TPU v7x, 32 devices: a whole 2x2x4 slice. The times are simulated.
32 devices in a mesh: mx: 8 (over z, core), my: 2 (over y), vz: 2 (over x).
Axes of the slice: x: 2, y: 2, z: 4, core: 2. Of those that a mesh axis runs over, the one named last changes fastest.
Arguments:
- viscosity: float32 [16, 128, 256], P('vz', 'mx', 'my'), may hold values from 0.1 to 2.5
- friction: float32 [128, 256], P('mx', 'my'), may hold values from 0.3 to 3
- base_velocity: float32 [2, 128, 256], P(None, 'mx', 'my'), may hold values from -6 to 6
- grounded: int32 [128, 256], P('mx', 'my'), may hold values 0 or 1
- ice_free: int32 [128, 256], P('mx', 'my'), may hold values 0 or 1
- direction: float32 [128, 256], P('mx', 'my'), may hold values from -6 to 6
Outputs:
- hess_action: float32 [128, 256], P('mx', 'my')
- velocity_step: float32 [2, 16, 128, 256], P(None, 'vz', 'mx', 'my')
All inputs are finite; a program needn't handle non-finite values. No bound on the sum of `grounded` or of `ice_free` on one device may be relied on, other than what follows from the above.
Results may differ from a plain program's by a relative error of at most 0.00002.
Values sent between devices are 32-bit elements; how exact they have to be, the bound alone decides.
No kernel may reach another device: no remote copies, remote signals or barrier semaphores. Data moves between devices by JAX's collectives and lax.ppermute only.
A program may use at most 64 MiB of HBM per device.

v0:
```python
import jax
import jax.numpy as jnp
from jax import lax
from jax.sharding import PartitionSpec as P

LAYERS = 16
STEPS = 16
SWEEPS = 2


weight_z = 128.0
shift_mass = 0.05
theta_center = 1.05
delta_half = 0.95
obs_weight = 200.0
reg_weight = 0.5


def padded(block, sides, width):
    for axis, dim in sides:
        count = lax.axis_size(axis)
        forward = [(i, i + 1) for i in range(count - 1)]
        backward = [(target, source) for source, target in forward]
        low = lax.ppermute(
            lax.slice_in_dim(block, block.shape[dim] - width, None, axis=dim), axis, forward
        )
        high = lax.ppermute(lax.slice_in_dim(block, 0, width, axis=dim), axis, backward)
        block = jnp.concatenate([low, block, high], axis=dim)
    return block


def harmonic(left, right):
    return 2.0 * left * right / (left + right)


def coefficients(padded_eta):
    core = padded_eta[1:-1, 1:-1, 1:-1]
    coefs = (
        weight_z * harmonic(core, padded_eta[:-2, 1:-1, 1:-1]),
        weight_z * harmonic(core, padded_eta[2:, 1:-1, 1:-1]),
        harmonic(core, padded_eta[1:-1, :-2, 1:-1]),
        harmonic(core, padded_eta[1:-1, 2:, 1:-1]),
        harmonic(core, padded_eta[1:-1, 1:-1, :-2]),
        harmonic(core, padded_eta[1:-1, 1:-1, 2:]),
    )
    return (core, coefs)


def stencil(pad, coefs, diag, masked, act, field):
    beside_all = coefs[0] * pad[:, :-2, 1:-1, 1:-1] + coefs[1] * pad[:, 2:, 1:-1, 1:-1]
    beside_all = beside_all + coefs[2] * pad[:, 1:-1, :-2, 1:-1] + coefs[3] * pad[:, 1:-1, 2:, 1:-1]
    beside_all = beside_all + coefs[4] * pad[:, 1:-1, 1:-1, :-2] + coefs[5] * pad[:, 1:-1, 1:-1, 2:]
    return act * (diag * masked - beside_all) + (1.0 - act) * field


def operate_split(field, coefs, diag, act):
    masked = field * act
    pad = padded(masked, (("mx", 2), ("my", 3), ("vz", 1)), 1)
    return stencil(pad, coefs, diag, masked, act, field)


def chebyshev(rhs, operate, jacobi):
    sigma = theta_center / delta_half
    rho = 1.0 / sigma
    keep_list = []
    push_list = []
    for inner in range(STEPS - 1):
        rho_new = 1.0 / (2.0 * sigma - rho)
        keep_list.append(rho_new * rho)
        push_list.append(2.0 * rho_new / delta_half)
        rho = rho_new
    keep_table = jnp.array(keep_list, jnp.float32)
    push_table = jnp.array(push_list, jnp.float32)

    def inner_step(position, state_pair):
        iterate, step_dir = state_pair
        iterate = iterate + step_dir
        resid = rhs - operate(iterate)
        step_dir = keep_table[position] * step_dir + push_table[position] * (jacobi * resid)
        return (iterate, step_dir)

    iterate = jnp.zeros_like(rhs)
    for sweep in range(SWEEPS):
        resid = rhs if sweep == 0 else rhs - operate(iterate)
        step_dir = jacobi * resid / theta_center
        iterate, step_dir = lax.fori_loop(0, STEPS - 1, inner_step, (iterate, step_dir))
        iterate = iterate + step_dir
    return iterate


def local(viscosity, friction, base_velocity, grounded, ice_free, direction):
    act = (1 - ice_free).astype(jnp.float32)
    ground = grounded.astype(jnp.float32)
    layer_index = lax.axis_index("vz")
    column_devices = lax.axis_size("vz")
    bed_coef = ground * friction
    padded_eta = padded(viscosity, (("mx", 1), ("my", 2), ("vz", 0)), 1)
    on_bed = jnp.where(layer_index == 0, 1.0, 0.0).astype(jnp.float32)
    core, coefs = coefficients(padded_eta)
    basal = jnp.zeros_like(core).at[0].set(on_bed * bed_coef)
    diag = (
        coefs[0] + coefs[1] + coefs[2] + coefs[3] + coefs[4] + coefs[5] + shift_mass * core + basal
    )
    jacobi = 1.0 / (act * diag + 1.0 - act)
    forcing = jnp.zeros((2,) + core.shape, jnp.float32)
    forcing = forcing.at[:, 0].set(-(on_bed * bed_coef * direction)[None] * base_velocity)
    forcing = forcing * act
    pad_dir = padded(direction, (("mx", 0), ("my", 1)), 1)
    lap = (
        4.0 * direction
        - pad_dir[:-2, 1:-1]
        - pad_dir[2:, 1:-1]
        - pad_dir[1:-1, :-2]
        - pad_dir[1:-1, 2:]
    )

    def operate(field):
        return operate_split(field, coefs, diag, act)

    velocity_step = chebyshev(forcing, operate, jacobi)
    column = lax.psum(jnp.sum(velocity_step, axis=1), "vz") / LAYERS
    adjoint_rhs = obs_weight * act * jnp.broadcast_to(column[:, None], velocity_step.shape)
    adjoint = chebyshev(adjoint_rhs, operate, jacobi)
    on_top = jnp.where(layer_index == column_devices - 1, 1.0, 0.0).astype(jnp.float32)
    bed_part = on_bed * bed_coef * jnp.sum(base_velocity * adjoint[:, 0], axis=0)
    own_part = on_top * (reg_weight * lap) - bed_part
    hess_action = lax.psum(own_part, "vz")
    return (hess_action, velocity_step)


def solution(mesh):
    return jax.shard_map(
        local,
        mesh=mesh,
        in_specs=(
            P("vz", "mx", "my"),
            P("mx", "my"),
            P(None, "mx", "my"),
            P("mx", "my"),
            P("mx", "my"),
            P("mx", "my"),
        ),
        out_specs=(P("mx", "my"), P(None, "vz", "mx", "my")),
        check_vma=False,
    )
```

profile of v0, /device:TPU:1, one launch (start us, length us, event | category | flops | bytes accessed | tf_op | source)
XLA Modules:
  0.0 1636.9 jit_solution(17196852787620336504)
XLA Ops:
  29.9 381.7 %while.71 = (s32[]{:T(128)}, f32[2,8,16,128]{3,2,1,0:T(8,128)S(1)}, f32[2,8,16,128]{3,2,1,0:T(8,128)S(1)}, f32[8,16,128]{2,1,0:T(8,128)S(1)}, f32[16,128]{1,0:T(...) while((s32[]{:T(128)}, f32[2,8,16,128]{3,2,1,0:T(8,128)S(1)}, ...), condition=%wide.region_1.2_spmd.clone.clone, body=%wide.region_0.1_spmd.sunk.clone.clone.sunk | while | flops 1489475 | bytes 2545463 | solution.py:86
  82.5 6.4 collective-permute-start.13
  159.0 6.2 collective-permute-start.13
  184.4 6.2 collective-permute-start.13
  209.9 6.2 collective-permute-start.13
  235.4 6.2 collective-permute-start.13
  311.8 6.2 collective-permute-start.13
  337.2 6.2 collective-permute-start.13
  362.7 6.2 collective-permute-start.13
  388.2 6.2 collective-permute-start.13
  411.7 6.2 collective-permute-start.34
  444.4 380.5 %while.69 = (s32[]{:T(128)}, f32[2,8,16,128]{3,2,1,0:T(8,128)S(1)}, f32[2,8,16,128]{3,2,1,0:T(8,128)S(1)}, f32[8,16,128]{2,1,0:T(8,128)S(1)}, f32[16,128]{1,0:T(...) while((s32[]{:T(128)}, f32[2,8,16,128]{3,2,1,0:T(8,128)S(1)}, ...), condition=%wide.region_3.4_spmd.clone, body=%wide.region_2.3_spmd.sunk.clone.sunk | while | flops 1456706 | bytes 2545445 | solution.py:86
  496.4 6.3 collective-permute-start.1
  521.8 6.3 collective-permute-start.1
  547.2 6.3 collective-permute-start.1
  572.6 6.3 collective-permute-start.1
  598.1 6.3 collective-permute-start.1
  623.5 6.3 collective-permute-start.1
  648.9 6.3 collective-permute-start.1
  674.3 6.3 collective-permute-start.1
  699.8 6.3 collective-permute-start.1
  725.2 6.3 collective-permute-start.1
  750.6 6.3 collective-permute-start.1
  776.0 6.3 collective-permute-start.1
  801.5 6.3 collective-permute-start.1
  825.5 6.9 psum.14
  832.5 383.4 %while.72 = (s32[]{:T(128)}, f32[2,8,16,128]{3,2,1,0:T(8,128)S(1)}, f32[2,8,16,128]{3,2,1,0:T(8,128)S(1)}, f32[8,16,128]{2,1,0:T(8,128)S(1)}, f32[16,128]{1,0:T(...) while((s32[]{:T(128)}, f32[2,8,16,128]{3,2,1,0:T(8,128)S(1)}, ...), condition=%wide.region_7.8_spmd.clone.clone, body=%wide.region_6.7_spmd.sunk.clone.clone.sunk | while | flops 1522243 | bytes 2438975 | solution.py:86
  834.9 8.0 collective-permute-start.19
  862.0 6.3 collective-permute-start.19
  887.4 6.3 collective-permute-start.19
  912.8 6.3 collective-permute-start.19
  938.3 6.3 collective-permute-start.19
  963.7 6.3 collective-permute-start.19
  989.1 6.3 collective-permute-start.19
  1014.5 6.3 collective-permute-start.19
  1040.0 6.3 collective-permute-start.19
  1065.4 6.3 collective-permute-start.19
  1090.8 6.3 collective-permute-start.19
  1116.2 6.3 collective-permute-start.19
  1141.7 6.3 collective-permute-start.19
  1167.1 6.3 collective-permute-start.19
  1192.5 6.3 collective-permute-start.19
  1216.0 6.3 collective-permute-start.40
  1251.3 380.9 %while.70 = (s32[]{:T(128)}, f32[2,8,16,128]{3,2,1,0:T(8,128)S(1)}, f32[2,8,16,128]{3,2,1,0:T(8,128)S(1)}, f32[8,16,128]{2,1,0:T(8,128)S(1)}, f32[16,128]{1,0:T(...) while((s32[]{:T(128)}, f32[2,8,16,128]{3,2,1,0:T(8,128)S(1)}, ...), condition=%wide.region_9.10_spmd.clone.clone, body=%wide.region_8.9_spmd.sunk.clone.clone.sunk | while | flops 1489474 | bytes 2438957 | solution.py:86
  1328.6 6.2 collective-permute-start.7
  1379.5 6.2 collective-permute-start.7
  1430.5 6.2 collective-permute-start.7
  1481.4 6.2 collective-permute-start.7
  (1313 shorter events, 1350.9 us)
Async XLA Ops:
  80.5 8.3 collective-permute-start.12
  106.1 8.2 collective-permute-start.12
  131.6 8.2 collective-permute-start.12
  157.0 8.2 collective-permute-start.12
  182.5 8.2 collective-permute-start.12
  208.0 8.2 collective-permute-start.12
  233.4 8.2 collective-permute-start.12
  258.9 8.2 collective-permute-start.12
  284.4 8.2 collective-permute-start.12
  309.8 8.2 collective-permute-start.12
  335.3 8.2 collective-permute-start.12
  360.8 8.2 collective-permute-start.12
  386.2 8.2 collective-permute-start.12
  411.7 8.2 collective-permute-start.34
  494.4 8.2 collective-permute-start
  519.9 8.2 collective-permute-start
  545.3 8.2 collective-permute-start
  570.7 8.2 collective-permute-start
  596.1 8.2 collective-permute-start
  621.5 8.2 collective-permute-start
  647.0 8.2 collective-permute-start
  672.4 8.2 collective-permute-start
  697.8 8.2 collective-permute-start
  723.2 8.2 collective-permute-start
  748.7 8.2 collective-permute-start
  774.1 8.2 collective-permute-start
  799.5 8.2 collective-permute-start
  832.6 10.3 collective-permute-start.18
  834.9 8.8 collective-permute-start.19
  860.1 8.2 collective-permute-start.18
  885.5 8.2 collective-permute-start.18
  910.9 8.2 collective-permute-start.18
  936.3 8.2 collective-permute-start.18
  961.8 8.2 collective-permute-start.18
  987.2 8.2 collective-permute-start.18
  1012.6 8.2 collective-permute-start.18
  1038.0 8.2 collective-permute-start.18
  1063.5 8.2 collective-permute-start.18
  1088.9 8.2 collective-permute-start.18
  1114.3 8.2 collective-permute-start.18
  1139.7 8.2 collective-permute-start.18
  1165.1 8.2 collective-permute-start.18
  1190.6 8.2 collective-permute-start.18
  1216.0 13.8 collective-permute-start.40
  1224.2 11.2 collective-permute-start.24
  1247.0 385.2 %collective-permute-start.26 = (f32[18,1]{1,0:T(8,128)S(1)}, f32[18,1]{1,0:T(8,128)S(1)}, u32[]{:S(2)}, u32[]{:S(2)}) collective-permute-start(f32[18,1]{1,0:T(8,128)S(1)} %get-tuple-element.1488), channel_id=1, source_target_pairs={{0,2},{1,3},{4,6},{5,7},{8,10},{9,11},{12,14},{13,15},{16,18},{17,... | collective-permute-start | bytes 224 | tf_op jit(solution)/shard_map/ppermute | solution.py:24
  1248.4 383.7 %collective-permute-start.27 = (f32[18,1]{1,0:T(8,128)S(1)}, f32[18,1]{1,0:T(8,128)S(1)}, u32[]{:S(2)}, u32[]{:S(2)}) collective-permute-start(f32[18,1]{1,0:T(8,128)S(1)} %get-tuple-element.1489), channel_id=1, source_target_pairs={{2,0},{3,1},{6,4},{7,5},{10,8},{11,9},{14,12},{15,13},{18,16},{19,... | collective-permute-start | bytes 224 | tf_op jit(solution)/shard_map/ppermute | solution.py:27
  1326.7 8.2 collective-permute-start.6
  (342 other events, 2185.0 us)
where the time goes:
time: 1650 us; the launch traced here: 1640 us
  starting transfers between devices  1190 us (72%)
  waiting for transfers between devices  234 us (14%)
  other arithmetic  109 us (7%)
  local copies, waits for them, and re-layouts  83.4 us (5%)
    ppermute x191, starting transfers between devices, padded(): lax.ppermute(lax.slice_in_dim(block, block.shape[dim] - width, None, axis...  901 us
    ppermute x191, starting transfers between devices, padded(): lax.ppermute(lax.slice_in_dim(block, 0, width, axis=dim), axis, backward)  290 us
    ppermute x191, waiting for transfers between devices, padded(): lax.ppermute(lax.slice_in_dim(block, block.shape[dim] - width, None, axis...  140 us
    ppermute x191, waiting for transfers between devices, padded(): lax.ppermute(lax.slice_in_dim(block, 0, width, axis=dim), axis, backward)  93.9 us
    add x60, other arithmetic, inner_step(): keep_table[position] * step_dir + push_table[position] * (jacobi * resid)  92.4 us
    dynamic_slice x60, local copies, waits for them, and re-layouts, inner_step(): push_table[position] * (jacobi * resid)  37.5 us
    dynamic_slice x60, local copies, waits for them, and re-layouts, inner_step(): keep_table[position] * step_dir + push_table[position] * (jacobi * resid)  35.9 us
  transfers between devices with their start and end apart: 382, of which 193 were waited for; matrix products, arithmetic and copies ran while one was open for 6% of the time, Pallas kernels for 0%

commit v1 on v0

--- a/solution.py
+++ b/solution.py
@@ -6,7 +6,7 @@
 LAYERS = 16
 STEPS = 16
 SWEEPS = 2
-
+HALO = 16
 
 weight_z = 128.0
 shift_mass = 0.05
@@ -14,6 +14,158 @@
 delta_half = 0.95
 obs_weight = 200.0
 reg_weight = 0.5
+
+
+def step_constants():
+    sigma = theta_center / delta_half
+    table = []
+    for sweep in range(SWEEPS):
+        rho = 1.0 / sigma
+        if sweep > 0:
+            table.append((None, 1.0 / theta_center))
+        for inner in range(STEPS - 1):
+            rho_new = 1.0 / (2.0 * sigma - rho)
+            table.append((rho_new * rho, 2.0 * rho_new / delta_half))
+            rho = rho_new
+    return table
+
+
+def harmonic(left, right):
+    total = left + right
+    safe = jnp.where(total > 0, total, 1.0)
+    return jnp.where(total > 0, 2.0 * left * right / safe, 0.0)
+
+
+def exchange_rows(ext, k, rows, axis):
+    count = lax.axis_size("mx")
+    forward = [(i, i + 1) for i in range(count - 1)]
+    backward = [(i + 1, i) for i in range(count - 1)]
+    own = lax.slice_in_dim(ext, k, k + rows, axis=axis)
+    low = lax.ppermute(lax.slice_in_dim(own, rows - k, rows, axis=axis), "mx", forward)
+    high = lax.ppermute(lax.slice_in_dim(own, 0, k, axis=axis), "mx", backward)
+    return jnp.concatenate([low, own, high], axis=axis)
+
+
+def shift(a, axis, offset):
+    n = a.shape[axis]
+    zeros_shape = list(a.shape)
+    zeros_shape[axis] = 1
+    z = jnp.zeros(zeros_shape, a.dtype)
+    if offset > 0:
+        return jnp.concatenate([lax.slice_in_dim(a, 1, n, axis=axis), z], axis=axis)
+    return jnp.concatenate([z, lax.slice_in_dim(a, 0, n - 1, axis=axis)], axis=axis)
+
+
+def local(viscosity, friction, base_velocity, grounded, ice_free, direction):
+    layers_own, rows, cols_own = viscosity.shape
+    if cols_own * lax.axis_size("my") > 256:
+        return local_split(viscosity, friction, base_velocity, grounded, ice_free, direction)
+    k = min(HALO, rows)
+    act = (1 - ice_free).astype(jnp.float32)
+    bed_coef = grounded.astype(jnp.float32) * friction
+    planes = jnp.stack([act, bed_coef, base_velocity[0], base_velocity[1], direction])
+    planes = lax.all_gather(planes, "my", axis=2, tiled=True)
+    eta = lax.all_gather(viscosity, "my", axis=2, tiled=True)
+    eta = lax.all_gather(eta, "vz", axis=0, tiled=True)
+    layers = eta.shape[0]
+    joined = jnp.concatenate([eta, planes], axis=0)
+    zeros_halo = jnp.zeros(joined.shape[:1] + (k,) + joined.shape[2:], joined.dtype)
+    joined = exchange_rows(jnp.concatenate([zeros_halo, joined, zeros_halo], axis=1), k, rows, 1)
+    eta = joined[:layers]
+    act, bed_coef, bv0, bv1, dir_ext = (joined[layers + i] for i in range(5))
+    bv = jnp.stack([bv0, bv1])
+
+    c_zm = weight_z * harmonic(eta, shift(eta, 0, -1))
+    c_zp = weight_z * harmonic(eta, shift(eta, 0, 1))
+    c_xm = harmonic(eta, shift(eta, 1, -1))
+    c_xp = harmonic(eta, shift(eta, 1, 1))
+    c_ym = harmonic(eta, shift(eta, 2, -1))
+    c_yp = harmonic(eta, shift(eta, 2, 1))
+    basal = jnp.zeros_like(eta).at[0].set(bed_coef)
+    diag = c_zm + c_zp + c_xm + c_xp + c_ym + c_yp + shift_mass * eta + basal
+    jacobi = 1.0 / (act * diag + 1.0 - act)
+
+    def operate(field):
+        masked = field * act
+        beside_all = c_zm * shift(masked, 1, -1) + c_zp * shift(masked, 1, 1)
+        beside_all = beside_all + c_xm * shift(masked, 2, -1) + c_xp * shift(masked, 2, 1)
+        beside_all = beside_all + c_ym * shift(masked, 3, -1) + c_yp * shift(masked, 3, 1)
+        return act * (diag * masked - beside_all) + (1.0 - act) * field
+
+    table = step_constants()
+    keep_table = jnp.array([0.0 if kp is None else kp for kp, _ in table], jnp.float32)
+    push_table = jnp.array([ps for _, ps in table], jnp.float32)
+
+    def normal_step(position, state_pair, rhs):
+        iterate, step_dir = state_pair
+        iterate = iterate + step_dir
+        resid = rhs - operate(iterate)
+        step_dir = keep_table[position] * step_dir + push_table[position] * (jacobi * resid)
+        return (iterate, step_dir)
+
+    def chebyshev(rhs):
+        iterate = jnp.zeros_like(rhs)
+        step_dir = jacobi * rhs / theta_center
+        since = 1
+        run = []
+
+        def flush(state_pair):
+            if len(run) == 1:
+                return normal_step(run[0], state_pair, rhs)
+            if run:
+                return lax.fori_loop(
+                    run[0], run[-1] + 1, lambda i, sp: normal_step(i, sp, rhs), state_pair
+                )
+            return state_pair
+
+        for position, (keep, push) in enumerate(table):
+            if since == k:
+                iterate, step_dir = flush((iterate, step_dir))
+                run = []
+                both = exchange_rows(jnp.stack([iterate, step_dir]), k, rows, 3)
+                iterate, step_dir = both[0], both[1]
+                since = 0
+            if keep is None:
+                iterate, step_dir = flush((iterate, step_dir))
+                run = []
+                iterate = iterate + step_dir
+                resid = rhs - operate(iterate)
+                step_dir = jacobi * resid / theta_center
+            else:
+                run.append(position)
+            since += 1
+        iterate, step_dir = flush((iterate, step_dir))
+        return iterate + step_dir
+
+    forcing = jnp.zeros((2,) + eta.shape, jnp.float32)
+    forcing = forcing.at[:, 0].set(-(bed_coef * dir_ext)[None] * bv)
+    forcing = forcing * act
+    velocity_ext = chebyshev(forcing)
+    column = jnp.sum(velocity_ext, axis=1) / layers
+    column = exchange_rows(column, k, rows, 1)
+    adjoint_rhs = obs_weight * act * jnp.broadcast_to(column[:, None], velocity_ext.shape)
+    adjoint = chebyshev(adjoint_rhs)
+
+    bed_term = bed_coef * jnp.sum(bv * adjoint[:, 0], axis=0)
+    lap = (
+        4.0 * dir_ext
+        - shift(dir_ext, 0, -1)
+        - shift(dir_ext, 0, 1)
+        - shift(dir_ext, 1, -1)
+        - shift(dir_ext, 1, 1)
+    )
+    hess_ext = -bed_term + reg_weight * lap
+    col0 = lax.axis_index("my") * cols_own
+    layer0 = lax.axis_index("vz") * layers_own
+    hess_action = lax.dynamic_slice(hess_ext, (k, col0), (rows, cols_own))
+    velocity_step = lax.dynamic_slice(
+        velocity_ext, (0, layer0, k, col0), (2, layers_own, rows, cols_own)
+    )
+    return (hess_action, velocity_step)
+
+
+def plain_harmonic(left, right):
+    return 2.0 * left * right / (left + right)
 
 
 def padded(block, sides, width):
@@ -29,19 +181,15 @@
     return block
 
 
-def harmonic(left, right):
-    return 2.0 * left * right / (left + right)
-
-
 def coefficients(padded_eta):
     core = padded_eta[1:-1, 1:-1, 1:-1]
     coefs = (
-        weight_z * harmonic(core, padded_eta[:-2, 1:-1, 1:-1]),
-        weight_z * harmonic(core, padded_eta[2:, 1:-1, 1:-1]),
-        harmonic(core, padded_eta[1:-1, :-2, 1:-1]),
-        harmonic(core, padded_eta[1:-1, 2:, 1:-1]),
-        harmonic(core, padded_eta[1:-1, 1:-1, :-2]),
-        harmonic(core, padded_eta[1:-1, 1:-1, 2:]),
+        weight_z * plain_harmonic(core, padded_eta[:-2, 1:-1, 1:-1]),
+        weight_z * plain_harmonic(core, padded_eta[2:, 1:-1, 1:-1]),
+        plain_harmonic(core, padded_eta[1:-1, :-2, 1:-1]),
+        plain_harmonic(core, padded_eta[1:-1, 2:, 1:-1]),
+        plain_harmonic(core, padded_eta[1:-1, 1:-1, :-2]),
+        plain_harmonic(core, padded_eta[1:-1, 1:-1, 2:]),
     )
     return (core, coefs)
 
@@ -59,7 +207,7 @@
     return stencil(pad, coefs, diag, masked, act, field)
 
 
-def chebyshev(rhs, operate, jacobi):
+def chebyshev_split(rhs, operate, jacobi):
     sigma = theta_center / delta_half
     rho = 1.0 / sigma
     keep_list = []
@@ -88,7 +236,7 @@
     return iterate
 
 
-def local(viscosity, friction, base_velocity, grounded, ice_free, direction):
+def local_split(viscosity, friction, base_velocity, grounded, ice_free, direction):
     act = (1 - ice_free).astype(jnp.float32)
     ground = grounded.astype(jnp.float32)
     layer_index = lax.axis_index("vz")
@@ -117,10 +265,10 @@
     def operate(field):
         return operate_split(field, coefs, diag, act)
 
-    velocity_step = chebyshev(forcing, operate, jacobi)
+    velocity_step = chebyshev_split(forcing, operate, jacobi)
     column = lax.psum(jnp.sum(velocity_step, axis=1), "vz") / LAYERS
     adjoint_rhs = obs_weight * act * jnp.broadcast_to(column[:, None], velocity_step.shape)
-    adjoint = chebyshev(adjoint_rhs, operate, jacobi)
+    adjoint = chebyshev_split(adjoint_rhs, operate, jacobi)
     on_top = jnp.where(layer_index == column_devices - 1, 1.0, 0.0).astype(jnp.float32)
     bed_part = on_bed * bed_coef * jnp.sum(base_velocity * adjoint[:, 0], axis=0)
     own_part = on_top * (reg_weight * lap) - bed_part

time: 1650 us -> 917 us (0.56)
  starting transfers between devices: 1190 us -> 24.6 us
  other arithmetic: 109 us -> 580 us
  waiting for transfers between devices: 234 us -> 31.9 us
  local copies, waits for them, and re-layouts: 83.4 us -> 257 us
    ppermute x382 -> x8, starting transfers between devices: 1190 us -> 24.6 us  [the longest x4 13.1 us: exchange_rows(): lax.ppermute(lax.slice_in_dim(own, rows - k, rows, axis=axis), 'mx', forw...]
    add x62 -> x63, other arithmetic: 92.6 us -> 361 us  [the longest x60 357 us: normal_step(): keep_table[position] * step_dir + push_table[position] * (jacobi * resid)]
    ppermute x382 -> x8, waiting for transfers between devices: 234 us -> 31.9 us  [the longest x4 16 us: exchange_rows(): high = lax.ppermute(lax.slice_in_dim(own, 0, k, axis=axis), 'mx', backward)]
    mul x63 -> x64, other arithmetic: 4.17 us -> 197 us  [the longest x62 197 us: operate(): masked = field * act]
    while x0 -> x662, local copies, waits for them, and re-layouts: none -> 83.9 us
    slice x128 -> x190, local copies, waits for them, and re-layouts: 8.59 us -> 81.8 us  [the longest x187 80.7 us: shift(): lax.slice_in_dim(a, 0, n - 1, axis=axis)]
    dynamic_slice x120 -> x121, local copies, waits for them, and re-layouts: 73.4 us -> 77.3 us  [the longest x60 38.2 us: normal_step(): keep_table[position] * step_dir + push_table[position] * (jacobi * resid)]
  transfers between devices with their start and end apart: 382 -> 8, of which waited for: 193 -> 7; matrix products, arithmetic and copies ran while one was open for 6% -> 0% of each run, Pallas kernels for 0% -> 0%
where the time goes in v1:
time: 917 us; the launch traced here: 913 us
  other arithmetic  580 us (63%)
  local copies, waits for them, and re-layouts  257 us (28%)
  waiting for transfers between devices  31.9 us (3%)
  starting transfers between devices  24.6 us (3%)
  blocking collectives  12.7 us (1%)
    add x60, other arithmetic, normal_step(): keep_table[position] * step_dir + push_table[position] * (jacobi * resid)  357 us
    mul x62, other arithmetic, operate(): masked = field * act  197 us
    while x660, local copies, waits for them, and re-layouts  82.1 us
    slice x187, local copies, waits for them, and re-layouts, shift(): lax.slice_in_dim(a, 0, n - 1, axis=axis)  80.7 us
    dynamic_slice x60, local copies, waits for them, and re-layouts, normal_step(): keep_table[position] * step_dir + push_table[position] * (jacobi * resid)  38.2 us
    dynamic_slice x60, local copies, waits for them, and re-layouts, normal_step(): push_table[position] * (jacobi * resid)  37.5 us
  transfers between devices with their start and end apart: 8, of which 7 were waited for; matrix products, arithmetic and copies ran while one was open for 0% of the time, Pallas kernels for 0%

profile of v1, /device:TPU:1, one launch (start us, length us, event | category | flops | bytes accessed | tf_op | source)
XLA Modules:
  0.0 912.6 jit_solution(6068462144976788309)
XLA Ops:
  15.5 7.4 collective-permute-start
  39.6 192.4 %while.75 = (s32[]{:T(128)}, f32[2,16,48,256]{3,2,1,0:T(8,128)}, f32[2,16,48,256]{3,2,1,0:T(8,128)}, f32[16,48,256]{2,1,0:T(8,128)S(1)}, f32[1,48,256]{2,1,0:T(8...) while((s32[]{:T(128)}, f32[2,16,48,256]{3,2,1,0:T(8,128)}, ...), condition=%wide.region_1.2_spmd.clone.clone, body=%wide.region_0.1_spmd.sunk.clone.clone.sunk | while | flops 9842691 | bytes 71774584 | solution.py:116
  45.9 6.0 multiply_add_fusion.6
  58.8 6.0 multiply_add_fusion.6
  71.6 6.0 multiply_add_fusion.6
  84.5 6.0 multiply_add_fusion.6
  97.3 6.0 multiply_add_fusion.6
  110.2 6.0 multiply_add_fusion.6
  123.1 6.0 multiply_add_fusion.6
  135.9 6.0 multiply_add_fusion.6
  148.8 6.0 multiply_add_fusion.6
  161.6 6.0 multiply_add_fusion.6
  174.5 6.0 multiply_add_fusion.6
  187.3 6.0 multiply_add_fusion.6
  200.2 6.0 multiply_add_fusion.6
  213.1 6.0 multiply_add_fusion.6
  225.9 6.0 multiply_add_fusion.6
  240.7 8.4 collective-permute-done.2
  264.2 212.0 %while.73 = (s32[]{:T(128)}, f32[2,16,48,256]{3,2,1,0:T(8,128)}, f32[2,16,48,256]{3,2,1,0:T(8,128)}, f32[16,48,256]{2,1,0:T(8,128)S(1)}, f32[1,48,256]{2,1,0:T(8...) while((s32[]{:T(128)}, f32[2,16,48,256]{3,2,1,0:T(8,128)}, ...), condition=%wide.region_3.4_spmd.clone, body=%wide.region_2.3_spmd.sunk.clone.sunk | while | flops 9449478 | bytes 71774632 | solution.py:116
  272.2 6.0 multiply_add_fusion.5
  286.4 6.0 multiply_add_fusion.5
  300.5 6.0 multiply_add_fusion.5
  314.6 6.0 multiply_add_fusion.5
  328.8 6.0 multiply_add_fusion.5
  342.9 6.0 multiply_add_fusion.5
  357.0 6.0 multiply_add_fusion.5
  371.2 6.0 multiply_add_fusion.5
  385.3 6.0 multiply_add_fusion.5
  399.4 6.0 multiply_add_fusion.5
  413.5 6.0 multiply_add_fusion.5
  427.7 6.0 multiply_add_fusion.5
  441.8 6.0 multiply_add_fusion.5
  455.9 6.0 multiply_add_fusion.5
  470.1 6.0 multiply_add_fusion.5
  488.1 187.0 %while.76 = (s32[]{:T(128)}, f32[2,16,48,256]{3,2,1,0:T(8,128)}, f32[2,16,48,256]{3,2,1,0:T(8,128)}, f32[16,48,256]{2,1,0:T(8,128)S(1)}, f32[1,48,256]{2,1,0:T(8...) while((s32[]{:T(128)}, f32[2,16,48,256]{3,2,1,0:T(8,128)}, ...), condition=%wide.region_6.7_spmd.clone.clone, body=%wide.region_5.6_spmd.sunk.clone.clone.sunk | while | flops 10235907 | bytes 64057700 | solution.py:116
  494.2 5.9 fusion.90
  506.7 5.9 fusion.90
  519.2 5.9 fusion.90
  531.7 5.9 fusion.90
  544.2 5.9 fusion.90
  556.7 5.9 fusion.90
  569.2 5.9 fusion.90
  581.7 5.9 fusion.90
  594.2 5.9 fusion.90
  606.7 5.9 fusion.90
  619.2 5.9 fusion.90
  631.7 5.9 fusion.90
  707.1 203.0 %while.74 = (s32[]{:T(128)}, f32[2,16,48,256]{3,2,1,0:T(8,128)}, f32[2,16,48,256]{3,2,1,0:T(8,128)}, f32[16,48,256]{2,1,0:T(8,128)S(1)}, f32[1,48,256]{2,1,0:T(8...) while((s32[]{:T(128)}, f32[2,16,48,256]{3,2,1,0:T(8,128)}, ...), condition=%wide.region_8.9_spmd.clone.clone, body=%wide.region_7.8_spmd.sunk.clone.clone.sunk | while | flops 9842694 | bytes 64057748 | solution.py:116
  (1209 shorter events, 638.2 us)
Async XLA Ops:
  15.5 20.4 %copy-start.33 = (f32[21,16,256]{2,1,0:T(8,128)}, f32[21,16,256]{2,1,0:T(8,128)S(1)}, u32[]{:S(2)}) copy-start(f32[21,16,256]{2,1,0:T(8,128)S(1)} %constant_dynamic-update-slice_fusion) | copy-start | bytes 1032196
  15.5 11.6 %collective-permute-start = (f32[21,16,256]{2,1,0:T(8,128)S(1)}, f32[21,16,256]{2,1,0:T(8,128)S(1)}, u32[]{:S(2)}, u32[]{:S(2)}) collective-permute-start(f32[21,16,256]{2,1,0:T(8,128)S(1)} %constant_dynamic-update-slice_fusion), channel_id=1, source_target_pairs={{0,4},{4,8},{8,12},{12,16},{16,20},{20,24},{24,28},{1,5},{5,9},{9,... | collective-permute-start | bytes 1032200 | tf_op jit(solution)/shard_map/ppermute | solution.py:44
  22.9 8.6 collective-permute-start.1
  27.1 8.8 copy-start.34
  31.4 4.4 copy-start.35
  31.5 4.4 copy-start.31
  43.4 2.5 copy-start.28
  56.3 2.5 copy-start.28
  69.1 2.5 copy-start.28
  82.0 2.5 copy-start.28
  94.8 2.5 copy-start.28
  107.7 2.5 copy-start.28
  120.5 2.5 copy-start.28
  133.4 2.5 copy-start.28
  146.3 2.5 copy-start.28
  159.1 2.5 copy-start.28
  172.0 2.5 copy-start.28
  184.8 2.5 copy-start.28
  197.7 2.5 copy-start.28
  210.5 2.5 copy-start.28
  223.4 2.5 copy-start.28
  235.2 14.0 %collective-permute-start.2 = (f32[2,2,16,16,256]{4,3,1,2,0:T(8,128)}, f32[2,2,16,16,256]{4,3,1,2,0:T(8,128)}, u32[]{:S(2)}, u32[]{:S(2)}) collective-permute-start(f32[2,2,16,16,256]{4,3,1,2,0:T(8,128)} %pad_maximum_fusion.3), channel_id=1, source_target_pairs={{0,4},{4,8},{8,12},{12,16},{16,20},{20,24},{24,28},{1,5},{5,9},{9,... | collective-permute-start | bytes 3145736 | tf_op jit(solution)/shard_map/ppermute | solution.py:44
  237.2 16.4 %collective-permute-start.3 = (f32[2,2,16,16,256]{4,3,1,2,0:T(8,128)}, f32[2,2,16,16,256]{4,3,1,2,0:T(8,128)}, u32[]{:S(2)}, u32[]{:S(2)}) collective-permute-start(f32[2,2,16,16,256]{4,3,1,2,0:T(8,128)} %pad_maximum_fusion.3), channel_id=1, source_target_pairs={{4,0},{8,4},{12,8},{16,12},{20,16},{24,20},{28,24},{5,1},{9,5},{13... | collective-permute-start | bytes 3145736 | tf_op jit(solution)/shard_map/ppermute | solution.py:45
  257.4 2.4 copy-start.19
  269.7 2.5 copy-start.24
  283.9 2.5 copy-start.24
  298.0 2.5 copy-start.24
  312.1 2.5 copy-start.24
  326.3 2.5 copy-start.24
  340.4 2.5 copy-start.24
  354.5 2.5 copy-start.24
  368.6 2.5 copy-start.24
  382.8 2.5 copy-start.24
  396.9 2.5 copy-start.24
  411.0 2.5 copy-start.24
  425.2 2.5 copy-start.24
  439.3 2.5 copy-start.24
  453.4 2.5 copy-start.24
  467.6 2.5 copy-start.24
  476.1 10.5 %copy-start.32 = (f32[48,256]{1,0:T(8,128)S(1)}, f32[48,256]{1,0:T(8,128)}, u32[]{:S(2)}) copy-start(f32[48,256]{1,0:T(8,128)} %get-tuple-element.2535) | copy-start | bytes 147460
  479.4 4.3 collective-permute-start.4
  481.3 5.2 collective-permute-start.5
  677.1 7.5 copy-start.37
  678.2 14.0 %collective-permute-start.6 = (f32[2,2,16,16,256]{4,3,1,2,0:T(8,128)}, f32[2,2,16,16,256]{4,3,1,2,0:T(8,128)}, u32[]{:S(2)}, u32[]{:S(2)}) collective-permute-start(f32[2,2,16,16,256]{4,3,1,2,0:T(8,128)} %pad_maximum_fusion.2), channel_id=1, source_target_pairs={{0,4},{4,8},{8,12},{12,16},{16,20},{20,24},{24,28},{1,5},{5,9},{9,... | collective-permute-start | bytes 3145736 | tf_op jit(solution)/shard_map/ppermute | solution.py:44
  680.1 16.4 %collective-permute-start.7 = (f32[2,2,16,16,256]{4,3,1,2,0:T(8,128)}, f32[2,2,16,16,256]{4,3,1,2,0:T(8,128)}, u32[]{:S(2)}, u32[]{:S(2)}) collective-permute-start(f32[2,2,16,16,256]{4,3,1,2,0:T(8,128)} %pad_maximum_fusion.2), channel_id=1, source_target_pairs={{4,0},{8,4},{12,8},{16,12},{20,16},{24,20},{28,24},{5,1},{9,5},{13... | collective-permute-start | bytes 3145736 | tf_op jit(solution)/shard_map/ppermute | solution.py:45
  700.4 2.4 copy-start.22
  707.1 204.0 %copy-start.39 = (f32[48,255]{1,0:T(8,128)S(1)}, f32[48,255]{1,0:T(8,128)}, u32[]{:S(2)}) copy-start(f32[48,255]{1,0:T(8,128)} %get-tuple-element.1930) | copy-start | bytes 146884
  707.1 204.0 %copy-start.40 = (f32[48,255]{1,0:T(8,128)S(1)}, f32[48,255]{1,0:T(8,128)}, u32[]{:S(2)}) copy-start(f32[48,255]{1,0:T(8,128)} %get-tuple-element.1931) | copy-start | bytes 146884
  (311 other events, 541.5 us)

commit v2 on v1

--- a/solution.py
+++ b/solution.py
@@ -1,6 +1,8 @@
 import jax
 import jax.numpy as jnp
 from jax import lax
+from jax.experimental import pallas as pl
+from jax.experimental.pallas import tpu as pltpu
 from jax.sharding import PartitionSpec as P
 
 LAYERS = 16
@@ -54,6 +56,66 @@
     if offset > 0:
         return jnp.concatenate([lax.slice_in_dim(a, 1, n, axis=axis), z], axis=axis)
     return jnp.concatenate([z, lax.slice_in_dim(a, 0, n - 1, axis=axis)], axis=axis)
+
+
+def segment_kernel(steps, op_ref, act_ref, rhs_ref, x_in, d_in, x_ref, d_ref, m_ref):
+    comps, layers = rhs_ref.shape[0], rhs_ref.shape[1]
+    rows, cols = act_ref.shape
+    x_ref[...] = x_in[...]
+    d_ref[...] = d_in[...]
+    zero = jnp.zeros((rows, cols), jnp.float32)
+    for c in range(comps):
+        m_ref[c, 0] = zero
+        m_ref[c, layers + 1] = zero
+
+    for keep, push in steps:
+
+        def advance(layer, carry):
+            for c in range(comps):
+                moved = x_ref[c, layer] + d_ref[c, layer]
+                x_ref[c, layer] = moved
+                m_ref[c, layer + 1] = moved * act_ref[...]
+            return carry
+
+        lax.fori_loop(0, layers, advance, 0)
+
+        def update(layer, carry):
+            act = act_ref[...]
+            for c in range(comps):
+                centre = m_ref[c, layer + 1]
+                beside = op_ref[0, layer] * m_ref[c, layer] + op_ref[1, layer] * m_ref[c, layer + 2]
+                beside = beside + op_ref[2, layer] * pltpu.roll(centre, 1, 0)
+                beside = beside + op_ref[3, layer] * pltpu.roll(centre, rows - 1, 0)
+                beside = beside + op_ref[4, layer] * pltpu.roll(centre, 1, 1)
+                beside = beside + op_ref[5, layer] * pltpu.roll(centre, cols - 1, 1)
+                applied = act * (op_ref[6, layer] * centre - beside) + (1.0 - act) * x_ref[c, layer]
+                resid = rhs_ref[c, layer] - applied
+                if keep is None:
+                    d_ref[c, layer] = op_ref[7, layer] * resid / theta_center
+                else:
+                    d_ref[c, layer] = keep * d_ref[c, layer] + push * (op_ref[7, layer] * resid)
+            return carry
+
+        lax.fori_loop(0, layers, update, 0)
+
+
+def run_segment(steps, op_stack, act, rhs, iterate, step_dir):
+    comps, layers, rows, cols = rhs.shape
+    vmem = pl.BlockSpec(memory_space=pltpu.VMEM)
+    cells = comps * layers * rows * cols
+    return pl.pallas_call(
+        lambda *refs: segment_kernel(steps, *refs),
+        out_shape=(
+            jax.ShapeDtypeStruct(rhs.shape, jnp.float32),
+            jax.ShapeDtypeStruct(rhs.shape, jnp.float32),
+        ),
+        in_specs=[vmem] * 5,
+        out_specs=(vmem, vmem),
+        scratch_shapes=[pltpu.VMEM((comps, layers + 2, rows, cols), jnp.float32)],
+        cost_estimate=pl.CostEstimate(
+            flops=30 * cells * len(steps), bytes_accessed=4 * cells * 9, transcendentals=0
+        ),
+    )(op_stack, act, rhs, iterate, step_dir)
 
 
 def local(viscosity, friction, base_velocity, grounded, ice_free, direction):
@@ -85,56 +147,24 @@
     diag = c_zm + c_zp + c_xm + c_xp + c_ym + c_yp + shift_mass * eta + basal
     jacobi = 1.0 / (act * diag + 1.0 - act)
 
-    def operate(field):
-        masked = field * act
-        beside_all = c_zm * shift(masked, 1, -1) + c_zp * shift(masked, 1, 1)
-        beside_all = beside_all + c_xm * shift(masked, 2, -1) + c_xp * shift(masked, 2, 1)
-        beside_all = beside_all + c_ym * shift(masked, 3, -1) + c_yp * shift(masked, 3, 1)
-        return act * (diag * masked - beside_all) + (1.0 - act) * field
-
+    op_stack = jnp.stack([c_zm, c_zp, c_xm, c_xp, c_ym, c_yp, diag, jacobi])
     table = step_constants()
-    keep_table = jnp.array([0.0 if kp is None else kp for kp, _ in table], jnp.float32)
-    push_table = jnp.array([ps for _, ps in table], jnp.float32)
-
-    def normal_step(position, state_pair, rhs):
-        iterate, step_dir = state_pair
-        iterate = iterate + step_dir
-        resid = rhs - operate(iterate)
-        step_dir = keep_table[position] * step_dir + push_table[position] * (jacobi * resid)
-        return (iterate, step_dir)
 
     def chebyshev(rhs):
         iterate = jnp.zeros_like(rhs)
         step_dir = jacobi * rhs / theta_center
         since = 1
         run = []
-
-        def flush(state_pair):
-            if len(run) == 1:
-                return normal_step(run[0], state_pair, rhs)
-            if run:
-                return lax.fori_loop(
-                    run[0], run[-1] + 1, lambda i, sp: normal_step(i, sp, rhs), state_pair
-                )
-            return state_pair
-
-        for position, (keep, push) in enumerate(table):
+        for keep, push in table:
             if since == k:
-                iterate, step_dir = flush((iterate, step_dir))
+                iterate, step_dir = run_segment(tuple(run), op_stack, act, rhs, iterate, step_dir)
                 run = []
                 both = exchange_rows(jnp.stack([iterate, step_dir]), k, rows, 3)
                 iterate, step_dir = both[0], both[1]
                 since = 0
-            if keep is None:
-                iterate, step_dir = flush((iterate, step_dir))
-                run = []
-                iterate = iterate + step_dir
-                resid = rhs - operate(iterate)
-                step_dir = jacobi * resid / theta_center
-            else:
-                run.append(position)
+            run.append((keep, push))
             since += 1
-        iterate, step_dir = flush((iterate, step_dir))
+        iterate, step_dir = run_segment(tuple(run), op_stack, act, rhs, iterate, step_dir)
         return iterate + step_dir
 
     forcing = jnp.zeros((2,) + eta.shape, jnp.float32)

time: 917 us -> 292 us (0.32)
  other arithmetic: 580 us -> 26.3 us
  local copies, waits for them, and re-layouts: 257 us -> 8.28 us
  Pallas kernels: 0 us -> 186 us
    add x60 -> x0, other arithmetic: 357 us -> none  [normal_step(): keep_table[position] * step_dir + push_table[position] * (jacobi * resid)]
    mul x63 -> x0, other arithmetic: 197 us -> none  [the longest x62 197 us: operate(): masked = field * act]
    pallas_call x0 -> x4, Pallas kernels: none -> 186 us  [run_segment(): pl.pallas_call(lambda *refs: segment_kernel(steps, *refs), out_shape=(jax...]
    while x662 -> x0, local copies, waits for them, and re-layouts: 83.9 us -> none
    slice x187 -> x0, local copies, waits for them, and re-layouts: 80.7 us -> none  [shift(): lax.slice_in_dim(a, 0, n - 1, axis=axis)]
    dynamic_slice x120 -> x0, local copies, waits for them, and re-layouts: 75.7 us -> none  [the longest x60 38.2 us: normal_step(): keep_table[position] * step_dir + push_table[position] * (jacobi * resid)]
    unnamed x50 -> x4, local copies, waits for them, and re-layouts: 12.1 us -> 0.97 us
  transfers between devices with their start and end apart: 8 -> 8, of which waited for: 7 -> 7; matrix products, arithmetic and copies ran while one was open for 0% -> 1% of each run, Pallas kernels for 0% -> 0%
where the time goes in v2:
time: 292 us; the launch traced here: 291 us
  Pallas kernels  186 us (64%)
  waiting for transfers between devices  35.2 us (12%)
  other arithmetic  26.3 us (9%)
  starting transfers between devices  22.6 us (8%)
  blocking collectives  12.7 us (4%)
  local copies, waits for them, and re-layouts  8.28 us (3%)
    pallas_call x4, Pallas kernels, run_segment(): pl.pallas_call(lambda *refs: segment_kernel(steps, *refs), out_shape=(jax...  186 us
    ppermute x4, waiting for transfers between devices, exchange_rows(): lax.ppermute(lax.slice_in_dim(own, rows - k, rows, axis=axis), 'mx', forw...  19.4 us
    ppermute x4, waiting for transfers between devices, exchange_rows(): high = lax.ppermute(lax.slice_in_dim(own, 0, k, axis=axis), 'mx', backward)  15.8 us
    ppermute x4, starting transfers between devices, exchange_rows(): lax.ppermute(lax.slice_in_dim(own, rows - k, rows, axis=axis), 'mx', forw...  13.1 us
    ppermute x4, starting transfers between devices, exchange_rows(): high = lax.ppermute(lax.slice_in_dim(own, 0, k, axis=axis), 'mx', backward)  9.44 us
    unnamed x6, other arithmetic  6.87 us
  transfers between devices with their start and end apart: 8, of which 7 were waited for; matrix products, arithmetic and copies ran while one was open for 1% of the time, Pallas kernels for 0%

profile of v2, /device:TPU:1, one launch (start us, length us, event | category | flops | bytes accessed | tf_op | source)
XLA Modules:
  0.0 291.4 jit_solution(11649642772741240759)
XLA Ops:
  0.6 4.7 %all_gather.9 = f32[8,16,256]{2,1,0:T(8,128)S(1)} all-gather(f32[8,16,128]{2,1,0:T(8,128)} %param.10), channel_id=1, replica_groups=mesh['mx'=8,'my'=2,'vz'=2] {'my'}, dimensions={2}, use_global_device_ids=true | all-gather | bytes 196608 | tf_op jit(solution)/shard_map/all_gather | solution.py:130
  5.3 4.5 %all_gather.10 = f32[16,16,256]{2,1,0:T(8,128)S(1)} all-gather(f32[8,16,256]{2,1,0:T(8,128)S(1)} %all_gather.9), channel_id=1, replica_groups=mesh['mx'=8,'my'=2,'vz'=2] {'vz'}, dimensions={0}, use_global_device_ids=true | all-gather | bytes 393216 | tf_op jit(solution)/shard_map/all_gather | solution.py:131
  9.8 0.7 convert_bitcast_fusion
  10.5 0.7 multiply_bitcast_fusion.1
  11.2 0.7 pad_maximum_fusion.8
  11.9 3.5 %all_gather.11 = f32[5,16,256]{2,1,0:T(8,128)S(1)} all-gather(f32[5,16,128]{2,1,0:T(8,128)S(1)} %pad_maximum_fusion.8), channel_id=1, replica_groups=mesh['mx'=8,'my'=2,'vz'=2] {'my'}, dimensions={2}, use_global_device_ids=true | all-gather | bytes 122880 | tf_op jit(solution)/shard_map/all_gather | solution.py:129
  15.5 7.4 %collective-permute-start = (f32[21,16,256]{2,1,0:T(8,128)S(1)}, f32[21,16,256]{2,1,0:T(8,128)S(1)}, u32[]{:S(2)}, u32[]{:S(2)}) collective-permute-start(f32[21,16,256]{2,1,0:T(8,128)S(1)} %constant_dynamic-update-slice_fusion), channel_id=1, source_target_pairs={{0,4},{4,8},{8,12},{12,16},{16,20},{20,24},{24,28},{1,5},{5,9},{9,... | collective-permute-start | bytes 1032200 | tf_op jit(solution)/shard_map/ppermute | solution.py:46
  22.9 1.9 collective-permute-start.1
  24.8 2.2 collective-permute-done
  27.0 4.4 %collective-permute-done.1 = f32[21,16,256]{2,1,0:T(8,128)S(1)} collective-permute-done((f32[21,16,256]{2,1,0:T(8,128)S(1)}, f32[21,16,256]{2,1,0:T(8,128)S(1)}, u32[]{:S(2)}, u32[]{:S(2)}) %collective-permute-start.1) | collective-permute-done | bytes 344096 | tf_op jit(solution)/shard_map/ppermute | solution.py:47
  31.8 0.3 fusion.20
  32.1 1.1 bitcast_dynamic-update-slice_fusion.7
  33.2 1.2 bitcast_dynamic-update-slice_fusion.6
  34.4 1.1 bitcast_dynamic-update-slice_fusion.5
  35.5 1.1 bitcast_dynamic-update-slice_fusion.4
  36.6 1.2 bitcast_dynamic-update-slice_fusion.3
  37.9 1.4 multiply_add_fusion
  39.3 1.1 bitcast_dynamic-update-slice_fusion.2
  40.5 1.0 bitcast_dynamic-update-slice_fusion.1
  41.5 1.1 bitcast_dynamic-update-slice_fusion
  42.6 2.1 multiply_multiply_fusion.1
  44.7 1.3 broadcast_14_refs_3_.2.refs_3_
  46.0 45.2 %shard_map.77 = (f32[2,16,48,256]{3,2,1,0:T(8,128)}, f32[2,16,48,256]{3,2,1,0:T(8,128)}) custom-call(f32[8,16,48,256]{3,2,1,0:T(8,128)} %get-tuple-element.50.refs_0_, f32[48,256]{1,0:T(8,128)} %copy-done, f32[2,16,48,256]{3,2,1,0:T(8,128)} %get-tuple-element.69.refs_2_, f32[2,16,48,256]{3,2,1,0:T(8,128)} %broadcast_14_refs_3_.2.refs_3_, ...), custom_call_target="tpu_custom_call" | custom-call | flops 176947200 | bytes 14155776 | tf_op jit(solution)/shard_map/pallas_call | solution.py:106
  91.2 1.3 pad_maximum_fusion.3
  92.5 1.9 collective-permute-start.2
  94.4 2.5 collective-permute-start.3
  96.9 9.2 %collective-permute-done.2 = f32[2,2,16,16,256]{4,3,2,1,0:T(8,128)S(1)} collective-permute-done((f32[2,2,16,16,256]{4,3,2,1,0:T(8,128)S(1)}, f32[2,2,16,16,256]{4,3,2,1,0:T(8,128)S(1)}, u32[]{:S(2)}, u32[]{:S(2)}) %collective-permute-start.2) | collective-permute-done | bytes 1048608 | tf_op jit(solution)/shard_map/ppermute | solution.py:46
  106.1 4.4 %collective-permute-done.3 = f32[2,2,16,16,256]{4,3,2,1,0:T(8,128)S(1)} collective-permute-done((f32[2,2,16,16,256]{4,3,2,1,0:T(8,128)S(1)}, f32[2,2,16,16,256]{4,3,2,1,0:T(8,128)S(1)}, u32[]{:S(2)}, u32[]{:S(2)}) %collective-permute-start.3) | collective-permute-done | bytes 1048608 | tf_op jit(solution)/shard_map/ppermute | solution.py:47
  110.5 0.2 pad_maximum_fusion
  110.7 1.9 slice_bitcast_fusion.2
  112.6 47.7 %shard_map.78 = (f32[2,16,48,256]{3,2,1,0:T(8,128)}, f32[2,16,48,256]{3,2,1,0:T(8,128)}) custom-call(f32[8,16,48,256]{3,2,1,0:T(8,128)} %get-tuple-element.50.refs_0_, f32[48,256]{1,0:T(8,128)} %copy-done, f32[2,16,48,256]{3,2,1,0:T(8,128)} %get-tuple-element.69.refs_2_, f32[2,16,48,256]{3,2,1,0:T(8,128)} %get-tuple-element.55.refs_3_, ...), custom_call_target="tpu_custom_call" | custom-call | flops 188743680 | bytes 14155776 | tf_op jit(solution)/shard_map/pallas_call | solution.py:106
  160.3 3.3 %fusion.19 = (f32[2,48,256]{2,1,0:T(8,128)S(1)}, f32[2,16,48,256]{3,2,1,0:T(8,128)}) fusion(f32[2,16,48,256]{3,2,1,0:T(8,128)} %get-tuple-element.36, f32[2,16,48,256]{3,2,1,0:T(8,128)} %get-tuple-element.37), kind=kLoop, calls=%fused_computation.78 | loop fusion | flops 761856 | bytes 4816896 | tf_op jit(solution)/shard_map/reduce_sum | solution.py:174
  163.6 1.9 collective-permute-start.4
  165.5 2.6 collective-permute-start.5
  168.1 2.6 collective-permute-done.5
  170.7 2.0 multiply_multiply_fusion
  172.7 45.0 %shard_map.79 = (f32[2,16,48,256]{3,2,1,0:T(8,128)}, f32[2,16,48,256]{3,2,1,0:T(8,128)}) custom-call(f32[8,16,48,256]{3,2,1,0:T(8,128)} %get-tuple-element.50.refs_0_, f32[48,256]{1,0:T(8,128)} %copy-done, f32[2,16,48,256]{3,2,1,0:T(8,128)} %get-tuple-element.67.refs_2_, f32[2,16,48,256]{3,2,1,0:T(8,128)} %broadcast_14_refs_3_.2.refs_3_, ...), custom_call_target="tpu_custom_call" | custom-call | flops 176947200 | bytes 14155776 | tf_op jit(solution)/shard_map/pallas_call | solution.py:106
  217.8 2.2 pad_maximum_fusion.2
  220.0 1.9 collective-permute-start.6
  221.9 2.5 collective-permute-start.7
  224.5 1.6 constant_dynamic-slice_fusion
  226.1 7.9 %collective-permute-done.6 = f32[2,2,16,16,256]{4,3,2,1,0:T(8,128)S(1)} collective-permute-done((f32[2,2,16,16,256]{4,3,2,1,0:T(8,128)}, f32[2,2,16,16,256]{4,3,2,1,0:T(8,128)S(1)}, u32[]{:S(2)}, u32[]{:S(2)}) %collective-permute-start.6) | collective-permute-done | bytes 1048608 | tf_op jit(solution)/shard_map/ppermute | solution.py:46
  234.0 4.4 %collective-permute-done.7 = f32[2,2,16,16,256]{4,3,2,1,0:T(8,128)} collective-permute-done((f32[2,2,16,16,256]{4,3,2,1,0:T(8,128)}, f32[2,2,16,16,256]{4,3,2,1,0:T(8,128)}, u32[]{:S(2)}, u32[]{:S(2)}) %collective-permute-start.7) | collective-permute-done | bytes 1048608 | tf_op jit(solution)/shard_map/ppermute | solution.py:47
  238.4 1.8 pad_maximum_fusion.1
  240.2 1.9 slice_bitcast_fusion
  242.0 47.7 %shard_map.80 = (f32[2,16,48,256]{3,2,1,0:T(8,128)}, f32[2,16,48,256]{3,2,1,0:T(8,128)}) custom-call(f32[8,16,48,256]{3,2,1,0:T(8,128)} %get-tuple-element.50.refs_0_, f32[48,256]{1,0:T(8,128)} %copy-done, f32[2,16,48,256]{3,2,1,0:T(8,128)} %get-tuple-element.67.refs_2_, f32[2,16,48,256]{3,2,1,0:T(8,128)} %get-tuple-element.53.refs_3_, ...), custom_call_target="tpu_custom_call" | custom-call | flops 188743680 | bytes 14155776 | tf_op jit(solution)/shard_map/pallas_call | solution.py:106
  289.7 1.0 fusion.10
  290.7 0.7 fusion.17
  (16 shorter events, 0.6 us)
Async XLA Ops:
  15.5 11.6 %collective-permute-start = (f32[21,16,256]{2,1,0:T(8,128)S(1)}, f32[21,16,256]{2,1,0:T(8,128)S(1)}, u32[]{:S(2)}, u32[]{:S(2)}) collective-permute-start(f32[21,16,256]{2,1,0:T(8,128)S(1)} %constant_dynamic-update-slice_fusion), channel_id=1, source_target_pairs={{0,4},{4,8},{8,12},{12,16},{16,20},{20,24},{24,28},{1,5},{5,9},{9,... | collective-permute-start | bytes 1032200 | tf_op jit(solution)/shard_map/ppermute | solution.py:46
  22.9 8.6 %collective-permute-start.1 = (f32[21,16,256]{2,1,0:T(8,128)S(1)}, f32[21,16,256]{2,1,0:T(8,128)S(1)}, u32[]{:S(2)}, u32[]{:S(2)}) collective-permute-start(f32[21,16,256]{2,1,0:T(8,128)S(1)} %constant_dynamic-update-slice_fusion), channel_id=1, source_target_pairs={{4,0},{8,4},{12,8},{16,12},{20,16},{24,20},{28,24},{5,1},{9,5},{13... | collective-permute-start | bytes 1032200 | tf_op jit(solution)/shard_map/ppermute | solution.py:47
  40.5 2.1 copy-start
  92.5 13.7 %collective-permute-start.2 = (f32[2,2,16,16,256]{4,3,2,1,0:T(8,128)S(1)}, f32[2,2,16,16,256]{4,3,2,1,0:T(8,128)S(1)}, u32[]{:S(2)}, u32[]{:S(2)}) collective-permute-start(f32[2,2,16,16,256]{4,3,2,1,0:T(8,128)S(1)} %pad_maximum_fusion.3), channel_id=1, source_target_pairs={{0,4},{4,8},{8,12},{12,16},{16,20},{20,24},{24,28},{1,5},{5,9},{9,... | collective-permute-start | bytes 3145736 | tf_op jit(solution)/shard_map/ppermute | solution.py:46
  94.4 16.1 %collective-permute-start.3 = (f32[2,2,16,16,256]{4,3,2,1,0:T(8,128)S(1)}, f32[2,2,16,16,256]{4,3,2,1,0:T(8,128)S(1)}, u32[]{:S(2)}, u32[]{:S(2)}) collective-permute-start(f32[2,2,16,16,256]{4,3,2,1,0:T(8,128)S(1)} %pad_maximum_fusion.3), channel_id=1, source_target_pairs={{4,0},{8,4},{12,8},{16,12},{20,16},{24,20},{28,24},{5,1},{9,5},{13... | collective-permute-start | bytes 3145736 | tf_op jit(solution)/shard_map/ppermute | solution.py:47
  163.6 4.5 %collective-permute-start.4 = (f32[2,16,256]{2,1,0:T(8,128)S(1)}, f32[2,16,256]{2,1,0:T(8,128)S(1)}, u32[]{:S(2)}, u32[]{:S(2)}) collective-permute-start(f32[2,16,256]{2,1,0:T(8,128)S(1)} %slice_multiply_fusion), channel_id=1, source_target_pairs={{0,4},{4,8},{8,12},{12,16},{16,20},{20,24},{24,28},{1,5},{5,9},{9,... | collective-permute-start | bytes 98312 | tf_op jit(solution)/shard_map/ppermute | solution.py:46
  165.5 5.2 %collective-permute-start.5 = (f32[2,16,256]{2,1,0:T(8,128)S(1)}, f32[2,16,256]{2,1,0:T(8,128)S(1)}, u32[]{:S(2)}, u32[]{:S(2)}) collective-permute-start(f32[2,16,256]{2,1,0:T(8,128)S(1)} %slice_multiply_fusion), channel_id=1, source_target_pairs={{4,0},{8,4},{12,8},{16,12},{20,16},{24,20},{28,24},{5,1},{9,5},{13... | collective-permute-start | bytes 98312 | tf_op jit(solution)/shard_map/ppermute | solution.py:47
  220.0 14.0 %collective-permute-start.6 = (f32[2,2,16,16,256]{4,3,2,1,0:T(8,128)}, f32[2,2,16,16,256]{4,3,2,1,0:T(8,128)S(1)}, u32[]{:S(2)}, u32[]{:S(2)}) collective-permute-start(f32[2,2,16,16,256]{4,3,2,1,0:T(8,128)} %pad_maximum_fusion.2), channel_id=1, source_target_pairs={{0,4},{4,8},{8,12},{12,16},{16,20},{20,24},{24,28},{1,5},{5,9},{9,... | collective-permute-start | bytes 3145736 | tf_op jit(solution)/shard_map/ppermute | solution.py:46
  221.9 16.4 %collective-permute-start.7 = (f32[2,2,16,16,256]{4,3,2,1,0:T(8,128)}, f32[2,2,16,16,256]{4,3,2,1,0:T(8,128)}, u32[]{:S(2)}, u32[]{:S(2)}) collective-permute-start(f32[2,2,16,16,256]{4,3,2,1,0:T(8,128)} %pad_maximum_fusion.2), channel_id=1, source_target_pairs={{4,0},{8,4},{12,8},{16,12},{20,16},{24,20},{28,24},{5,1},{9,5},{13... | collective-permute-start | bytes 3145736 | tf_op jit(solution)/shard_map/ppermute | solution.py:47

commit v3 on v2

--- a/solution.py
+++ b/solution.py
@@ -58,64 +58,52 @@
     return jnp.concatenate([z, lax.slice_in_dim(a, 0, n - 1, axis=axis)], axis=axis)
 
 
-def segment_kernel(steps, op_ref, act_ref, rhs_ref, x_in, d_in, x_ref, d_ref, m_ref):
+def segment_kernel(steps, op_ref, rhs_ref, x_in, d_in, x_ref, d_ref):
     comps, layers = rhs_ref.shape[0], rhs_ref.shape[1]
-    rows, cols = act_ref.shape
+    rows, cols = rhs_ref.shape[2], rhs_ref.shape[3]
     x_ref[...] = x_in[...]
     d_ref[...] = d_in[...]
-    zero = jnp.zeros((rows, cols), jnp.float32)
-    for c in range(comps):
-        m_ref[c, 0] = zero
-        m_ref[c, layers + 1] = zero
 
     for keep, push in steps:
-
-        def advance(layer, carry):
+        for c in range(comps):
+            x_ref[c, 1] = x_ref[c, 1] + d_ref[c, 1]
+
+        def update(layer, carry):
+            p = layer + 1
             for c in range(comps):
-                moved = x_ref[c, layer] + d_ref[c, layer]
-                x_ref[c, layer] = moved
-                m_ref[c, layer + 1] = moved * act_ref[...]
-            return carry
-
-        lax.fori_loop(0, layers, advance, 0)
-
-        def update(layer, carry):
-            act = act_ref[...]
-            for c in range(comps):
-                centre = m_ref[c, layer + 1]
-                beside = op_ref[0, layer] * m_ref[c, layer] + op_ref[1, layer] * m_ref[c, layer + 2]
+                x_ref[c, p + 1] = x_ref[c, p + 1] + d_ref[c, p + 1]
+                centre = x_ref[c, p]
+                beside = op_ref[0, layer] * x_ref[c, p - 1] + op_ref[1, layer] * x_ref[c, p + 1]
                 beside = beside + op_ref[2, layer] * pltpu.roll(centre, 1, 0)
                 beside = beside + op_ref[3, layer] * pltpu.roll(centre, rows - 1, 0)
                 beside = beside + op_ref[4, layer] * pltpu.roll(centre, 1, 1)
                 beside = beside + op_ref[5, layer] * pltpu.roll(centre, cols - 1, 1)
-                applied = act * (op_ref[6, layer] * centre - beside) + (1.0 - act) * x_ref[c, layer]
-                resid = rhs_ref[c, layer] - applied
+                resid = rhs_ref[c, layer] - (op_ref[6, layer] * centre - beside)
                 if keep is None:
-                    d_ref[c, layer] = op_ref[7, layer] * resid / theta_center
+                    d_ref[c, p] = op_ref[7, layer] * resid / theta_center
                 else:
-                    d_ref[c, layer] = keep * d_ref[c, layer] + push * (op_ref[7, layer] * resid)
+                    d_ref[c, p] = keep * d_ref[c, p] + push * (op_ref[7, layer] * resid)
             return carry
 
         lax.fori_loop(0, layers, update, 0)
 
 
-def run_segment(steps, op_stack, act, rhs, iterate, step_dir):
+def run_segment(steps, op_stack, rhs, iterate, step_dir):
     comps, layers, rows, cols = rhs.shape
     vmem = pl.BlockSpec(memory_space=pltpu.VMEM)
     cells = comps * layers * rows * cols
     return pl.pallas_call(
         lambda *refs: segment_kernel(steps, *refs),
         out_shape=(
-            jax.ShapeDtypeStruct(rhs.shape, jnp.float32),
-            jax.ShapeDtypeStruct(rhs.shape, jnp.float32),
+            jax.ShapeDtypeStruct(iterate.shape, jnp.float32),
+            jax.ShapeDtypeStruct(iterate.shape, jnp.float32),
         ),
-        in_specs=[vmem] * 5,
+        in_specs=[vmem] * 4,
         out_specs=(vmem, vmem),
-        scratch_shapes=[pltpu.VMEM((comps, layers + 2, rows, cols), jnp.float32)],
         cost_estimate=pl.CostEstimate(
-            flops=30 * cells * len(steps), bytes_accessed=4 * cells * 9, transcendentals=0
+            flops=20 * cells * len(steps), bytes_accessed=4 * cells * 9, transcendentals=0
         ),
-    )(op_stack, act, rhs, iterate, step_dir)
+    )(op_stack, rhs, iterate, step_dir)
 
 
 def local(viscosity, friction, base_velocity, grounded, ice_free, direction):
@@ -147,25 +135,38 @@
     diag = c_zm + c_zp + c_xm + c_xp + c_ym + c_yp + shift_mass * eta + basal
     jacobi = 1.0 / (act * diag + 1.0 - act)
 
-    op_stack = jnp.stack([c_zm, c_zp, c_xm, c_xp, c_ym, c_yp, diag, jacobi])
+    on = act > 0
+    op_stack = jnp.stack(
+        [
+            act * c_zm,
+            act * c_zp,
+            act * c_xm * shift(act, 0, -1),
+            act * c_xp * shift(act, 0, 1),
+            act * c_ym * shift(act, 1, -1),
+            act * c_yp * shift(act, 1, 1),
+            jnp.where(on, diag, 1.0),
+            jacobi,
+        ]
+    )
     table = step_constants()
+    layer_pad = ((0, 0), (1, 1), (0, 0), (0, 0))
 
     def chebyshev(rhs):
-        iterate = jnp.zeros_like(rhs)
-        step_dir = jacobi * rhs / theta_center
+        iterate = jnp.zeros((2, layers + 2) + rhs.shape[2:], jnp.float32)
+        step_dir = jnp.pad(jacobi * rhs / theta_center, layer_pad)
         since = 1
         run = []
         for keep, push in table:
             if since == k:
-                iterate, step_dir = run_segment(tuple(run), op_stack, act, rhs, iterate, step_dir)
+                iterate, step_dir = run_segment(tuple(run), op_stack, rhs, iterate, step_dir)
                 run = []
                 both = exchange_rows(jnp.stack([iterate, step_dir]), k, rows, 3)
                 iterate, step_dir = both[0], both[1]
                 since = 0
             run.append((keep, push))
             since += 1
-        iterate, step_dir = run_segment(tuple(run), op_stack, act, rhs, iterate, step_dir)
-        return iterate + step_dir
+        iterate, step_dir = run_segment(tuple(run), op_stack, rhs, iterate, step_dir)
+        return (iterate + step_dir)[:, 1 : layers + 1]
 
     forcing = jnp.zeros((2,) + eta.shape, jnp.float32)
     forcing = forcing.at[:, 0].set(-(bed_coef * dir_ext)[None] * bv)

time: 292 us -> 274 us (0.938)
  Pallas kernels: 186 us -> 162 us
  local copies, waits for them, and re-layouts: 8.28 us -> 11.6 us
    pallas_call x4, Pallas kernels: 186 us -> 162 us  [run_segment(): pl.pallas_call(lambda *refs: segment_kernel(steps, *refs), out_shape=(jax...]
    pad x0 -> x2, local copies, waits for them, and re-layouts: none -> 2.95 us  [chebyshev(): step_dir = jnp.pad(jacobi * rhs / theta_center, layer_pad)]
    unnamed x6 -> x7, other arithmetic: 6.87 us -> 8.01 us
where the time goes in v3:
time: 274 us; the launch traced here: 273 us
  Pallas kernels  162 us (59%)
  waiting for transfers between devices  37.2 us (14%)
  other arithmetic  27.1 us (10%)
  starting transfers between devices  22.6 us (8%)
  blocking collectives  12.7 us (5%)
  local copies, waits for them, and re-layouts  11.6 us (4%)
    pallas_call x4, Pallas kernels, run_segment(): pl.pallas_call(lambda *refs: segment_kernel(steps, *refs), out_shape=(jax...  162 us
    ppermute x4, waiting for transfers between devices, exchange_rows(): lax.ppermute(lax.slice_in_dim(own, rows - k, rows, axis=axis), 'mx', forw...  21.2 us
    ppermute x4, waiting for transfers between devices, exchange_rows(): high = lax.ppermute(lax.slice_in_dim(own, 0, k, axis=axis), 'mx', backward)  15.9 us
    ppermute x4, starting transfers between devices, exchange_rows(): lax.ppermute(lax.slice_in_dim(own, rows - k, rows, axis=axis), 'mx', forw...  13.1 us
    ppermute x4, starting transfers between devices, exchange_rows(): high = lax.ppermute(lax.slice_in_dim(own, 0, k, axis=axis), 'mx', backward)  9.46 us
    unnamed x7, other arithmetic  8.01 us
  transfers between devices with their start and end apart: 8, of which 7 were waited for; matrix products, arithmetic and copies ran while one was open for 1% of the time, Pallas kernels for 0%

profile of v3, /device:TPU:1, one launch (start us, length us, event | category | flops | bytes accessed | tf_op | source)
XLA Modules:
  0.0 273.5 jit_solution(1031477926042434608)
XLA Ops:
  0.6 4.7 %all_gather.9 = f32[8,16,256]{2,1,0:T(8,128)S(1)} all-gather(f32[8,16,128]{2,1,0:T(8,128)} %param.10), channel_id=1, replica_groups=mesh['mx'=8,'my'=2,'vz'=2] {'my'}, dimensions={2}, use_global_device_ids=true | all-gather | bytes 196608 | tf_op jit(solution)/shard_map/all_gather | solution.py:118
  5.3 4.5 %all_gather.10 = f32[16,16,256]{2,1,0:T(8,128)S(1)} all-gather(f32[8,16,256]{2,1,0:T(8,128)S(1)} %all_gather.9), channel_id=1, replica_groups=mesh['mx'=8,'my'=2,'vz'=2] {'vz'}, dimensions={0}, use_global_device_ids=true | all-gather | bytes 393216 | tf_op jit(solution)/shard_map/all_gather | solution.py:119
  9.8 0.7 convert_bitcast_fusion
  10.5 0.7 multiply_bitcast_fusion.1
  11.2 0.7 pad_maximum_fusion.8
  11.9 3.5 %all_gather.11 = f32[5,16,256]{2,1,0:T(8,128)S(1)} all-gather(f32[5,16,128]{2,1,0:T(8,128)S(1)} %pad_maximum_fusion.8), channel_id=1, replica_groups=mesh['mx'=8,'my'=2,'vz'=2] {'my'}, dimensions={2}, use_global_device_ids=true | all-gather | bytes 122880 | tf_op jit(solution)/shard_map/all_gather | solution.py:117
  15.5 7.4 %collective-permute-start = (f32[21,16,256]{2,1,0:T(8,128)S(1)}, f32[21,16,256]{2,1,0:T(8,128)S(1)}, u32[]{:S(2)}, u32[]{:S(2)}) collective-permute-start(f32[21,16,256]{2,1,0:T(8,128)S(1)} %constant_dynamic-update-slice_fusion), channel_id=1, source_target_pairs={{0,4},{4,8},{8,12},{12,16},{16,20},{20,24},{24,28},{1,5},{5,9},{9,... | collective-permute-start | bytes 1032200 | tf_op jit(solution)/shard_map/ppermute | solution.py:46
  22.9 1.9 collective-permute-start.1
  24.8 2.2 collective-permute-done
  27.0 4.4 %collective-permute-done.1 = f32[21,16,256]{2,1,0:T(8,128)S(1)} collective-permute-done((f32[21,16,256]{2,1,0:T(8,128)S(1)}, f32[21,16,256]{2,1,0:T(8,128)S(1)}, u32[]{:S(2)}, u32[]{:S(2)}) %collective-permute-start.1) | collective-permute-done | bytes 344096 | tf_op jit(solution)/shard_map/ppermute | solution.py:47
  33.6 1.1 bitcast_dynamic-update-slice_fusion.7
  34.7 1.2 bitcast_dynamic-update-slice_fusion.6
  35.9 1.2 bitcast_dynamic-update-slice_fusion.5
  37.1 1.2 bitcast_dynamic-update-slice_fusion.4
  38.2 1.4 multiply_add_fusion
  39.6 1.2 bitcast_dynamic-update-slice_fusion.3
  40.9 1.2 bitcast_dynamic-update-slice_fusion.2
  42.1 1.0 bitcast_dynamic-update-slice_fusion.1
  43.0 1.1 bitcast_dynamic-update-slice_fusion
  44.1 1.5 multiply_multiply_fusion.1
  45.6 1.5 pad.26.refs_3_
  47.1 1.4 broadcast_12_refs_2_.2.refs_2_
  48.5 39.3 %shard_map.77 = (f32[2,18,48,256]{3,2,1,0:T(8,128)}, f32[2,18,48,256]{3,2,1,0:T(8,128)}) custom-call(f32[8,16,48,256]{3,2,1,0:T(8,128)} %get-tuple-element.50.refs_0_, f32[2,16,48,256]{3,2,1,0:T(8,128)} %get-tuple-element.71.refs_1_, f32[2,18,48,256]{3,2,1,0:T(8,128)} %broadcast_12_refs_2_.2.refs_2_, f32[2,18,48,256]{3,2,1,0:T(8,128)} %pad.26.refs_3_), custom_call_target="tpu_custom_call" | custom-call | flops 117964800 | bytes 14155776 | tf_op jit(solution)/shard_map/pallas_call | solution.py:95
  87.9 1.3 pad_maximum_fusion.3
  89.2 1.9 collective-permute-start.2
  91.1 2.5 collective-permute-start.3
  93.6 10.6 %collective-permute-done.2 = f32[2,2,18,16,256]{4,3,2,1,0:T(8,128)S(1)} collective-permute-done((f32[2,2,18,16,256]{4,3,2,1,0:T(8,128)S(1)}, f32[2,2,18,16,256]{4,3,2,1,0:T(8,128)S(1)}, u32[]{:S(2)}, u32[]{:S(2)}) %collective-permute-start.2) | collective-permute-done | bytes 1179680 | tf_op jit(solution)/shard_map/ppermute | solution.py:46
  104.3 4.4 %collective-permute-done.3 = f32[2,2,18,16,256]{4,3,2,1,0:T(8,128)S(1)} collective-permute-done((f32[2,2,18,16,256]{4,3,2,1,0:T(8,128)S(1)}, f32[2,2,18,16,256]{4,3,2,1,0:T(8,128)S(1)}, u32[]{:S(2)}, u32[]{:S(2)}) %collective-permute-start.3) | collective-permute-done | bytes 1179680 | tf_op jit(solution)/shard_map/ppermute | solution.py:47
  108.9 2.1 slice_bitcast_fusion.2
  111.0 41.4 %shard_map.78 = (f32[2,18,48,256]{3,2,1,0:T(8,128)}, f32[2,18,48,256]{3,2,1,0:T(8,128)}) custom-call(f32[8,16,48,256]{3,2,1,0:T(8,128)} %get-tuple-element.50.refs_0_, f32[2,16,48,256]{3,2,1,0:T(8,128)} %get-tuple-element.71.refs_1_, f32[2,18,48,256]{3,2,1,0:T(8,128)} %get-tuple-element.55.refs_2_, f32[2,18,48,256]{3,2,1,0:T(8,128)} %get-tuple-element.54.refs_3_), custom_call_target="tpu_custom_call" | custom-call | flops 125829120 | bytes 14155776 | tf_op jit(solution)/shard_map/pallas_call | solution.py:95
  152.4 3.3 %fusion.17 = (f32[2,48,256]{2,1,0:T(8,128)S(1)}, f32[2,16,48,256]{3,2,1,0:T(8,128)}) fusion(f32[2,18,48,256]{3,2,1,0:T(8,128)} %get-tuple-element.37, f32[2,18,48,256]{3,2,1,0:T(8,128)} %get-tuple-element.36), kind=kLoop, calls=%fused_computation.81 | loop fusion | flops 761856 | bytes 4816896 | tf_op jit(solution)/shard_map/reduce_sum | solution.py:175
  155.7 1.9 collective-permute-start.4
  157.6 2.6 collective-permute-start.5
  160.2 2.6 collective-permute-done.5
  162.9 1.5 multiply_multiply_fusion
  164.3 1.5 pad.27.refs_3_
  165.8 39.3 %shard_map.79 = (f32[2,18,48,256]{3,2,1,0:T(8,128)}, f32[2,18,48,256]{3,2,1,0:T(8,128)}) custom-call(f32[8,16,48,256]{3,2,1,0:T(8,128)} %get-tuple-element.50.refs_0_, f32[2,16,48,256]{3,2,1,0:T(8,128)} %get-tuple-element.69.refs_1_, f32[2,18,48,256]{3,2,1,0:T(8,128)} %broadcast_12_refs_2_.2.refs_2_, f32[2,18,48,256]{3,2,1,0:T(8,128)} %pad.27.refs_3_), custom_call_target="tpu_custom_call" | custom-call | flops 117964800 | bytes 14155776 | tf_op jit(solution)/shard_map/pallas_call | solution.py:95
  205.2 1.3 pad_maximum_fusion.2
  206.5 1.9 collective-permute-start.6
  208.4 2.5 collective-permute-start.7
  211.6 1.6 constant_dynamic-slice_fusion
  213.2 8.4 %collective-permute-done.6 = f32[2,2,18,16,256]{4,3,2,1,0:T(8,128)S(1)} collective-permute-done((f32[2,2,18,16,256]{4,3,2,1,0:T(8,128)S(1)}, f32[2,2,18,16,256]{4,3,2,1,0:T(8,128)S(1)}, u32[]{:S(2)}, u32[]{:S(2)}) %collective-permute-start.6) | collective-permute-done | bytes 1179680 | tf_op jit(solution)/shard_map/ppermute | solution.py:46
  221.5 4.5 %collective-permute-done.7 = f32[2,2,18,16,256]{4,3,2,1,0:T(8,128)} collective-permute-done((f32[2,2,18,16,256]{4,3,2,1,0:T(8,128)S(1)}, f32[2,2,18,16,256]{4,3,2,1,0:T(8,128)}, u32[]{:S(2)}, u32[]{:S(2)}) %collective-permute-start.7) | collective-permute-done | bytes 1179680 | tf_op jit(solution)/shard_map/ppermute | solution.py:47
  226.0 1.5 pad_maximum_fusion.1
  227.6 2.1 slice_bitcast_fusion
  229.6 41.5 %shard_map.80 = (f32[2,18,48,256]{3,2,1,0:T(8,128)}, f32[2,18,48,256]{3,2,1,0:T(8,128)}) custom-call(f32[8,16,48,256]{3,2,1,0:T(8,128)} %get-tuple-element.50.refs_0_, f32[2,16,48,256]{3,2,1,0:T(8,128)} %get-tuple-element.69.refs_1_, f32[2,18,48,256]{3,2,1,0:T(8,128)} %get-tuple-element.53.refs_2_, f32[2,18,48,256]{3,2,1,0:T(8,128)} %get-tuple-element.52.refs_3_), custom_call_target="tpu_custom_call" | custom-call | flops 125829120 | bytes 14155776 | tf_op jit(solution)/shard_map/pallas_call | solution.py:95
  271.1 1.0 fusion.8
  272.1 1.4 fusion.15
  (29 shorter events, 3.1 us)
Async XLA Ops:
  15.5 11.6 %collective-permute-start = (f32[21,16,256]{2,1,0:T(8,128)S(1)}, f32[21,16,256]{2,1,0:T(8,128)S(1)}, u32[]{:S(2)}, u32[]{:S(2)}) collective-permute-start(f32[21,16,256]{2,1,0:T(8,128)S(1)} %constant_dynamic-update-slice_fusion), channel_id=1, source_target_pairs={{0,4},{4,8},{8,12},{12,16},{16,20},{20,24},{24,28},{1,5},{5,9},{9,... | collective-permute-start | bytes 1032200 | tf_op jit(solution)/shard_map/ppermute | solution.py:46
  22.9 8.6 %collective-permute-start.1 = (f32[21,16,256]{2,1,0:T(8,128)S(1)}, f32[21,16,256]{2,1,0:T(8,128)S(1)}, u32[]{:S(2)}, u32[]{:S(2)}) collective-permute-start(f32[21,16,256]{2,1,0:T(8,128)S(1)} %constant_dynamic-update-slice_fusion), channel_id=1, source_target_pairs={{4,0},{8,4},{12,8},{16,12},{20,16},{24,20},{28,24},{5,1},{9,5},{13... | collective-permute-start | bytes 1032200 | tf_op jit(solution)/shard_map/ppermute | solution.py:47
  89.2 15.1 %collective-permute-start.2 = (f32[2,2,18,16,256]{4,3,2,1,0:T(8,128)S(1)}, f32[2,2,18,16,256]{4,3,2,1,0:T(8,128)S(1)}, u32[]{:S(2)}, u32[]{:S(2)}) collective-permute-start(f32[2,2,18,16,256]{4,3,2,1,0:T(8,128)S(1)} %pad_maximum_fusion.3), channel_id=1, source_target_pairs={{0,4},{4,8},{8,12},{12,16},{16,20},{20,24},{24,28},{1,5},{5,9},{9,... | collective-permute-start | bytes 3538952 | tf_op jit(solution)/shard_map/ppermute | solution.py:46
  91.1 17.5 %collective-permute-start.3 = (f32[2,2,18,16,256]{4,3,2,1,0:T(8,128)S(1)}, f32[2,2,18,16,256]{4,3,2,1,0:T(8,128)S(1)}, u32[]{:S(2)}, u32[]{:S(2)}) collective-permute-start(f32[2,2,18,16,256]{4,3,2,1,0:T(8,128)S(1)} %pad_maximum_fusion.3), channel_id=1, source_target_pairs={{4,0},{8,4},{12,8},{16,12},{20,16},{24,20},{28,24},{5,1},{9,5},{13... | collective-permute-start | bytes 3538952 | tf_op jit(solution)/shard_map/ppermute | solution.py:47
  155.7 4.5 %collective-permute-start.4 = (f32[2,16,256]{2,1,0:T(8,128)S(1)}, f32[2,16,256]{2,1,0:T(8,128)S(1)}, u32[]{:S(2)}, u32[]{:S(2)}) collective-permute-start(f32[2,16,256]{2,1,0:T(8,128)S(1)} %slice_multiply_fusion), channel_id=1, source_target_pairs={{0,4},{4,8},{8,12},{12,16},{16,20},{20,24},{24,28},{1,5},{5,9},{9,... | collective-permute-start | bytes 98312 | tf_op jit(solution)/shard_map/ppermute | solution.py:46
  157.6 5.2 %collective-permute-start.5 = (f32[2,16,256]{2,1,0:T(8,128)S(1)}, f32[2,16,256]{2,1,0:T(8,128)S(1)}, u32[]{:S(2)}, u32[]{:S(2)}) collective-permute-start(f32[2,16,256]{2,1,0:T(8,128)S(1)} %slice_multiply_fusion), channel_id=1, source_target_pairs={{4,0},{8,4},{12,8},{16,12},{20,16},{24,20},{28,24},{5,1},{9,5},{13... | collective-permute-start | bytes 98312 | tf_op jit(solution)/shard_map/ppermute | solution.py:47
  206.5 15.1 %collective-permute-start.6 = (f32[2,2,18,16,256]{4,3,2,1,0:T(8,128)S(1)}, f32[2,2,18,16,256]{4,3,2,1,0:T(8,128)S(1)}, u32[]{:S(2)}, u32[]{:S(2)}) collective-permute-start(f32[2,2,18,16,256]{4,3,2,1,0:T(8,128)S(1)} %pad_maximum_fusion.2), channel_id=1, source_target_pairs={{0,4},{4,8},{8,12},{12,16},{16,20},{20,24},{24,28},{1,5},{5,9},{9,... | collective-permute-start | bytes 3538952 | tf_op jit(solution)/shard_map/ppermute | solution.py:46
  208.4 17.6 %collective-permute-start.7 = (f32[2,2,18,16,256]{4,3,2,1,0:T(8,128)S(1)}, f32[2,2,18,16,256]{4,3,2,1,0:T(8,128)}, u32[]{:S(2)}, u32[]{:S(2)}) collective-permute-start(f32[2,2,18,16,256]{4,3,2,1,0:T(8,128)S(1)} %pad_maximum_fusion.2), channel_id=1, source_target_pairs={{4,0},{8,4},{12,8},{16,12},{20,16},{24,20},{28,24},{5,1},{9,5},{13... | collective-permute-start | bytes 3538952 | tf_op jit(solution)/shard_map/ppermute | solution.py:47
  229.6 42.5 %copy-start = (f32[47,256]{1,0:T(8,128)S(1)}, f32[47,256]{1,0:T(8,128)}, u32[]{:S(2)}) copy-start(f32[47,256]{1,0:T(8,128)} %get-tuple-element.62) | copy-start | bytes 144388
  229.6 42.5 %copy-start.1 = (f32[48,255]{1,0:T(8,128)S(1)}, f32[48,255]{1,0:T(8,128)}, u32[]{:S(2)}) copy-start(f32[48,255]{1,0:T(8,128)} %get-tuple-element.74) | copy-start | bytes 146884
  229.6 42.5 %copy-start.2 = (f32[48,255]{1,0:T(8,128)S(1)}, f32[48,255]{1,0:T(8,128)}, u32[]{:S(2)}) copy-start(f32[48,255]{1,0:T(8,128)} %get-tuple-element.75) | copy-start | bytes 146884

commit v4 on v3

--- a/solution.py
+++ b/solution.py
@@ -46,6 +46,18 @@
     low = lax.ppermute(lax.slice_in_dim(own, rows - k, rows, axis=axis), "mx", forward)
     high = lax.ppermute(lax.slice_in_dim(own, 0, k, axis=axis), "mx", backward)
     return jnp.concatenate([low, own, high], axis=axis)
+
+
+def gather_axis(block, axis, dim):
+    count = lax.axis_size(axis)
+    me = lax.axis_index(axis)
+    seq = [block]
+    for s in range(1, count):
+        pairs = [(j, (j - s) % count) for j in range(count)]
+        seq.append(lax.ppermute(block, axis, pairs))
+    size = block.shape[dim]
+    doubled = jnp.concatenate(seq + seq, axis=dim)
+    return lax.dynamic_slice_in_dim(doubled, ((count - me) % count) * size, count * size, axis=dim)
 
 
 def shift(a, axis, offset):
@@ -114,9 +126,9 @@
     act = (1 - ice_free).astype(jnp.float32)
     bed_coef = grounded.astype(jnp.float32) * friction
     planes = jnp.stack([act, bed_coef, base_velocity[0], base_velocity[1], direction])
-    planes = lax.all_gather(planes, "my", axis=2, tiled=True)
-    eta = lax.all_gather(viscosity, "my", axis=2, tiled=True)
-    eta = lax.all_gather(eta, "vz", axis=0, tiled=True)
+    both = gather_axis(jnp.concatenate([viscosity, planes], axis=0), "my", 2)
+    planes = both[layers_own:]
+    eta = gather_axis(both[:layers_own], "vz", 0)
     layers = eta.shape[0]
     joined = jnp.concatenate([eta, planes], axis=0)
     zeros_halo = jnp.zeros(joined.shape[:1] + (k,) + joined.shape[2:], joined.dtype)

time: 274 us -> 270 us (0.985)
  blocking collectives: 12.7 us -> 0 us
  waiting for transfers between devices: 37.2 us -> 42.8 us
    all_gather x3 -> x0, blocking collectives: 12.7 us -> none  [the longest x1 4.65 us: local(): eta = lax.all_gather(viscosity, 'my', axis=2, tiled=True)]
    ppermute x0 -> x2, waiting for transfers between devices: none -> 5.67 us  [gather_axis(): seq.append(lax.ppermute(block, axis, pairs))]
    ppermute x0 -> x2, starting transfers between devices: none -> 2.97 us  [gather_axis(): seq.append(lax.ppermute(block, axis, pairs))]
    unnamed x7 -> x9, other arithmetic: 8.01 us -> 9.44 us
  transfers between devices with their start and end apart: 8 -> 10, of which waited for: 7 -> 9; matrix products, arithmetic and copies ran while one was open for 1% -> 1% of each run, Pallas kernels for 0% -> 0%
where the time goes in v4:
time: 270 us
  Pallas kernels  162 us (60%)
  waiting for transfers between devices  42.8 us (16%)
  other arithmetic  26.6 us (10%)
  starting transfers between devices  23.9 us (9%)
  local copies, waits for them, and re-layouts  13.9 us (5%)
    pallas_call x4, Pallas kernels, run_segment(): pl.pallas_call(lambda *refs: segment_kernel(steps, *refs), out_shape=(jax...  162 us
    ppermute x4, waiting for transfers between devices, exchange_rows(): lax.ppermute(lax.slice_in_dim(own, rows - k, rows, axis=axis), 'mx', forw...  21.2 us
    ppermute x4, waiting for transfers between devices, exchange_rows(): high = lax.ppermute(lax.slice_in_dim(own, 0, k, axis=axis), 'mx', backward)  15.9 us
    ppermute x4, starting transfers between devices, exchange_rows(): lax.ppermute(lax.slice_in_dim(own, rows - k, rows, axis=axis), 'mx', forw...  11.4 us
    ppermute x4, starting transfers between devices, exchange_rows(): high = lax.ppermute(lax.slice_in_dim(own, 0, k, axis=axis), 'mx', backward)  9.46 us
    unnamed x9, other arithmetic  9.44 us
    ppermute x2, waiting for transfers between devices, gather_axis(): seq.append(lax.ppermute(block, axis, pairs))  5.67 us
  transfers between devices with their start and end apart: 10, of which 9 were waited for; matrix products, arithmetic and copies ran while one was open for 1% of the time, Pallas kernels for 0%

profile of v4, /device:TPU:1, one launch (start us, length us, event | category | flops | bytes accessed | tf_op | source)
XLA Modules:
  0.0 269.6 jit_solution(13142357958590194398)
XLA Ops:
  0.6 0.8 constant_dynamic-update-slice_fusion.4
  2.9 0.7 constant_dynamic-update-slice_fusion.1
  4.3 2.1 collective-permute-start
  6.4 2.7 collective-permute-done
  9.2 0.9 collective-permute-start.1
  10.1 3.0 %collective-permute-done.1 = f32[8,16,256]{2,1,0:T(8,128)S(1)} collective-permute-done((f32[8,16,256]{2,1,0:T(8,128)S(1)}, f32[8,16,256]{2,1,0:T(8,128)S(1)}, u32[]{:S(2)}, u32[]{:S(2)}) %collective-permute-start.1) | collective-permute-done | bytes 131104 | tf_op jit(solution)/shard_map/ppermute | solution.py:57
  13.2 5.7 %collective-permute-start.2 = (f32[21,16,256]{2,1,0:T(8,128)S(1)}, f32[21,16,256]{2,1,0:T(8,128)S(1)}, u32[]{:S(2)}, u32[]{:S(2)}) collective-permute-start(f32[21,16,256]{2,1,0:T(8,128)S(1)} %pad_maximum_fusion.5), channel_id=1, source_target_pairs={{0,4},{4,8},{8,12},{12,16},{16,20},{20,24},{24,28},{1,5},{5,9},{9,... | collective-permute-start | bytes 1032200 | tf_op jit(solution)/shard_map/ppermute | solution.py:46
  18.9 1.9 collective-permute-start.3
  20.8 2.2 collective-permute-done.2
  23.0 4.4 %collective-permute-done.3 = f32[21,16,256]{2,1,0:T(8,128)S(1)} collective-permute-done((f32[21,16,256]{2,1,0:T(8,128)S(1)}, f32[21,16,256]{2,1,0:T(8,128)S(1)}, u32[]{:S(2)}, u32[]{:S(2)}) %collective-permute-start.3) | collective-permute-done | bytes 344096 | tf_op jit(solution)/shard_map/ppermute | solution.py:47
  29.6 1.1 bitcast_dynamic-update-slice_fusion.7
  30.7 1.2 bitcast_dynamic-update-slice_fusion.6
  31.9 1.4 multiply_add_fusion
  33.3 1.2 bitcast_dynamic-update-slice_fusion.5
  34.5 1.2 bitcast_dynamic-update-slice_fusion.4
  35.7 1.2 bitcast_dynamic-update-slice_fusion.3
  36.9 1.2 bitcast_dynamic-update-slice_fusion.2
  38.1 1.0 bitcast_dynamic-update-slice_fusion.1
  39.1 1.1 bitcast_dynamic-update-slice_fusion
  40.2 1.5 multiply_multiply_fusion.1
  41.7 1.5 pad.26.refs_3_
  43.2 1.4 broadcast_12_refs_2_.2.refs_2_
  44.6 39.3 %shard_map.77 = (f32[2,18,48,256]{3,2,1,0:T(8,128)}, f32[2,18,48,256]{3,2,1,0:T(8,128)}) custom-call(f32[8,16,48,256]{3,2,1,0:T(8,128)} %get-tuple-element.50.refs_0_, f32[2,16,48,256]{3,2,1,0:T(8,128)} %get-tuple-element.71.refs_1_, f32[2,18,48,256]{3,2,1,0:T(8,128)} %broadcast_12_refs_2_.2.refs_2_, f32[2,18,48,256]{3,2,1,0:T(8,128)} %pad.26.refs_3_), custom_call_target="tpu_custom_call" | custom-call | flops 117964800 | bytes 14155776 | tf_op jit(solution)/shard_map/pallas_call | solution.py:107
  83.9 1.3 pad_maximum_fusion.3
  85.3 1.9 collective-permute-start.4
  87.2 2.5 collective-permute-start.5
  89.7 10.6 %collective-permute-done.4 = f32[2,2,18,16,256]{4,3,2,1,0:T(8,128)S(1)} collective-permute-done((f32[2,2,18,16,256]{4,3,2,1,0:T(8,128)S(1)}, f32[2,2,18,16,256]{4,3,2,1,0:T(8,128)S(1)}, u32[]{:S(2)}, u32[]{:S(2)}) %collective-permute-start.4) | collective-permute-done | bytes 1179680 | tf_op jit(solution)/shard_map/ppermute | solution.py:46
  100.3 4.4 %collective-permute-done.5 = f32[2,2,18,16,256]{4,3,2,1,0:T(8,128)S(1)} collective-permute-done((f32[2,2,18,16,256]{4,3,2,1,0:T(8,128)S(1)}, f32[2,2,18,16,256]{4,3,2,1,0:T(8,128)S(1)}, u32[]{:S(2)}, u32[]{:S(2)}) %collective-permute-start.5) | collective-permute-done | bytes 1179680 | tf_op jit(solution)/shard_map/ppermute | solution.py:47
  105.0 2.1 slice_bitcast_fusion.2
  107.0 41.4 %shard_map.78 = (f32[2,18,48,256]{3,2,1,0:T(8,128)}, f32[2,18,48,256]{3,2,1,0:T(8,128)}) custom-call(f32[8,16,48,256]{3,2,1,0:T(8,128)} %get-tuple-element.50.refs_0_, f32[2,16,48,256]{3,2,1,0:T(8,128)} %get-tuple-element.71.refs_1_, f32[2,18,48,256]{3,2,1,0:T(8,128)} %get-tuple-element.55.refs_2_, f32[2,18,48,256]{3,2,1,0:T(8,128)} %get-tuple-element.54.refs_3_), custom_call_target="tpu_custom_call" | custom-call | flops 125829120 | bytes 14155776 | tf_op jit(solution)/shard_map/pallas_call | solution.py:107
  148.4 3.3 %fusion.23 = (f32[2,48,256]{2,1,0:T(8,128)S(1)}, f32[2,16,48,256]{3,2,1,0:T(8,128)}) fusion(f32[2,18,48,256]{3,2,1,0:T(8,128)} %get-tuple-element.37, f32[2,18,48,256]{3,2,1,0:T(8,128)} %get-tuple-element.36), kind=kLoop, calls=%fused_computation.96 | loop fusion | flops 761856 | bytes 4816896 | tf_op jit(solution)/shard_map/reduce_sum | solution.py:187
  151.7 1.9 collective-permute-start.6
  153.7 2.6 collective-permute-start.7
  156.3 2.6 collective-permute-done.7
  158.9 1.5 multiply_multiply_fusion
  160.4 1.5 pad.27.refs_3_
  161.9 39.3 %shard_map.79 = (f32[2,18,48,256]{3,2,1,0:T(8,128)}, f32[2,18,48,256]{3,2,1,0:T(8,128)}) custom-call(f32[8,16,48,256]{3,2,1,0:T(8,128)} %get-tuple-element.50.refs_0_, f32[2,16,48,256]{3,2,1,0:T(8,128)} %get-tuple-element.69.refs_1_, f32[2,18,48,256]{3,2,1,0:T(8,128)} %broadcast_12_refs_2_.2.refs_2_, f32[2,18,48,256]{3,2,1,0:T(8,128)} %pad.27.refs_3_), custom_call_target="tpu_custom_call" | custom-call | flops 117964800 | bytes 14155776 | tf_op jit(solution)/shard_map/pallas_call | solution.py:107
  201.2 1.3 pad_maximum_fusion.2
  202.6 1.9 collective-permute-start.8
  204.5 2.5 collective-permute-start.9
  207.7 1.6 constant_dynamic-slice_fusion
  209.3 8.4 %collective-permute-done.8 = f32[2,2,18,16,256]{4,3,2,1,0:T(8,128)S(1)} collective-permute-done((f32[2,2,18,16,256]{4,3,2,1,0:T(8,128)S(1)}, f32[2,2,18,16,256]{4,3,2,1,0:T(8,128)S(1)}, u32[]{:S(2)}, u32[]{:S(2)}) %collective-permute-start.8) | collective-permute-done | bytes 1179680 | tf_op jit(solution)/shard_map/ppermute | solution.py:46
  217.6 4.5 %collective-permute-done.9 = f32[2,2,18,16,256]{4,3,2,1,0:T(8,128)} collective-permute-done((f32[2,2,18,16,256]{4,3,2,1,0:T(8,128)S(1)}, f32[2,2,18,16,256]{4,3,2,1,0:T(8,128)}, u32[]{:S(2)}, u32[]{:S(2)}) %collective-permute-start.9) | collective-permute-done | bytes 1179680 | tf_op jit(solution)/shard_map/ppermute | solution.py:47
  222.1 1.5 pad_maximum_fusion.1
  223.6 2.1 slice_bitcast_fusion
  225.7 41.5 %shard_map.80 = (f32[2,18,48,256]{3,2,1,0:T(8,128)}, f32[2,18,48,256]{3,2,1,0:T(8,128)}) custom-call(f32[8,16,48,256]{3,2,1,0:T(8,128)} %get-tuple-element.50.refs_0_, f32[2,16,48,256]{3,2,1,0:T(8,128)} %get-tuple-element.69.refs_1_, f32[2,18,48,256]{3,2,1,0:T(8,128)} %get-tuple-element.53.refs_2_, f32[2,18,48,256]{3,2,1,0:T(8,128)} %get-tuple-element.52.refs_3_), custom_call_target="tpu_custom_call" | custom-call | flops 125829120 | bytes 14155776 | tf_op jit(solution)/shard_map/pallas_call | solution.py:107
  267.2 1.0 fusion.14
  268.2 1.4 fusion.21
  (35 shorter events, 5.4 us)
Async XLA Ops:
  4.3 4.8 %collective-permute-start = (f32[13,16,128]{2,1,0:T(8,128)S(1)}, f32[13,16,128]{2,1,0:T(8,128)S(1)}, u32[]{:S(2)}, u32[]{:S(2)}) collective-permute-start(f32[13,16,128]{2,1,0:T(8,128)S(1)} %constant_dynamic-update-slice_fusion), channel_id=1, source_target_pairs={{0,2},{2,0},{1,3},{3,1},{4,6},{6,4},{5,7},{7,5},{8,10},{10,8},{9,1... | collective-permute-start | bytes 319496 | tf_op jit(solution)/shard_map/ppermute | solution.py:57
  9.2 3.9 %collective-permute-start.1 = (f32[8,16,256]{2,1,0:T(8,128)S(1)}, f32[8,16,256]{2,1,0:T(8,128)S(1)}, u32[]{:S(2)}, u32[]{:S(2)}) collective-permute-start(f32[8,16,256]{2,1,0:T(8,128)S(1)} %slice.194), channel_id=1, source_target_pairs={{0,1},{1,0},{2,3},{3,2},{4,5},{5,4},{6,7},{7,6},{8,9},{9,8},{10,11... | collective-permute-start | bytes 393224 | tf_op jit(solution)/shard_map/ppermute | solution.py:57
  13.2 9.9 %collective-permute-start.2 = (f32[21,16,256]{2,1,0:T(8,128)S(1)}, f32[21,16,256]{2,1,0:T(8,128)S(1)}, u32[]{:S(2)}, u32[]{:S(2)}) collective-permute-start(f32[21,16,256]{2,1,0:T(8,128)S(1)} %pad_maximum_fusion.5), channel_id=1, source_target_pairs={{0,4},{4,8},{8,12},{12,16},{16,20},{20,24},{24,28},{1,5},{5,9},{9,... | collective-permute-start | bytes 1032200 | tf_op jit(solution)/shard_map/ppermute | solution.py:46
  18.9 8.6 %collective-permute-start.3 = (f32[21,16,256]{2,1,0:T(8,128)S(1)}, f32[21,16,256]{2,1,0:T(8,128)S(1)}, u32[]{:S(2)}, u32[]{:S(2)}) collective-permute-start(f32[21,16,256]{2,1,0:T(8,128)S(1)} %pad_maximum_fusion.5), channel_id=1, source_target_pairs={{4,0},{8,4},{12,8},{16,12},{20,16},{24,20},{28,24},{5,1},{9,5},{13... | collective-permute-start | bytes 1032200 | tf_op jit(solution)/shard_map/ppermute | solution.py:47
  85.3 15.1 %collective-permute-start.4 = (f32[2,2,18,16,256]{4,3,2,1,0:T(8,128)S(1)}, f32[2,2,18,16,256]{4,3,2,1,0:T(8,128)S(1)}, u32[]{:S(2)}, u32[]{:S(2)}) collective-permute-start(f32[2,2,18,16,256]{4,3,2,1,0:T(8,128)S(1)} %pad_maximum_fusion.3), channel_id=1, source_target_pairs={{0,4},{4,8},{8,12},{12,16},{16,20},{20,24},{24,28},{1,5},{5,9},{9,... | collective-permute-start | bytes 3538952 | tf_op jit(solution)/shard_map/ppermute | solution.py:46
  87.2 17.5 %collective-permute-start.5 = (f32[2,2,18,16,256]{4,3,2,1,0:T(8,128)S(1)}, f32[2,2,18,16,256]{4,3,2,1,0:T(8,128)S(1)}, u32[]{:S(2)}, u32[]{:S(2)}) collective-permute-start(f32[2,2,18,16,256]{4,3,2,1,0:T(8,128)S(1)} %pad_maximum_fusion.3), channel_id=1, source_target_pairs={{4,0},{8,4},{12,8},{16,12},{20,16},{24,20},{28,24},{5,1},{9,5},{13... | collective-permute-start | bytes 3538952 | tf_op jit(solution)/shard_map/ppermute | solution.py:47
  151.7 4.5 %collective-permute-start.6 = (f32[2,16,256]{2,1,0:T(8,128)S(1)}, f32[2,16,256]{2,1,0:T(8,128)S(1)}, u32[]{:S(2)}, u32[]{:S(2)}) collective-permute-start(f32[2,16,256]{2,1,0:T(8,128)S(1)} %slice_multiply_fusion), channel_id=1, source_target_pairs={{0,4},{4,8},{8,12},{12,16},{16,20},{20,24},{24,28},{1,5},{5,9},{9,... | collective-permute-start | bytes 98312 | tf_op jit(solution)/shard_map/ppermute | solution.py:46
  153.7 5.2 %collective-permute-start.7 = (f32[2,16,256]{2,1,0:T(8,128)S(1)}, f32[2,16,256]{2,1,0:T(8,128)S(1)}, u32[]{:S(2)}, u32[]{:S(2)}) collective-permute-start(f32[2,16,256]{2,1,0:T(8,128)S(1)} %slice_multiply_fusion), channel_id=1, source_target_pairs={{4,0},{8,4},{12,8},{16,12},{20,16},{24,20},{28,24},{5,1},{9,5},{13... | collective-permute-start | bytes 98312 | tf_op jit(solution)/shard_map/ppermute | solution.py:47
  202.6 15.1 %collective-permute-start.8 = (f32[2,2,18,16,256]{4,3,2,1,0:T(8,128)S(1)}, f32[2,2,18,16,256]{4,3,2,1,0:T(8,128)S(1)}, u32[]{:S(2)}, u32[]{:S(2)}) collective-permute-start(f32[2,2,18,16,256]{4,3,2,1,0:T(8,128)S(1)} %pad_maximum_fusion.2), channel_id=1, source_target_pairs={{0,4},{4,8},{8,12},{12,16},{16,20},{20,24},{24,28},{1,5},{5,9},{9,... | collective-permute-start | bytes 3538952 | tf_op jit(solution)/shard_map/ppermute | solution.py:46
  204.5 17.6 %collective-permute-start.9 = (f32[2,2,18,16,256]{4,3,2,1,0:T(8,128)S(1)}, f32[2,2,18,16,256]{4,3,2,1,0:T(8,128)}, u32[]{:S(2)}, u32[]{:S(2)}) collective-permute-start(f32[2,2,18,16,256]{4,3,2,1,0:T(8,128)S(1)} %pad_maximum_fusion.2), channel_id=1, source_target_pairs={{4,0},{8,4},{12,8},{16,12},{20,16},{24,20},{28,24},{5,1},{9,5},{13... | collective-permute-start | bytes 3538952 | tf_op jit(solution)/shard_map/ppermute | solution.py:47
  225.7 42.5 %copy-start = (f32[47,256]{1,0:T(8,128)S(1)}, f32[47,256]{1,0:T(8,128)}, u32[]{:S(2)}) copy-start(f32[47,256]{1,0:T(8,128)} %get-tuple-element.62) | copy-start | bytes 144388
  225.7 42.5 %copy-start.1 = (f32[48,255]{1,0:T(8,128)S(1)}, f32[48,255]{1,0:T(8,128)}, u32[]{:S(2)}) copy-start(f32[48,255]{1,0:T(8,128)} %get-tuple-element.74) | copy-start | bytes 146884
  225.7 42.5 %copy-start.2 = (f32[48,255]{1,0:T(8,128)S(1)}, f32[48,255]{1,0:T(8,128)}, u32[]{:S(2)}) copy-start(f32[48,255]{1,0:T(8,128)} %get-tuple-element.75) | copy-start | bytes 146884

commit v5 on v4

--- a/solution.py
+++ b/solution.py
@@ -163,31 +163,48 @@
     table = step_constants()
     layer_pad = ((0, 0), (1, 1), (0, 0), (0, 0))
 
-    def chebyshev(rhs):
-        iterate = jnp.zeros((2, layers + 2) + rhs.shape[2:], jnp.float32)
-        step_dir = jnp.pad(jacobi * rhs / theta_center, layer_pad)
+    def exchange_state(iterate, step_dir):
+        inner = jnp.stack([iterate, step_dir])[:, :, 1 : layers + 1]
+        both = jnp.pad(exchange_rows(inner, k, rows, 3), ((0, 0),) + layer_pad)
+        return both[0], both[1]
+
+    def chebyshev(rhs_list):
+        states = [
+            (
+                jnp.zeros((1, layers + 2) + rhs.shape[2:], jnp.float32),
+                jnp.pad(jacobi * rhs / theta_center, layer_pad),
+            )
+            for rhs in rhs_list
+        ]
         since = 1
         run = []
         for keep, push in table:
             if since == k:
-                iterate, step_dir = run_segment(tuple(run), op_stack, rhs, iterate, step_dir)
+                states = [
+                    exchange_state(*run_segment(tuple(run), op_stack, rhs, *state))
+                    for rhs, state in zip(rhs_list, states)
+                ]
                 run = []
-                both = exchange_rows(jnp.stack([iterate, step_dir]), k, rows, 3)
-                iterate, step_dir = both[0], both[1]
                 since = 0
             run.append((keep, push))
             since += 1
-        iterate, step_dir = run_segment(tuple(run), op_stack, rhs, iterate, step_dir)
-        return (iterate + step_dir)[:, 1 : layers + 1]
+        finals = []
+        for rhs, state in zip(rhs_list, states):
+            iterate, step_dir = run_segment(tuple(run), op_stack, rhs, *state)
+            finals.append((iterate + step_dir)[:, 1 : layers + 1])
+        return finals
 
     forcing = jnp.zeros((2,) + eta.shape, jnp.float32)
     forcing = forcing.at[:, 0].set(-(bed_coef * dir_ext)[None] * bv)
     forcing = forcing * act
-    velocity_ext = chebyshev(forcing)
-    column = jnp.sum(velocity_ext, axis=1) / layers
-    column = exchange_rows(column, k, rows, 1)
-    adjoint_rhs = obs_weight * act * jnp.broadcast_to(column[:, None], velocity_ext.shape)
-    adjoint = chebyshev(adjoint_rhs)
+    velocity_parts = chebyshev([forcing[0:1], forcing[1:2]])
+    adjoint_rhs = []
+    for part in velocity_parts:
+        column = jnp.sum(part, axis=1) / layers
+        column = exchange_rows(column, k, rows, 1)
+        adjoint_rhs.append(obs_weight * act * jnp.broadcast_to(column[:, None], part.shape))
+    adjoint = jnp.concatenate(chebyshev(adjoint_rhs), axis=0)
+    velocity_ext = jnp.concatenate(velocity_parts, axis=0)
 
     bed_term = bed_coef * jnp.sum(bv * adjoint[:, 0], axis=0)
     lap = (

time: 270 us -> 365 us (1.35)
  Pallas kernels: 162 us -> 251 us
  waiting for transfers between devices: 42.8 us -> 25.9 us
  starting transfers between devices: 23.9 us -> 39.1 us
  other arithmetic: 26.6 us -> 31.1 us
    pallas_call x4 -> x8, Pallas kernels: 162 us -> 251 us  [run_segment(): pl.pallas_call(lambda *refs: segment_kernel(steps, *refs), out_shape=(jax...]
    ppermute x4 -> x7, waiting for transfers between devices: 21.2 us -> 4.09 us  [exchange_rows(): lax.ppermute(lax.slice_in_dim(own, rows - k, rows, axis=axis), 'mx', forw...]
    ppermute x4 -> x7, starting transfers between devices: 11.4 us -> 19.4 us  [exchange_rows(): lax.ppermute(lax.slice_in_dim(own, rows - k, rows, axis=axis), 'mx', forw...]
    ppermute x4 -> x7, starting transfers between devices: 9.46 us -> 16.7 us  [exchange_rows(): high = lax.ppermute(lax.slice_in_dim(own, 0, k, axis=axis), 'mx', backward)]
    ppermute x4 -> x7, waiting for transfers between devices: 15.9 us -> 16.1 us  [exchange_rows(): high = lax.ppermute(lax.slice_in_dim(own, 0, k, axis=axis), 'mx', backward)]
  transfers between devices with their start and end apart: 10 -> 16, of which waited for: 9 -> 9; matrix products, arithmetic and copies ran while one was open for 1% -> 3% of each run, Pallas kernels for 0% -> 17%
where the time goes in v5:
time: 365 us; the launch traced here: 364 us
  Pallas kernels  251 us (69%)
  starting transfers between devices  39.1 us (11%)
  other arithmetic  31.1 us (9%)
  waiting for transfers between devices  25.9 us (7%)
  local copies, waits for them, and re-layouts  16.2 us (4%)
    pallas_call x8, Pallas kernels, run_segment(): pl.pallas_call(lambda *refs: segment_kernel(steps, *refs), out_shape=(jax...  251 us
    ppermute x7, starting transfers between devices, exchange_rows(): lax.ppermute(lax.slice_in_dim(own, rows - k, rows, axis=axis), 'mx', forw...  19.4 us
    ppermute x7, starting transfers between devices, exchange_rows(): high = lax.ppermute(lax.slice_in_dim(own, 0, k, axis=axis), 'mx', backward)  16.7 us
    ppermute x7, waiting for transfers between devices, exchange_rows(): high = lax.ppermute(lax.slice_in_dim(own, 0, k, axis=axis), 'mx', backward)  16.1 us
    unnamed x9, other arithmetic  9.43 us
  transfers between devices with their start and end apart: 16, of which 9 were waited for; matrix products, arithmetic and copies ran while one was open for 3% of the time, Pallas kernels for 17%

profile of v5, /device:TPU:1, one launch (start us, length us, event | category | flops | bytes accessed | tf_op | source)
XLA Modules:
  0.0 364.0 jit_solution(11180688340180516821)
XLA Ops:
  4.3 2.1 collective-permute-start
  6.4 2.7 collective-permute-done
  10.1 3.0 collective-permute-done.1
  13.2 5.7 %collective-permute-start.2 = (f32[21,16,256]{2,1,0:T(8,128)S(1)}, f32[21,16,256]{2,1,0:T(8,128)S(1)}, u32[]{:S(2)}, u32[]{:S(2)}) collective-permute-start(f32[21,16,256]{2,1,0:T(8,128)S(1)} %pad_maximum_fusion.5), channel_id=1, source_target_pairs={{0,4},{4,8},{8,12},{12,16},{16,20},{20,24},{24,28},{1,5},{5,9},{9,... | collective-permute-start | bytes 1032200 | tf_op jit(solution)/shard_map/ppermute | solution.py:46
  18.9 1.9 collective-permute-start.3
  20.8 2.2 collective-permute-done.2
  23.0 4.4 %collective-permute-done.3 = f32[21,16,256]{2,1,0:T(8,128)S(1)} collective-permute-done((f32[21,16,256]{2,1,0:T(8,128)S(1)}, f32[21,16,256]{2,1,0:T(8,128)S(1)}, u32[]{:S(2)}, u32[]{:S(2)}) %collective-permute-start.3) | collective-permute-done | bytes 344096 | tf_op jit(solution)/shard_map/ppermute | solution.py:47
  32.1 1.2 bitcast_dynamic-update-slice_fusion.5
  34.5 1.4 multiply_add_fusion
  35.9 1.2 bitcast_dynamic-update-slice_fusion.3
  37.1 1.2 bitcast_dynamic-update-slice_fusion.2
  39.3 1.6 fusion.7
  42.9 30.4 %shard_map.81 = (f32[1,18,48,256]{3,2,1,0:T(8,128)}, f32[1,18,48,256]{3,2,1,0:T(8,128)}) custom-call(f32[8,16,48,256]{3,2,1,0:T(8,128)} %get-tuple-element.92.refs_0_, f32[1,16,48,256]{3,2,1,0:T(8,128)} %get-tuple-element.78.refs_1_, f32[1,18,48,256]{3,2,1,0:T(8,128)} %broadcast_16_refs_2_.2.refs_2_, f32[1,18,48,256]{3,2,1,0:T(8,128)} %pad.49.refs_3_), custom_call_target="tpu_custom_call" | custom-call | flops 58982400 | bytes 7077888 | tf_op jit(solution)/shard_map/pallas_call | solution.py:107
  74.4 1.9 collective-permute-start.10
  76.3 3.2 collective-permute-start.11
  80.5 30.5 %shard_map.77 = (f32[1,18,48,256]{3,2,1,0:T(8,128)}, f32[1,18,48,256]{3,2,1,0:T(8,128)}) custom-call(f32[8,16,48,256]{3,2,1,0:T(8,128)} %get-tuple-element.92.refs_0_, f32[1,16,48,256]{3,2,1,0:T(8,128)} %get-tuple-element.79.refs_1_, f32[1,18,48,256]{3,2,1,0:T(8,128)} %broadcast_16_refs_2_.2.refs_2_, f32[1,18,48,256]{3,2,1,0:T(8,128)} %pad.45.refs_3_), custom_call_target="tpu_custom_call" | custom-call | flops 58982400 | bytes 7077888 | tf_op jit(solution)/shard_map/pallas_call | solution.py:107
  112.1 2.4 collective-permute-start.4
  114.5 2.0 collective-permute-start.5
  116.5 1.4 select_maximum_fusion.2
  117.9 1.4 slice_bitcast_fusion.2
  119.3 1.3 collective-permute-done.4
  120.6 4.4 %collective-permute-done.5 = f32[2,1,16,16,256]{4,3,2,1,0:T(8,128)S(1)} collective-permute-done((f32[2,1,16,16,256]{4,3,2,1,0:T(8,128)S(1)}, f32[2,1,16,16,256]{4,3,2,1,0:T(8,128)S(1)}, u32[]{:S(2)}, u32[]{:S(2)}) %collective-permute-start.5) | collective-permute-done | bytes 524320 | tf_op jit(solution)/shard_map/ppermute | solution.py:47
  125.2 1.3 slice_bitcast_fusion.6
  126.5 32.2 %shard_map.82 = (f32[1,18,48,256]{3,2,1,0:T(8,128)}, f32[1,18,48,256]{3,2,1,0:T(8,128)}) custom-call(f32[8,16,48,256]{3,2,1,0:T(8,128)} %get-tuple-element.92.refs_0_, f32[1,16,48,256]{3,2,1,0:T(8,128)} %get-tuple-element.78.refs_1_, f32[1,18,48,256]{3,2,1,0:T(8,128)} %get-tuple-element.77.refs_2_, f32[1,18,48,256]{3,2,1,0:T(8,128)} %get-tuple-element.76.refs_3_), custom_call_target="tpu_custom_call" | custom-call | flops 62914560 | bytes 7077888 | tf_op jit(solution)/shard_map/pallas_call | solution.py:107
  158.7 32.1 %shard_map.78 = (f32[1,18,48,256]{3,2,1,0:T(8,128)}, f32[1,18,48,256]{3,2,1,0:T(8,128)}) custom-call(f32[8,16,48,256]{3,2,1,0:T(8,128)} %get-tuple-element.92.refs_0_, f32[1,16,48,256]{3,2,1,0:T(8,128)} %get-tuple-element.79.refs_1_, f32[1,18,48,256]{3,2,1,0:T(8,128)} %get-tuple-element.73.refs_2_, f32[1,18,48,256]{3,2,1,0:T(8,128)} %get-tuple-element.72.refs_3_), custom_call_target="tpu_custom_call" | custom-call | flops 62914560 | bytes 7077888 | tf_op jit(solution)/shard_map/pallas_call | solution.py:107
  190.8 2.1 fusion.29
  193.0 1.9 collective-permute-start.12
  194.9 2.4 collective-permute-start.13
  197.3 3.2 collective-permute-start.6
  200.5 2.1 collective-permute-start.7
  202.6 2.9 collective-permute-done.7
  205.6 1.2 multiply_bitcast_fusion.1
  208.9 30.5 %shard_map.79 = (f32[1,18,48,256]{3,2,1,0:T(8,128)}, f32[1,18,48,256]{3,2,1,0:T(8,128)}) custom-call(f32[8,16,48,256]{3,2,1,0:T(8,128)} %get-tuple-element.92.refs_0_, f32[1,16,48,256]{3,2,1,0:T(8,128)} %mul.259.refs_1_, f32[1,18,48,256]{3,2,1,0:T(8,128)} %broadcast_16_refs_2_.2.refs_2_, f32[1,18,48,256]{3,2,1,0:T(8,128)} %pad.47.refs_3_), custom_call_target="tpu_custom_call" | custom-call | flops 58982400 | bytes 7077888 | tf_op jit(solution)/shard_map/pallas_call | solution.py:107
  239.3 1.9 pad_maximum_fusion.3
  241.3 1.9 collective-permute-start.8
  243.2 3.2 collective-permute-start.9
  249.1 30.5 %shard_map.83 = (f32[1,18,48,256]{3,2,1,0:T(8,128)}, f32[1,18,48,256]{3,2,1,0:T(8,128)}) custom-call(f32[8,16,48,256]{3,2,1,0:T(8,128)} %get-tuple-element.92.refs_0_, f32[1,16,48,256]{3,2,1,0:T(8,128)} %mul.264.refs_1_, f32[1,18,48,256]{3,2,1,0:T(8,128)} %broadcast_16_refs_2_.2.refs_2_, f32[1,18,48,256]{3,2,1,0:T(8,128)} %pad.51.refs_3_), custom_call_target="tpu_custom_call" | custom-call | flops 58982400 | bytes 7077888 | tf_op jit(solution)/shard_map/pallas_call | solution.py:107
  280.7 2.4 collective-permute-start.14
  283.1 2.0 collective-permute-start.15
  285.8 1.6 select_maximum_fusion.4
  287.4 1.3 slice_bitcast_fusion.4
  289.2 4.4 %collective-permute-done.15 = f32[2,1,16,16,256]{4,3,2,1,0:T(8,128)S(1)} collective-permute-done((f32[2,1,16,16,256]{4,3,2,1,0:T(8,128)S(1)}, f32[2,1,16,16,256]{4,3,2,1,0:T(8,128)S(1)}, u32[]{:S(2)}, u32[]{:S(2)}) %collective-permute-start.15) | collective-permute-done | bytes 524320 | tf_op jit(solution)/shard_map/ppermute | solution.py:47
  293.8 1.3 slice_bitcast_fusion
  295.1 32.2 %shard_map.80 = (f32[1,18,48,256]{3,2,1,0:T(8,128)}, f32[1,18,48,256]{3,2,1,0:T(8,128)}) custom-call(f32[8,16,48,256]{3,2,1,0:T(8,128)} %get-tuple-element.92.refs_0_, f32[1,16,48,256]{3,2,1,0:T(8,128)} %mul.259.refs_1_, f32[1,18,48,256]{3,2,1,0:T(8,128)} %get-tuple-element.71.refs_2_, f32[1,18,48,256]{3,2,1,0:T(8,128)} %get-tuple-element.70.refs_3_), custom_call_target="tpu_custom_call" | custom-call | flops 62914560 | bytes 7077888 | tf_op jit(solution)/shard_map/pallas_call | solution.py:107
  327.4 1.5 slice_add_fusion.2
  328.9 32.1 %shard_map.84 = (f32[1,18,48,256]{3,2,1,0:T(8,128)}, f32[1,18,48,256]{3,2,1,0:T(8,128)}) custom-call(f32[8,16,48,256]{3,2,1,0:T(8,128)} %get-tuple-element.92.refs_0_, f32[1,16,48,256]{3,2,1,0:T(8,128)} %mul.264.refs_1_, f32[1,18,48,256]{3,2,1,0:T(8,128)} %get-tuple-element.75.refs_2_, f32[1,18,48,256]{3,2,1,0:T(8,128)} %get-tuple-element.74.refs_3_), custom_call_target="tpu_custom_call" | custom-call | flops 62914560 | bytes 7077888 | tf_op jit(solution)/shard_map/pallas_call | solution.py:107
  361.0 1.5 slice_add_fusion
  362.5 1.4 fusion.27
  (70 shorter events, 24.2 us)
Async XLA Ops:
  4.3 4.8 %collective-permute-start = (f32[13,16,128]{2,1,0:T(8,128)S(1)}, f32[13,16,128]{2,1,0:T(8,128)S(1)}, u32[]{:S(2)}, u32[]{:S(2)}) collective-permute-start(f32[13,16,128]{2,1,0:T(8,128)S(1)} %constant_dynamic-update-slice_fusion), channel_id=1, source_target_pairs={{0,2},{2,0},{1,3},{3,1},{4,6},{6,4},{5,7},{7,5},{8,10},{10,8},{9,1... | collective-permute-start | bytes 319496 | tf_op jit(solution)/shard_map/ppermute | solution.py:57
  9.2 3.9 %collective-permute-start.1 = (f32[8,16,256]{2,1,0:T(8,128)S(1)}, f32[8,16,256]{2,1,0:T(8,128)S(1)}, u32[]{:S(2)}, u32[]{:S(2)}) collective-permute-start(f32[8,16,256]{2,1,0:T(8,128)S(1)} %slice.248), channel_id=1, source_target_pairs={{0,1},{1,0},{2,3},{3,2},{4,5},{5,4},{6,7},{7,6},{8,9},{9,8},{10,11... | collective-permute-start | bytes 393224 | tf_op jit(solution)/shard_map/ppermute | solution.py:57
  13.2 9.9 %collective-permute-start.2 = (f32[21,16,256]{2,1,0:T(8,128)S(1)}, f32[21,16,256]{2,1,0:T(8,128)S(1)}, u32[]{:S(2)}, u32[]{:S(2)}) collective-permute-start(f32[21,16,256]{2,1,0:T(8,128)S(1)} %pad_maximum_fusion.5), channel_id=1, source_target_pairs={{0,4},{4,8},{8,12},{12,16},{16,20},{20,24},{24,28},{1,5},{5,9},{9,... | collective-permute-start | bytes 1032200 | tf_op jit(solution)/shard_map/ppermute | solution.py:46
  18.9 8.6 %collective-permute-start.3 = (f32[21,16,256]{2,1,0:T(8,128)S(1)}, f32[21,16,256]{2,1,0:T(8,128)S(1)}, u32[]{:S(2)}, u32[]{:S(2)}) collective-permute-start(f32[21,16,256]{2,1,0:T(8,128)S(1)} %pad_maximum_fusion.5), channel_id=1, source_target_pairs={{4,0},{8,4},{12,8},{16,12},{20,16},{24,20},{28,24},{5,1},{9,5},{13... | collective-permute-start | bytes 1032200 | tf_op jit(solution)/shard_map/ppermute | solution.py:47
  29.6 8.7 %copy-start.1 = (f32[1,48,256]{2,1,0:T(8,128)}, f32[1,48,256]{2,1,0:T(8,128)S(1)}, u32[]{:S(2)}) copy-start(f32[1,48,256]{2,1,0:T(8,128)S(1)} %get-tuple-element.65) | copy-start | bytes 147460
  74.4 42.1 %collective-permute-start.10 = (f32[2,1,16,16,256]{4,3,2,1,0:T(8,128)S(1)}, f32[2,1,16,16,256]{4,3,2,1,0:T(8,128)}, u32[]{:S(2)}, u32[]{:S(2)}) collective-permute-start(f32[2,1,16,16,256]{4,3,2,1,0:T(8,128)S(1)} %pad_maximum_fusion.2), channel_id=1, source_target_pairs={{0,4},{4,8},{8,12},{12,16},{16,20},{20,24},{24,28},{1,5},{5,9},{9,... | collective-permute-start | bytes 1572872 | tf_op jit(solution)/shard_map/ppermute | solution.py:46
  76.3 40.2 %collective-permute-start.11 = (f32[2,1,16,16,256]{4,3,2,1,0:T(8,128)S(1)}, f32[2,1,16,16,256]{4,3,2,1,0:T(8,128)}, u32[]{:S(2)}, u32[]{:S(2)}) collective-permute-start(f32[2,1,16,16,256]{4,3,2,1,0:T(8,128)S(1)} %pad_maximum_fusion.2), channel_id=1, source_target_pairs={{4,0},{8,4},{12,8},{16,12},{20,16},{24,20},{28,24},{5,1},{9,5},{13... | collective-permute-start | bytes 1572872 | tf_op jit(solution)/shard_map/ppermute | solution.py:47
  112.1 8.5 %collective-permute-start.4 = (f32[2,1,16,16,256]{4,3,2,1,0:T(8,128)S(1)}, f32[2,1,16,16,256]{4,3,2,1,0:T(8,128)S(1)}, u32[]{:S(2)}, u32[]{:S(2)}) collective-permute-start(f32[2,1,16,16,256]{4,3,2,1,0:T(8,128)S(1)} %pad_maximum_fusion.4), channel_id=1, source_target_pairs={{0,4},{4,8},{8,12},{12,16},{16,20},{20,24},{24,28},{1,5},{5,9},{9,... | collective-permute-start | bytes 1572872 | tf_op jit(solution)/shard_map/ppermute | solution.py:46
  114.5 10.5 %collective-permute-start.5 = (f32[2,1,16,16,256]{4,3,2,1,0:T(8,128)S(1)}, f32[2,1,16,16,256]{4,3,2,1,0:T(8,128)S(1)}, u32[]{:S(2)}, u32[]{:S(2)}) collective-permute-start(f32[2,1,16,16,256]{4,3,2,1,0:T(8,128)S(1)} %pad_maximum_fusion.4), channel_id=1, source_target_pairs={{4,0},{8,4},{12,8},{16,12},{20,16},{24,20},{28,24},{5,1},{9,5},{13... | collective-permute-start | bytes 1572872 | tf_op jit(solution)/shard_map/ppermute | solution.py:47
  193.0 9.6 %collective-permute-start.12 = (f32[1,16,256]{2,1,0:T(8,128)S(1)}, f32[1,16,256]{2,1,0:T(8,128)S(1)}, u32[]{:S(2)}, u32[]{:S(2)}) collective-permute-start(f32[1,16,256]{2,1,0:T(8,128)S(1)} %slice.274), channel_id=1, source_target_pairs={{0,4},{4,8},{8,12},{12,16},{16,20},{20,24},{24,28},{1,5},{5,9},{9,... | collective-permute-start | bytes 49160 | tf_op jit(solution)/shard_map/ppermute | solution.py:46
  194.9 7.7 %collective-permute-start.13 = (f32[1,16,256]{2,1,0:T(8,128)S(1)}, f32[1,16,256]{2,1,0:T(8,128)S(1)}, u32[]{:S(2)}, u32[]{:S(2)}) collective-permute-start(f32[1,16,256]{2,1,0:T(8,128)S(1)} %slice.274), channel_id=1, source_target_pairs={{4,0},{8,4},{12,8},{16,12},{20,16},{24,20},{28,24},{5,1},{9,5},{13... | collective-permute-start | bytes 49160 | tf_op jit(solution)/shard_map/ppermute | solution.py:47
  197.3 5.3 %collective-permute-start.6 = (f32[1,16,256]{2,1,0:T(8,128)S(1)}, f32[1,16,256]{2,1,0:T(8,128)S(1)}, u32[]{:S(2)}, u32[]{:S(2)}) collective-permute-start(f32[1,16,256]{2,1,0:T(8,128)S(1)} %slice.264), channel_id=1, source_target_pairs={{0,4},{4,8},{8,12},{12,16},{16,20},{20,24},{24,28},{1,5},{5,9},{9,... | collective-permute-start | bytes 49160 | tf_op jit(solution)/shard_map/ppermute | solution.py:46
  200.5 5.1 %collective-permute-start.7 = (f32[1,16,256]{2,1,0:T(8,128)S(1)}, f32[1,16,256]{2,1,0:T(8,128)S(1)}, u32[]{:S(2)}, u32[]{:S(2)}) collective-permute-start(f32[1,16,256]{2,1,0:T(8,128)S(1)} %slice.264), channel_id=1, source_target_pairs={{4,0},{8,4},{12,8},{16,12},{20,16},{24,20},{28,24},{5,1},{9,5},{13... | collective-permute-start | bytes 49160 | tf_op jit(solution)/shard_map/ppermute | solution.py:47
  239.3 7.7 %copy-start = (f32[1,16,48,256]{3,2,1,0:T(8,128)S(1)}, f32[1,16,48,256]{3,2,1,0:T(8,128)}, u32[]{:S(2)}) copy-start(f32[1,16,48,256]{3,2,1,0:T(8,128)} %get-tuple-element.91) | copy-start | bytes 2359300
  241.3 44.5 %collective-permute-start.8 = (f32[2,1,16,16,256]{4,3,2,1,0:T(8,128)}, f32[2,1,16,16,256]{4,3,2,1,0:T(8,128)}, u32[]{:S(2)}, u32[]{:S(2)}) collective-permute-start(f32[2,1,16,16,256]{4,3,2,1,0:T(8,128)} %pad_maximum_fusion.3), channel_id=1, source_target_pairs={{0,4},{4,8},{8,12},{12,16},{16,20},{20,24},{24,28},{1,5},{5,9},{9,... | collective-permute-start | bytes 1572872 | tf_op jit(solution)/shard_map/ppermute | solution.py:46
  243.2 42.6 %collective-permute-start.9 = (f32[2,1,16,16,256]{4,3,2,1,0:T(8,128)}, f32[2,1,16,16,256]{4,3,2,1,0:T(8,128)}, u32[]{:S(2)}, u32[]{:S(2)}) collective-permute-start(f32[2,1,16,16,256]{4,3,2,1,0:T(8,128)} %pad_maximum_fusion.3), channel_id=1, source_target_pairs={{4,0},{8,4},{12,8},{16,12},{20,16},{24,20},{28,24},{5,1},{9,5},{13... | collective-permute-start | bytes 1572872 | tf_op jit(solution)/shard_map/ppermute | solution.py:47
  280.7 8.5 %collective-permute-start.14 = (f32[2,1,16,16,256]{4,3,2,1,0:T(8,128)S(1)}, f32[2,1,16,16,256]{4,3,2,1,0:T(8,128)S(1)}, u32[]{:S(2)}, u32[]{:S(2)}) collective-permute-start(f32[2,1,16,16,256]{4,3,2,1,0:T(8,128)S(1)} %pad_maximum_fusion.1), channel_id=1, source_target_pairs={{0,4},{4,8},{8,12},{12,16},{16,20},{20,24},{24,28},{1,5},{5,9},{9,... | collective-permute-start | bytes 1572872 | tf_op jit(solution)/shard_map/ppermute | solution.py:46
  283.1 10.5 %collective-permute-start.15 = (f32[2,1,16,16,256]{4,3,2,1,0:T(8,128)S(1)}, f32[2,1,16,16,256]{4,3,2,1,0:T(8,128)S(1)}, u32[]{:S(2)}, u32[]{:S(2)}) collective-permute-start(f32[2,1,16,16,256]{4,3,2,1,0:T(8,128)S(1)} %pad_maximum_fusion.1), channel_id=1, source_target_pairs={{4,0},{8,4},{12,8},{16,12},{20,16},{24,20},{28,24},{5,1},{9,5},{13... | collective-permute-start | bytes 1572872 | tf_op jit(solution)/shard_map/ppermute | solution.py:47
  361.0 1.5 copy-start.2
  361.0 1.5 copy-start.3
  361.0 1.5 copy-start.4

commit v6 on v4

--- a/solution.py
+++ b/solution.py
@@ -70,42 +70,51 @@
     return jnp.concatenate([z, lax.slice_in_dim(a, 0, n - 1, axis=axis)], axis=axis)
 
 
-def segment_kernel(steps, op_ref, rhs_ref, x_in, d_in, x_ref, d_ref):
+def segment_kernel(steps, start_valid, op_ref, rhs_ref, x_in, d_in, x_ref, d_ref):
     comps, layers = rhs_ref.shape[0], rhs_ref.shape[1]
     rows, cols = rhs_ref.shape[2], rhs_ref.shape[3]
     x_ref[...] = x_in[...]
     d_ref[...] = d_in[...]
 
-    for keep, push in steps:
+    for j, (keep, push) in enumerate(steps):
+        lo = min(8 * ((start_valid + j) // 8), rows // 2 - 8)
+        lo = max(lo, 0)
+        span = pl.ds(lo, rows - 2 * lo)
+        height = rows - 2 * lo
         for c in range(comps):
-            x_ref[c, 1] = x_ref[c, 1] + d_ref[c, 1]
+            x_ref[c, 1, span] = x_ref[c, 1, span] + d_ref[c, 1, span]
 
         def update(layer, carry):
             p = layer + 1
+            c_xm = op_ref[2, layer, span]
+            c_ym = op_ref[3, layer, span]
+            c_xp = pltpu.roll(c_xm, height - 1, 0)
+            c_yp = pltpu.roll(c_ym, cols - 1, 1)
             for c in range(comps):
-                x_ref[c, p + 1] = x_ref[c, p + 1] + d_ref[c, p + 1]
-                centre = x_ref[c, p]
-                beside = op_ref[0, layer] * x_ref[c, p - 1] + op_ref[1, layer] * x_ref[c, p + 1]
-                beside = beside + op_ref[2, layer] * pltpu.roll(centre, 1, 0)
-                beside = beside + op_ref[3, layer] * pltpu.roll(centre, rows - 1, 0)
-                beside = beside + op_ref[4, layer] * pltpu.roll(centre, 1, 1)
-                beside = beside + op_ref[5, layer] * pltpu.roll(centre, cols - 1, 1)
-                resid = rhs_ref[c, layer] - (op_ref[6, layer] * centre - beside)
+                above = x_ref[c, p + 1, span] + d_ref[c, p + 1, span]
+                x_ref[c, p + 1, span] = above
+                centre = x_ref[c, p, span]
+                beside = op_ref[0, layer, span] * x_ref[c, p - 1, span] + op_ref[1, layer, span] * above
+                beside = beside + c_xm * pltpu.roll(centre, 1, 0)
+                beside = beside + c_xp * pltpu.roll(centre, height - 1, 0)
+                beside = beside + c_ym * pltpu.roll(centre, 1, 1)
+                beside = beside + c_yp * pltpu.roll(centre, cols - 1, 1)
+                resid = rhs_ref[c, layer, span] - (op_ref[4, layer, span] * centre - beside)
                 if keep is None:
-                    d_ref[c, p] = op_ref[7, layer] * resid / theta_center
+                    d_ref[c, p, span] = op_ref[5, layer, span] * resid / theta_center
                 else:
-                    d_ref[c, p] = keep * d_ref[c, p] + push * (op_ref[7, layer] * resid)
+                    d_ref[c, p, span] = keep * d_ref[c, p, span] + push * (op_ref[5, layer, span] * resid)
             return carry
 
         lax.fori_loop(0, layers, update, 0)
 
 
-def run_segment(steps, op_stack, rhs, iterate, step_dir):
+def run_segment(steps, start_valid, op_stack, rhs, iterate, step_dir):
     comps, layers, rows, cols = rhs.shape
     vmem = pl.BlockSpec(memory_space=pltpu.VMEM)
     cells = comps * layers * rows * cols
     return pl.pallas_call(
-        lambda *refs: segment_kernel(steps, *refs),
+        lambda *refs: segment_kernel(steps, start_valid, *refs),
         out_shape=(
             jax.ShapeDtypeStruct(iterate.shape, jnp.float32),
             jax.ShapeDtypeStruct(iterate.shape, jnp.float32),
@@ -153,9 +162,7 @@
             act * c_zm,
             act * c_zp,
             act * c_xm * shift(act, 0, -1),
-            act * c_xp * shift(act, 0, 1),
             act * c_ym * shift(act, 1, -1),
-            act * c_yp * shift(act, 1, 1),
             jnp.where(on, diag, 1.0),
             jacobi,
         ]
@@ -167,17 +174,19 @@
         iterate = jnp.zeros((2, layers + 2) + rhs.shape[2:], jnp.float32)
         step_dir = jnp.pad(jacobi * rhs / theta_center, layer_pad)
         since = 1
+        start_valid = 1
         run = []
         for keep, push in table:
             if since == k:
-                iterate, step_dir = run_segment(tuple(run), op_stack, rhs, iterate, step_dir)
+                iterate, step_dir = run_segment(tuple(run), start_valid, op_stack, rhs, iterate, step_dir)
                 run = []
+                start_valid = 0
                 both = exchange_rows(jnp.stack([iterate, step_dir]), k, rows, 3)
                 iterate, step_dir = both[0], both[1]
                 since = 0
             run.append((keep, push))
             since += 1
-        iterate, step_dir = run_segment(tuple(run), op_stack, rhs, iterate, step_dir)
+        iterate, step_dir = run_segment(tuple(run), start_valid, op_stack, rhs, iterate, step_dir)
         return (iterate + step_dir)[:, 1 : layers + 1]
 
     forcing = jnp.zeros((2,) + eta.shape, jnp.float32)

time: 270 us -> 266 us (0.985)
    unnamed x9 -> x7, other arithmetic: 9.44 us -> 7.11 us
where the time goes in v6:
time: 266 us; the launch traced here: 265 us
  Pallas kernels  160 us (60%)
  waiting for transfers between devices  42.8 us (16%)
  other arithmetic  24.3 us (9%)
  starting transfers between devices  23.9 us (9%)
  local copies, waits for them, and re-layouts  13.8 us (5%)
    pallas_call x4, Pallas kernels, run_segment(): pl.pallas_call(lambda *refs: segment_kernel(steps, start_valid, *refs), o...  160 us
    ppermute x4, waiting for transfers between devices, exchange_rows(): lax.ppermute(lax.slice_in_dim(own, rows - k, rows, axis=axis), 'mx', forw...  21.2 us
    ppermute x4, waiting for transfers between devices, exchange_rows(): high = lax.ppermute(lax.slice_in_dim(own, 0, k, axis=axis), 'mx', backward)  15.9 us
    ppermute x4, starting transfers between devices, exchange_rows(): lax.ppermute(lax.slice_in_dim(own, rows - k, rows, axis=axis), 'mx', forw...  11.4 us
    ppermute x4, starting transfers between devices, exchange_rows(): high = lax.ppermute(lax.slice_in_dim(own, 0, k, axis=axis), 'mx', backward)  9.46 us
    unnamed x7, other arithmetic  7.11 us
    ppermute x2, waiting for transfers between devices, gather_axis(): seq.append(lax.ppermute(block, axis, pairs))  5.67 us
  transfers between devices with their start and end apart: 10, of which 9 were waited for; matrix products, arithmetic and copies ran while one was open for 1% of the time, Pallas kernels for 0%

profile of v6, /device:TPU:1, one launch (start us, length us, event | category | flops | bytes accessed | tf_op | source)
XLA Modules:
  0.0 265.2 jit_solution(8414600728612061233)
XLA Ops:
  0.6 0.8 constant_dynamic-update-slice_fusion.4
  2.2 0.7 constant_dynamic-update-slice_fusion.2
  2.9 0.7 constant_dynamic-update-slice_fusion.1
  4.3 2.1 collective-permute-start
  6.4 2.7 %collective-permute-done = f32[13,16,128]{2,1,0:T(8,128)S(1)} collective-permute-done((f32[13,16,128]{2,1,0:T(8,128)S(1)}, f32[13,16,128]{2,1,0:T(8,128)S(1)}, u32[]{:S(2)}, u32[]{:S(2)}) %collective-permute-start) | collective-permute-done | bytes 106528 | tf_op jit(solution)/shard_map/ppermute | solution.py:57
  9.2 0.9 collective-permute-start.1
  10.1 3.0 %collective-permute-done.1 = f32[8,16,256]{2,1,0:T(8,128)S(1)} collective-permute-done((f32[8,16,256]{2,1,0:T(8,128)S(1)}, f32[8,16,256]{2,1,0:T(8,128)S(1)}, u32[]{:S(2)}, u32[]{:S(2)}) %collective-permute-start.1) | collective-permute-done | bytes 131104 | tf_op jit(solution)/shard_map/ppermute | solution.py:57
  13.2 5.7 %collective-permute-start.2 = (f32[21,16,256]{2,1,0:T(8,128)S(1)}, f32[21,16,256]{2,1,0:T(8,128)S(1)}, u32[]{:S(2)}, u32[]{:S(2)}) collective-permute-start(f32[21,16,256]{2,1,0:T(8,128)S(1)} %pad_maximum_fusion.5), channel_id=1, source_target_pairs={{0,4},{4,8},{8,12},{12,16},{16,20},{20,24},{24,28},{1,5},{5,9},{9,... | collective-permute-start | bytes 1032200 | tf_op jit(solution)/shard_map/ppermute | solution.py:46
  18.9 1.9 collective-permute-start.3
  20.8 2.2 collective-permute-done.2
  23.0 4.4 %collective-permute-done.3 = f32[21,16,256]{2,1,0:T(8,128)S(1)} collective-permute-done((f32[21,16,256]{2,1,0:T(8,128)S(1)}, f32[21,16,256]{2,1,0:T(8,128)S(1)}, u32[]{:S(2)}, u32[]{:S(2)}) %collective-permute-start.3) | collective-permute-done | bytes 344096 | tf_op jit(solution)/shard_map/ppermute | solution.py:47
  29.5 1.1 bitcast_dynamic-update-slice_fusion.5
  30.6 1.2 bitcast_dynamic-update-slice_fusion.4
  31.8 1.4 fusion.8
  33.2 1.2 bitcast_dynamic-update-slice_fusion.3
  34.4 1.3 bitcast_dynamic-update-slice_fusion.2
  35.7 0.9 bitcast_dynamic-update-slice_fusion.1
  36.6 1.1 bitcast_dynamic-update-slice_fusion
  37.7 1.5 multiply_multiply_fusion.1
  39.3 1.5 pad.24.refs_3_
  40.7 1.5 broadcast_12_refs_2_.2.refs_2_
  42.2 38.7 %shard_map.77 = (f32[2,18,48,256]{3,2,1,0:T(8,128)}, f32[2,18,48,256]{3,2,1,0:T(8,128)}) custom-call(f32[6,16,48,256]{3,2,1,0:T(8,128)} %get-tuple-element.50.refs_0_, f32[2,16,48,256]{3,2,1,0:T(8,128)} %get-tuple-element.70.refs_1_, f32[2,18,48,256]{3,2,1,0:T(8,128)} %broadcast_12_refs_2_.2.refs_2_, f32[2,18,48,256]{3,2,1,0:T(8,128)} %pad.24.refs_3_), custom_call_target="tpu_custom_call" | custom-call | flops 117964800 | bytes 14155776 | tf_op jit(solution)/shard_map/pallas_call | solution.py:116
  80.9 1.3 pad_maximum_fusion.3
  82.2 1.9 collective-permute-start.4
  84.1 2.5 collective-permute-start.5
  86.6 10.6 %collective-permute-done.4 = f32[2,2,18,16,256]{4,3,2,1,0:T(8,128)S(1)} collective-permute-done((f32[2,2,18,16,256]{4,3,2,1,0:T(8,128)S(1)}, f32[2,2,18,16,256]{4,3,2,1,0:T(8,128)S(1)}, u32[]{:S(2)}, u32[]{:S(2)}) %collective-permute-start.4) | collective-permute-done | bytes 1179680 | tf_op jit(solution)/shard_map/ppermute | solution.py:46
  97.3 4.4 %collective-permute-done.5 = f32[2,2,18,16,256]{4,3,2,1,0:T(8,128)S(1)} collective-permute-done((f32[2,2,18,16,256]{4,3,2,1,0:T(8,128)S(1)}, f32[2,2,18,16,256]{4,3,2,1,0:T(8,128)S(1)}, u32[]{:S(2)}, u32[]{:S(2)}) %collective-permute-start.5) | collective-permute-done | bytes 1179680 | tf_op jit(solution)/shard_map/ppermute | solution.py:47
  101.9 2.1 slice_bitcast_fusion.2
  104.0 41.1 %shard_map.78 = (f32[2,18,48,256]{3,2,1,0:T(8,128)}, f32[2,18,48,256]{3,2,1,0:T(8,128)}) custom-call(f32[6,16,48,256]{3,2,1,0:T(8,128)} %get-tuple-element.50.refs_0_, f32[2,16,48,256]{3,2,1,0:T(8,128)} %get-tuple-element.70.refs_1_, f32[2,18,48,256]{3,2,1,0:T(8,128)} %get-tuple-element.55.refs_2_, f32[2,18,48,256]{3,2,1,0:T(8,128)} %get-tuple-element.54.refs_3_), custom_call_target="tpu_custom_call" | custom-call | flops 125829120 | bytes 14155776 | tf_op jit(solution)/shard_map/pallas_call | solution.py:116
  145.2 3.3 %fusion.27 = (f32[2,48,256]{2,1,0:T(8,128)S(1)}, f32[2,16,48,256]{3,2,1,0:T(8,128)}) fusion(f32[2,18,48,256]{3,2,1,0:T(8,128)} %get-tuple-element.37, f32[2,18,48,256]{3,2,1,0:T(8,128)} %get-tuple-element.36), kind=kLoop, calls=%fused_computation.100 | loop fusion | flops 761856 | bytes 4816896 | tf_op jit(solution)/shard_map/reduce_sum | solution.py:196
  148.5 1.9 collective-permute-start.6
  150.4 2.6 collective-permute-start.7
  153.0 2.6 collective-permute-done.7
  155.6 1.6 multiply_multiply_fusion
  157.2 1.5 pad.25.refs_3_
  158.6 38.7 %shard_map.79 = (f32[2,18,48,256]{3,2,1,0:T(8,128)}, f32[2,18,48,256]{3,2,1,0:T(8,128)}) custom-call(f32[6,16,48,256]{3,2,1,0:T(8,128)} %get-tuple-element.50.refs_0_, f32[2,16,48,256]{3,2,1,0:T(8,128)} %get-tuple-element.68.refs_1_, f32[2,18,48,256]{3,2,1,0:T(8,128)} %broadcast_12_refs_2_.2.refs_2_, f32[2,18,48,256]{3,2,1,0:T(8,128)} %pad.25.refs_3_), custom_call_target="tpu_custom_call" | custom-call | flops 117964800 | bytes 14155776 | tf_op jit(solution)/shard_map/pallas_call | solution.py:116
  197.3 1.3 pad_maximum_fusion.2
  198.6 1.9 collective-permute-start.8
  200.6 2.5 collective-permute-start.9
  203.1 0.7 fusion.31
  203.8 1.6 constant_dynamic-slice_fusion
  205.3 8.4 %collective-permute-done.8 = f32[2,2,18,16,256]{4,3,2,1,0:T(8,128)S(1)} collective-permute-done((f32[2,2,18,16,256]{4,3,2,1,0:T(8,128)S(1)}, f32[2,2,18,16,256]{4,3,2,1,0:T(8,128)S(1)}, u32[]{:S(2)}, u32[]{:S(2)}) %collective-permute-start.8) | collective-permute-done | bytes 1179680 | tf_op jit(solution)/shard_map/ppermute | solution.py:46
  213.7 4.5 %collective-permute-done.9 = f32[2,2,18,16,256]{4,3,2,1,0:T(8,128)} collective-permute-done((f32[2,2,18,16,256]{4,3,2,1,0:T(8,128)S(1)}, f32[2,2,18,16,256]{4,3,2,1,0:T(8,128)}, u32[]{:S(2)}, u32[]{:S(2)}) %collective-permute-start.9) | collective-permute-done | bytes 1179680 | tf_op jit(solution)/shard_map/ppermute | solution.py:47
  218.2 1.5 pad_maximum_fusion.1
  219.7 2.0 slice_bitcast_fusion
  221.7 41.1 %shard_map.80 = (f32[2,18,48,256]{3,2,1,0:T(8,128)}, f32[2,18,48,256]{3,2,1,0:T(8,128)}) custom-call(f32[6,16,48,256]{3,2,1,0:T(8,128)} %get-tuple-element.50.refs_0_, f32[2,16,48,256]{3,2,1,0:T(8,128)} %get-tuple-element.68.refs_1_, f32[2,18,48,256]{3,2,1,0:T(8,128)} %get-tuple-element.53.refs_2_, f32[2,18,48,256]{3,2,1,0:T(8,128)} %get-tuple-element.52.refs_3_), custom_call_target="tpu_custom_call" | custom-call | flops 125829120 | bytes 14155776 | tf_op jit(solution)/shard_map/pallas_call | solution.py:116
  262.8 1.0 fusion.18
  263.8 1.4 fusion.25
  (30 shorter events, 3.9 us)
Async XLA Ops:
  4.3 4.8 %collective-permute-start = (f32[13,16,128]{2,1,0:T(8,128)S(1)}, f32[13,16,128]{2,1,0:T(8,128)S(1)}, u32[]{:S(2)}, u32[]{:S(2)}) collective-permute-start(f32[13,16,128]{2,1,0:T(8,128)S(1)} %constant_dynamic-update-slice_fusion), channel_id=1, source_target_pairs={{0,2},{2,0},{1,3},{3,1},{4,6},{6,4},{5,7},{7,5},{8,10},{10,8},{9,1... | collective-permute-start | bytes 319496 | tf_op jit(solution)/shard_map/ppermute | solution.py:57
  9.2 3.9 %collective-permute-start.1 = (f32[8,16,256]{2,1,0:T(8,128)S(1)}, f32[8,16,256]{2,1,0:T(8,128)S(1)}, u32[]{:S(2)}, u32[]{:S(2)}) collective-permute-start(f32[8,16,256]{2,1,0:T(8,128)S(1)} %slice.181), channel_id=1, source_target_pairs={{0,1},{1,0},{2,3},{3,2},{4,5},{5,4},{6,7},{7,6},{8,9},{9,8},{10,11... | collective-permute-start | bytes 393224 | tf_op jit(solution)/shard_map/ppermute | solution.py:57
  13.2 9.9 %collective-permute-start.2 = (f32[21,16,256]{2,1,0:T(8,128)S(1)}, f32[21,16,256]{2,1,0:T(8,128)S(1)}, u32[]{:S(2)}, u32[]{:S(2)}) collective-permute-start(f32[21,16,256]{2,1,0:T(8,128)S(1)} %pad_maximum_fusion.5), channel_id=1, source_target_pairs={{0,4},{4,8},{8,12},{12,16},{16,20},{20,24},{24,28},{1,5},{5,9},{9,... | collective-permute-start | bytes 1032200 | tf_op jit(solution)/shard_map/ppermute | solution.py:46
  18.9 8.6 %collective-permute-start.3 = (f32[21,16,256]{2,1,0:T(8,128)S(1)}, f32[21,16,256]{2,1,0:T(8,128)S(1)}, u32[]{:S(2)}, u32[]{:S(2)}) collective-permute-start(f32[21,16,256]{2,1,0:T(8,128)S(1)} %pad_maximum_fusion.5), channel_id=1, source_target_pairs={{4,0},{8,4},{12,8},{16,12},{20,16},{24,20},{28,24},{5,1},{9,5},{13... | collective-permute-start | bytes 1032200 | tf_op jit(solution)/shard_map/ppermute | solution.py:47
  82.2 15.1 %collective-permute-start.4 = (f32[2,2,18,16,256]{4,3,2,1,0:T(8,128)S(1)}, f32[2,2,18,16,256]{4,3,2,1,0:T(8,128)S(1)}, u32[]{:S(2)}, u32[]{:S(2)}) collective-permute-start(f32[2,2,18,16,256]{4,3,2,1,0:T(8,128)S(1)} %pad_maximum_fusion.3), channel_id=1, source_target_pairs={{0,4},{4,8},{8,12},{12,16},{16,20},{20,24},{24,28},{1,5},{5,9},{9,... | collective-permute-start | bytes 3538952 | tf_op jit(solution)/shard_map/ppermute | solution.py:46
  84.1 17.5 %collective-permute-start.5 = (f32[2,2,18,16,256]{4,3,2,1,0:T(8,128)S(1)}, f32[2,2,18,16,256]{4,3,2,1,0:T(8,128)S(1)}, u32[]{:S(2)}, u32[]{:S(2)}) collective-permute-start(f32[2,2,18,16,256]{4,3,2,1,0:T(8,128)S(1)} %pad_maximum_fusion.3), channel_id=1, source_target_pairs={{4,0},{8,4},{12,8},{16,12},{20,16},{24,20},{28,24},{5,1},{9,5},{13... | collective-permute-start | bytes 3538952 | tf_op jit(solution)/shard_map/ppermute | solution.py:47
  148.5 4.5 %collective-permute-start.6 = (f32[2,16,256]{2,1,0:T(8,128)S(1)}, f32[2,16,256]{2,1,0:T(8,128)S(1)}, u32[]{:S(2)}, u32[]{:S(2)}) collective-permute-start(f32[2,16,256]{2,1,0:T(8,128)S(1)} %slice_multiply_fusion), channel_id=1, source_target_pairs={{0,4},{4,8},{8,12},{12,16},{16,20},{20,24},{24,28},{1,5},{5,9},{9,... | collective-permute-start | bytes 98312 | tf_op jit(solution)/shard_map/ppermute | solution.py:46
  150.4 5.2 %collective-permute-start.7 = (f32[2,16,256]{2,1,0:T(8,128)S(1)}, f32[2,16,256]{2,1,0:T(8,128)S(1)}, u32[]{:S(2)}, u32[]{:S(2)}) collective-permute-start(f32[2,16,256]{2,1,0:T(8,128)S(1)} %slice_multiply_fusion), channel_id=1, source_target_pairs={{4,0},{8,4},{12,8},{16,12},{20,16},{24,20},{28,24},{5,1},{9,5},{13... | collective-permute-start | bytes 98312 | tf_op jit(solution)/shard_map/ppermute | solution.py:47
  198.6 15.1 %collective-permute-start.8 = (f32[2,2,18,16,256]{4,3,2,1,0:T(8,128)S(1)}, f32[2,2,18,16,256]{4,3,2,1,0:T(8,128)S(1)}, u32[]{:S(2)}, u32[]{:S(2)}) collective-permute-start(f32[2,2,18,16,256]{4,3,2,1,0:T(8,128)S(1)} %pad_maximum_fusion.2), channel_id=1, source_target_pairs={{0,4},{4,8},{8,12},{12,16},{16,20},{20,24},{24,28},{1,5},{5,9},{9,... | collective-permute-start | bytes 3538952 | tf_op jit(solution)/shard_map/ppermute | solution.py:46
  200.6 17.6 %collective-permute-start.9 = (f32[2,2,18,16,256]{4,3,2,1,0:T(8,128)S(1)}, f32[2,2,18,16,256]{4,3,2,1,0:T(8,128)}, u32[]{:S(2)}, u32[]{:S(2)}) collective-permute-start(f32[2,2,18,16,256]{4,3,2,1,0:T(8,128)S(1)} %pad_maximum_fusion.2), channel_id=1, source_target_pairs={{4,0},{8,4},{12,8},{16,12},{20,16},{24,20},{28,24},{5,1},{9,5},{13... | collective-permute-start | bytes 3538952 | tf_op jit(solution)/shard_map/ppermute | solution.py:47
  221.7 42.1 %copy-start = (f32[47,256]{1,0:T(8,128)S(1)}, f32[47,256]{1,0:T(8,128)}, u32[]{:S(2)}) copy-start(f32[47,256]{1,0:T(8,128)} %get-tuple-element.62) | copy-start | bytes 144388
  221.7 42.1 %copy-start.1 = (f32[48,255]{1,0:T(8,128)S(1)}, f32[48,255]{1,0:T(8,128)}, u32[]{:S(2)}) copy-start(f32[48,255]{1,0:T(8,128)} %get-tuple-element.71) | copy-start | bytes 146884
  221.7 42.1 %copy-start.2 = (f32[48,255]{1,0:T(8,128)S(1)}, f32[48,255]{1,0:T(8,128)}, u32[]{:S(2)}) copy-start(f32[48,255]{1,0:T(8,128)} %get-tuple-element.72) | copy-start | bytes 146884

commit v7 on v6

--- a/solution.py
+++ b/solution.py
@@ -106,7 +106,7 @@
                     d_ref[c, p, span] = keep * d_ref[c, p, span] + push * (op_ref[5, layer, span] * resid)
             return carry
 
-        lax.fori_loop(0, layers, update, 0)
+        lax.fori_loop(0, layers, update, 0, unroll=4)
 
 
 def run_segment(steps, start_valid, op_stack, rhs, iterate, step_dir):

time: 266 us -> 219 us (0.82)
  Pallas kernels: 160 us -> 113 us
    pallas_call x4, Pallas kernels: 160 us -> 113 us  [run_segment(): pl.pallas_call(lambda *refs: segment_kernel(steps, start_valid, *refs), o...]
where the time goes in v7:
time: 219 us; the launch traced here: 218 us
  Pallas kernels  113 us (52%)
  waiting for transfers between devices  42.4 us (19%)
  other arithmetic  24.3 us (11%)
  starting transfers between devices  24.3 us (11%)
  local copies, waits for them, and re-layouts  13.8 us (6%)
    pallas_call x4, Pallas kernels, run_segment(): pl.pallas_call(lambda *refs: segment_kernel(steps, start_valid, *refs), o...  113 us
    ppermute x4, waiting for transfers between devices, exchange_rows(): lax.ppermute(lax.slice_in_dim(own, rows - k, rows, axis=axis), 'mx', forw...  20.8 us
    ppermute x4, waiting for transfers between devices, exchange_rows(): high = lax.ppermute(lax.slice_in_dim(own, 0, k, axis=axis), 'mx', backward)  15.9 us
    ppermute x4, starting transfers between devices, exchange_rows(): lax.ppermute(lax.slice_in_dim(own, rows - k, rows, axis=axis), 'mx', forw...  11.4 us
    ppermute x4, starting transfers between devices, exchange_rows(): high = lax.ppermute(lax.slice_in_dim(own, 0, k, axis=axis), 'mx', backward)  9.94 us
    unnamed x7, other arithmetic  7.11 us
    ppermute x2, waiting for transfers between devices, gather_axis(): seq.append(lax.ppermute(block, axis, pairs))  5.67 us
  transfers between devices with their start and end apart: 10, of which 9 were waited for; matrix products, arithmetic and copies ran while one was open for 1% of the time, Pallas kernels for 0%

profile of v7, /device:TPU:1, one launch (start us, length us, event | category | flops | bytes accessed | tf_op | source)
XLA Modules:
  0.0 218.4 jit_solution(8326651573530609971)
XLA Ops:
  0.6 0.8 constant_dynamic-update-slice_fusion.4
  2.2 0.7 constant_dynamic-update-slice_fusion.2
  2.9 0.7 constant_dynamic-update-slice_fusion.1
  4.3 2.1 collective-permute-start
  6.4 2.7 %collective-permute-done = f32[13,16,128]{2,1,0:T(8,128)S(1)} collective-permute-done((f32[13,16,128]{2,1,0:T(8,128)S(1)}, f32[13,16,128]{2,1,0:T(8,128)S(1)}, u32[]{:S(2)}, u32[]{:S(2)}) %collective-permute-start) | collective-permute-done | bytes 106528 | tf_op jit(solution)/shard_map/ppermute | solution.py:57
  9.2 0.9 collective-permute-start.1
  10.1 3.0 %collective-permute-done.1 = f32[8,16,256]{2,1,0:T(8,128)S(1)} collective-permute-done((f32[8,16,256]{2,1,0:T(8,128)S(1)}, f32[8,16,256]{2,1,0:T(8,128)S(1)}, u32[]{:S(2)}, u32[]{:S(2)}) %collective-permute-start.1) | collective-permute-done | bytes 131104 | tf_op jit(solution)/shard_map/ppermute | solution.py:57
  13.2 5.7 %collective-permute-start.2 = (f32[21,16,256]{2,1,0:T(8,128)S(1)}, f32[21,16,256]{2,1,0:T(8,128)S(1)}, u32[]{:S(2)}, u32[]{:S(2)}) collective-permute-start(f32[21,16,256]{2,1,0:T(8,128)S(1)} %pad_maximum_fusion.5), channel_id=1, source_target_pairs={{0,4},{4,8},{8,12},{12,16},{16,20},{20,24},{24,28},{1,5},{5,9},{9,... | collective-permute-start | bytes 1032200 | tf_op jit(solution)/shard_map/ppermute | solution.py:46
  18.9 1.9 collective-permute-start.3
  20.8 2.2 %collective-permute-done.2 = f32[21,16,256]{2,1,0:T(8,128)S(1)} collective-permute-done((f32[21,16,256]{2,1,0:T(8,128)S(1)}, f32[21,16,256]{2,1,0:T(8,128)S(1)}, u32[]{:S(2)}, u32[]{:S(2)}) %collective-permute-start.2) | collective-permute-done | bytes 344096 | tf_op jit(solution)/shard_map/ppermute | solution.py:46
  23.0 4.4 %collective-permute-done.3 = f32[21,16,256]{2,1,0:T(8,128)S(1)} collective-permute-done((f32[21,16,256]{2,1,0:T(8,128)S(1)}, f32[21,16,256]{2,1,0:T(8,128)S(1)}, u32[]{:S(2)}, u32[]{:S(2)}) %collective-permute-start.3) | collective-permute-done | bytes 344096 | tf_op jit(solution)/shard_map/ppermute | solution.py:47
  29.5 1.1 bitcast_dynamic-update-slice_fusion.5
  30.6 1.2 bitcast_dynamic-update-slice_fusion.4
  31.8 1.4 fusion.8
  33.2 1.2 bitcast_dynamic-update-slice_fusion.3
  34.4 1.3 bitcast_dynamic-update-slice_fusion.2
  35.7 0.9 bitcast_dynamic-update-slice_fusion.1
  36.6 1.1 bitcast_dynamic-update-slice_fusion
  37.7 1.5 multiply_multiply_fusion.1
  39.3 1.5 pad.24.refs_3_
  40.7 1.5 broadcast_12_refs_2_.2.refs_2_
  42.2 27.4 %shard_map.77 = (f32[2,18,48,256]{3,2,1,0:T(8,128)}, f32[2,18,48,256]{3,2,1,0:T(8,128)}) custom-call(f32[6,16,48,256]{3,2,1,0:T(8,128)} %get-tuple-element.50.refs_0_, f32[2,16,48,256]{3,2,1,0:T(8,128)} %get-tuple-element.70.refs_1_, f32[2,18,48,256]{3,2,1,0:T(8,128)} %broadcast_12_refs_2_.2.refs_2_, f32[2,18,48,256]{3,2,1,0:T(8,128)} %pad.24.refs_3_), custom_call_target="tpu_custom_call" | custom-call | flops 117964800 | bytes 14155776 | tf_op jit(solution)/shard_map/pallas_call | solution.py:116
  69.6 1.3 pad_maximum_fusion.3
  70.9 1.9 collective-permute-start.4
  72.8 2.7 %collective-permute-start.5 = (f32[2,2,18,16,256]{4,3,2,1,0:T(8,128)S(1)}, f32[2,2,18,16,256]{4,3,2,1,0:T(8,128)S(1)}, u32[]{:S(2)}, u32[]{:S(2)}) collective-permute-start(f32[2,2,18,16,256]{4,3,2,1,0:T(8,128)S(1)} %pad_maximum_fusion.3), channel_id=1, source_target_pairs={{4,0},{8,4},{12,8},{16,12},{20,16},{24,20},{28,24},{5,1},{9,5},{13... | collective-permute-start | bytes 3538952 | tf_op jit(solution)/shard_map/ppermute | solution.py:47
  75.5 10.5 %collective-permute-done.4 = f32[2,2,18,16,256]{4,3,2,1,0:T(8,128)S(1)} collective-permute-done((f32[2,2,18,16,256]{4,3,2,1,0:T(8,128)S(1)}, f32[2,2,18,16,256]{4,3,2,1,0:T(8,128)S(1)}, u32[]{:S(2)}, u32[]{:S(2)}) %collective-permute-start.4) | collective-permute-done | bytes 1179680 | tf_op jit(solution)/shard_map/ppermute | solution.py:46
  86.0 4.4 %collective-permute-done.5 = f32[2,2,18,16,256]{4,3,2,1,0:T(8,128)S(1)} collective-permute-done((f32[2,2,18,16,256]{4,3,2,1,0:T(8,128)S(1)}, f32[2,2,18,16,256]{4,3,2,1,0:T(8,128)S(1)}, u32[]{:S(2)}, u32[]{:S(2)}) %collective-permute-start.5) | collective-permute-done | bytes 1179680 | tf_op jit(solution)/shard_map/ppermute | solution.py:47
  90.6 2.1 slice_bitcast_fusion.2
  92.7 29.0 %shard_map.78 = (f32[2,18,48,256]{3,2,1,0:T(8,128)}, f32[2,18,48,256]{3,2,1,0:T(8,128)}) custom-call(f32[6,16,48,256]{3,2,1,0:T(8,128)} %get-tuple-element.50.refs_0_, f32[2,16,48,256]{3,2,1,0:T(8,128)} %get-tuple-element.70.refs_1_, f32[2,18,48,256]{3,2,1,0:T(8,128)} %get-tuple-element.55.refs_2_, f32[2,18,48,256]{3,2,1,0:T(8,128)} %get-tuple-element.54.refs_3_), custom_call_target="tpu_custom_call" | custom-call | flops 125829120 | bytes 14155776 | tf_op jit(solution)/shard_map/pallas_call | solution.py:116
  121.8 3.3 %fusion.27 = (f32[2,48,256]{2,1,0:T(8,128)S(1)}, f32[2,16,48,256]{3,2,1,0:T(8,128)}) fusion(f32[2,18,48,256]{3,2,1,0:T(8,128)} %get-tuple-element.37, f32[2,18,48,256]{3,2,1,0:T(8,128)} %get-tuple-element.36), kind=kLoop, calls=%fused_computation.100 | loop fusion | flops 761856 | bytes 4816896 | tf_op jit(solution)/shard_map/reduce_sum | solution.py:196
  125.1 1.9 collective-permute-start.6
  127.0 2.6 %collective-permute-start.7 = (f32[2,16,256]{2,1,0:T(8,128)S(1)}, f32[2,16,256]{2,1,0:T(8,128)S(1)}, u32[]{:S(2)}, u32[]{:S(2)}) collective-permute-start(f32[2,16,256]{2,1,0:T(8,128)S(1)} %slice_multiply_fusion), channel_id=1, source_target_pairs={{4,0},{8,4},{12,8},{16,12},{20,16},{24,20},{28,24},{5,1},{9,5},{13... | collective-permute-start | bytes 98312 | tf_op jit(solution)/shard_map/ppermute | solution.py:47
  129.6 2.6 %collective-permute-done.7 = f32[2,16,256]{2,1,0:T(8,128)S(1)} collective-permute-done((f32[2,16,256]{2,1,0:T(8,128)S(1)}, f32[2,16,256]{2,1,0:T(8,128)S(1)}, u32[]{:S(2)}, u32[]{:S(2)}) %collective-permute-start.7) | collective-permute-done | bytes 32800 | tf_op jit(solution)/shard_map/ppermute | solution.py:47
  132.2 1.6 multiply_multiply_fusion
  133.8 1.5 pad.25.refs_3_
  135.2 27.4 %shard_map.79 = (f32[2,18,48,256]{3,2,1,0:T(8,128)}, f32[2,18,48,256]{3,2,1,0:T(8,128)}) custom-call(f32[6,16,48,256]{3,2,1,0:T(8,128)} %get-tuple-element.50.refs_0_, f32[2,16,48,256]{3,2,1,0:T(8,128)} %get-tuple-element.68.refs_1_, f32[2,18,48,256]{3,2,1,0:T(8,128)} %broadcast_12_refs_2_.2.refs_2_, f32[2,18,48,256]{3,2,1,0:T(8,128)} %pad.25.refs_3_), custom_call_target="tpu_custom_call" | custom-call | flops 117964800 | bytes 14155776 | tf_op jit(solution)/shard_map/pallas_call | solution.py:116
  162.6 1.3 pad_maximum_fusion.2
  163.9 1.9 collective-permute-start.8
  165.9 2.7 %collective-permute-start.9 = (f32[2,2,18,16,256]{4,3,2,1,0:T(8,128)S(1)}, f32[2,2,18,16,256]{4,3,2,1,0:T(8,128)}, u32[]{:S(2)}, u32[]{:S(2)}) collective-permute-start(f32[2,2,18,16,256]{4,3,2,1,0:T(8,128)S(1)} %pad_maximum_fusion.2), channel_id=1, source_target_pairs={{4,0},{8,4},{12,8},{16,12},{20,16},{24,20},{28,24},{5,1},{9,5},{13... | collective-permute-start | bytes 3538952 | tf_op jit(solution)/shard_map/ppermute | solution.py:47
  168.6 0.7 fusion.31
  169.3 1.6 constant_dynamic-slice_fusion
  170.9 8.1 %collective-permute-done.8 = f32[2,2,18,16,256]{4,3,2,1,0:T(8,128)S(1)} collective-permute-done((f32[2,2,18,16,256]{4,3,2,1,0:T(8,128)S(1)}, f32[2,2,18,16,256]{4,3,2,1,0:T(8,128)S(1)}, u32[]{:S(2)}, u32[]{:S(2)}) %collective-permute-start.8) | collective-permute-done | bytes 1179680 | tf_op jit(solution)/shard_map/ppermute | solution.py:46
  179.0 4.5 %collective-permute-done.9 = f32[2,2,18,16,256]{4,3,2,1,0:T(8,128)} collective-permute-done((f32[2,2,18,16,256]{4,3,2,1,0:T(8,128)S(1)}, f32[2,2,18,16,256]{4,3,2,1,0:T(8,128)}, u32[]{:S(2)}, u32[]{:S(2)}) %collective-permute-start.9) | collective-permute-done | bytes 1179680 | tf_op jit(solution)/shard_map/ppermute | solution.py:47
  183.5 1.5 pad_maximum_fusion.1
  185.0 2.0 slice_bitcast_fusion
  187.0 29.0 %shard_map.80 = (f32[2,18,48,256]{3,2,1,0:T(8,128)}, f32[2,18,48,256]{3,2,1,0:T(8,128)}) custom-call(f32[6,16,48,256]{3,2,1,0:T(8,128)} %get-tuple-element.50.refs_0_, f32[2,16,48,256]{3,2,1,0:T(8,128)} %get-tuple-element.68.refs_1_, f32[2,18,48,256]{3,2,1,0:T(8,128)} %get-tuple-element.53.refs_2_, f32[2,18,48,256]{3,2,1,0:T(8,128)} %get-tuple-element.52.refs_3_), custom_call_target="tpu_custom_call" | custom-call | flops 125829120 | bytes 14155776 | tf_op jit(solution)/shard_map/pallas_call | solution.py:116
  216.0 1.0 fusion.18
  217.0 1.4 fusion.25
  (30 shorter events, 3.9 us)
Async XLA Ops:
  4.3 4.8 %collective-permute-start = (f32[13,16,128]{2,1,0:T(8,128)S(1)}, f32[13,16,128]{2,1,0:T(8,128)S(1)}, u32[]{:S(2)}, u32[]{:S(2)}) collective-permute-start(f32[13,16,128]{2,1,0:T(8,128)S(1)} %constant_dynamic-update-slice_fusion), channel_id=1, source_target_pairs={{0,2},{2,0},{1,3},{3,1},{4,6},{6,4},{5,7},{7,5},{8,10},{10,8},{9,1... | collective-permute-start | bytes 319496 | tf_op jit(solution)/shard_map/ppermute | solution.py:57
  9.2 3.9 %collective-permute-start.1 = (f32[8,16,256]{2,1,0:T(8,128)S(1)}, f32[8,16,256]{2,1,0:T(8,128)S(1)}, u32[]{:S(2)}, u32[]{:S(2)}) collective-permute-start(f32[8,16,256]{2,1,0:T(8,128)S(1)} %slice.181), channel_id=1, source_target_pairs={{0,1},{1,0},{2,3},{3,2},{4,5},{5,4},{6,7},{7,6},{8,9},{9,8},{10,11... | collective-permute-start | bytes 393224 | tf_op jit(solution)/shard_map/ppermute | solution.py:57
  13.2 9.9 %collective-permute-start.2 = (f32[21,16,256]{2,1,0:T(8,128)S(1)}, f32[21,16,256]{2,1,0:T(8,128)S(1)}, u32[]{:S(2)}, u32[]{:S(2)}) collective-permute-start(f32[21,16,256]{2,1,0:T(8,128)S(1)} %pad_maximum_fusion.5), channel_id=1, source_target_pairs={{0,4},{4,8},{8,12},{12,16},{16,20},{20,24},{24,28},{1,5},{5,9},{9,... | collective-permute-start | bytes 1032200 | tf_op jit(solution)/shard_map/ppermute | solution.py:46
  18.9 8.6 %collective-permute-start.3 = (f32[21,16,256]{2,1,0:T(8,128)S(1)}, f32[21,16,256]{2,1,0:T(8,128)S(1)}, u32[]{:S(2)}, u32[]{:S(2)}) collective-permute-start(f32[21,16,256]{2,1,0:T(8,128)S(1)} %pad_maximum_fusion.5), channel_id=1, source_target_pairs={{4,0},{8,4},{12,8},{16,12},{20,16},{24,20},{28,24},{5,1},{9,5},{13... | collective-permute-start | bytes 1032200 | tf_op jit(solution)/shard_map/ppermute | solution.py:47
  70.9 15.1 %collective-permute-start.4 = (f32[2,2,18,16,256]{4,3,2,1,0:T(8,128)S(1)}, f32[2,2,18,16,256]{4,3,2,1,0:T(8,128)S(1)}, u32[]{:S(2)}, u32[]{:S(2)}) collective-permute-start(f32[2,2,18,16,256]{4,3,2,1,0:T(8,128)S(1)} %pad_maximum_fusion.3), channel_id=1, source_target_pairs={{0,4},{4,8},{8,12},{12,16},{16,20},{20,24},{24,28},{1,5},{5,9},{9,... | collective-permute-start | bytes 3538952 | tf_op jit(solution)/shard_map/ppermute | solution.py:46
  72.8 17.5 %collective-permute-start.5 = (f32[2,2,18,16,256]{4,3,2,1,0:T(8,128)S(1)}, f32[2,2,18,16,256]{4,3,2,1,0:T(8,128)S(1)}, u32[]{:S(2)}, u32[]{:S(2)}) collective-permute-start(f32[2,2,18,16,256]{4,3,2,1,0:T(8,128)S(1)} %pad_maximum_fusion.3), channel_id=1, source_target_pairs={{4,0},{8,4},{12,8},{16,12},{20,16},{24,20},{28,24},{5,1},{9,5},{13... | collective-permute-start | bytes 3538952 | tf_op jit(solution)/shard_map/ppermute | solution.py:47
  125.1 4.6 %collective-permute-start.6 = (f32[2,16,256]{2,1,0:T(8,128)S(1)}, f32[2,16,256]{2,1,0:T(8,128)S(1)}, u32[]{:S(2)}, u32[]{:S(2)}) collective-permute-start(f32[2,16,256]{2,1,0:T(8,128)S(1)} %slice_multiply_fusion), channel_id=1, source_target_pairs={{0,4},{4,8},{8,12},{12,16},{16,20},{20,24},{24,28},{1,5},{5,9},{9,... | collective-permute-start | bytes 98312 | tf_op jit(solution)/shard_map/ppermute | solution.py:46
  127.0 5.2 %collective-permute-start.7 = (f32[2,16,256]{2,1,0:T(8,128)S(1)}, f32[2,16,256]{2,1,0:T(8,128)S(1)}, u32[]{:S(2)}, u32[]{:S(2)}) collective-permute-start(f32[2,16,256]{2,1,0:T(8,128)S(1)} %slice_multiply_fusion), channel_id=1, source_target_pairs={{4,0},{8,4},{12,8},{16,12},{20,16},{24,20},{28,24},{5,1},{9,5},{13... | collective-permute-start | bytes 98312 | tf_op jit(solution)/shard_map/ppermute | solution.py:47
  163.9 15.1 %collective-permute-start.8 = (f32[2,2,18,16,256]{4,3,2,1,0:T(8,128)S(1)}, f32[2,2,18,16,256]{4,3,2,1,0:T(8,128)S(1)}, u32[]{:S(2)}, u32[]{:S(2)}) collective-permute-start(f32[2,2,18,16,256]{4,3,2,1,0:T(8,128)S(1)} %pad_maximum_fusion.2), channel_id=1, source_target_pairs={{0,4},{4,8},{8,12},{12,16},{16,20},{20,24},{24,28},{1,5},{5,9},{9,... | collective-permute-start | bytes 3538952 | tf_op jit(solution)/shard_map/ppermute | solution.py:46
  165.9 17.6 %collective-permute-start.9 = (f32[2,2,18,16,256]{4,3,2,1,0:T(8,128)S(1)}, f32[2,2,18,16,256]{4,3,2,1,0:T(8,128)}, u32[]{:S(2)}, u32[]{:S(2)}) collective-permute-start(f32[2,2,18,16,256]{4,3,2,1,0:T(8,128)S(1)} %pad_maximum_fusion.2), channel_id=1, source_target_pairs={{4,0},{8,4},{12,8},{16,12},{20,16},{24,20},{28,24},{5,1},{9,5},{13... | collective-permute-start | bytes 3538952 | tf_op jit(solution)/shard_map/ppermute | solution.py:47
  187.0 30.0 %copy-start = (f32[47,256]{1,0:T(8,128)S(1)}, f32[47,256]{1,0:T(8,128)}, u32[]{:S(2)}) copy-start(f32[47,256]{1,0:T(8,128)} %get-tuple-element.62) | copy-start | bytes 144388
  187.0 30.0 %copy-start.1 = (f32[48,255]{1,0:T(8,128)S(1)}, f32[48,255]{1,0:T(8,128)}, u32[]{:S(2)}) copy-start(f32[48,255]{1,0:T(8,128)} %get-tuple-element.71) | copy-start | bytes 146884
  187.0 30.0 %copy-start.2 = (f32[48,255]{1,0:T(8,128)S(1)}, f32[48,255]{1,0:T(8,128)}, u32[]{:S(2)}) copy-start(f32[48,255]{1,0:T(8,128)} %get-tuple-element.72) | copy-start | bytes 146884

commit v8 on v7

--- a/solution.py
+++ b/solution.py
@@ -70,15 +70,13 @@
     return jnp.concatenate([z, lax.slice_in_dim(a, 0, n - 1, axis=axis)], axis=axis)
 
 
-def segment_kernel(steps, start_valid, op_ref, rhs_ref, x_in, d_in, x_ref, d_ref):
+def segment_kernel(steps, start_valid, table_ref, op_ref, rhs_ref, x_in, d_in, x_ref, d_ref):
     comps, layers = rhs_ref.shape[0], rhs_ref.shape[1]
     rows, cols = rhs_ref.shape[2], rhs_ref.shape[3]
     x_ref[...] = x_in[...]
     d_ref[...] = d_in[...]
 
-    for j, (keep, push) in enumerate(steps):
-        lo = min(8 * ((start_valid + j) // 8), rows // 2 - 8)
-        lo = max(lo, 0)
+    def one_step(lo, keep, push):
         span = pl.ds(lo, rows - 2 * lo)
         height = rows - 2 * lo
         for c in range(comps):
@@ -106,25 +104,50 @@
                     d_ref[c, p, span] = keep * d_ref[c, p, span] + push * (op_ref[5, layer, span] * resid)
             return carry
 
-        lax.fori_loop(0, layers, update, 0, unroll=4)
+        lax.fori_loop(0, layers, update, 0, unroll=True)
+
+    def row_start(j):
+        return max(min(8 * ((start_valid + j) // 8), rows // 2 - 8), 0)
+
+    j = 0
+    if steps[0][0] is None:
+        one_step(row_start(0), None, None)
+        j = 1
+    while j < len(steps):
+        lo = row_start(j)
+        end = j
+        while end < len(steps) and row_start(end) == lo:
+            end += 1
+
+        def body(i, carry, lo=lo):
+            one_step(lo, table_ref[0, i], table_ref[1, i])
+            return carry
+
+        lax.fori_loop(j, end, body, 0)
+        j = end
 
 
 def run_segment(steps, start_valid, op_stack, rhs, iterate, step_dir):
     comps, layers, rows, cols = rhs.shape
     vmem = pl.BlockSpec(memory_space=pltpu.VMEM)
+    smem = pl.BlockSpec(memory_space=pltpu.SMEM)
     cells = comps * layers * rows * cols
+    table = jnp.array(
+        [[0.0 if kp is None else kp for kp, _ in steps], [0.0 if kp is None else ps for kp, ps in steps]],
+        jnp.float32,
+    )
     return pl.pallas_call(
         lambda *refs: segment_kernel(steps, start_valid, *refs),
         out_shape=(
             jax.ShapeDtypeStruct(iterate.shape, jnp.float32),
             jax.ShapeDtypeStruct(iterate.shape, jnp.float32),
         ),
-        in_specs=[vmem] * 4,
+        in_specs=[smem] + [vmem] * 4,
         out_specs=(vmem, vmem),
         cost_estimate=pl.CostEstimate(
             flops=20 * cells * len(steps), bytes_accessed=4 * cells * 9, transcendentals=0
         ),
-    )(op_stack, rhs, iterate, step_dir)
+    )(table, op_stack, rhs, iterate, step_dir)
 
 
 def local(viscosity, friction, base_velocity, grounded, ice_free, direction):

time: 219 us -> 213 us (0.973)
  Pallas kernels: 113 us -> 107 us
    pallas_call x4, Pallas kernels: 113 us -> 107 us  [run_segment(): pl.pallas_call(lambda *refs: segment_kernel(steps, start_valid, *refs), o...]
where the time goes in v8:
time: 213 us; the launch traced here: 212 us
  Pallas kernels  107 us (50%)
  waiting for transfers between devices  42.6 us (20%)
  other arithmetic  24.3 us (11%)
  starting transfers between devices  24.1 us (11%)
  local copies, waits for them, and re-layouts  13.8 us (6%)
    pallas_call x4, Pallas kernels, run_segment(): pl.pallas_call(lambda *refs: segment_kernel(steps, start_valid, *refs), o...  107 us
    ppermute x4, waiting for transfers between devices, exchange_rows(): lax.ppermute(lax.slice_in_dim(own, rows - k, rows, axis=axis), 'mx', forw...  20.8 us
    ppermute x4, waiting for transfers between devices, exchange_rows(): high = lax.ppermute(lax.slice_in_dim(own, 0, k, axis=axis), 'mx', backward)  16.1 us
    ppermute x4, starting transfers between devices, exchange_rows(): lax.ppermute(lax.slice_in_dim(own, rows - k, rows, axis=axis), 'mx', forw...  11.4 us
    ppermute x4, starting transfers between devices, exchange_rows(): high = lax.ppermute(lax.slice_in_dim(own, 0, k, axis=axis), 'mx', backward)  9.68 us
    unnamed x7, other arithmetic  7.11 us
    ppermute x2, waiting for transfers between devices, gather_axis(): seq.append(lax.ppermute(block, axis, pairs))  5.67 us
  transfers between devices with their start and end apart: 10, of which 9 were waited for; matrix products, arithmetic and copies ran while one was open for 1% of the time, Pallas kernels for 0%

profile of v8, /device:TPU:1, one launch (start us, length us, event | category | flops | bytes accessed | tf_op | source)
XLA Modules:
  0.0 212.2 jit_solution(4825759938905876205)
XLA Ops:
  0.6 0.8 constant_dynamic-update-slice_fusion.4
  2.2 0.7 constant_dynamic-update-slice_fusion.2
  2.9 0.7 constant_dynamic-update-slice_fusion.1
  4.3 2.1 collective-permute-start
  6.4 2.7 %collective-permute-done = f32[13,16,128]{2,1,0:T(8,128)S(1)} collective-permute-done((f32[13,16,128]{2,1,0:T(8,128)S(1)}, f32[13,16,128]{2,1,0:T(8,128)S(1)}, u32[]{:S(2)}, u32[]{:S(2)}) %collective-permute-start) | collective-permute-done | bytes 106528 | tf_op jit(solution)/shard_map/ppermute | solution.py:57
  9.2 0.9 collective-permute-start.1
  10.1 3.0 %collective-permute-done.1 = f32[8,16,256]{2,1,0:T(8,128)S(1)} collective-permute-done((f32[8,16,256]{2,1,0:T(8,128)S(1)}, f32[8,16,256]{2,1,0:T(8,128)S(1)}, u32[]{:S(2)}, u32[]{:S(2)}) %collective-permute-start.1) | collective-permute-done | bytes 131104 | tf_op jit(solution)/shard_map/ppermute | solution.py:57
  13.2 5.7 %collective-permute-start.2 = (f32[21,16,256]{2,1,0:T(8,128)S(1)}, f32[21,16,256]{2,1,0:T(8,128)S(1)}, u32[]{:S(2)}, u32[]{:S(2)}) collective-permute-start(f32[21,16,256]{2,1,0:T(8,128)S(1)} %pad_maximum_fusion.5), channel_id=1, source_target_pairs={{0,4},{4,8},{8,12},{12,16},{16,20},{20,24},{24,28},{1,5},{5,9},{9,... | collective-permute-start | bytes 1032200 | tf_op jit(solution)/shard_map/ppermute | solution.py:46
  18.9 1.9 collective-permute-start.3
  20.8 2.2 %collective-permute-done.2 = f32[21,16,256]{2,1,0:T(8,128)S(1)} collective-permute-done((f32[21,16,256]{2,1,0:T(8,128)S(1)}, f32[21,16,256]{2,1,0:T(8,128)S(1)}, u32[]{:S(2)}, u32[]{:S(2)}) %collective-permute-start.2) | collective-permute-done | bytes 344096 | tf_op jit(solution)/shard_map/ppermute | solution.py:46
  23.0 4.4 %collective-permute-done.3 = f32[21,16,256]{2,1,0:T(8,128)S(1)} collective-permute-done((f32[21,16,256]{2,1,0:T(8,128)S(1)}, f32[21,16,256]{2,1,0:T(8,128)S(1)}, u32[]{:S(2)}, u32[]{:S(2)}) %collective-permute-start.3) | collective-permute-done | bytes 344096 | tf_op jit(solution)/shard_map/ppermute | solution.py:47
  29.5 1.1 bitcast_dynamic-update-slice_fusion.5
  30.6 1.2 bitcast_dynamic-update-slice_fusion.4
  31.8 1.4 fusion.8
  33.2 1.2 bitcast_dynamic-update-slice_fusion.3
  34.4 1.3 bitcast_dynamic-update-slice_fusion.2
  35.7 0.9 bitcast_dynamic-update-slice_fusion.1
  36.6 1.1 bitcast_dynamic-update-slice_fusion
  37.7 1.5 multiply_multiply_fusion.1
  39.3 1.5 pad.24.refs_4_
  40.7 1.5 broadcast_12_refs_3_.2.refs_3_
  42.2 26.0 %shard_map.113 = (f32[2,18,48,256]{3,2,1,0:T(8,128)}, f32[2,18,48,256]{3,2,1,0:T(8,128)}) custom-call(f32[2,15]{1,0:T(2,128)} %constant.124.clone.refs_0_, f32[6,16,48,256]{3,2,1,0:T(8,128)} %get-tuple-element.50.refs_1_, f32[2,16,48,256]{3,2,1,0:T(8,128)} %get-tuple-element.70.refs_2_, f32[2,18,48,256]{3,2,1,0:T(8,128)} %broadcast_12_refs_3_.2.refs_3_, ...), custom_call_target="tpu_custom_call" | custom-call | flops 117964800 | bytes 14155776 | tf_op jit(solution)/shard_map/pallas_call | solution.py:139
  68.2 1.3 pad_maximum_fusion.3
  69.5 1.9 collective-permute-start.4
  71.4 2.7 %collective-permute-start.5 = (f32[2,2,18,16,256]{4,3,2,1,0:T(8,128)S(1)}, f32[2,2,18,16,256]{4,3,2,1,0:T(8,128)S(1)}, u32[]{:S(2)}, u32[]{:S(2)}) collective-permute-start(f32[2,2,18,16,256]{4,3,2,1,0:T(8,128)S(1)} %pad_maximum_fusion.3), channel_id=1, source_target_pairs={{4,0},{8,4},{12,8},{16,12},{20,16},{24,20},{28,24},{5,1},{9,5},{13... | collective-permute-start | bytes 3538952 | tf_op jit(solution)/shard_map/ppermute | solution.py:47
  74.1 10.5 %collective-permute-done.4 = f32[2,2,18,16,256]{4,3,2,1,0:T(8,128)S(1)} collective-permute-done((f32[2,2,18,16,256]{4,3,2,1,0:T(8,128)S(1)}, f32[2,2,18,16,256]{4,3,2,1,0:T(8,128)S(1)}, u32[]{:S(2)}, u32[]{:S(2)}) %collective-permute-start.4) | collective-permute-done | bytes 1179680 | tf_op jit(solution)/shard_map/ppermute | solution.py:46
  84.6 4.4 %collective-permute-done.5 = f32[2,2,18,16,256]{4,3,2,1,0:T(8,128)S(1)} collective-permute-done((f32[2,2,18,16,256]{4,3,2,1,0:T(8,128)S(1)}, f32[2,2,18,16,256]{4,3,2,1,0:T(8,128)S(1)}, u32[]{:S(2)}, u32[]{:S(2)}) %collective-permute-start.5) | collective-permute-done | bytes 1179680 | tf_op jit(solution)/shard_map/ppermute | solution.py:47
  89.2 2.1 %slice_bitcast_fusion.2 = (f32[2,18,48,256]{3,2,1,0:T(8,128)}, f32[2,18,48,256]{3,2,1,0:T(8,128)}) fusion(f32[2,2,18,48,256]{4,3,2,1,0:T(8,128)S(1)} %pad_maximum_fusion), kind=kLoop, calls=%fused_computation.4 | loop fusion | bytes 7077888 | tf_op jit(solution)/shard_map/squeeze | solution.py:208
  91.3 27.4 %shard_map.114 = (f32[2,18,48,256]{3,2,1,0:T(8,128)}, f32[2,18,48,256]{3,2,1,0:T(8,128)}) custom-call(f32[2,16]{1,0:T(2,128)} %constant.125.clone.refs_0_, f32[6,16,48,256]{3,2,1,0:T(8,128)} %get-tuple-element.50.refs_1_, f32[2,16,48,256]{3,2,1,0:T(8,128)} %get-tuple-element.70.refs_2_, f32[2,18,48,256]{3,2,1,0:T(8,128)} %get-tuple-element.55.refs_3_, ...), custom_call_target="tpu_custom_call" | custom-call | flops 125829120 | bytes 14155776 | tf_op jit(solution)/shard_map/pallas_call | solution.py:139
  118.7 3.3 %fusion.27 = (f32[2,48,256]{2,1,0:T(8,128)S(1)}, f32[2,16,48,256]{3,2,1,0:T(8,128)}) fusion(f32[2,18,48,256]{3,2,1,0:T(8,128)} %get-tuple-element.37, f32[2,18,48,256]{3,2,1,0:T(8,128)} %get-tuple-element.36), kind=kLoop, calls=%fused_computation.100 | loop fusion | flops 761856 | bytes 4816896 | tf_op jit(solution)/shard_map/reduce_sum | solution.py:219
  122.0 1.9 collective-permute-start.6
  123.9 2.4 %collective-permute-start.7 = (f32[2,16,256]{2,1,0:T(8,128)S(1)}, f32[2,16,256]{2,1,0:T(8,128)S(1)}, u32[]{:S(2)}, u32[]{:S(2)}) collective-permute-start(f32[2,16,256]{2,1,0:T(8,128)S(1)} %slice_multiply_fusion), channel_id=1, source_target_pairs={{4,0},{8,4},{12,8},{16,12},{20,16},{24,20},{28,24},{5,1},{9,5},{13... | collective-permute-start | bytes 98312 | tf_op jit(solution)/shard_map/ppermute | solution.py:47
  126.3 2.8 %collective-permute-done.7 = f32[2,16,256]{2,1,0:T(8,128)S(1)} collective-permute-done((f32[2,16,256]{2,1,0:T(8,128)S(1)}, f32[2,16,256]{2,1,0:T(8,128)S(1)}, u32[]{:S(2)}, u32[]{:S(2)}) %collective-permute-start.7) | collective-permute-done | bytes 32800 | tf_op jit(solution)/shard_map/ppermute | solution.py:47
  129.1 1.6 multiply_multiply_fusion
  130.7 1.5 pad.25.refs_4_
  132.2 26.0 %shard_map.115 = (f32[2,18,48,256]{3,2,1,0:T(8,128)}, f32[2,18,48,256]{3,2,1,0:T(8,128)}) custom-call(f32[2,15]{1,0:T(2,128)} %constant.124.clone.refs_0_, f32[6,16,48,256]{3,2,1,0:T(8,128)} %get-tuple-element.50.refs_1_, f32[2,16,48,256]{3,2,1,0:T(8,128)} %get-tuple-element.68.refs_2_, f32[2,18,48,256]{3,2,1,0:T(8,128)} %broadcast_12_refs_3_.2.refs_3_, ...), custom_call_target="tpu_custom_call" | custom-call | flops 117964800 | bytes 14155776 | tf_op jit(solution)/shard_map/pallas_call | solution.py:139
  158.1 1.3 pad_maximum_fusion.2
  159.5 1.9 collective-permute-start.8
  161.4 2.7 %collective-permute-start.9 = (f32[2,2,18,16,256]{4,3,2,1,0:T(8,128)S(1)}, f32[2,2,18,16,256]{4,3,2,1,0:T(8,128)}, u32[]{:S(2)}, u32[]{:S(2)}) collective-permute-start(f32[2,2,18,16,256]{4,3,2,1,0:T(8,128)S(1)} %pad_maximum_fusion.2), channel_id=1, source_target_pairs={{4,0},{8,4},{12,8},{16,12},{20,16},{24,20},{28,24},{5,1},{9,5},{13... | collective-permute-start | bytes 3538952 | tf_op jit(solution)/shard_map/ppermute | solution.py:47
  164.1 0.7 fusion.31
  164.8 1.6 constant_dynamic-slice_fusion
  166.4 8.1 %collective-permute-done.8 = f32[2,2,18,16,256]{4,3,2,1,0:T(8,128)S(1)} collective-permute-done((f32[2,2,18,16,256]{4,3,2,1,0:T(8,128)S(1)}, f32[2,2,18,16,256]{4,3,2,1,0:T(8,128)S(1)}, u32[]{:S(2)}, u32[]{:S(2)}) %collective-permute-start.8) | collective-permute-done | bytes 1179680 | tf_op jit(solution)/shard_map/ppermute | solution.py:46
  174.5 4.5 %collective-permute-done.9 = f32[2,2,18,16,256]{4,3,2,1,0:T(8,128)} collective-permute-done((f32[2,2,18,16,256]{4,3,2,1,0:T(8,128)S(1)}, f32[2,2,18,16,256]{4,3,2,1,0:T(8,128)}, u32[]{:S(2)}, u32[]{:S(2)}) %collective-permute-start.9) | collective-permute-done | bytes 1179680 | tf_op jit(solution)/shard_map/ppermute | solution.py:47
  179.0 1.5 pad_maximum_fusion.1
  180.5 2.0 slice_bitcast_fusion
  182.5 27.3 %shard_map.116 = (f32[2,18,48,256]{3,2,1,0:T(8,128)}, f32[2,18,48,256]{3,2,1,0:T(8,128)}) custom-call(f32[2,16]{1,0:T(2,128)} %constant.125.clone.refs_0_, f32[6,16,48,256]{3,2,1,0:T(8,128)} %get-tuple-element.50.refs_1_, f32[2,16,48,256]{3,2,1,0:T(8,128)} %get-tuple-element.68.refs_2_, f32[2,18,48,256]{3,2,1,0:T(8,128)} %get-tuple-element.53.refs_3_, ...), custom_call_target="tpu_custom_call" | custom-call | flops 125829120 | bytes 14155776 | tf_op jit(solution)/shard_map/pallas_call | solution.py:139
  209.9 1.0 fusion.18
  210.9 1.4 fusion.25
  (30 shorter events, 3.9 us)
Async XLA Ops:
  4.3 4.8 %collective-permute-start = (f32[13,16,128]{2,1,0:T(8,128)S(1)}, f32[13,16,128]{2,1,0:T(8,128)S(1)}, u32[]{:S(2)}, u32[]{:S(2)}) collective-permute-start(f32[13,16,128]{2,1,0:T(8,128)S(1)} %constant_dynamic-update-slice_fusion), channel_id=1, source_target_pairs={{0,2},{2,0},{1,3},{3,1},{4,6},{6,4},{5,7},{7,5},{8,10},{10,8},{9,1... | collective-permute-start | bytes 319496 | tf_op jit(solution)/shard_map/ppermute | solution.py:57
  9.2 3.9 %collective-permute-start.1 = (f32[8,16,256]{2,1,0:T(8,128)S(1)}, f32[8,16,256]{2,1,0:T(8,128)S(1)}, u32[]{:S(2)}, u32[]{:S(2)}) collective-permute-start(f32[8,16,256]{2,1,0:T(8,128)S(1)} %slice.181), channel_id=1, source_target_pairs={{0,1},{1,0},{2,3},{3,2},{4,5},{5,4},{6,7},{7,6},{8,9},{9,8},{10,11... | collective-permute-start | bytes 393224 | tf_op jit(solution)/shard_map/ppermute | solution.py:57
  13.2 9.9 %collective-permute-start.2 = (f32[21,16,256]{2,1,0:T(8,128)S(1)}, f32[21,16,256]{2,1,0:T(8,128)S(1)}, u32[]{:S(2)}, u32[]{:S(2)}) collective-permute-start(f32[21,16,256]{2,1,0:T(8,128)S(1)} %pad_maximum_fusion.5), channel_id=1, source_target_pairs={{0,4},{4,8},{8,12},{12,16},{16,20},{20,24},{24,28},{1,5},{5,9},{9,... | collective-permute-start | bytes 1032200 | tf_op jit(solution)/shard_map/ppermute | solution.py:46
  18.9 8.6 %collective-permute-start.3 = (f32[21,16,256]{2,1,0:T(8,128)S(1)}, f32[21,16,256]{2,1,0:T(8,128)S(1)}, u32[]{:S(2)}, u32[]{:S(2)}) collective-permute-start(f32[21,16,256]{2,1,0:T(8,128)S(1)} %pad_maximum_fusion.5), channel_id=1, source_target_pairs={{4,0},{8,4},{12,8},{16,12},{20,16},{24,20},{28,24},{5,1},{9,5},{13... | collective-permute-start | bytes 1032200 | tf_op jit(solution)/shard_map/ppermute | solution.py:47
  69.5 15.1 %collective-permute-start.4 = (f32[2,2,18,16,256]{4,3,2,1,0:T(8,128)S(1)}, f32[2,2,18,16,256]{4,3,2,1,0:T(8,128)S(1)}, u32[]{:S(2)}, u32[]{:S(2)}) collective-permute-start(f32[2,2,18,16,256]{4,3,2,1,0:T(8,128)S(1)} %pad_maximum_fusion.3), channel_id=1, source_target_pairs={{0,4},{4,8},{8,12},{12,16},{16,20},{20,24},{24,28},{1,5},{5,9},{9,... | collective-permute-start | bytes 3538952 | tf_op jit(solution)/shard_map/ppermute | solution.py:46
  71.4 17.5 %collective-permute-start.5 = (f32[2,2,18,16,256]{4,3,2,1,0:T(8,128)S(1)}, f32[2,2,18,16,256]{4,3,2,1,0:T(8,128)S(1)}, u32[]{:S(2)}, u32[]{:S(2)}) collective-permute-start(f32[2,2,18,16,256]{4,3,2,1,0:T(8,128)S(1)} %pad_maximum_fusion.3), channel_id=1, source_target_pairs={{4,0},{8,4},{12,8},{16,12},{20,16},{24,20},{28,24},{5,1},{9,5},{13... | collective-permute-start | bytes 3538952 | tf_op jit(solution)/shard_map/ppermute | solution.py:47
  122.0 4.3 %collective-permute-start.6 = (f32[2,16,256]{2,1,0:T(8,128)S(1)}, f32[2,16,256]{2,1,0:T(8,128)S(1)}, u32[]{:S(2)}, u32[]{:S(2)}) collective-permute-start(f32[2,16,256]{2,1,0:T(8,128)S(1)} %slice_multiply_fusion), channel_id=1, source_target_pairs={{0,4},{4,8},{8,12},{12,16},{16,20},{20,24},{24,28},{1,5},{5,9},{9,... | collective-permute-start | bytes 98312 | tf_op jit(solution)/shard_map/ppermute | solution.py:46
  123.9 5.2 %collective-permute-start.7 = (f32[2,16,256]{2,1,0:T(8,128)S(1)}, f32[2,16,256]{2,1,0:T(8,128)S(1)}, u32[]{:S(2)}, u32[]{:S(2)}) collective-permute-start(f32[2,16,256]{2,1,0:T(8,128)S(1)} %slice_multiply_fusion), channel_id=1, source_target_pairs={{4,0},{8,4},{12,8},{16,12},{20,16},{24,20},{28,24},{5,1},{9,5},{13... | collective-permute-start | bytes 98312 | tf_op jit(solution)/shard_map/ppermute | solution.py:47
  159.5 15.1 %collective-permute-start.8 = (f32[2,2,18,16,256]{4,3,2,1,0:T(8,128)S(1)}, f32[2,2,18,16,256]{4,3,2,1,0:T(8,128)S(1)}, u32[]{:S(2)}, u32[]{:S(2)}) collective-permute-start(f32[2,2,18,16,256]{4,3,2,1,0:T(8,128)S(1)} %pad_maximum_fusion.2), channel_id=1, source_target_pairs={{0,4},{4,8},{8,12},{12,16},{16,20},{20,24},{24,28},{1,5},{5,9},{9,... | collective-permute-start | bytes 3538952 | tf_op jit(solution)/shard_map/ppermute | solution.py:46
  161.4 17.6 %collective-permute-start.9 = (f32[2,2,18,16,256]{4,3,2,1,0:T(8,128)S(1)}, f32[2,2,18,16,256]{4,3,2,1,0:T(8,128)}, u32[]{:S(2)}, u32[]{:S(2)}) collective-permute-start(f32[2,2,18,16,256]{4,3,2,1,0:T(8,128)S(1)} %pad_maximum_fusion.2), channel_id=1, source_target_pairs={{4,0},{8,4},{12,8},{16,12},{20,16},{24,20},{28,24},{5,1},{9,5},{13... | collective-permute-start | bytes 3538952 | tf_op jit(solution)/shard_map/ppermute | solution.py:47
  182.5 28.3 %copy-start = (f32[47,256]{1,0:T(8,128)S(1)}, f32[47,256]{1,0:T(8,128)}, u32[]{:S(2)}) copy-start(f32[47,256]{1,0:T(8,128)} %get-tuple-element.62) | copy-start | bytes 144388
  182.5 28.3 %copy-start.1 = (f32[48,255]{1,0:T(8,128)S(1)}, f32[48,255]{1,0:T(8,128)}, u32[]{:S(2)}) copy-start(f32[48,255]{1,0:T(8,128)} %get-tuple-element.71) | copy-start | bytes 146884
  182.5 28.3 %copy-start.2 = (f32[48,255]{1,0:T(8,128)S(1)}, f32[48,255]{1,0:T(8,128)}, u32[]{:S(2)}) copy-start(f32[48,255]{1,0:T(8,128)} %get-tuple-element.72) | copy-start | bytes 146884

commit v9 on v8

--- a/solution.py
+++ b/solution.py
@@ -70,11 +70,29 @@
     return jnp.concatenate([z, lax.slice_in_dim(a, 0, n - 1, axis=axis)], axis=axis)
 
 
-def segment_kernel(steps, start_valid, table_ref, op_ref, rhs_ref, x_in, d_in, x_ref, d_ref):
+def segment_kernel(steps, start_valid, table_ref, op_ref, rhs_ref, *refs):
     comps, layers = rhs_ref.shape[0], rhs_ref.shape[1]
     rows, cols = rhs_ref.shape[2], rhs_ref.shape[3]
-    x_ref[...] = x_in[...]
-    d_ref[...] = d_in[...]
+    if len(refs) == 4:
+        x_in, d_in, x_ref, d_ref = refs
+        x_ref[...] = x_in[...]
+        d_ref[...] = d_in[...]
+    else:
+        x_ref, d_ref = refs
+        zero = jnp.zeros((rows, cols), jnp.float32)
+        for c in range(comps):
+            x_ref[c, 0] = zero
+            d_ref[c, 0] = zero
+            x_ref[c, layers + 1] = zero
+            d_ref[c, layers + 1] = zero
+
+        def start(layer, carry):
+            for c in range(comps):
+                x_ref[c, layer + 1] = zero
+                d_ref[c, layer + 1] = op_ref[5, layer] * rhs_ref[c, layer] / theta_center
+            return carry
+
+        lax.fori_loop(0, layers, start, 0)
 
     def one_step(lo, keep, push):
         span = pl.ds(lo, rows - 2 * lo)
@@ -136,18 +154,20 @@
         [[0.0 if kp is None else kp for kp, _ in steps], [0.0 if kp is None else ps for kp, ps in steps]],
         jnp.float32,
     )
+    state = () if iterate is None else (iterate, step_dir)
+    padded_shape = (comps, layers + 2, rows, cols)
     return pl.pallas_call(
         lambda *refs: segment_kernel(steps, start_valid, *refs),
         out_shape=(
-            jax.ShapeDtypeStruct(iterate.shape, jnp.float32),
-            jax.ShapeDtypeStruct(iterate.shape, jnp.float32),
+            jax.ShapeDtypeStruct(padded_shape, jnp.float32),
+            jax.ShapeDtypeStruct(padded_shape, jnp.float32),
         ),
-        in_specs=[smem] + [vmem] * 4,
+        in_specs=[smem] + [vmem] * (2 + len(state)),
         out_specs=(vmem, vmem),
         cost_estimate=pl.CostEstimate(
             flops=20 * cells * len(steps), bytes_accessed=4 * cells * 9, transcendentals=0
         ),
-    )(table, op_stack, rhs, iterate, step_dir)
+    )(table, op_stack, rhs, *state)
 
 
 def local(viscosity, friction, base_velocity, grounded, ice_free, direction):
@@ -191,11 +211,9 @@
         ]
     )
     table = step_constants()
-    layer_pad = ((0, 0), (1, 1), (0, 0), (0, 0))
 
     def chebyshev(rhs):
-        iterate = jnp.zeros((2, layers + 2) + rhs.shape[2:], jnp.float32)
-        step_dir = jnp.pad(jacobi * rhs / theta_center, layer_pad)
+        iterate, step_dir = None, None
         since = 1
         start_valid = 1
         run = []

time: 213 us -> 204 us (0.958)
  waiting for transfers between devices: 42.6 us -> 34.4 us
  starting transfers between devices: 24.1 us -> 29.7 us
  local copies, waits for them, and re-layouts: 13.8 us -> 10.6 us
    ppermute x4, waiting for transfers between devices: 20.8 us -> 4.54 us  [exchange_rows(): lax.ppermute(lax.slice_in_dim(own, rows - k, rows, axis=axis), 'mx', forw...]
    ppermute x4, waiting for transfers between devices: 16.1 us -> 24.2 us  [exchange_rows(): high = lax.ppermute(lax.slice_in_dim(own, 0, k, axis=axis), 'mx', backward)]
    ppermute x4, starting transfers between devices: 11.4 us -> 16.7 us  [exchange_rows(): lax.ppermute(lax.slice_in_dim(own, rows - k, rows, axis=axis), 'mx', forw...]
    div x2 -> x0, other arithmetic: 3.07 us -> none  [chebyshev(): step_dir = jnp.pad(jacobi * rhs / theta_center, layer_pad)]
    pad x2 -> x0, local copies, waits for them, and re-layouts: 2.93 us -> none  [chebyshev(): step_dir = jnp.pad(jacobi * rhs / theta_center, layer_pad)]
where the time goes in v9:
time: 204 us; the launch traced here: 203 us
  Pallas kernels  105 us (51%)
  waiting for transfers between devices  34.4 us (17%)
  starting transfers between devices  29.7 us (15%)
  other arithmetic  22.7 us (11%)
  local copies, waits for them, and re-layouts  10.6 us (5%)
    pallas_call x4, Pallas kernels, run_segment(): pl.pallas_call(lambda *refs: segment_kernel(steps, start_valid, *refs), o...  105 us
    ppermute x4, waiting for transfers between devices, exchange_rows(): high = lax.ppermute(lax.slice_in_dim(own, 0, k, axis=axis), 'mx', backward)  24.2 us
    ppermute x4, starting transfers between devices, exchange_rows(): lax.ppermute(lax.slice_in_dim(own, rows - k, rows, axis=axis), 'mx', forw...  16.7 us
    ppermute x4, starting transfers between devices, exchange_rows(): high = lax.ppermute(lax.slice_in_dim(own, 0, k, axis=axis), 'mx', backward)  10 us
    unnamed x7, other arithmetic  7.08 us
    ppermute x2, waiting for transfers between devices, gather_axis(): seq.append(lax.ppermute(block, axis, pairs))  5.67 us
    ppermute x4, waiting for transfers between devices, exchange_rows(): lax.ppermute(lax.slice_in_dim(own, rows - k, rows, axis=axis), 'mx', forw...  4.54 us
  transfers between devices with their start and end apart: 10, of which 9 were waited for; matrix products, arithmetic and copies ran while one was open for 1% of the time, Pallas kernels for 0%

profile of v9, /device:TPU:1, one launch (start us, length us, event | category | flops | bytes accessed | tf_op | source)
XLA Modules:
  0.0 203.0 jit_solution(2002569933940668371)
XLA Ops:
  0.6 0.8 constant_dynamic-update-slice_fusion.4
  1.5 0.7 constant_dynamic-update-slice_fusion.3
  2.2 0.7 constant_dynamic-update-slice_fusion.2
  2.9 0.7 constant_dynamic-update-slice_fusion.1
  3.6 0.7 constant_dynamic-update-slice_fusion
  4.3 2.1 %collective-permute-start = (f32[13,16,128]{2,1,0:T(8,128)S(1)}, f32[13,16,128]{2,1,0:T(8,128)S(1)}, u32[]{:S(2)}, u32[]{:S(2)}) collective-permute-start(f32[13,16,128]{2,1,0:T(8,128)S(1)} %constant_dynamic-update-slice_fusion), channel_id=1, source_target_pairs={{0,2},{2,0},{1,3},{3,1},{4,6},{6,4},{5,7},{7,5},{8,10},{10,8},{9,1... | collective-permute-start | bytes 319496 | tf_op jit(solution)/shard_map/ppermute | solution.py:57
  6.4 2.7 %collective-permute-done = f32[13,16,128]{2,1,0:T(8,128)S(1)} collective-permute-done((f32[13,16,128]{2,1,0:T(8,128)S(1)}, f32[13,16,128]{2,1,0:T(8,128)S(1)}, u32[]{:S(2)}, u32[]{:S(2)}) %collective-permute-start) | collective-permute-done | bytes 106528 | tf_op jit(solution)/shard_map/ppermute | solution.py:57
  9.2 0.9 collective-permute-start.1
  10.1 3.0 %collective-permute-done.1 = f32[8,16,256]{2,1,0:T(8,128)S(1)} collective-permute-done((f32[8,16,256]{2,1,0:T(8,128)S(1)}, f32[8,16,256]{2,1,0:T(8,128)S(1)}, u32[]{:S(2)}, u32[]{:S(2)}) %collective-permute-start.1) | collective-permute-done | bytes 131104 | tf_op jit(solution)/shard_map/ppermute | solution.py:57
  13.2 4.3 %collective-permute-start.3 = (f32[21,16,256]{2,1,0:T(8,128)S(1)}, f32[21,16,256]{2,1,0:T(8,128)S(1)}, u32[]{:S(2)}, u32[]{:S(2)}) collective-permute-start(f32[21,16,256]{2,1,0:T(8,128)S(1)} %pad_maximum_fusion.5), channel_id=1, source_target_pairs={{4,0},{8,4},{12,8},{16,12},{20,16},{24,20},{28,24},{5,1},{9,5},{13... | collective-permute-start | bytes 1032200 | tf_op jit(solution)/shard_map/ppermute | solution.py:47
  17.5 3.3 %collective-permute-start.2 = (f32[21,16,256]{2,1,0:T(8,128)S(1)}, f32[21,16,256]{2,1,0:T(8,128)S(1)}, u32[]{:S(2)}, u32[]{:S(2)}) collective-permute-start(f32[21,16,256]{2,1,0:T(8,128)S(1)} %pad_maximum_fusion.5), channel_id=1, source_target_pairs={{0,4},{4,8},{8,12},{12,16},{16,20},{20,24},{24,28},{1,5},{5,9},{9,... | collective-permute-start | bytes 1032200 | tf_op jit(solution)/shard_map/ppermute | solution.py:46
  20.8 3.0 %collective-permute-done.3 = f32[21,16,256]{2,1,0:T(8,128)S(1)} collective-permute-done((f32[21,16,256]{2,1,0:T(8,128)S(1)}, f32[21,16,256]{2,1,0:T(8,128)S(1)}, u32[]{:S(2)}, u32[]{:S(2)}) %collective-permute-start.3) | collective-permute-done | bytes 344096 | tf_op jit(solution)/shard_map/ppermute | solution.py:47
  23.8 1.2 collective-permute-done.2
  25.0 0.6 broadcast_multiply_fusion.2
  27.2 1.3 copy.13.refs_2_
  28.6 1.1 bitcast_dynamic-update-slice_fusion.5
  29.7 1.1 bitcast_dynamic-update-slice_fusion.4
  30.9 1.4 fusion.8
  32.3 1.2 bitcast_dynamic-update-slice_fusion.3
  33.5 1.2 bitcast_dynamic-update-slice_fusion.2
  34.7 1.0 bitcast_dynamic-update-slice_fusion.1
  35.7 1.0 bitcast_dynamic-update-slice_fusion.refs_1_
  36.7 25.0 %shard_map.113 = (f32[2,18,48,256]{3,2,1,0:T(8,128)}, f32[2,18,48,256]{3,2,1,0:T(8,128)}) custom-call(f32[2,15]{1,0:T(2,128)} %constant.118.clone.refs_0_, f32[6,16,48,256]{3,2,1,0:T(8,128)} %bitcast_dynamic-update-slice_fusion.refs_1_, f32[2,16,48,256]{3,2,1,0:T(8,128)} %copy.13.refs_2_), custom_call_target="tpu_custom_call" | custom-call | flops 117964800 | bytes 14155776 | tf_op jit(solution)/shard_map/pallas_call | solution.py:159
  61.7 1.3 pad_maximum_fusion.3
  63.0 1.9 collective-permute-start.5
  65.0 4.6 %collective-permute-start.4 = (f32[2,2,18,16,256]{4,3,2,1,0:T(8,128)S(1)}, f32[2,2,18,16,256]{4,3,2,1,0:T(8,128)S(1)}, u32[]{:S(2)}, u32[]{:S(2)}) collective-permute-start(f32[2,2,18,16,256]{4,3,2,1,0:T(8,128)S(1)} %pad_maximum_fusion.3), channel_id=1, source_target_pairs={{0,4},{4,8},{8,12},{12,16},{16,20},{20,24},{24,28},{1,5},{5,9},{9,... | collective-permute-start | bytes 3538952 | tf_op jit(solution)/shard_map/ppermute | solution.py:46
  69.5 11.8 %collective-permute-done.5 = f32[2,2,18,16,256]{4,3,2,1,0:T(8,128)S(1)} collective-permute-done((f32[2,2,18,16,256]{4,3,2,1,0:T(8,128)S(1)}, f32[2,2,18,16,256]{4,3,2,1,0:T(8,128)S(1)}, u32[]{:S(2)}, u32[]{:S(2)}) %collective-permute-start.5) | collective-permute-done | bytes 1179680 | tf_op jit(solution)/shard_map/ppermute | solution.py:47
  81.3 1.2 collective-permute-done.4
  82.7 2.0 %slice_bitcast_fusion.2 = (f32[2,18,48,256]{3,2,1,0:T(8,128)}, f32[2,18,48,256]{3,2,1,0:T(8,128)}) fusion(f32[2,2,18,48,256]{4,3,2,1,0:T(8,128)S(1)} %pad_maximum_fusion), kind=kLoop, calls=%fused_computation.4 | loop fusion | bytes 7077888 | tf_op jit(solution)/shard_map/squeeze | solution.py:226
  84.8 27.3 %shard_map.114 = (f32[2,18,48,256]{3,2,1,0:T(8,128)}, f32[2,18,48,256]{3,2,1,0:T(8,128)}) custom-call(f32[2,16]{1,0:T(2,128)} %constant.119.clone.refs_0_, f32[6,16,48,256]{3,2,1,0:T(8,128)} %bitcast_dynamic-update-slice_fusion.refs_1_, f32[2,16,48,256]{3,2,1,0:T(8,128)} %copy.13.refs_2_, f32[2,18,48,256]{3,2,1,0:T(8,128)} %get-tuple-element.53.refs_3_, ...), custom_call_target="tpu_custom_call" | custom-call | flops 125829120 | bytes 14155776 | tf_op jit(solution)/shard_map/pallas_call | solution.py:159
  112.1 3.3 %fusion.27 = (f32[2,48,256]{2,1,0:T(8,128)S(1)}, f32[2,16,48,256]{3,2,1,0:T(8,128)}) fusion(f32[2,18,48,256]{3,2,1,0:T(8,128)} %get-tuple-element.37, f32[2,18,48,256]{3,2,1,0:T(8,128)} %get-tuple-element.36), kind=kLoop, calls=%fused_computation.97 | loop fusion | flops 761856 | bytes 4816896 | tf_op jit(solution)/shard_map/reduce_sum | solution.py:237
  115.4 1.9 collective-permute-start.7
  117.3 4.4 %collective-permute-start.6 = (f32[2,16,256]{2,1,0:T(8,128)S(1)}, f32[2,16,256]{2,1,0:T(8,128)S(1)}, u32[]{:S(2)}, u32[]{:S(2)}) collective-permute-start(f32[2,16,256]{2,1,0:T(8,128)S(1)} %slice_multiply_fusion), channel_id=1, source_target_pairs={{0,4},{4,8},{8,12},{12,16},{16,20},{20,24},{24,28},{1,5},{5,9},{9,... | collective-permute-start | bytes 98312 | tf_op jit(solution)/shard_map/ppermute | solution.py:46
  121.7 1.0 collective-permute-done.6
  122.7 1.4 broadcast_multiply_fusion.refs_2_
  124.1 25.0 %shard_map.115 = (f32[2,18,48,256]{3,2,1,0:T(8,128)}, f32[2,18,48,256]{3,2,1,0:T(8,128)}) custom-call(f32[2,15]{1,0:T(2,128)} %constant.118.clone.refs_0_, f32[6,16,48,256]{3,2,1,0:T(8,128)} %bitcast_dynamic-update-slice_fusion.refs_1_, f32[2,16,48,256]{3,2,1,0:T(8,128)} %broadcast_multiply_fusion.refs_2_), custom_call_target="tpu_custom_call" | custom-call | flops 117964800 | bytes 14155776 | tf_op jit(solution)/shard_map/pallas_call | solution.py:159
  149.1 1.3 pad_maximum_fusion.2
  150.5 1.9 collective-permute-start.9
  152.4 4.4 %collective-permute-start.8 = (f32[2,2,18,16,256]{4,3,2,1,0:T(8,128)S(1)}, f32[2,2,18,16,256]{4,3,2,1,0:T(8,128)}, u32[]{:S(2)}, u32[]{:S(2)}) collective-permute-start(f32[2,2,18,16,256]{4,3,2,1,0:T(8,128)S(1)} %pad_maximum_fusion.2), channel_id=1, source_target_pairs={{0,4},{4,8},{8,12},{12,16},{16,20},{20,24},{24,28},{1,5},{5,9},{9,... | collective-permute-start | bytes 3538952 | tf_op jit(solution)/shard_map/ppermute | solution.py:46
  156.8 0.7 fusion.31
  157.5 1.6 constant_dynamic-slice_fusion
  159.1 9.4 %collective-permute-done.9 = f32[2,2,18,16,256]{4,3,2,1,0:T(8,128)S(1)} collective-permute-done((f32[2,2,18,16,256]{4,3,2,1,0:T(8,128)S(1)}, f32[2,2,18,16,256]{4,3,2,1,0:T(8,128)S(1)}, u32[]{:S(2)}, u32[]{:S(2)}) %collective-permute-start.9) | collective-permute-done | bytes 1179680 | tf_op jit(solution)/shard_map/ppermute | solution.py:47
  168.6 1.2 collective-permute-done.8
  169.7 1.5 pad_maximum_fusion.1
  171.3 2.0 slice_bitcast_fusion
  173.3 27.3 %shard_map.116 = (f32[2,18,48,256]{3,2,1,0:T(8,128)}, f32[2,18,48,256]{3,2,1,0:T(8,128)}) custom-call(f32[2,16]{1,0:T(2,128)} %constant.119.clone.refs_0_, f32[6,16,48,256]{3,2,1,0:T(8,128)} %bitcast_dynamic-update-slice_fusion.refs_1_, f32[2,16,48,256]{3,2,1,0:T(8,128)} %broadcast_multiply_fusion.refs_2_, f32[2,18,48,256]{3,2,1,0:T(8,128)} %get-tuple-element.51.refs_3_, ...), custom_call_target="tpu_custom_call" | custom-call | flops 125829120 | bytes 14155776 | tf_op jit(solution)/shard_map/pallas_call | solution.py:159
  200.6 1.0 fusion.18
  201.6 1.4 fusion.25
  (28 shorter events, 2.1 us)
Async XLA Ops:
  4.3 4.8 %collective-permute-start = (f32[13,16,128]{2,1,0:T(8,128)S(1)}, f32[13,16,128]{2,1,0:T(8,128)S(1)}, u32[]{:S(2)}, u32[]{:S(2)}) collective-permute-start(f32[13,16,128]{2,1,0:T(8,128)S(1)} %constant_dynamic-update-slice_fusion), channel_id=1, source_target_pairs={{0,2},{2,0},{1,3},{3,1},{4,6},{6,4},{5,7},{7,5},{8,10},{10,8},{9,1... | collective-permute-start | bytes 319496 | tf_op jit(solution)/shard_map/ppermute | solution.py:57
  9.2 3.9 %collective-permute-start.1 = (f32[8,16,256]{2,1,0:T(8,128)S(1)}, f32[8,16,256]{2,1,0:T(8,128)S(1)}, u32[]{:S(2)}, u32[]{:S(2)}) collective-permute-start(f32[8,16,256]{2,1,0:T(8,128)S(1)} %slice.181), channel_id=1, source_target_pairs={{0,1},{1,0},{2,3},{3,2},{4,5},{5,4},{6,7},{7,6},{8,9},{9,8},{10,11... | collective-permute-start | bytes 393224 | tf_op jit(solution)/shard_map/ppermute | solution.py:57
  13.2 10.6 %collective-permute-start.3 = (f32[21,16,256]{2,1,0:T(8,128)S(1)}, f32[21,16,256]{2,1,0:T(8,128)S(1)}, u32[]{:S(2)}, u32[]{:S(2)}) collective-permute-start(f32[21,16,256]{2,1,0:T(8,128)S(1)} %pad_maximum_fusion.5), channel_id=1, source_target_pairs={{4,0},{8,4},{12,8},{16,12},{20,16},{24,20},{28,24},{5,1},{9,5},{13... | collective-permute-start | bytes 1032200 | tf_op jit(solution)/shard_map/ppermute | solution.py:47
  17.5 7.5 %collective-permute-start.2 = (f32[21,16,256]{2,1,0:T(8,128)S(1)}, f32[21,16,256]{2,1,0:T(8,128)S(1)}, u32[]{:S(2)}, u32[]{:S(2)}) collective-permute-start(f32[21,16,256]{2,1,0:T(8,128)S(1)} %pad_maximum_fusion.5), channel_id=1, source_target_pairs={{0,4},{4,8},{8,12},{12,16},{16,20},{20,24},{24,28},{1,5},{5,9},{9,... | collective-permute-start | bytes 1032200 | tf_op jit(solution)/shard_map/ppermute | solution.py:46
  63.0 18.3 %collective-permute-start.5 = (f32[2,2,18,16,256]{4,3,2,1,0:T(8,128)S(1)}, f32[2,2,18,16,256]{4,3,2,1,0:T(8,128)S(1)}, u32[]{:S(2)}, u32[]{:S(2)}) collective-permute-start(f32[2,2,18,16,256]{4,3,2,1,0:T(8,128)S(1)} %pad_maximum_fusion.3), channel_id=1, source_target_pairs={{4,0},{8,4},{12,8},{16,12},{20,16},{24,20},{28,24},{5,1},{9,5},{13... | collective-permute-start | bytes 3538952 | tf_op jit(solution)/shard_map/ppermute | solution.py:47
  65.0 17.5 %collective-permute-start.4 = (f32[2,2,18,16,256]{4,3,2,1,0:T(8,128)S(1)}, f32[2,2,18,16,256]{4,3,2,1,0:T(8,128)S(1)}, u32[]{:S(2)}, u32[]{:S(2)}) collective-permute-start(f32[2,2,18,16,256]{4,3,2,1,0:T(8,128)S(1)} %pad_maximum_fusion.3), channel_id=1, source_target_pairs={{0,4},{4,8},{8,12},{12,16},{16,20},{20,24},{24,28},{1,5},{5,9},{9,... | collective-permute-start | bytes 3538952 | tf_op jit(solution)/shard_map/ppermute | solution.py:46
  115.4 6.3 %collective-permute-start.7 = (f32[2,16,256]{2,1,0:T(8,128)S(1)}, f32[2,16,256]{2,1,0:T(8,128)S(1)}, u32[]{:S(2)}, u32[]{:S(2)}) collective-permute-start(f32[2,16,256]{2,1,0:T(8,128)S(1)} %slice_multiply_fusion), channel_id=1, source_target_pairs={{4,0},{8,4},{12,8},{16,12},{20,16},{24,20},{28,24},{5,1},{9,5},{13... | collective-permute-start | bytes 98312 | tf_op jit(solution)/shard_map/ppermute | solution.py:47
  117.3 5.4 %collective-permute-start.6 = (f32[2,16,256]{2,1,0:T(8,128)S(1)}, f32[2,16,256]{2,1,0:T(8,128)S(1)}, u32[]{:S(2)}, u32[]{:S(2)}) collective-permute-start(f32[2,16,256]{2,1,0:T(8,128)S(1)} %slice_multiply_fusion), channel_id=1, source_target_pairs={{0,4},{4,8},{8,12},{12,16},{16,20},{20,24},{24,28},{1,5},{5,9},{9,... | collective-permute-start | bytes 98312 | tf_op jit(solution)/shard_map/ppermute | solution.py:46
  150.5 18.1 %collective-permute-start.9 = (f32[2,2,18,16,256]{4,3,2,1,0:T(8,128)S(1)}, f32[2,2,18,16,256]{4,3,2,1,0:T(8,128)S(1)}, u32[]{:S(2)}, u32[]{:S(2)}) collective-permute-start(f32[2,2,18,16,256]{4,3,2,1,0:T(8,128)S(1)} %pad_maximum_fusion.2), channel_id=1, source_target_pairs={{4,0},{8,4},{12,8},{16,12},{20,16},{24,20},{28,24},{5,1},{9,5},{13... | collective-permute-start | bytes 3538952 | tf_op jit(solution)/shard_map/ppermute | solution.py:47
  152.4 17.4 %collective-permute-start.8 = (f32[2,2,18,16,256]{4,3,2,1,0:T(8,128)S(1)}, f32[2,2,18,16,256]{4,3,2,1,0:T(8,128)}, u32[]{:S(2)}, u32[]{:S(2)}) collective-permute-start(f32[2,2,18,16,256]{4,3,2,1,0:T(8,128)S(1)} %pad_maximum_fusion.2), channel_id=1, source_target_pairs={{0,4},{4,8},{8,12},{12,16},{16,20},{20,24},{24,28},{1,5},{5,9},{9,... | collective-permute-start | bytes 3538952 | tf_op jit(solution)/shard_map/ppermute | solution.py:46
  173.3 28.3 %copy-start = (f32[47,256]{1,0:T(8,128)S(1)}, f32[47,256]{1,0:T(8,128)}, u32[]{:S(2)}) copy-start(f32[47,256]{1,0:T(8,128)} %get-tuple-element.60) | copy-start | bytes 144388
  173.3 28.3 %copy-start.1 = (f32[48,255]{1,0:T(8,128)S(1)}, f32[48,255]{1,0:T(8,128)}, u32[]{:S(2)}) copy-start(f32[48,255]{1,0:T(8,128)} %get-tuple-element.65) | copy-start | bytes 146884
  173.3 28.3 %copy-start.2 = (f32[48,255]{1,0:T(8,128)S(1)}, f32[48,255]{1,0:T(8,128)}, u32[]{:S(2)}) copy-start(f32[48,255]{1,0:T(8,128)} %get-tuple-element.66) | copy-start | bytes 146884

commit v10 on v9

--- a/solution.py
+++ b/solution.py
@@ -70,13 +70,25 @@
     return jnp.concatenate([z, lax.slice_in_dim(a, 0, n - 1, axis=axis)], axis=axis)
 
 
-def segment_kernel(steps, start_valid, table_ref, op_ref, rhs_ref, *refs):
+def segment_kernel(steps, start_valid, halo, send, table_ref, op_ref, rhs_ref, *refs):
     comps, layers = rhs_ref.shape[0], rhs_ref.shape[1]
     rows, cols = rhs_ref.shape[2], rhs_ref.shape[3]
-    if len(refs) == 4:
-        x_in, d_in, x_ref, d_ref = refs
+    own = rows - 2 * halo
+    if send:
+        refs, up_ref, down_ref = refs[:-2], refs[-2], refs[-1]
+    if len(refs) == 6:
+        x_in, d_in, low_in, high_in, x_ref, d_ref = refs
         x_ref[...] = x_in[...]
         d_ref[...] = d_in[...]
+
+        def place(layer, carry):
+            for c in range(comps):
+                for f, ref in enumerate((x_ref, d_ref)):
+                    ref[c, layer + 1, pl.ds(0, halo)] = low_in[f, c, layer]
+                    ref[c, layer + 1, pl.ds(halo + own, halo)] = high_in[f, c, layer]
+            return carry
+
+        lax.fori_loop(0, layers, place, 0)
     else:
         x_ref, d_ref = refs
         zero = jnp.zeros((rows, cols), jnp.float32)
@@ -144,8 +156,18 @@
         lax.fori_loop(j, end, body, 0)
         j = end
 
-
-def run_segment(steps, start_valid, op_stack, rhs, iterate, step_dir):
+    if send:
+        def pack(layer, carry):
+            for c in range(comps):
+                for f, ref in enumerate((x_ref, d_ref)):
+                    up_ref[f, c, layer] = ref[c, layer + 1, pl.ds(own, halo)]
+                    down_ref[f, c, layer] = ref[c, layer + 1, pl.ds(halo, halo)]
+            return carry
+
+        lax.fori_loop(0, layers, pack, 0)
+
+
+def run_segment(steps, start_valid, halo, send, op_stack, rhs, state):
     comps, layers, rows, cols = rhs.shape
     vmem = pl.BlockSpec(memory_space=pltpu.VMEM)
     smem = pl.BlockSpec(memory_space=pltpu.SMEM)
@@ -154,16 +176,14 @@
         [[0.0 if kp is None else kp for kp, _ in steps], [0.0 if kp is None else ps for kp, ps in steps]],
         jnp.float32,
     )
-    state = () if iterate is None else (iterate, step_dir)
-    padded_shape = (comps, layers + 2, rows, cols)
+    padded_shape = jax.ShapeDtypeStruct((comps, layers + 2, rows, cols), jnp.float32)
+    slab_shape = jax.ShapeDtypeStruct((2, comps, layers, halo, cols), jnp.float32)
+    out_shape = (padded_shape, padded_shape) + ((slab_shape, slab_shape) if send else ())
     return pl.pallas_call(
-        lambda *refs: segment_kernel(steps, start_valid, *refs),
-        out_shape=(
-            jax.ShapeDtypeStruct(padded_shape, jnp.float32),
-            jax.ShapeDtypeStruct(padded_shape, jnp.float32),
-        ),
+        lambda *refs: segment_kernel(steps, start_valid, halo, send, *refs),
+        out_shape=out_shape,
         in_specs=[smem] + [vmem] * (2 + len(state)),
-        out_specs=(vmem, vmem),
+        out_specs=tuple(vmem for _ in out_shape),
         cost_estimate=pl.CostEstimate(
             flops=20 * cells * len(steps), bytes_accessed=4 * cells * 9, transcendentals=0
         ),
@@ -213,21 +233,27 @@
     table = step_constants()
 
     def chebyshev(rhs):
-        iterate, step_dir = None, None
+        count = lax.axis_size("mx")
+        forward = [(i, i + 1) for i in range(count - 1)]
+        backward = [(i + 1, i) for i in range(count - 1)]
+        state = ()
         since = 1
         start_valid = 1
         run = []
         for keep, push in table:
             if since == k:
-                iterate, step_dir = run_segment(tuple(run), start_valid, op_stack, rhs, iterate, step_dir)
+                iterate, step_dir, up, down = run_segment(
+                    tuple(run), start_valid, k, True, op_stack, rhs, state
+                )
+                low = lax.ppermute(up, "mx", forward)
+                high = lax.ppermute(down, "mx", backward)
+                state = (iterate, step_dir, low, high)
                 run = []
                 start_valid = 0
-                both = exchange_rows(jnp.stack([iterate, step_dir]), k, rows, 3)
-                iterate, step_dir = both[0], both[1]
                 since = 0
             run.append((keep, push))
             since += 1
-        iterate, step_dir = run_segment(tuple(run), start_valid, op_stack, rhs, iterate, step_dir)
+        iterate, step_dir = run_segment(tuple(run), start_valid, k, False, op_stack, rhs, state)
         return (iterate + step_dir)[:, 1 : layers + 1]
 
     forcing = jnp.zeros((2,) + eta.shape, jnp.float32)

time: 204 us -> 199 us (0.975)
  other arithmetic: 22.7 us -> 15.2 us
  local copies, waits for them, and re-layouts: 10.6 us -> 6.07 us
  waiting for transfers between devices: 34.4 us -> 38.6 us
  Pallas kernels: 105 us -> 108 us
    ppermute x0 -> x4, waiting for transfers between devices: none -> 27.7 us  [the longest x2 19.1 us: chebyshev(): low = lax.ppermute(up, 'mx', forward)]
    ppermute x4 -> x2, waiting for transfers between devices: 24.2 us -> 2.99 us  [exchange_rows(): high = lax.ppermute(lax.slice_in_dim(own, 0, k, axis=axis), 'mx', backward)]
    ppermute x0 -> x4, starting transfers between devices: none -> 12.8 us  [the longest x2 8.59 us: chebyshev(): low = lax.ppermute(up, 'mx', forward)]
    ppermute x4 -> x2, starting transfers between devices: 16.7 us -> 6.97 us  [exchange_rows(): lax.ppermute(lax.slice_in_dim(own, rows - k, rows, axis=axis), 'mx', forw...]
    squeeze x2 -> x0, local copies, waits for them, and re-layouts: 4.04 us -> none  [chebyshev(): iterate, step_dir = (both[0], both[1])]
    ppermute x4 -> x2, starting transfers between devices: 10 us -> 6.21 us  [exchange_rows(): high = lax.ppermute(lax.slice_in_dim(own, 0, k, axis=axis), 'mx', backward)]
    pallas_call x4, Pallas kernels: 105 us -> 108 us  [run_segment(): pl.pallas_call(lambda *refs: segment_kernel(steps, start_valid, halo, sen...]
    another operation x3 -> x1, other arithmetic: 2.67 us -> 0.01 us  [the longest x2 2.66 us: chebyshev(): both = exchange_rows(jnp.stack([iterate, step_dir]), k, rows, 3)]
  transfers between devices with their start and end apart: 10 -> 10, of which waited for: 9 -> 9; matrix products, arithmetic and copies ran while one was open for 1% -> 0% of each run, Pallas kernels for 0% -> 0%
where the time goes in v10:
time: 199 us; the launch traced here: 198 us
  Pallas kernels  108 us (54%)
  waiting for transfers between devices  38.6 us (19%)
  starting transfers between devices  29 us (15%)
  other arithmetic  15.2 us (8%)
  local copies, waits for them, and re-layouts  6.07 us (3%)
    pallas_call x4, Pallas kernels, run_segment(): pl.pallas_call(lambda *refs: segment_kernel(steps, start_valid, halo, sen...  108 us
    ppermute x2, waiting for transfers between devices, chebyshev(): low = lax.ppermute(up, 'mx', forward)  19.1 us
    ppermute x2, waiting for transfers between devices, chebyshev(): high = lax.ppermute(down, 'mx', backward)  8.68 us
    ppermute x2, starting transfers between devices, chebyshev(): low = lax.ppermute(up, 'mx', forward)  8.59 us
    unnamed x7, other arithmetic  7.08 us
    ppermute x2, starting transfers between devices, exchange_rows(): lax.ppermute(lax.slice_in_dim(own, rows - k, rows, axis=axis), 'mx', forw...  6.97 us
    ppermute x2, starting transfers between devices, exchange_rows(): high = lax.ppermute(lax.slice_in_dim(own, 0, k, axis=axis), 'mx', backward)  6.21 us
    ppermute x2, waiting for transfers between devices, gather_axis(): seq.append(lax.ppermute(block, axis, pairs))  5.67 us
  transfers between devices with their start and end apart: 10, of which 9 were waited for; matrix products, arithmetic and copies ran while one was open for 0% of the time, Pallas kernels for 0%

profile of v10, /device:TPU:1, one launch (start us, length us, event | category | flops | bytes accessed | tf_op | source)
XLA Modules:
  0.0 198.0 jit_solution(11181225974064841897)
XLA Ops:
  0.6 0.8 constant_dynamic-update-slice_fusion.4
  1.5 0.7 constant_dynamic-update-slice_fusion.3
  2.2 0.7 constant_dynamic-update-slice_fusion.2
  2.9 0.7 constant_dynamic-update-slice_fusion.1
  3.6 0.7 constant_dynamic-update-slice_fusion
  4.3 2.1 %collective-permute-start = (f32[13,16,128]{2,1,0:T(8,128)S(1)}, f32[13,16,128]{2,1,0:T(8,128)S(1)}, u32[]{:S(2)}, u32[]{:S(2)}) collective-permute-start(f32[13,16,128]{2,1,0:T(8,128)S(1)} %constant_dynamic-update-slice_fusion), channel_id=1, source_target_pairs={{0,2},{2,0},{1,3},{3,1},{4,6},{6,4},{5,7},{7,5},{8,10},{10,8},{9,1... | collective-permute-start | bytes 319496 | tf_op jit(solution)/shard_map/ppermute | solution.py:57
  6.4 2.7 %collective-permute-done = f32[13,16,128]{2,1,0:T(8,128)S(1)} collective-permute-done((f32[13,16,128]{2,1,0:T(8,128)S(1)}, f32[13,16,128]{2,1,0:T(8,128)S(1)}, u32[]{:S(2)}, u32[]{:S(2)}) %collective-permute-start) | collective-permute-done | bytes 106528 | tf_op jit(solution)/shard_map/ppermute | solution.py:57
  9.2 0.9 collective-permute-start.1
  10.1 3.0 %collective-permute-done.1 = f32[8,16,256]{2,1,0:T(8,128)S(1)} collective-permute-done((f32[8,16,256]{2,1,0:T(8,128)S(1)}, f32[8,16,256]{2,1,0:T(8,128)S(1)}, u32[]{:S(2)}, u32[]{:S(2)}) %collective-permute-start.1) | collective-permute-done | bytes 131104 | tf_op jit(solution)/shard_map/ppermute | solution.py:57
  13.0 0.1 fusion.12
  13.2 4.3 %collective-permute-start.3 = (f32[21,16,256]{2,1,0:T(8,128)S(1)}, f32[21,16,256]{2,1,0:T(8,128)S(1)}, u32[]{:S(2)}, u32[]{:S(2)}) collective-permute-start(f32[21,16,256]{2,1,0:T(8,128)S(1)} %pad_maximum_fusion.1), channel_id=1, source_target_pairs={{4,0},{8,4},{12,8},{16,12},{20,16},{24,20},{28,24},{5,1},{9,5},{13... | collective-permute-start | bytes 1032200 | tf_op jit(solution)/shard_map/ppermute | solution.py:47
  17.5 3.3 %collective-permute-start.2 = (f32[21,16,256]{2,1,0:T(8,128)S(1)}, f32[21,16,256]{2,1,0:T(8,128)S(1)}, u32[]{:S(2)}, u32[]{:S(2)}) collective-permute-start(f32[21,16,256]{2,1,0:T(8,128)S(1)} %pad_maximum_fusion.1), channel_id=1, source_target_pairs={{0,4},{4,8},{8,12},{12,16},{16,20},{20,24},{24,28},{1,5},{5,9},{9,... | collective-permute-start | bytes 1032200 | tf_op jit(solution)/shard_map/ppermute | solution.py:46
  20.8 3.0 %collective-permute-done.3 = f32[21,16,256]{2,1,0:T(8,128)S(1)} collective-permute-done((f32[21,16,256]{2,1,0:T(8,128)S(1)}, f32[21,16,256]{2,1,0:T(8,128)S(1)}, u32[]{:S(2)}, u32[]{:S(2)}) %collective-permute-start.3) | collective-permute-done | bytes 344096 | tf_op jit(solution)/shard_map/ppermute | solution.py:47
  23.8 1.2 collective-permute-done.2
  25.1 0.2 fusion.30
  25.3 0.3 fusion.29
  25.6 0.2 fusion.28
  25.8 0.1 concatenate.69
  25.9 0.2 pad_multiply_fusion
  26.1 1.4 copy.13.refs_2_
  27.4 1.1 bitcast_dynamic-update-slice_fusion.5
  28.5 1.1 bitcast_dynamic-update-slice_fusion.4
  29.7 1.4 fusion.8
  31.1 1.2 bitcast_dynamic-update-slice_fusion.3
  32.3 1.2 bitcast_dynamic-update-slice_fusion.2
  33.6 1.0 bitcast_dynamic-update-slice_fusion.1
  34.5 1.0 bitcast_dynamic-update-slice_fusion.refs_1_
  35.5 25.9 %shard_map.113 = (f32[2,18,48,256]{3,2,1,0:T(8,128)}, f32[2,18,48,256]{3,2,1,0:T(8,128)}, f32[2,2,16,16,256]{4,3,2,1,0:T(8,128)}, f32[2,2,16,16,256]{4,3,2,1,0:T(8,128)}) custom-call(f32[2,15]{1,0:T(2,128)} %constant.118.clone.refs_0_, f32[6,16,48,256]{3,2,1,0:T(8,128)} %bitcast_dynamic-update-slice_fusion.refs_1_, f32[2,16,48,256]{3,2,1,0:T(8,128)} %copy.13.refs_2_), custom_call_target="tpu_custom_call" | custom-call | flops 117964800 | bytes 14155776 | tf_op jit(solution)/shard_map/pallas_call | solution.py:182
  61.5 4.4 %collective-permute-start.4 = (f32[2,2,16,16,256]{4,3,2,1,0:T(8,128)}, f32[2,2,16,16,256]{4,3,2,1,0:T(8,128)S(1)}, u32[]{:S(2)}, u32[]{:S(2)}) collective-permute-start(f32[2,2,16,16,256]{4,3,2,1,0:T(8,128)} %get-tuple-element.40), channel_id=1, source_target_pairs={{0,4},{4,8},{8,12},{12,16},{16,20},{20,24},{24,28},{1,5},{5,9},{9,... | collective-permute-start | bytes 3145736 | tf_op jit(solution)/shard_map/ppermute | solution.py:248
  65.8 2.1 %collective-permute-start.5 = (f32[2,2,16,16,256]{4,3,2,1,0:T(8,128)}, f32[2,2,16,16,256]{4,3,2,1,0:T(8,128)S(1)}, u32[]{:S(2)}, u32[]{:S(2)}) collective-permute-start(f32[2,2,16,16,256]{4,3,2,1,0:T(8,128)} %get-tuple-element.41), channel_id=1, source_target_pairs={{4,0},{8,4},{12,8},{16,12},{20,16},{24,20},{28,24},{5,1},{9,5},{13... | collective-permute-start | bytes 3145736 | tf_op jit(solution)/shard_map/ppermute | solution.py:249
  67.9 9.9 %collective-permute-done.4.refs_5_ = f32[2,2,16,16,256]{4,3,2,1,0:T(8,128)S(1)} collective-permute-done((f32[2,2,16,16,256]{4,3,2,1,0:T(8,128)}, f32[2,2,16,16,256]{4,3,2,1,0:T(8,128)S(1)}, u32[]{:S(2)}, u32[]{:S(2)}) %collective-permute-start.4) | collective-permute-done | bytes 1048608 | tf_op jit(solution)/shard_map/ppermute | solution.py:248
  77.9 4.3 %collective-permute-done.5.refs_6_ = f32[2,2,16,16,256]{4,3,2,1,0:T(8,128)S(1)} collective-permute-done((f32[2,2,16,16,256]{4,3,2,1,0:T(8,128)}, f32[2,2,16,16,256]{4,3,2,1,0:T(8,128)S(1)}, u32[]{:S(2)}, u32[]{:S(2)}) %collective-permute-start.5) | collective-permute-done | bytes 1048608 | tf_op jit(solution)/shard_map/ppermute | solution.py:249
  82.2 1.0 copy-done.1
  83.2 28.2 %shard_map.114 = (f32[2,18,48,256]{3,2,1,0:T(8,128)}, f32[2,18,48,256]{3,2,1,0:T(8,128)}) custom-call(f32[2,16]{1,0:T(2,128)} %constant.119.clone.refs_0_, f32[6,16,48,256]{3,2,1,0:T(8,128)} %bitcast_dynamic-update-slice_fusion.refs_1_, f32[2,16,48,256]{3,2,1,0:T(8,128)} %copy.13.refs_2_, f32[2,18,48,256]{3,2,1,0:T(8,128)} %get-tuple-element.38.refs_3_, ...), custom_call_target="tpu_custom_call" | custom-call | flops 125829120 | bytes 14155776 | tf_op jit(solution)/shard_map/pallas_call | solution.py:182
  111.4 2.1 %fusion.27 = (f32[2,48,256]{2,1,0:T(8,128)S(1)}, f32[2,16,48,256]{3,2,1,0:T(8,128)S(1)}) fusion(f32[2,18,48,256]{3,2,1,0:T(8,128)} %get-tuple-element.43, f32[2,18,48,256]{3,2,1,0:T(8,128)} %get-tuple-element.42), kind=kLoop, calls=%fused_computation.89 | loop fusion | flops 761856 | bytes 4816896 | tf_op jit(solution)/shard_map/reduce_sum | solution.py:263
  113.5 1.9 collective-permute-start.7
  115.4 3.6 %collective-permute-start.6 = (f32[2,16,256]{2,1,0:T(8,128)S(1)}, f32[2,16,256]{2,1,0:T(8,128)S(1)}, u32[]{:S(2)}, u32[]{:S(2)}) collective-permute-start(f32[2,16,256]{2,1,0:T(8,128)S(1)} %slice_multiply_fusion), channel_id=1, source_target_pairs={{0,4},{4,8},{8,12},{12,16},{16,20},{20,24},{24,28},{1,5},{5,9},{9,... | collective-permute-start | bytes 98312 | tf_op jit(solution)/shard_map/ppermute | solution.py:46
  119.1 1.0 collective-permute-done.6
  120.1 1.4 broadcast_multiply_fusion.refs_2_
  121.5 25.9 %shard_map.115 = (f32[2,18,48,256]{3,2,1,0:T(8,128)}, f32[2,18,48,256]{3,2,1,0:T(8,128)}, f32[2,2,16,16,256]{4,3,2,1,0:T(8,128)}, f32[2,2,16,16,256]{4,3,2,1,0:T(8,128)}) custom-call(f32[2,15]{1,0:T(2,128)} %constant.118.clone.refs_0_, f32[6,16,48,256]{3,2,1,0:T(8,128)} %bitcast_dynamic-update-slice_fusion.refs_1_, ...), custom_call_target="tpu_custom_call" | custom-call | flops 117964800 | bytes 14155776 | tf_op jit(solution)/shard_map/pallas_call | solution.py:182
  147.4 4.2 %collective-permute-start.8 = (f32[2,2,16,16,256]{4,3,2,1,0:T(8,128)}, f32[2,2,16,16,256]{4,3,2,1,0:T(8,128)}, u32[]{:S(2)}, u32[]{:S(2)}) collective-permute-start(f32[2,2,16,16,256]{4,3,2,1,0:T(8,128)} %get-tuple-element.46), channel_id=1, source_target_pairs={{0,4},{4,8},{8,12},{12,16},{16,20},{20,24},{24,28},{1,5},{5,9},{9,... | collective-permute-start | bytes 3145736 | tf_op jit(solution)/shard_map/ppermute | solution.py:248
  151.7 2.1 %collective-permute-start.9 = (f32[2,2,16,16,256]{4,3,2,1,0:T(8,128)}, f32[2,2,16,16,256]{4,3,2,1,0:T(8,128)}, u32[]{:S(2)}, u32[]{:S(2)}) collective-permute-start(f32[2,2,16,16,256]{4,3,2,1,0:T(8,128)} %get-tuple-element.47), channel_id=1, source_target_pairs={{4,0},{8,4},{12,8},{16,12},{20,16},{24,20},{28,24},{5,1},{9,5},{13... | collective-permute-start | bytes 3145736 | tf_op jit(solution)/shard_map/ppermute | solution.py:249
  153.9 0.7 constant_dynamic-slice_fusion
  154.6 9.1 %collective-permute-done.8.refs_5_ = f32[2,2,16,16,256]{4,3,2,1,0:T(8,128)} collective-permute-done((f32[2,2,16,16,256]{4,3,2,1,0:T(8,128)}, f32[2,2,16,16,256]{4,3,2,1,0:T(8,128)}, u32[]{:S(2)}, u32[]{:S(2)}) %collective-permute-start.8) | collective-permute-done | bytes 1048608 | tf_op jit(solution)/shard_map/ppermute | solution.py:248
  163.7 4.4 %collective-permute-done.9.refs_6_ = f32[2,2,16,16,256]{4,3,2,1,0:T(8,128)} collective-permute-done((f32[2,2,16,16,256]{4,3,2,1,0:T(8,128)}, f32[2,2,16,16,256]{4,3,2,1,0:T(8,128)}, u32[]{:S(2)}, u32[]{:S(2)}) %collective-permute-start.9) | collective-permute-done | bytes 1048608 | tf_op jit(solution)/shard_map/ppermute | solution.py:249
  168.1 28.2 %shard_map.116 = (f32[2,18,48,256]{3,2,1,0:T(8,128)}, f32[2,18,48,256]{3,2,1,0:T(8,128)}) custom-call(f32[2,16]{1,0:T(2,128)} %constant.119.clone.refs_0_, f32[6,16,48,256]{3,2,1,0:T(8,128)} %bitcast_dynamic-update-slice_fusion.refs_1_, f32[2,16,48,256]{3,2,1,0:T(8,128)} %broadcast_multiply_fusion.refs_2_, f32[2,18,48,256]{3,2,1,0:T(8,128)} %get-tuple-element.44.refs_3_, ...), custom_call_target="tpu_custom_call" | custom-call | flops 125829120 | bytes 14155776 | tf_op jit(solution)/shard_map/pallas_call | solution.py:182
  196.3 1.0 fusion.18
  197.3 0.7 fusion.25
  (20 shorter events, 0.4 us)
Async XLA Ops:
  4.3 4.8 %collective-permute-start = (f32[13,16,128]{2,1,0:T(8,128)S(1)}, f32[13,16,128]{2,1,0:T(8,128)S(1)}, u32[]{:S(2)}, u32[]{:S(2)}) collective-permute-start(f32[13,16,128]{2,1,0:T(8,128)S(1)} %constant_dynamic-update-slice_fusion), channel_id=1, source_target_pairs={{0,2},{2,0},{1,3},{3,1},{4,6},{6,4},{5,7},{7,5},{8,10},{10,8},{9,1... | collective-permute-start | bytes 319496 | tf_op jit(solution)/shard_map/ppermute | solution.py:57
  9.2 3.9 %collective-permute-start.1 = (f32[8,16,256]{2,1,0:T(8,128)S(1)}, f32[8,16,256]{2,1,0:T(8,128)S(1)}, u32[]{:S(2)}, u32[]{:S(2)}) collective-permute-start(f32[8,16,256]{2,1,0:T(8,128)S(1)} %slice.157), channel_id=1, source_target_pairs={{0,1},{1,0},{2,3},{3,2},{4,5},{5,4},{6,7},{7,6},{8,9},{9,8},{10,11... | collective-permute-start | bytes 393224 | tf_op jit(solution)/shard_map/ppermute | solution.py:57
  13.2 10.6 %collective-permute-start.3 = (f32[21,16,256]{2,1,0:T(8,128)S(1)}, f32[21,16,256]{2,1,0:T(8,128)S(1)}, u32[]{:S(2)}, u32[]{:S(2)}) collective-permute-start(f32[21,16,256]{2,1,0:T(8,128)S(1)} %pad_maximum_fusion.1), channel_id=1, source_target_pairs={{4,0},{8,4},{12,8},{16,12},{20,16},{24,20},{28,24},{5,1},{9,5},{13... | collective-permute-start | bytes 1032200 | tf_op jit(solution)/shard_map/ppermute | solution.py:47
  17.5 7.5 %collective-permute-start.2 = (f32[21,16,256]{2,1,0:T(8,128)S(1)}, f32[21,16,256]{2,1,0:T(8,128)S(1)}, u32[]{:S(2)}, u32[]{:S(2)}) collective-permute-start(f32[21,16,256]{2,1,0:T(8,128)S(1)} %pad_maximum_fusion.1), channel_id=1, source_target_pairs={{0,4},{4,8},{8,12},{12,16},{16,20},{20,24},{24,28},{1,5},{5,9},{9,... | collective-permute-start | bytes 1032200 | tf_op jit(solution)/shard_map/ppermute | solution.py:46
  61.5 16.4 %collective-permute-start.4 = (f32[2,2,16,16,256]{4,3,2,1,0:T(8,128)}, f32[2,2,16,16,256]{4,3,2,1,0:T(8,128)S(1)}, u32[]{:S(2)}, u32[]{:S(2)}) collective-permute-start(f32[2,2,16,16,256]{4,3,2,1,0:T(8,128)} %get-tuple-element.40), channel_id=1, source_target_pairs={{0,4},{4,8},{8,12},{12,16},{16,20},{20,24},{24,28},{1,5},{5,9},{9,... | collective-permute-start | bytes 3145736 | tf_op jit(solution)/shard_map/ppermute | solution.py:248
  65.8 16.3 %collective-permute-start.5 = (f32[2,2,16,16,256]{4,3,2,1,0:T(8,128)}, f32[2,2,16,16,256]{4,3,2,1,0:T(8,128)S(1)}, u32[]{:S(2)}, u32[]{:S(2)}) collective-permute-start(f32[2,2,16,16,256]{4,3,2,1,0:T(8,128)} %get-tuple-element.41), channel_id=1, source_target_pairs={{4,0},{8,4},{12,8},{16,12},{20,16},{24,20},{28,24},{5,1},{9,5},{13... | collective-permute-start | bytes 3145736 | tf_op jit(solution)/shard_map/ppermute | solution.py:249
  77.9 4.3 %copy-start = (f32[2,2,16,16,256]{4,3,2,1,0:T(8,128)}, f32[2,2,16,16,256]{4,3,2,1,0:T(8,128)S(1)}, u32[]{:S(2)}) copy-start(f32[2,2,16,16,256]{4,3,2,1,0:T(8,128)S(1)} %collective-permute-done.4.refs_5_) | copy-start | bytes 3145732
  82.2 1.0 copy-start.1
  113.5 5.6 %collective-permute-start.7 = (f32[2,16,256]{2,1,0:T(8,128)S(1)}, f32[2,16,256]{2,1,0:T(8,128)S(1)}, u32[]{:S(2)}, u32[]{:S(2)}) collective-permute-start(f32[2,16,256]{2,1,0:T(8,128)S(1)} %slice_multiply_fusion), channel_id=1, source_target_pairs={{4,0},{8,4},{12,8},{16,12},{20,16},{24,20},{28,24},{5,1},{9,5},{13... | collective-permute-start | bytes 98312 | tf_op jit(solution)/shard_map/ppermute | solution.py:47
  115.4 4.7 %collective-permute-start.6 = (f32[2,16,256]{2,1,0:T(8,128)S(1)}, f32[2,16,256]{2,1,0:T(8,128)S(1)}, u32[]{:S(2)}, u32[]{:S(2)}) collective-permute-start(f32[2,16,256]{2,1,0:T(8,128)S(1)} %slice_multiply_fusion), channel_id=1, source_target_pairs={{0,4},{4,8},{8,12},{12,16},{16,20},{20,24},{24,28},{1,5},{5,9},{9,... | collective-permute-start | bytes 98312 | tf_op jit(solution)/shard_map/ppermute | solution.py:46
  147.4 16.3 %collective-permute-start.8 = (f32[2,2,16,16,256]{4,3,2,1,0:T(8,128)}, f32[2,2,16,16,256]{4,3,2,1,0:T(8,128)}, u32[]{:S(2)}, u32[]{:S(2)}) collective-permute-start(f32[2,2,16,16,256]{4,3,2,1,0:T(8,128)} %get-tuple-element.46), channel_id=1, source_target_pairs={{0,4},{4,8},{8,12},{12,16},{16,20},{20,24},{24,28},{1,5},{5,9},{9,... | collective-permute-start | bytes 3145736 | tf_op jit(solution)/shard_map/ppermute | solution.py:248
  151.7 16.4 %collective-permute-start.9 = (f32[2,2,16,16,256]{4,3,2,1,0:T(8,128)}, f32[2,2,16,16,256]{4,3,2,1,0:T(8,128)}, u32[]{:S(2)}, u32[]{:S(2)}) collective-permute-start(f32[2,2,16,16,256]{4,3,2,1,0:T(8,128)} %get-tuple-element.47), channel_id=1, source_target_pairs={{4,0},{8,4},{12,8},{16,12},{20,16},{24,20},{28,24},{5,1},{9,5},{13... | collective-permute-start | bytes 3145736 | tf_op jit(solution)/shard_map/ppermute | solution.py:249

commit v11 on v10

--- a/solution.py
+++ b/solution.py
@@ -197,10 +197,32 @@
     k = min(HALO, rows)
     act = (1 - ice_free).astype(jnp.float32)
     bed_coef = grounded.astype(jnp.float32) * friction
-    planes = jnp.stack([act, bed_coef, base_velocity[0], base_velocity[1], direction])
-    both = gather_axis(jnp.concatenate([viscosity, planes], axis=0), "my", 2)
+    local_stack = jnp.concatenate(
+        [viscosity, act[None], bed_coef[None], base_velocity, direction[None]], axis=0
+    )
+    if lax.axis_size("vz") == 2 and lax.axis_size("my") == 2:
+        swap = [(0, 1), (1, 0)]
+        across_my = lax.ppermute(local_stack, "my", swap)
+        across_vz = lax.ppermute(viscosity, "vz", swap)
+        diagonal = lax.ppermute(viscosity, ("my", "vz"), [(i, 3 - i) for i in range(4)])
+        first_my = lax.axis_index("my") == 0
+        first_vz = lax.axis_index("vz") == 0
+
+        def by_my(mine, other):
+            return jnp.where(first_my, jnp.concatenate([mine, other], axis=2), jnp.concatenate([other, mine], axis=2))
+
+        both = by_my(local_stack, across_my)
+        other_half = by_my(across_vz, diagonal)
+        mine_half = both[:layers_own]
+        eta = jnp.where(
+            first_vz,
+            jnp.concatenate([mine_half, other_half], axis=0),
+            jnp.concatenate([other_half, mine_half], axis=0),
+        )
+    else:
+        both = gather_axis(local_stack, "my", 2)
+        eta = gather_axis(both[:layers_own], "vz", 0)
     planes = both[layers_own:]
-    eta = gather_axis(both[:layers_own], "vz", 0)
     layers = eta.shape[0]
     joined = jnp.concatenate([eta, planes], axis=0)
     zeros_halo = jnp.zeros(joined.shape[:1] + (k,) + joined.shape[2:], joined.dtype)

time: 199 us -> 196 us (0.985)
  waiting for transfers between devices: 38.6 us -> 36.3 us
    ppermute x2 -> x3, waiting for transfers between devices: 5.67 us -> 3.43 us  [the longest x1 3.43 us: local(): across_my = lax.ppermute(local_stack, 'my', swap)]
  transfers between devices with their start and end apart: 10 -> 11, of which waited for: 9 -> 8; matrix products, arithmetic and copies ran while one was open for 0% -> 2% of each run, Pallas kernels for 0% -> 0%
where the time goes in v11:
time: 196 us
  Pallas kernels  108 us (55%)
  waiting for transfers between devices  36.3 us (19%)
  starting transfers between devices  29.2 us (15%)
  other arithmetic  15.1 us (8%)
  local copies, waits for them, and re-layouts  6.09 us (3%)
    pallas_call x4, Pallas kernels, run_segment(): pl.pallas_call(lambda *refs: segment_kernel(steps, start_valid, halo, sen...  108 us
    ppermute x2, waiting for transfers between devices, chebyshev(): low = lax.ppermute(up, 'mx', forward)  19.1 us
    ppermute x2, waiting for transfers between devices, chebyshev(): high = lax.ppermute(down, 'mx', backward)  8.68 us
    ppermute x2, starting transfers between devices, chebyshev(): low = lax.ppermute(up, 'mx', forward)  8.59 us
    unnamed x7, other arithmetic  7.08 us
    ppermute x2, starting transfers between devices, exchange_rows(): lax.ppermute(lax.slice_in_dim(own, rows - k, rows, axis=axis), 'mx', forw...  6.74 us
    ppermute x2, starting transfers between devices, exchange_rows(): high = lax.ppermute(lax.slice_in_dim(own, 0, k, axis=axis), 'mx', backward)  6.21 us
    ppermute x2, starting transfers between devices, chebyshev(): high = lax.ppermute(down, 'mx', backward)  4.24 us
  transfers between devices with their start and end apart: 11, of which 8 were waited for; matrix products, arithmetic and copies ran while one was open for 2% of the time, Pallas kernels for 0%

profile of v11, /device:TPU:1, one launch (start us, length us, event | category | flops | bytes accessed | tf_op | source)
XLA Modules:
  0.0 195.9 jit_solution(7611217325725198746)
XLA Ops:
  0.6 3.1 %collective-permute-start.2 = (f32[8,16,128]{2,1,0:T(8,128)}, f32[8,16,128]{2,1,0:T(8,128)S(1)}, u32[]{:S(2)}, u32[]{:S(2)}) collective-permute-start(f32[8,16,128]{2,1,0:T(8,128)} %param.14), channel_id=1, source_target_pairs={{0,3},{1,2},{2,1},{3,0},{4,7},{5,6},{6,5},{7,4},{8,11},{9,10},{10,... | collective-permute-start | bytes 196616 | tf_op jit(solution)/shard_map/ppermute | solution.py:207
  3.7 0.3 collective-permute-start.1
  3.9 0.9 constant_dynamic-update-slice_fusion.4
  4.8 0.7 constant_dynamic-update-slice_fusion.3
  5.5 0.7 constant_dynamic-update-slice_fusion.2
  6.2 0.7 constant_dynamic-update-slice_fusion.1
  7.0 0.7 constant_dynamic-update-slice_fusion
  7.7 0.1 collective-permute-start
  7.8 3.4 %collective-permute-done = f32[13,16,128]{2,1,0:T(8,128)S(1)} collective-permute-done((f32[13,16,128]{2,1,0:T(8,128)S(1)}, f32[13,16,128]{2,1,0:T(8,128)S(1)}, u32[]{:S(2)}, u32[]{:S(2)}) %collective-permute-start) | collective-permute-done | bytes 106528 | tf_op jit(solution)/shard_map/ppermute | solution.py:205
  11.3 4.3 %collective-permute-start.4 = (f32[21,16,256]{2,1,0:T(8,128)S(1)}, f32[21,16,256]{2,1,0:T(8,128)S(1)}, u32[]{:S(2)}, u32[]{:S(2)}) collective-permute-start(f32[21,16,256]{2,1,0:T(8,128)S(1)} %pad_maximum_fusion.1), channel_id=1, source_target_pairs={{4,0},{8,4},{12,8},{16,12},{20,16},{24,20},{28,24},{5,1},{9,5},{13... | collective-permute-start | bytes 1032200 | tf_op jit(solution)/shard_map/ppermute | solution.py:47
  15.6 3.1 %collective-permute-start.3 = (f32[21,16,256]{2,1,0:T(8,128)S(1)}, f32[21,16,256]{2,1,0:T(8,128)S(1)}, u32[]{:S(2)}, u32[]{:S(2)}) collective-permute-start(f32[21,16,256]{2,1,0:T(8,128)S(1)} %pad_maximum_fusion.1), channel_id=1, source_target_pairs={{0,4},{4,8},{8,12},{12,16},{16,20},{20,24},{24,28},{1,5},{5,9},{9,... | collective-permute-start | bytes 1032200 | tf_op jit(solution)/shard_map/ppermute | solution.py:46
  18.7 3.0 %collective-permute-done.4 = f32[21,16,256]{2,1,0:T(8,128)S(1)} collective-permute-done((f32[21,16,256]{2,1,0:T(8,128)S(1)}, f32[21,16,256]{2,1,0:T(8,128)S(1)}, u32[]{:S(2)}, u32[]{:S(2)}) %collective-permute-start.4) | collective-permute-done | bytes 344096 | tf_op jit(solution)/shard_map/ppermute | solution.py:47
  21.7 1.2 collective-permute-done.3
  23.0 0.2 fusion.24
  23.2 0.3 fusion.23
  23.5 0.2 fusion.22
  23.7 0.1 concatenate.84
  23.8 0.2 pad_multiply_fusion
  24.0 1.4 copy.13.refs_2_
  25.3 1.1 bitcast_dynamic-update-slice_fusion.5
  26.5 1.1 bitcast_dynamic-update-slice_fusion.4
  27.6 1.4 fusion.8
  29.0 1.2 bitcast_dynamic-update-slice_fusion.3
  30.2 1.2 bitcast_dynamic-update-slice_fusion.2
  31.5 1.0 bitcast_dynamic-update-slice_fusion.1
  32.5 1.0 bitcast_dynamic-update-slice_fusion.refs_1_
  33.4 25.9 %shard_map.113 = (f32[2,18,48,256]{3,2,1,0:T(8,128)}, f32[2,18,48,256]{3,2,1,0:T(8,128)}, f32[2,2,16,16,256]{4,3,2,1,0:T(8,128)}, f32[2,2,16,16,256]{4,3,2,1,0:T(8,128)}) custom-call(f32[2,15]{1,0:T(2,128)} %constant.99.clone.refs_0_, f32[6,16,48,256]{3,2,1,0:T(8,128)} %bitcast_dynamic-update-slice_fusion.refs_1_, f32[2,16,48,256]{3,2,1,0:T(8,128)} %copy.13.refs_2_), custom_call_target="tpu_custom_call" | custom-call | flops 117964800 | bytes 14155776 | tf_op jit(solution)/shard_map/pallas_call | solution.py:182
  59.4 4.4 %collective-permute-start.5 = (f32[2,2,16,16,256]{4,3,2,1,0:T(8,128)}, f32[2,2,16,16,256]{4,3,2,1,0:T(8,128)S(1)}, u32[]{:S(2)}, u32[]{:S(2)}) collective-permute-start(f32[2,2,16,16,256]{4,3,2,1,0:T(8,128)} %get-tuple-element.40), channel_id=1, source_target_pairs={{0,4},{4,8},{8,12},{12,16},{16,20},{20,24},{24,28},{1,5},{5,9},{9,... | collective-permute-start | bytes 3145736 | tf_op jit(solution)/shard_map/ppermute | solution.py:270
  63.8 2.1 %collective-permute-start.6 = (f32[2,2,16,16,256]{4,3,2,1,0:T(8,128)}, f32[2,2,16,16,256]{4,3,2,1,0:T(8,128)S(1)}, u32[]{:S(2)}, u32[]{:S(2)}) collective-permute-start(f32[2,2,16,16,256]{4,3,2,1,0:T(8,128)} %get-tuple-element.41), channel_id=1, source_target_pairs={{4,0},{8,4},{12,8},{16,12},{20,16},{24,20},{28,24},{5,1},{9,5},{13... | collective-permute-start | bytes 3145736 | tf_op jit(solution)/shard_map/ppermute | solution.py:271
  65.9 9.9 %collective-permute-done.5.refs_5_ = f32[2,2,16,16,256]{4,3,2,1,0:T(8,128)S(1)} collective-permute-done((f32[2,2,16,16,256]{4,3,2,1,0:T(8,128)}, f32[2,2,16,16,256]{4,3,2,1,0:T(8,128)S(1)}, u32[]{:S(2)}, u32[]{:S(2)}) %collective-permute-start.5) | collective-permute-done | bytes 1048608 | tf_op jit(solution)/shard_map/ppermute | solution.py:270
  75.8 4.3 %collective-permute-done.6.refs_6_ = f32[2,2,16,16,256]{4,3,2,1,0:T(8,128)S(1)} collective-permute-done((f32[2,2,16,16,256]{4,3,2,1,0:T(8,128)}, f32[2,2,16,16,256]{4,3,2,1,0:T(8,128)S(1)}, u32[]{:S(2)}, u32[]{:S(2)}) %collective-permute-start.6) | collective-permute-done | bytes 1048608 | tf_op jit(solution)/shard_map/ppermute | solution.py:271
  80.1 1.0 copy-done.1
  81.1 28.2 %shard_map.114 = (f32[2,18,48,256]{3,2,1,0:T(8,128)}, f32[2,18,48,256]{3,2,1,0:T(8,128)}) custom-call(f32[2,16]{1,0:T(2,128)} %constant.100.clone.refs_0_, f32[6,16,48,256]{3,2,1,0:T(8,128)} %bitcast_dynamic-update-slice_fusion.refs_1_, f32[2,16,48,256]{3,2,1,0:T(8,128)} %copy.13.refs_2_, f32[2,18,48,256]{3,2,1,0:T(8,128)} %get-tuple-element.38.refs_3_, ...), custom_call_target="tpu_custom_call" | custom-call | flops 125829120 | bytes 14155776 | tf_op jit(solution)/shard_map/pallas_call | solution.py:182
  109.3 2.1 %fusion.21 = (f32[2,48,256]{2,1,0:T(8,128)S(1)}, f32[2,16,48,256]{3,2,1,0:T(8,128)S(1)}) fusion(f32[2,18,48,256]{3,2,1,0:T(8,128)} %get-tuple-element.43, f32[2,18,48,256]{3,2,1,0:T(8,128)} %get-tuple-element.42), kind=kLoop, calls=%fused_computation.78 | loop fusion | flops 761856 | bytes 4816896 | tf_op jit(solution)/shard_map/reduce_sum | solution.py:285
  111.4 1.9 collective-permute-start.8
  113.4 3.6 %collective-permute-start.7 = (f32[2,16,256]{2,1,0:T(8,128)S(1)}, f32[2,16,256]{2,1,0:T(8,128)S(1)}, u32[]{:S(2)}, u32[]{:S(2)}) collective-permute-start(f32[2,16,256]{2,1,0:T(8,128)S(1)} %slice_multiply_fusion), channel_id=1, source_target_pairs={{0,4},{4,8},{8,12},{12,16},{16,20},{20,24},{24,28},{1,5},{5,9},{9,... | collective-permute-start | bytes 98312 | tf_op jit(solution)/shard_map/ppermute | solution.py:46
  117.0 1.0 collective-permute-done.7
  118.0 1.4 broadcast_multiply_fusion.refs_2_
  119.4 25.9 %shard_map.115 = (f32[2,18,48,256]{3,2,1,0:T(8,128)}, f32[2,18,48,256]{3,2,1,0:T(8,128)}, f32[2,2,16,16,256]{4,3,2,1,0:T(8,128)}, f32[2,2,16,16,256]{4,3,2,1,0:T(8,128)}) custom-call(f32[2,15]{1,0:T(2,128)} %constant.99.clone.refs_0_, f32[6,16,48,256]{3,2,1,0:T(8,128)} %bitcast_dynamic-update-slice_fusion.refs_1_, ...), custom_call_target="tpu_custom_call" | custom-call | flops 117964800 | bytes 14155776 | tf_op jit(solution)/shard_map/pallas_call | solution.py:182
  145.3 4.2 %collective-permute-start.9 = (f32[2,2,16,16,256]{4,3,2,1,0:T(8,128)}, f32[2,2,16,16,256]{4,3,2,1,0:T(8,128)}, u32[]{:S(2)}, u32[]{:S(2)}) collective-permute-start(f32[2,2,16,16,256]{4,3,2,1,0:T(8,128)} %get-tuple-element.46), channel_id=1, source_target_pairs={{0,4},{4,8},{8,12},{12,16},{16,20},{20,24},{24,28},{1,5},{5,9},{9,... | collective-permute-start | bytes 3145736 | tf_op jit(solution)/shard_map/ppermute | solution.py:270
  149.6 2.1 %collective-permute-start.10 = (f32[2,2,16,16,256]{4,3,2,1,0:T(8,128)}, f32[2,2,16,16,256]{4,3,2,1,0:T(8,128)}, u32[]{:S(2)}, u32[]{:S(2)}) collective-permute-start(f32[2,2,16,16,256]{4,3,2,1,0:T(8,128)} %get-tuple-element.47), channel_id=1, source_target_pairs={{4,0},{8,4},{12,8},{16,12},{20,16},{24,20},{28,24},{5,1},{9,5},{13... | collective-permute-start | bytes 3145736 | tf_op jit(solution)/shard_map/ppermute | solution.py:271
  151.7 0.1 fusion.25
  151.8 0.7 constant_dynamic-slice_fusion
  152.5 9.1 %collective-permute-done.9.refs_5_ = f32[2,2,16,16,256]{4,3,2,1,0:T(8,128)} collective-permute-done((f32[2,2,16,16,256]{4,3,2,1,0:T(8,128)}, f32[2,2,16,16,256]{4,3,2,1,0:T(8,128)}, u32[]{:S(2)}, u32[]{:S(2)}) %collective-permute-start.9) | collective-permute-done | bytes 1048608 | tf_op jit(solution)/shard_map/ppermute | solution.py:270
  161.6 4.4 %collective-permute-done.10.refs_6_ = f32[2,2,16,16,256]{4,3,2,1,0:T(8,128)} collective-permute-done((f32[2,2,16,16,256]{4,3,2,1,0:T(8,128)}, f32[2,2,16,16,256]{4,3,2,1,0:T(8,128)}, u32[]{:S(2)}, u32[]{:S(2)}) %collective-permute-start.10) | collective-permute-done | bytes 1048608 | tf_op jit(solution)/shard_map/ppermute | solution.py:271
  166.0 28.2 %shard_map.116 = (f32[2,18,48,256]{3,2,1,0:T(8,128)}, f32[2,18,48,256]{3,2,1,0:T(8,128)}) custom-call(f32[2,16]{1,0:T(2,128)} %constant.100.clone.refs_0_, f32[6,16,48,256]{3,2,1,0:T(8,128)} %bitcast_dynamic-update-slice_fusion.refs_1_, f32[2,16,48,256]{3,2,1,0:T(8,128)} %broadcast_multiply_fusion.refs_2_, f32[2,18,48,256]{3,2,1,0:T(8,128)} %get-tuple-element.44.refs_3_, ...), custom_call_target="tpu_custom_call" | custom-call | flops 125829120 | bytes 14155776 | tf_op jit(solution)/shard_map/pallas_call | solution.py:182
  194.2 1.0 fusion.12
  195.2 0.7 fusion.19
  (23 shorter events, 0.3 us)
Async XLA Ops:
  0.6 7.1 %collective-permute-start.2 = (f32[8,16,128]{2,1,0:T(8,128)}, f32[8,16,128]{2,1,0:T(8,128)S(1)}, u32[]{:S(2)}, u32[]{:S(2)}) collective-permute-start(f32[8,16,128]{2,1,0:T(8,128)} %param.14), channel_id=1, source_target_pairs={{0,3},{1,2},{2,1},{3,0},{4,7},{5,6},{6,5},{7,4},{8,11},{9,10},{10,... | collective-permute-start | bytes 196616 | tf_op jit(solution)/shard_map/ppermute | solution.py:207
  3.7 4.1 %collective-permute-start.1 = (f32[8,16,128]{2,1,0:T(8,128)}, f32[8,16,128]{2,1,0:T(8,128)S(1)}, u32[]{:S(2)}, u32[]{:S(2)}) collective-permute-start(f32[8,16,128]{2,1,0:T(8,128)} %param.14), channel_id=1, source_target_pairs={{0,1},{1,0},{2,3},{3,2},{4,5},{5,4},{6,7},{7,6},{8,9},{9,8},{10,11... | collective-permute-start | bytes 196616 | tf_op jit(solution)/shard_map/ppermute | solution.py:206
  7.7 3.6 %collective-permute-start = (f32[13,16,128]{2,1,0:T(8,128)S(1)}, f32[13,16,128]{2,1,0:T(8,128)S(1)}, u32[]{:S(2)}, u32[]{:S(2)}) collective-permute-start(f32[13,16,128]{2,1,0:T(8,128)S(1)} %constant_dynamic-update-slice_fusion), channel_id=1, source_target_pairs={{0,2},{2,0},{1,3},{3,1},{4,6},{6,4},{5,7},{7,5},{8,10},{10,8},{9,1... | collective-permute-start | bytes 319496 | tf_op jit(solution)/shard_map/ppermute | solution.py:205
  11.3 10.4 %collective-permute-start.4 = (f32[21,16,256]{2,1,0:T(8,128)S(1)}, f32[21,16,256]{2,1,0:T(8,128)S(1)}, u32[]{:S(2)}, u32[]{:S(2)}) collective-permute-start(f32[21,16,256]{2,1,0:T(8,128)S(1)} %pad_maximum_fusion.1), channel_id=1, source_target_pairs={{4,0},{8,4},{12,8},{16,12},{20,16},{24,20},{28,24},{5,1},{9,5},{13... | collective-permute-start | bytes 1032200 | tf_op jit(solution)/shard_map/ppermute | solution.py:47
  15.6 7.3 %collective-permute-start.3 = (f32[21,16,256]{2,1,0:T(8,128)S(1)}, f32[21,16,256]{2,1,0:T(8,128)S(1)}, u32[]{:S(2)}, u32[]{:S(2)}) collective-permute-start(f32[21,16,256]{2,1,0:T(8,128)S(1)} %pad_maximum_fusion.1), channel_id=1, source_target_pairs={{0,4},{4,8},{8,12},{12,16},{16,20},{20,24},{24,28},{1,5},{5,9},{9,... | collective-permute-start | bytes 1032200 | tf_op jit(solution)/shard_map/ppermute | solution.py:46
  59.4 16.4 %collective-permute-start.5 = (f32[2,2,16,16,256]{4,3,2,1,0:T(8,128)}, f32[2,2,16,16,256]{4,3,2,1,0:T(8,128)S(1)}, u32[]{:S(2)}, u32[]{:S(2)}) collective-permute-start(f32[2,2,16,16,256]{4,3,2,1,0:T(8,128)} %get-tuple-element.40), channel_id=1, source_target_pairs={{0,4},{4,8},{8,12},{12,16},{16,20},{20,24},{24,28},{1,5},{5,9},{9,... | collective-permute-start | bytes 3145736 | tf_op jit(solution)/shard_map/ppermute | solution.py:270
  63.8 16.3 %collective-permute-start.6 = (f32[2,2,16,16,256]{4,3,2,1,0:T(8,128)}, f32[2,2,16,16,256]{4,3,2,1,0:T(8,128)S(1)}, u32[]{:S(2)}, u32[]{:S(2)}) collective-permute-start(f32[2,2,16,16,256]{4,3,2,1,0:T(8,128)} %get-tuple-element.41), channel_id=1, source_target_pairs={{4,0},{8,4},{12,8},{16,12},{20,16},{24,20},{28,24},{5,1},{9,5},{13... | collective-permute-start | bytes 3145736 | tf_op jit(solution)/shard_map/ppermute | solution.py:271
  75.8 4.3 %copy-start = (f32[2,2,16,16,256]{4,3,2,1,0:T(8,128)}, f32[2,2,16,16,256]{4,3,2,1,0:T(8,128)S(1)}, u32[]{:S(2)}) copy-start(f32[2,2,16,16,256]{4,3,2,1,0:T(8,128)S(1)} %collective-permute-done.5.refs_5_) | copy-start | bytes 3145732
  80.1 1.0 copy-start.1
  111.4 5.6 %collective-permute-start.8 = (f32[2,16,256]{2,1,0:T(8,128)S(1)}, f32[2,16,256]{2,1,0:T(8,128)S(1)}, u32[]{:S(2)}, u32[]{:S(2)}) collective-permute-start(f32[2,16,256]{2,1,0:T(8,128)S(1)} %slice_multiply_fusion), channel_id=1, source_target_pairs={{4,0},{8,4},{12,8},{16,12},{20,16},{24,20},{28,24},{5,1},{9,5},{13... | collective-permute-start | bytes 98312 | tf_op jit(solution)/shard_map/ppermute | solution.py:47
  113.4 4.7 %collective-permute-start.7 = (f32[2,16,256]{2,1,0:T(8,128)S(1)}, f32[2,16,256]{2,1,0:T(8,128)S(1)}, u32[]{:S(2)}, u32[]{:S(2)}) collective-permute-start(f32[2,16,256]{2,1,0:T(8,128)S(1)} %slice_multiply_fusion), channel_id=1, source_target_pairs={{0,4},{4,8},{8,12},{12,16},{16,20},{20,24},{24,28},{1,5},{5,9},{9,... | collective-permute-start | bytes 98312 | tf_op jit(solution)/shard_map/ppermute | solution.py:46
  145.3 16.3 %collective-permute-start.9 = (f32[2,2,16,16,256]{4,3,2,1,0:T(8,128)}, f32[2,2,16,16,256]{4,3,2,1,0:T(8,128)}, u32[]{:S(2)}, u32[]{:S(2)}) collective-permute-start(f32[2,2,16,16,256]{4,3,2,1,0:T(8,128)} %get-tuple-element.46), channel_id=1, source_target_pairs={{0,4},{4,8},{8,12},{12,16},{16,20},{20,24},{24,28},{1,5},{5,9},{9,... | collective-permute-start | bytes 3145736 | tf_op jit(solution)/shard_map/ppermute | solution.py:270
  149.6 16.4 %collective-permute-start.10 = (f32[2,2,16,16,256]{4,3,2,1,0:T(8,128)}, f32[2,2,16,16,256]{4,3,2,1,0:T(8,128)}, u32[]{:S(2)}, u32[]{:S(2)}) collective-permute-start(f32[2,2,16,16,256]{4,3,2,1,0:T(8,128)} %get-tuple-element.47), channel_id=1, source_target_pairs={{4,0},{8,4},{12,8},{16,12},{20,16},{24,20},{28,24},{5,1},{9,5},{13... | collective-permute-start | bytes 3145736 | tf_op jit(solution)/shard_map/ppermute | solution.py:271

commit v12 on v11

--- a/solution.py
+++ b/solution.py
@@ -1,3 +1,5 @@
+import functools
+
 import jax
 import jax.numpy as jnp
 from jax import lax
@@ -112,13 +114,13 @@
         for c in range(comps):
             x_ref[c, 1, span] = x_ref[c, 1, span] + d_ref[c, 1, span]
 
-        def update(layer, carry):
+        def update(c, layer, carry):
             p = layer + 1
             c_xm = op_ref[2, layer, span]
             c_ym = op_ref[3, layer, span]
             c_xp = pltpu.roll(c_xm, height - 1, 0)
             c_yp = pltpu.roll(c_ym, cols - 1, 1)
-            for c in range(comps):
+            if True:
                 above = x_ref[c, p + 1, span] + d_ref[c, p + 1, span]
                 x_ref[c, p + 1, span] = above
                 centre = x_ref[c, p, span]
@@ -134,7 +136,8 @@
                     d_ref[c, p, span] = keep * d_ref[c, p, span] + push * (op_ref[5, layer, span] * resid)
             return carry
 
-        lax.fori_loop(0, layers, update, 0, unroll=True)
+        for c in range(comps):
+            lax.fori_loop(0, layers, functools.partial(update, c), 0, unroll=True)
 
     def row_start(j):
         return max(min(8 * ((start_valid + j) // 8), rows // 2 - 8), 0)

time: 196 us -> 200 us (1.020)
  Pallas kernels: 108 us -> 112 us
    pallas_call x4, Pallas kernels: 108 us -> 112 us  [run_segment(): pl.pallas_call(lambda *refs: segment_kernel(steps, start_valid, halo, sen...]
where the time goes in v12:
time: 200 us; the launch traced here: 199 us
  Pallas kernels  112 us (56%)
  waiting for transfers between devices  36.3 us (18%)
  starting transfers between devices  29.2 us (15%)
  other arithmetic  15.1 us (8%)
  local copies, waits for them, and re-layouts  6.09 us (3%)
    pallas_call x4, Pallas kernels, run_segment(): pl.pallas_call(lambda *refs: segment_kernel(steps, start_valid, halo, sen...  112 us
    ppermute x2, waiting for transfers between devices, chebyshev(): low = lax.ppermute(up, 'mx', forward)  19.1 us
    ppermute x2, waiting for transfers between devices, chebyshev(): high = lax.ppermute(down, 'mx', backward)  8.68 us
    ppermute x2, starting transfers between devices, chebyshev(): low = lax.ppermute(up, 'mx', forward)  8.59 us
    unnamed x7, other arithmetic  7.08 us
    ppermute x2, starting transfers between devices, exchange_rows(): lax.ppermute(lax.slice_in_dim(own, rows - k, rows, axis=axis), 'mx', forw...  6.74 us
    ppermute x2, starting transfers between devices, exchange_rows(): high = lax.ppermute(lax.slice_in_dim(own, 0, k, axis=axis), 'mx', backward)  6.21 us
    ppermute x2, starting transfers between devices, chebyshev(): high = lax.ppermute(down, 'mx', backward)  4.24 us
  transfers between devices with their start and end apart: 11, of which 8 were waited for; matrix products, arithmetic and copies ran while one was open for 2% of the time, Pallas kernels for 0%

profile of v12, /device:TPU:1, one launch (start us, length us, event | category | flops | bytes accessed | tf_op | source)
XLA Modules:
  0.0 199.2 jit_solution(3631775966684152541)
XLA Ops:
  0.6 3.1 %collective-permute-start.2 = (f32[8,16,128]{2,1,0:T(8,128)}, f32[8,16,128]{2,1,0:T(8,128)S(1)}, u32[]{:S(2)}, u32[]{:S(2)}) collective-permute-start(f32[8,16,128]{2,1,0:T(8,128)} %param.14), channel_id=1, source_target_pairs={{0,3},{1,2},{2,1},{3,0},{4,7},{5,6},{6,5},{7,4},{8,11},{9,10},{10,... | collective-permute-start | bytes 196616 | tf_op jit(solution)/shard_map/ppermute | solution.py:210
  3.7 0.3 collective-permute-start.1
  3.9 0.9 constant_dynamic-update-slice_fusion.4
  4.8 0.7 constant_dynamic-update-slice_fusion.3
  5.5 0.7 constant_dynamic-update-slice_fusion.2
  6.2 0.7 constant_dynamic-update-slice_fusion.1
  7.0 0.7 constant_dynamic-update-slice_fusion
  7.7 0.1 collective-permute-start
  7.8 3.4 %collective-permute-done = f32[13,16,128]{2,1,0:T(8,128)S(1)} collective-permute-done((f32[13,16,128]{2,1,0:T(8,128)S(1)}, f32[13,16,128]{2,1,0:T(8,128)S(1)}, u32[]{:S(2)}, u32[]{:S(2)}) %collective-permute-start) | collective-permute-done | bytes 106528 | tf_op jit(solution)/shard_map/ppermute | solution.py:208
  11.3 4.3 %collective-permute-start.4 = (f32[21,16,256]{2,1,0:T(8,128)S(1)}, f32[21,16,256]{2,1,0:T(8,128)S(1)}, u32[]{:S(2)}, u32[]{:S(2)}) collective-permute-start(f32[21,16,256]{2,1,0:T(8,128)S(1)} %pad_maximum_fusion.1), channel_id=1, source_target_pairs={{4,0},{8,4},{12,8},{16,12},{20,16},{24,20},{28,24},{5,1},{9,5},{13... | collective-permute-start | bytes 1032200 | tf_op jit(solution)/shard_map/ppermute | solution.py:49
  15.6 3.1 %collective-permute-start.3 = (f32[21,16,256]{2,1,0:T(8,128)S(1)}, f32[21,16,256]{2,1,0:T(8,128)S(1)}, u32[]{:S(2)}, u32[]{:S(2)}) collective-permute-start(f32[21,16,256]{2,1,0:T(8,128)S(1)} %pad_maximum_fusion.1), channel_id=1, source_target_pairs={{0,4},{4,8},{8,12},{12,16},{16,20},{20,24},{24,28},{1,5},{5,9},{9,... | collective-permute-start | bytes 1032200 | tf_op jit(solution)/shard_map/ppermute | solution.py:48
  18.7 3.0 %collective-permute-done.4 = f32[21,16,256]{2,1,0:T(8,128)S(1)} collective-permute-done((f32[21,16,256]{2,1,0:T(8,128)S(1)}, f32[21,16,256]{2,1,0:T(8,128)S(1)}, u32[]{:S(2)}, u32[]{:S(2)}) %collective-permute-start.4) | collective-permute-done | bytes 344096 | tf_op jit(solution)/shard_map/ppermute | solution.py:49
  21.7 1.2 collective-permute-done.3
  23.0 0.2 fusion.24
  23.2 0.3 fusion.23
  23.5 0.2 fusion.22
  23.7 0.1 concatenate.84
  23.8 0.2 pad_multiply_fusion
  24.0 1.4 copy.13.refs_2_
  25.3 1.1 bitcast_dynamic-update-slice_fusion.5
  26.5 1.1 bitcast_dynamic-update-slice_fusion.4
  27.6 1.4 fusion.8
  29.0 1.2 bitcast_dynamic-update-slice_fusion.3
  30.2 1.2 bitcast_dynamic-update-slice_fusion.2
  31.5 1.0 bitcast_dynamic-update-slice_fusion.1
  32.5 1.0 bitcast_dynamic-update-slice_fusion.refs_1_
  33.4 26.8 %shard_map.113 = (f32[2,18,48,256]{3,2,1,0:T(8,128)}, f32[2,18,48,256]{3,2,1,0:T(8,128)}, f32[2,2,16,16,256]{4,3,2,1,0:T(8,128)}, f32[2,2,16,16,256]{4,3,2,1,0:T(8,128)}) custom-call(f32[2,15]{1,0:T(2,128)} %constant.99.clone.refs_0_, f32[6,16,48,256]{3,2,1,0:T(8,128)} %bitcast_dynamic-update-slice_fusion.refs_1_, f32[2,16,48,256]{3,2,1,0:T(8,128)} %copy.13.refs_2_), custom_call_target="tpu_custom_call" | custom-call | flops 117964800 | bytes 14155776 | tf_op jit(solution)/shard_map/pallas_call | solution.py:185
  60.2 4.4 %collective-permute-start.5 = (f32[2,2,16,16,256]{4,3,2,1,0:T(8,128)}, f32[2,2,16,16,256]{4,3,2,1,0:T(8,128)S(1)}, u32[]{:S(2)}, u32[]{:S(2)}) collective-permute-start(f32[2,2,16,16,256]{4,3,2,1,0:T(8,128)} %get-tuple-element.40), channel_id=1, source_target_pairs={{0,4},{4,8},{8,12},{12,16},{16,20},{20,24},{24,28},{1,5},{5,9},{9,... | collective-permute-start | bytes 3145736 | tf_op jit(solution)/shard_map/ppermute | solution.py:273
  64.6 2.1 %collective-permute-start.6 = (f32[2,2,16,16,256]{4,3,2,1,0:T(8,128)}, f32[2,2,16,16,256]{4,3,2,1,0:T(8,128)S(1)}, u32[]{:S(2)}, u32[]{:S(2)}) collective-permute-start(f32[2,2,16,16,256]{4,3,2,1,0:T(8,128)} %get-tuple-element.41), channel_id=1, source_target_pairs={{4,0},{8,4},{12,8},{16,12},{20,16},{24,20},{28,24},{5,1},{9,5},{13... | collective-permute-start | bytes 3145736 | tf_op jit(solution)/shard_map/ppermute | solution.py:274
  66.7 9.9 %collective-permute-done.5.refs_5_ = f32[2,2,16,16,256]{4,3,2,1,0:T(8,128)S(1)} collective-permute-done((f32[2,2,16,16,256]{4,3,2,1,0:T(8,128)}, f32[2,2,16,16,256]{4,3,2,1,0:T(8,128)S(1)}, u32[]{:S(2)}, u32[]{:S(2)}) %collective-permute-start.5) | collective-permute-done | bytes 1048608 | tf_op jit(solution)/shard_map/ppermute | solution.py:273
  76.6 4.3 %collective-permute-done.6.refs_6_ = f32[2,2,16,16,256]{4,3,2,1,0:T(8,128)S(1)} collective-permute-done((f32[2,2,16,16,256]{4,3,2,1,0:T(8,128)}, f32[2,2,16,16,256]{4,3,2,1,0:T(8,128)S(1)}, u32[]{:S(2)}, u32[]{:S(2)}) %collective-permute-start.6) | collective-permute-done | bytes 1048608 | tf_op jit(solution)/shard_map/ppermute | solution.py:274
  80.9 1.0 copy-done.1
  81.9 29.1 %shard_map.114 = (f32[2,18,48,256]{3,2,1,0:T(8,128)}, f32[2,18,48,256]{3,2,1,0:T(8,128)}) custom-call(f32[2,16]{1,0:T(2,128)} %constant.100.clone.refs_0_, f32[6,16,48,256]{3,2,1,0:T(8,128)} %bitcast_dynamic-update-slice_fusion.refs_1_, f32[2,16,48,256]{3,2,1,0:T(8,128)} %copy.13.refs_2_, f32[2,18,48,256]{3,2,1,0:T(8,128)} %get-tuple-element.38.refs_3_, ...), custom_call_target="tpu_custom_call" | custom-call | flops 125829120 | bytes 14155776 | tf_op jit(solution)/shard_map/pallas_call | solution.py:185
  111.0 2.1 %fusion.21 = (f32[2,48,256]{2,1,0:T(8,128)S(1)}, f32[2,16,48,256]{3,2,1,0:T(8,128)S(1)}) fusion(f32[2,18,48,256]{3,2,1,0:T(8,128)} %get-tuple-element.43, f32[2,18,48,256]{3,2,1,0:T(8,128)} %get-tuple-element.42), kind=kLoop, calls=%fused_computation.78 | loop fusion | flops 761856 | bytes 4816896 | tf_op jit(solution)/shard_map/reduce_sum | solution.py:288
  113.1 1.9 collective-permute-start.8
  115.0 3.6 %collective-permute-start.7 = (f32[2,16,256]{2,1,0:T(8,128)S(1)}, f32[2,16,256]{2,1,0:T(8,128)S(1)}, u32[]{:S(2)}, u32[]{:S(2)}) collective-permute-start(f32[2,16,256]{2,1,0:T(8,128)S(1)} %slice_multiply_fusion), channel_id=1, source_target_pairs={{0,4},{4,8},{8,12},{12,16},{16,20},{20,24},{24,28},{1,5},{5,9},{9,... | collective-permute-start | bytes 98312 | tf_op jit(solution)/shard_map/ppermute | solution.py:48
  118.7 1.0 collective-permute-done.7
  119.7 1.4 broadcast_multiply_fusion.refs_2_
  121.1 26.8 %shard_map.115 = (f32[2,18,48,256]{3,2,1,0:T(8,128)}, f32[2,18,48,256]{3,2,1,0:T(8,128)}, f32[2,2,16,16,256]{4,3,2,1,0:T(8,128)}, f32[2,2,16,16,256]{4,3,2,1,0:T(8,128)}) custom-call(f32[2,15]{1,0:T(2,128)} %constant.99.clone.refs_0_, f32[6,16,48,256]{3,2,1,0:T(8,128)} %bitcast_dynamic-update-slice_fusion.refs_1_, ...), custom_call_target="tpu_custom_call" | custom-call | flops 117964800 | bytes 14155776 | tf_op jit(solution)/shard_map/pallas_call | solution.py:185
  147.9 4.2 %collective-permute-start.9 = (f32[2,2,16,16,256]{4,3,2,1,0:T(8,128)}, f32[2,2,16,16,256]{4,3,2,1,0:T(8,128)}, u32[]{:S(2)}, u32[]{:S(2)}) collective-permute-start(f32[2,2,16,16,256]{4,3,2,1,0:T(8,128)} %get-tuple-element.46), channel_id=1, source_target_pairs={{0,4},{4,8},{8,12},{12,16},{16,20},{20,24},{24,28},{1,5},{5,9},{9,... | collective-permute-start | bytes 3145736 | tf_op jit(solution)/shard_map/ppermute | solution.py:273
  152.1 2.1 %collective-permute-start.10 = (f32[2,2,16,16,256]{4,3,2,1,0:T(8,128)}, f32[2,2,16,16,256]{4,3,2,1,0:T(8,128)}, u32[]{:S(2)}, u32[]{:S(2)}) collective-permute-start(f32[2,2,16,16,256]{4,3,2,1,0:T(8,128)} %get-tuple-element.47), channel_id=1, source_target_pairs={{4,0},{8,4},{12,8},{16,12},{20,16},{24,20},{28,24},{5,1},{9,5},{13... | collective-permute-start | bytes 3145736 | tf_op jit(solution)/shard_map/ppermute | solution.py:274
  154.2 0.1 fusion.25
  154.3 0.7 constant_dynamic-slice_fusion
  155.0 9.1 %collective-permute-done.9.refs_5_ = f32[2,2,16,16,256]{4,3,2,1,0:T(8,128)} collective-permute-done((f32[2,2,16,16,256]{4,3,2,1,0:T(8,128)}, f32[2,2,16,16,256]{4,3,2,1,0:T(8,128)}, u32[]{:S(2)}, u32[]{:S(2)}) %collective-permute-start.9) | collective-permute-done | bytes 1048608 | tf_op jit(solution)/shard_map/ppermute | solution.py:273
  164.1 4.4 %collective-permute-done.10.refs_6_ = f32[2,2,16,16,256]{4,3,2,1,0:T(8,128)} collective-permute-done((f32[2,2,16,16,256]{4,3,2,1,0:T(8,128)}, f32[2,2,16,16,256]{4,3,2,1,0:T(8,128)}, u32[]{:S(2)}, u32[]{:S(2)}) %collective-permute-start.10) | collective-permute-done | bytes 1048608 | tf_op jit(solution)/shard_map/ppermute | solution.py:274
  168.5 29.1 %shard_map.116 = (f32[2,18,48,256]{3,2,1,0:T(8,128)}, f32[2,18,48,256]{3,2,1,0:T(8,128)}) custom-call(f32[2,16]{1,0:T(2,128)} %constant.100.clone.refs_0_, f32[6,16,48,256]{3,2,1,0:T(8,128)} %bitcast_dynamic-update-slice_fusion.refs_1_, f32[2,16,48,256]{3,2,1,0:T(8,128)} %broadcast_multiply_fusion.refs_2_, f32[2,18,48,256]{3,2,1,0:T(8,128)} %get-tuple-element.44.refs_3_, ...), custom_call_target="tpu_custom_call" | custom-call | flops 125829120 | bytes 14155776 | tf_op jit(solution)/shard_map/pallas_call | solution.py:185
  197.6 1.0 fusion.12
  198.5 0.7 fusion.19
  (23 shorter events, 0.3 us)
Async XLA Ops:
  0.6 7.1 %collective-permute-start.2 = (f32[8,16,128]{2,1,0:T(8,128)}, f32[8,16,128]{2,1,0:T(8,128)S(1)}, u32[]{:S(2)}, u32[]{:S(2)}) collective-permute-start(f32[8,16,128]{2,1,0:T(8,128)} %param.14), channel_id=1, source_target_pairs={{0,3},{1,2},{2,1},{3,0},{4,7},{5,6},{6,5},{7,4},{8,11},{9,10},{10,... | collective-permute-start | bytes 196616 | tf_op jit(solution)/shard_map/ppermute | solution.py:210
  3.7 4.1 %collective-permute-start.1 = (f32[8,16,128]{2,1,0:T(8,128)}, f32[8,16,128]{2,1,0:T(8,128)S(1)}, u32[]{:S(2)}, u32[]{:S(2)}) collective-permute-start(f32[8,16,128]{2,1,0:T(8,128)} %param.14), channel_id=1, source_target_pairs={{0,1},{1,0},{2,3},{3,2},{4,5},{5,4},{6,7},{7,6},{8,9},{9,8},{10,11... | collective-permute-start | bytes 196616 | tf_op jit(solution)/shard_map/ppermute | solution.py:209
  7.7 3.6 %collective-permute-start = (f32[13,16,128]{2,1,0:T(8,128)S(1)}, f32[13,16,128]{2,1,0:T(8,128)S(1)}, u32[]{:S(2)}, u32[]{:S(2)}) collective-permute-start(f32[13,16,128]{2,1,0:T(8,128)S(1)} %constant_dynamic-update-slice_fusion), channel_id=1, source_target_pairs={{0,2},{2,0},{1,3},{3,1},{4,6},{6,4},{5,7},{7,5},{8,10},{10,8},{9,1... | collective-permute-start | bytes 319496 | tf_op jit(solution)/shard_map/ppermute | solution.py:208
  11.3 10.4 %collective-permute-start.4 = (f32[21,16,256]{2,1,0:T(8,128)S(1)}, f32[21,16,256]{2,1,0:T(8,128)S(1)}, u32[]{:S(2)}, u32[]{:S(2)}) collective-permute-start(f32[21,16,256]{2,1,0:T(8,128)S(1)} %pad_maximum_fusion.1), channel_id=1, source_target_pairs={{4,0},{8,4},{12,8},{16,12},{20,16},{24,20},{28,24},{5,1},{9,5},{13... | collective-permute-start | bytes 1032200 | tf_op jit(solution)/shard_map/ppermute | solution.py:49
  15.6 7.3 %collective-permute-start.3 = (f32[21,16,256]{2,1,0:T(8,128)S(1)}, f32[21,16,256]{2,1,0:T(8,128)S(1)}, u32[]{:S(2)}, u32[]{:S(2)}) collective-permute-start(f32[21,16,256]{2,1,0:T(8,128)S(1)} %pad_maximum_fusion.1), channel_id=1, source_target_pairs={{0,4},{4,8},{8,12},{12,16},{16,20},{20,24},{24,28},{1,5},{5,9},{9,... | collective-permute-start | bytes 1032200 | tf_op jit(solution)/shard_map/ppermute | solution.py:48
  60.2 16.4 %collective-permute-start.5 = (f32[2,2,16,16,256]{4,3,2,1,0:T(8,128)}, f32[2,2,16,16,256]{4,3,2,1,0:T(8,128)S(1)}, u32[]{:S(2)}, u32[]{:S(2)}) collective-permute-start(f32[2,2,16,16,256]{4,3,2,1,0:T(8,128)} %get-tuple-element.40), channel_id=1, source_target_pairs={{0,4},{4,8},{8,12},{12,16},{16,20},{20,24},{24,28},{1,5},{5,9},{9,... | collective-permute-start | bytes 3145736 | tf_op jit(solution)/shard_map/ppermute | solution.py:273
  64.6 16.3 %collective-permute-start.6 = (f32[2,2,16,16,256]{4,3,2,1,0:T(8,128)}, f32[2,2,16,16,256]{4,3,2,1,0:T(8,128)S(1)}, u32[]{:S(2)}, u32[]{:S(2)}) collective-permute-start(f32[2,2,16,16,256]{4,3,2,1,0:T(8,128)} %get-tuple-element.41), channel_id=1, source_target_pairs={{4,0},{8,4},{12,8},{16,12},{20,16},{24,20},{28,24},{5,1},{9,5},{13... | collective-permute-start | bytes 3145736 | tf_op jit(solution)/shard_map/ppermute | solution.py:274
  76.6 4.3 %copy-start = (f32[2,2,16,16,256]{4,3,2,1,0:T(8,128)}, f32[2,2,16,16,256]{4,3,2,1,0:T(8,128)S(1)}, u32[]{:S(2)}) copy-start(f32[2,2,16,16,256]{4,3,2,1,0:T(8,128)S(1)} %collective-permute-done.5.refs_5_) | copy-start | bytes 3145732
  80.9 1.0 copy-start.1
  113.1 5.6 %collective-permute-start.8 = (f32[2,16,256]{2,1,0:T(8,128)S(1)}, f32[2,16,256]{2,1,0:T(8,128)S(1)}, u32[]{:S(2)}, u32[]{:S(2)}) collective-permute-start(f32[2,16,256]{2,1,0:T(8,128)S(1)} %slice_multiply_fusion), channel_id=1, source_target_pairs={{4,0},{8,4},{12,8},{16,12},{20,16},{24,20},{28,24},{5,1},{9,5},{13... | collective-permute-start | bytes 98312 | tf_op jit(solution)/shard_map/ppermute | solution.py:49
  115.0 4.7 %collective-permute-start.7 = (f32[2,16,256]{2,1,0:T(8,128)S(1)}, f32[2,16,256]{2,1,0:T(8,128)S(1)}, u32[]{:S(2)}, u32[]{:S(2)}) collective-permute-start(f32[2,16,256]{2,1,0:T(8,128)S(1)} %slice_multiply_fusion), channel_id=1, source_target_pairs={{0,4},{4,8},{8,12},{12,16},{16,20},{20,24},{24,28},{1,5},{5,9},{9,... | collective-permute-start | bytes 98312 | tf_op jit(solution)/shard_map/ppermute | solution.py:48
  147.9 16.3 %collective-permute-start.9 = (f32[2,2,16,16,256]{4,3,2,1,0:T(8,128)}, f32[2,2,16,16,256]{4,3,2,1,0:T(8,128)}, u32[]{:S(2)}, u32[]{:S(2)}) collective-permute-start(f32[2,2,16,16,256]{4,3,2,1,0:T(8,128)} %get-tuple-element.46), channel_id=1, source_target_pairs={{0,4},{4,8},{8,12},{12,16},{16,20},{20,24},{24,28},{1,5},{5,9},{9,... | collective-permute-start | bytes 3145736 | tf_op jit(solution)/shard_map/ppermute | solution.py:273
  152.1 16.4 %collective-permute-start.10 = (f32[2,2,16,16,256]{4,3,2,1,0:T(8,128)}, f32[2,2,16,16,256]{4,3,2,1,0:T(8,128)}, u32[]{:S(2)}, u32[]{:S(2)}) collective-permute-start(f32[2,2,16,16,256]{4,3,2,1,0:T(8,128)} %get-tuple-element.47), channel_id=1, source_target_pairs={{4,0},{8,4},{12,8},{16,12},{20,16},{24,20},{28,24},{5,1},{9,5},{13... | collective-permute-start | bytes 3145736 | tf_op jit(solution)/shard_map/ppermute | solution.py:274

commit v13 on v11

--- a/solution.py
+++ b/solution.py
@@ -116,8 +116,8 @@
             p = layer + 1
             c_xm = op_ref[2, layer, span]
             c_ym = op_ref[3, layer, span]
-            c_xp = pltpu.roll(c_xm, height - 1, 0)
-            c_yp = pltpu.roll(c_ym, cols - 1, 1)
+            c_xp = op_ref[6, layer, span]
+            c_yp = op_ref[7, layer, span]
             for c in range(comps):
                 above = x_ref[c, p + 1, span] + d_ref[c, p + 1, span]
                 x_ref[c, p + 1, span] = above
@@ -250,6 +250,8 @@
             act * c_ym * shift(act, 1, -1),
             jnp.where(on, diag, 1.0),
             jacobi,
+            act * c_xp * shift(act, 0, 1),
+            act * c_yp * shift(act, 1, 1),
         ]
     )
     table = step_constants()

time: 196 us -> 191 us (0.974)
  Pallas kernels: 108 us -> 103 us
  starting transfers between devices: 29.2 us -> 25.4 us
  other arithmetic: 15.1 us -> 17.4 us
    ppermute x2, waiting for transfers between devices: 19.1 us -> 10.6 us  [chebyshev(): low = lax.ppermute(up, 'mx', forward)]
    ppermute x2, waiting for transfers between devices: 8.68 us -> 14.2 us  [chebyshev(): high = lax.ppermute(down, 'mx', backward)]
    pallas_call x4, Pallas kernels: 108 us -> 103 us  [run_segment(): pl.pallas_call(lambda *refs: segment_kernel(steps, start_valid, halo, sen...]
    ppermute x2, waiting for transfers between devices: 2.99 us -> 7.21 us  [exchange_rows(): high = lax.ppermute(lax.slice_in_dim(own, 0, k, axis=axis), 'mx', backward)]
    ppermute x2, starting transfers between devices: 8.59 us -> 5.77 us  [chebyshev(): low = lax.ppermute(up, 'mx', forward)]
    unnamed x7 -> x9, other arithmetic: 7.08 us -> 9.28 us
where the time goes in v13:
time: 191 us
  Pallas kernels  103 us (54%)
  waiting for transfers between devices  37.7 us (20%)
  starting transfers between devices  25.4 us (13%)
  other arithmetic  17.4 us (9%)
  local copies, waits for them, and re-layouts  6.08 us (3%)
    pallas_call x4, Pallas kernels, run_segment(): pl.pallas_call(lambda *refs: segment_kernel(steps, start_valid, halo, sen...  103 us
    ppermute x2, waiting for transfers between devices, chebyshev(): high = lax.ppermute(down, 'mx', backward)  14.2 us
    ppermute x2, waiting for transfers between devices, chebyshev(): low = lax.ppermute(up, 'mx', forward)  10.6 us
    unnamed x9, other arithmetic  9.28 us
    ppermute x2, starting transfers between devices, exchange_rows(): lax.ppermute(lax.slice_in_dim(own, rows - k, rows, axis=axis), 'mx', forw...  7.4 us
    ppermute x2, waiting for transfers between devices, exchange_rows(): high = lax.ppermute(lax.slice_in_dim(own, 0, k, axis=axis), 'mx', backward)  7.21 us
    ppermute x2, starting transfers between devices, chebyshev(): low = lax.ppermute(up, 'mx', forward)  5.77 us
    ppermute x2, starting transfers between devices, chebyshev(): high = lax.ppermute(down, 'mx', backward)  4.56 us
  transfers between devices with their start and end apart: 11, of which 8 were waited for; matrix products, arithmetic and copies ran while one was open for 2% of the time, Pallas kernels for 0%

profile of v13, /device:TPU:1, one launch (start us, length us, event | category | flops | bytes accessed | tf_op | source)
XLA Modules:
  0.0 190.5 jit_solution(10795732246206431224)
XLA Ops:
  0.6 2.1 %collective-permute-start.1 = (f32[8,16,128]{2,1,0:T(8,128)}, f32[8,16,128]{2,1,0:T(8,128)S(1)}, u32[]{:S(2)}, u32[]{:S(2)}) collective-permute-start(f32[8,16,128]{2,1,0:T(8,128)} %param.14), channel_id=1, source_target_pairs={{0,1},{1,0},{2,3},{3,2},{4,5},{5,4},{6,7},{7,6},{8,9},{9,8},{10,11... | collective-permute-start | bytes 196616 | tf_op jit(solution)/shard_map/ppermute | solution.py:206
  2.7 1.2 collective-permute-start.2
  3.9 0.9 constant_dynamic-update-slice_fusion.4
  4.8 0.7 constant_dynamic-update-slice_fusion.3
  5.5 0.7 constant_dynamic-update-slice_fusion.2
  6.2 0.7 constant_dynamic-update-slice_fusion.1
  7.0 0.7 constant_dynamic-update-slice_fusion
  7.7 3.5 %collective-permute-done = f32[13,16,128]{2,1,0:T(8,128)S(1)} collective-permute-done((f32[13,16,128]{2,1,0:T(8,128)S(1)}, f32[13,16,128]{2,1,0:T(8,128)S(1)}, u32[]{:S(2)}, u32[]{:S(2)}) %collective-permute-start) | collective-permute-done | bytes 106528 | tf_op jit(solution)/shard_map/ppermute | solution.py:205
  11.3 5.5 %collective-permute-start.3 = (f32[21,16,256]{2,1,0:T(8,128)S(1)}, f32[21,16,256]{2,1,0:T(8,128)S(1)}, u32[]{:S(2)}, u32[]{:S(2)}) collective-permute-start(f32[21,16,256]{2,1,0:T(8,128)S(1)} %pad_maximum_fusion.1), channel_id=1, source_target_pairs={{0,4},{4,8},{8,12},{12,16},{16,20},{20,24},{24,28},{1,5},{5,9},{9,... | collective-permute-start | bytes 1032200 | tf_op jit(solution)/shard_map/ppermute | solution.py:46
  16.8 1.9 %collective-permute-start.4 = (f32[21,16,256]{2,1,0:T(8,128)S(1)}, f32[21,16,256]{2,1,0:T(8,128)S(1)}, u32[]{:S(2)}, u32[]{:S(2)}) collective-permute-start(f32[21,16,256]{2,1,0:T(8,128)S(1)} %pad_maximum_fusion.1), channel_id=1, source_target_pairs={{4,0},{8,4},{12,8},{16,12},{20,16},{24,20},{28,24},{5,1},{9,5},{13... | collective-permute-start | bytes 1032200 | tf_op jit(solution)/shard_map/ppermute | solution.py:47
  18.7 2.2 %collective-permute-done.3 = f32[21,16,256]{2,1,0:T(8,128)S(1)} collective-permute-done((f32[21,16,256]{2,1,0:T(8,128)S(1)}, f32[21,16,256]{2,1,0:T(8,128)S(1)}, u32[]{:S(2)}, u32[]{:S(2)}) %collective-permute-start.3) | collective-permute-done | bytes 344096 | tf_op jit(solution)/shard_map/ppermute | solution.py:46
  21.0 4.4 %collective-permute-done.4 = f32[21,16,256]{2,1,0:T(8,128)S(1)} collective-permute-done((f32[21,16,256]{2,1,0:T(8,128)S(1)}, f32[21,16,256]{2,1,0:T(8,128)S(1)}, u32[]{:S(2)}, u32[]{:S(2)}) %collective-permute-start.4) | collective-permute-done | bytes 344096 | tf_op jit(solution)/shard_map/ppermute | solution.py:47
  25.5 0.3 fusion.18
  25.7 0.2 fusion.19
  25.9 0.2 fusion.20
  26.1 0.1 fusion.21
  26.3 1.1 bitcast_dynamic-update-slice_fusion.7
  27.5 1.2 bitcast_dynamic-update-slice_fusion.6
  28.6 1.4 multiply_add_fusion
  30.1 1.2 bitcast_dynamic-update-slice_fusion.5
  31.3 1.2 bitcast_dynamic-update-slice_fusion.4
  32.5 1.0 bitcast_dynamic-update-slice_fusion.3
  33.5 1.0 bitcast_dynamic-update-slice_fusion.2
  34.5 0.2 pad_multiply_fusion
  34.7 1.3 copy.13.refs_2_
  36.0 1.2 bitcast_dynamic-update-slice_fusion.1
  37.1 1.2 bitcast_dynamic-update-slice_fusion.refs_1_
  38.3 24.6 %shard_map.113 = (f32[2,18,48,256]{3,2,1,0:T(8,128)}, f32[2,18,48,256]{3,2,1,0:T(8,128)}, f32[2,2,16,16,256]{4,3,2,1,0:T(8,128)}, f32[2,2,16,16,256]{4,3,2,1,0:T(8,128)}) custom-call(f32[2,15]{1,0:T(2,128)} %constant.99.clone.refs_0_, f32[8,16,48,256]{3,2,1,0:T(8,128)} %bitcast_dynamic-update-slice_fusion.refs_1_, f32[2,16,48,256]{3,2,1,0:T(8,128)} %copy.13.refs_2_), custom_call_target="tpu_custom_call" | custom-call | flops 117964800 | bytes 14155776 | tf_op jit(solution)/shard_map/pallas_call | solution.py:182
  62.9 1.9 %collective-permute-start.5 = (f32[2,2,16,16,256]{4,3,2,1,0:T(8,128)}, f32[2,2,16,16,256]{4,3,2,1,0:T(8,128)S(1)}, u32[]{:S(2)}, u32[]{:S(2)}) collective-permute-start(f32[2,2,16,16,256]{4,3,2,1,0:T(8,128)} %get-tuple-element.40), channel_id=1, source_target_pairs={{0,4},{4,8},{8,12},{12,16},{16,20},{20,24},{24,28},{1,5},{5,9},{9,... | collective-permute-start | bytes 3145736 | tf_op jit(solution)/shard_map/ppermute | solution.py:272
  64.8 2.6 %collective-permute-start.6 = (f32[2,2,16,16,256]{4,3,2,1,0:T(8,128)}, f32[2,2,16,16,256]{4,3,2,1,0:T(8,128)S(1)}, u32[]{:S(2)}, u32[]{:S(2)}) collective-permute-start(f32[2,2,16,16,256]{4,3,2,1,0:T(8,128)} %get-tuple-element.41), channel_id=1, source_target_pairs={{4,0},{8,4},{12,8},{16,12},{20,16},{24,20},{28,24},{5,1},{9,5},{13... | collective-permute-start | bytes 3145736 | tf_op jit(solution)/shard_map/ppermute | solution.py:273
  67.5 9.4 %collective-permute-done.5.refs_5_ = f32[2,2,16,16,256]{4,3,2,1,0:T(8,128)S(1)} collective-permute-done((f32[2,2,16,16,256]{4,3,2,1,0:T(8,128)}, f32[2,2,16,16,256]{4,3,2,1,0:T(8,128)S(1)}, u32[]{:S(2)}, u32[]{:S(2)}) %collective-permute-start.5) | collective-permute-done | bytes 1048608 | tf_op jit(solution)/shard_map/ppermute | solution.py:272
  76.9 4.3 %collective-permute-done.6.refs_6_ = f32[2,2,16,16,256]{4,3,2,1,0:T(8,128)S(1)} collective-permute-done((f32[2,2,16,16,256]{4,3,2,1,0:T(8,128)}, f32[2,2,16,16,256]{4,3,2,1,0:T(8,128)S(1)}, u32[]{:S(2)}, u32[]{:S(2)}) %collective-permute-start.6) | collective-permute-done | bytes 1048608 | tf_op jit(solution)/shard_map/ppermute | solution.py:273
  81.1 1.0 copy-done.1
  82.1 26.9 %shard_map.114 = (f32[2,18,48,256]{3,2,1,0:T(8,128)}, f32[2,18,48,256]{3,2,1,0:T(8,128)}) custom-call(f32[2,16]{1,0:T(2,128)} %constant.100.clone.refs_0_, f32[8,16,48,256]{3,2,1,0:T(8,128)} %bitcast_dynamic-update-slice_fusion.refs_1_, f32[2,16,48,256]{3,2,1,0:T(8,128)} %copy.13.refs_2_, f32[2,18,48,256]{3,2,1,0:T(8,128)} %get-tuple-element.38.refs_3_, ...), custom_call_target="tpu_custom_call" | custom-call | flops 125829120 | bytes 14155776 | tf_op jit(solution)/shard_map/pallas_call | solution.py:182
  109.1 2.1 %fusion.17 = (f32[2,48,256]{2,1,0:T(8,128)S(1)}, f32[2,16,48,256]{3,2,1,0:T(8,128)S(1)}) fusion(f32[2,18,48,256]{3,2,1,0:T(8,128)} %get-tuple-element.43, f32[2,18,48,256]{3,2,1,0:T(8,128)} %get-tuple-element.42), kind=kLoop, calls=%fused_computation.74 | loop fusion | flops 761856 | bytes 4816896 | tf_op jit(solution)/shard_map/reduce_sum | solution.py:287
  111.2 1.9 %collective-permute-start.7 = (f32[2,16,256]{2,1,0:T(8,128)S(1)}, f32[2,16,256]{2,1,0:T(8,128)S(1)}, u32[]{:S(2)}, u32[]{:S(2)}) collective-permute-start(f32[2,16,256]{2,1,0:T(8,128)S(1)} %slice_multiply_fusion), channel_id=1, source_target_pairs={{0,4},{4,8},{8,12},{12,16},{16,20},{20,24},{24,28},{1,5},{5,9},{9,... | collective-permute-start | bytes 98312 | tf_op jit(solution)/shard_map/ppermute | solution.py:46
  113.2 2.4 %collective-permute-start.8 = (f32[2,16,256]{2,1,0:T(8,128)S(1)}, f32[2,16,256]{2,1,0:T(8,128)S(1)}, u32[]{:S(2)}, u32[]{:S(2)}) collective-permute-start(f32[2,16,256]{2,1,0:T(8,128)S(1)} %slice_multiply_fusion), channel_id=1, source_target_pairs={{4,0},{8,4},{12,8},{16,12},{20,16},{24,20},{28,24},{5,1},{9,5},{13... | collective-permute-start | bytes 98312 | tf_op jit(solution)/shard_map/ppermute | solution.py:47
  115.6 2.8 %collective-permute-done.8 = f32[2,16,256]{2,1,0:T(8,128)S(1)} collective-permute-done((f32[2,16,256]{2,1,0:T(8,128)S(1)}, f32[2,16,256]{2,1,0:T(8,128)S(1)}, u32[]{:S(2)}, u32[]{:S(2)}) %collective-permute-start.8) | collective-permute-done | bytes 32800 | tf_op jit(solution)/shard_map/ppermute | solution.py:47
  118.4 1.3 broadcast_multiply_fusion.refs_2_
  119.7 24.6 %shard_map.115 = (f32[2,18,48,256]{3,2,1,0:T(8,128)}, f32[2,18,48,256]{3,2,1,0:T(8,128)}, f32[2,2,16,16,256]{4,3,2,1,0:T(8,128)}, f32[2,2,16,16,256]{4,3,2,1,0:T(8,128)}) custom-call(f32[2,15]{1,0:T(2,128)} %constant.99.clone.refs_0_, f32[8,16,48,256]{3,2,1,0:T(8,128)} %bitcast_dynamic-update-slice_fusion.refs_1_, ...), custom_call_target="tpu_custom_call" | custom-call | flops 117964800 | bytes 14155776 | tf_op jit(solution)/shard_map/pallas_call | solution.py:182
  144.3 1.9 %collective-permute-start.10 = (f32[2,2,16,16,256]{4,3,2,1,0:T(8,128)}, f32[2,2,16,16,256]{4,3,2,1,0:T(8,128)}, u32[]{:S(2)}, u32[]{:S(2)}) collective-permute-start(f32[2,2,16,16,256]{4,3,2,1,0:T(8,128)} %get-tuple-element.47), channel_id=1, source_target_pairs={{4,0},{8,4},{12,8},{16,12},{20,16},{24,20},{28,24},{5,1},{9,5},{13... | collective-permute-start | bytes 3145736 | tf_op jit(solution)/shard_map/ppermute | solution.py:273
  146.2 3.9 %collective-permute-start.9 = (f32[2,2,16,16,256]{4,3,2,1,0:T(8,128)}, f32[2,2,16,16,256]{4,3,2,1,0:T(8,128)}, u32[]{:S(2)}, u32[]{:S(2)}) collective-permute-start(f32[2,2,16,16,256]{4,3,2,1,0:T(8,128)} %get-tuple-element.46), channel_id=1, source_target_pairs={{0,4},{4,8},{8,12},{12,16},{16,20},{20,24},{24,28},{1,5},{5,9},{9,... | collective-permute-start | bytes 3145736 | tf_op jit(solution)/shard_map/ppermute | solution.py:272
  150.2 0.7 constant_dynamic-slice_fusion
  150.9 9.9 %collective-permute-done.10.refs_6_ = f32[2,2,16,16,256]{4,3,2,1,0:T(8,128)} collective-permute-done((f32[2,2,16,16,256]{4,3,2,1,0:T(8,128)}, f32[2,2,16,16,256]{4,3,2,1,0:T(8,128)}, u32[]{:S(2)}, u32[]{:S(2)}) %collective-permute-start.10) | collective-permute-done | bytes 1048608 | tf_op jit(solution)/shard_map/ppermute | solution.py:273
  160.8 1.2 collective-permute-done.9.refs_5_
  161.9 26.9 %shard_map.116 = (f32[2,18,48,256]{3,2,1,0:T(8,128)}, f32[2,18,48,256]{3,2,1,0:T(8,128)}) custom-call(f32[2,16]{1,0:T(2,128)} %constant.100.clone.refs_0_, f32[8,16,48,256]{3,2,1,0:T(8,128)} %bitcast_dynamic-update-slice_fusion.refs_1_, f32[2,16,48,256]{3,2,1,0:T(8,128)} %broadcast_multiply_fusion.refs_2_, f32[2,18,48,256]{3,2,1,0:T(8,128)} %get-tuple-element.44.refs_3_, ...), custom_call_target="tpu_custom_call" | custom-call | flops 125829120 | bytes 14155776 | tf_op jit(solution)/shard_map/pallas_call | solution.py:182
  188.9 1.0 fusion.8
  189.9 0.7 fusion.15
  (28 shorter events, 0.5 us)
Async XLA Ops:
  0.6 7.1 %collective-permute-start.1 = (f32[8,16,128]{2,1,0:T(8,128)}, f32[8,16,128]{2,1,0:T(8,128)S(1)}, u32[]{:S(2)}, u32[]{:S(2)}) collective-permute-start(f32[8,16,128]{2,1,0:T(8,128)} %param.14), channel_id=1, source_target_pairs={{0,1},{1,0},{2,3},{3,2},{4,5},{5,4},{6,7},{7,6},{8,9},{9,8},{10,11... | collective-permute-start | bytes 196616 | tf_op jit(solution)/shard_map/ppermute | solution.py:206
  2.7 5.0 %collective-permute-start.2 = (f32[8,16,128]{2,1,0:T(8,128)}, f32[8,16,128]{2,1,0:T(8,128)S(1)}, u32[]{:S(2)}, u32[]{:S(2)}) collective-permute-start(f32[8,16,128]{2,1,0:T(8,128)} %param.14), channel_id=1, source_target_pairs={{0,3},{1,2},{2,1},{3,0},{4,7},{5,6},{6,5},{7,4},{8,11},{9,10},{10,... | collective-permute-start | bytes 196616 | tf_op jit(solution)/shard_map/ppermute | solution.py:207
  7.7 3.6 %collective-permute-start = (f32[13,16,128]{2,1,0:T(8,128)S(1)}, f32[13,16,128]{2,1,0:T(8,128)S(1)}, u32[]{:S(2)}, u32[]{:S(2)}) collective-permute-start(f32[13,16,128]{2,1,0:T(8,128)S(1)} %constant_dynamic-update-slice_fusion), channel_id=1, source_target_pairs={{0,2},{2,0},{1,3},{3,1},{4,6},{6,4},{5,7},{7,5},{8,10},{10,8},{9,1... | collective-permute-start | bytes 319496 | tf_op jit(solution)/shard_map/ppermute | solution.py:205
  11.3 9.7 %collective-permute-start.3 = (f32[21,16,256]{2,1,0:T(8,128)S(1)}, f32[21,16,256]{2,1,0:T(8,128)S(1)}, u32[]{:S(2)}, u32[]{:S(2)}) collective-permute-start(f32[21,16,256]{2,1,0:T(8,128)S(1)} %pad_maximum_fusion.1), channel_id=1, source_target_pairs={{0,4},{4,8},{8,12},{12,16},{16,20},{20,24},{24,28},{1,5},{5,9},{9,... | collective-permute-start | bytes 1032200 | tf_op jit(solution)/shard_map/ppermute | solution.py:46
  16.8 8.6 %collective-permute-start.4 = (f32[21,16,256]{2,1,0:T(8,128)S(1)}, f32[21,16,256]{2,1,0:T(8,128)S(1)}, u32[]{:S(2)}, u32[]{:S(2)}) collective-permute-start(f32[21,16,256]{2,1,0:T(8,128)S(1)} %pad_maximum_fusion.1), channel_id=1, source_target_pairs={{4,0},{8,4},{12,8},{16,12},{20,16},{24,20},{28,24},{5,1},{9,5},{13... | collective-permute-start | bytes 1032200 | tf_op jit(solution)/shard_map/ppermute | solution.py:47
  62.9 14.0 %collective-permute-start.5 = (f32[2,2,16,16,256]{4,3,2,1,0:T(8,128)}, f32[2,2,16,16,256]{4,3,2,1,0:T(8,128)S(1)}, u32[]{:S(2)}, u32[]{:S(2)}) collective-permute-start(f32[2,2,16,16,256]{4,3,2,1,0:T(8,128)} %get-tuple-element.40), channel_id=1, source_target_pairs={{0,4},{4,8},{8,12},{12,16},{16,20},{20,24},{24,28},{1,5},{5,9},{9,... | collective-permute-start | bytes 3145736 | tf_op jit(solution)/shard_map/ppermute | solution.py:272
  64.8 16.3 %collective-permute-start.6 = (f32[2,2,16,16,256]{4,3,2,1,0:T(8,128)}, f32[2,2,16,16,256]{4,3,2,1,0:T(8,128)S(1)}, u32[]{:S(2)}, u32[]{:S(2)}) collective-permute-start(f32[2,2,16,16,256]{4,3,2,1,0:T(8,128)} %get-tuple-element.41), channel_id=1, source_target_pairs={{4,0},{8,4},{12,8},{16,12},{20,16},{24,20},{28,24},{5,1},{9,5},{13... | collective-permute-start | bytes 3145736 | tf_op jit(solution)/shard_map/ppermute | solution.py:273
  76.8 4.3 %copy-start = (f32[2,2,16,16,256]{4,3,2,1,0:T(8,128)}, f32[2,2,16,16,256]{4,3,2,1,0:T(8,128)S(1)}, u32[]{:S(2)}) copy-start(f32[2,2,16,16,256]{4,3,2,1,0:T(8,128)S(1)} %collective-permute-done.5.refs_5_) | copy-start | bytes 3145732
  81.1 1.0 copy-start.1
  111.2 4.3 %collective-permute-start.7 = (f32[2,16,256]{2,1,0:T(8,128)S(1)}, f32[2,16,256]{2,1,0:T(8,128)S(1)}, u32[]{:S(2)}, u32[]{:S(2)}) collective-permute-start(f32[2,16,256]{2,1,0:T(8,128)S(1)} %slice_multiply_fusion), channel_id=1, source_target_pairs={{0,4},{4,8},{8,12},{12,16},{16,20},{20,24},{24,28},{1,5},{5,9},{9,... | collective-permute-start | bytes 98312 | tf_op jit(solution)/shard_map/ppermute | solution.py:46
  113.2 5.2 %collective-permute-start.8 = (f32[2,16,256]{2,1,0:T(8,128)S(1)}, f32[2,16,256]{2,1,0:T(8,128)S(1)}, u32[]{:S(2)}, u32[]{:S(2)}) collective-permute-start(f32[2,16,256]{2,1,0:T(8,128)S(1)} %slice_multiply_fusion), channel_id=1, source_target_pairs={{4,0},{8,4},{12,8},{16,12},{20,16},{24,20},{28,24},{5,1},{9,5},{13... | collective-permute-start | bytes 98312 | tf_op jit(solution)/shard_map/ppermute | solution.py:47
  144.3 16.4 %collective-permute-start.10 = (f32[2,2,16,16,256]{4,3,2,1,0:T(8,128)}, f32[2,2,16,16,256]{4,3,2,1,0:T(8,128)}, u32[]{:S(2)}, u32[]{:S(2)}) collective-permute-start(f32[2,2,16,16,256]{4,3,2,1,0:T(8,128)} %get-tuple-element.47), channel_id=1, source_target_pairs={{4,0},{8,4},{12,8},{16,12},{20,16},{24,20},{28,24},{5,1},{9,5},{13... | collective-permute-start | bytes 3145736 | tf_op jit(solution)/shard_map/ppermute | solution.py:273
  146.2 15.7 %collective-permute-start.9 = (f32[2,2,16,16,256]{4,3,2,1,0:T(8,128)}, f32[2,2,16,16,256]{4,3,2,1,0:T(8,128)}, u32[]{:S(2)}, u32[]{:S(2)}) collective-permute-start(f32[2,2,16,16,256]{4,3,2,1,0:T(8,128)} %get-tuple-element.46), channel_id=1, source_target_pairs={{0,4},{4,8},{8,12},{12,16},{16,20},{20,24},{24,28},{1,5},{5,9},{9,... | collective-permute-start | bytes 3145736 | tf_op jit(solution)/shard_map/ppermute | solution.py:272

commit v14 on v13

--- a/solution.py
+++ b/solution.py
@@ -88,7 +88,7 @@
                     ref[c, layer + 1, pl.ds(halo + own, halo)] = high_in[f, c, layer]
             return carry
 
-        lax.fori_loop(0, layers, place, 0)
+        lax.fori_loop(0, layers, place, 0, unroll=True)
     else:
         x_ref, d_ref = refs
         zero = jnp.zeros((rows, cols), jnp.float32)
@@ -104,7 +104,7 @@
                 d_ref[c, layer + 1] = op_ref[5, layer] * rhs_ref[c, layer] / theta_center
             return carry
 
-        lax.fori_loop(0, layers, start, 0)
+        lax.fori_loop(0, layers, start, 0, unroll=True)
 
     def one_step(lo, keep, push):
         span = pl.ds(lo, rows - 2 * lo)
@@ -164,7 +164,7 @@
                     down_ref[f, c, layer] = ref[c, layer + 1, pl.ds(halo, halo)]
             return carry
 
-        lax.fori_loop(0, layers, pack, 0)
+        lax.fori_loop(0, layers, pack, 0, unroll=True)
 
 
 def run_segment(steps, start_valid, halo, send, op_stack, rhs, state):

time: 191 us -> 190 us (level)
  no operation moved by 1% of the time
where the time goes in v14:
time: 190 us; the launch traced here: 189 us
  Pallas kernels  102 us (54%)
  waiting for transfers between devices  37.7 us (20%)
  starting transfers between devices  25.4 us (13%)
  other arithmetic  17.4 us (9%)
  local copies, waits for them, and re-layouts  6.08 us (3%)
    pallas_call x4, Pallas kernels, run_segment(): pl.pallas_call(lambda *refs: segment_kernel(steps, start_valid, halo, sen...  102 us
    ppermute x2, waiting for transfers between devices, chebyshev(): high = lax.ppermute(down, 'mx', backward)  14.2 us
    ppermute x2, waiting for transfers between devices, chebyshev(): low = lax.ppermute(up, 'mx', forward)  10.6 us
    unnamed x9, other arithmetic  9.28 us
    ppermute x2, starting transfers between devices, exchange_rows(): lax.ppermute(lax.slice_in_dim(own, rows - k, rows, axis=axis), 'mx', forw...  7.4 us
    ppermute x2, waiting for transfers between devices, exchange_rows(): high = lax.ppermute(lax.slice_in_dim(own, 0, k, axis=axis), 'mx', backward)  7.21 us
    ppermute x2, starting transfers between devices, chebyshev(): low = lax.ppermute(up, 'mx', forward)  5.77 us
    ppermute x2, starting transfers between devices, chebyshev(): high = lax.ppermute(down, 'mx', backward)  4.56 us
  transfers between devices with their start and end apart: 11, of which 8 were waited for; matrix products, arithmetic and copies ran while one was open for 2% of the time, Pallas kernels for 0%

profile of v14, /device:TPU:1, one launch (start us, length us, event | category | flops | bytes accessed | tf_op | source)
XLA Modules:
  0.0 189.2 jit_solution(18193692083392651027)
XLA Ops:
  0.6 2.1 %collective-permute-start.1 = (f32[8,16,128]{2,1,0:T(8,128)}, f32[8,16,128]{2,1,0:T(8,128)S(1)}, u32[]{:S(2)}, u32[]{:S(2)}) collective-permute-start(f32[8,16,128]{2,1,0:T(8,128)} %param.14), channel_id=1, source_target_pairs={{0,1},{1,0},{2,3},{3,2},{4,5},{5,4},{6,7},{7,6},{8,9},{9,8},{10,11... | collective-permute-start | bytes 196616 | tf_op jit(solution)/shard_map/ppermute | solution.py:206
  2.7 1.2 collective-permute-start.2
  3.9 0.9 constant_dynamic-update-slice_fusion.4
  4.8 0.7 constant_dynamic-update-slice_fusion.3
  5.5 0.7 constant_dynamic-update-slice_fusion.2
  6.2 0.7 constant_dynamic-update-slice_fusion.1
  7.0 0.7 constant_dynamic-update-slice_fusion
  7.7 3.5 %collective-permute-done = f32[13,16,128]{2,1,0:T(8,128)S(1)} collective-permute-done((f32[13,16,128]{2,1,0:T(8,128)S(1)}, f32[13,16,128]{2,1,0:T(8,128)S(1)}, u32[]{:S(2)}, u32[]{:S(2)}) %collective-permute-start) | collective-permute-done | bytes 106528 | tf_op jit(solution)/shard_map/ppermute | solution.py:205
  11.3 5.5 %collective-permute-start.3 = (f32[21,16,256]{2,1,0:T(8,128)S(1)}, f32[21,16,256]{2,1,0:T(8,128)S(1)}, u32[]{:S(2)}, u32[]{:S(2)}) collective-permute-start(f32[21,16,256]{2,1,0:T(8,128)S(1)} %pad_maximum_fusion.1), channel_id=1, source_target_pairs={{0,4},{4,8},{8,12},{12,16},{16,20},{20,24},{24,28},{1,5},{5,9},{9,... | collective-permute-start | bytes 1032200 | tf_op jit(solution)/shard_map/ppermute | solution.py:46
  16.8 1.9 %collective-permute-start.4 = (f32[21,16,256]{2,1,0:T(8,128)S(1)}, f32[21,16,256]{2,1,0:T(8,128)S(1)}, u32[]{:S(2)}, u32[]{:S(2)}) collective-permute-start(f32[21,16,256]{2,1,0:T(8,128)S(1)} %pad_maximum_fusion.1), channel_id=1, source_target_pairs={{4,0},{8,4},{12,8},{16,12},{20,16},{24,20},{28,24},{5,1},{9,5},{13... | collective-permute-start | bytes 1032200 | tf_op jit(solution)/shard_map/ppermute | solution.py:47
  18.7 2.2 %collective-permute-done.3 = f32[21,16,256]{2,1,0:T(8,128)S(1)} collective-permute-done((f32[21,16,256]{2,1,0:T(8,128)S(1)}, f32[21,16,256]{2,1,0:T(8,128)S(1)}, u32[]{:S(2)}, u32[]{:S(2)}) %collective-permute-start.3) | collective-permute-done | bytes 344096 | tf_op jit(solution)/shard_map/ppermute | solution.py:46
  21.0 4.4 %collective-permute-done.4 = f32[21,16,256]{2,1,0:T(8,128)S(1)} collective-permute-done((f32[21,16,256]{2,1,0:T(8,128)S(1)}, f32[21,16,256]{2,1,0:T(8,128)S(1)}, u32[]{:S(2)}, u32[]{:S(2)}) %collective-permute-start.4) | collective-permute-done | bytes 344096 | tf_op jit(solution)/shard_map/ppermute | solution.py:47
  25.5 0.3 fusion.18
  25.7 0.2 fusion.19
  25.9 0.2 fusion.20
  26.1 0.1 fusion.21
  26.3 1.1 bitcast_dynamic-update-slice_fusion.7
  27.5 1.2 bitcast_dynamic-update-slice_fusion.6
  28.6 1.4 multiply_add_fusion
  30.1 1.2 bitcast_dynamic-update-slice_fusion.5
  31.3 1.2 bitcast_dynamic-update-slice_fusion.4
  32.5 1.0 bitcast_dynamic-update-slice_fusion.3
  33.5 1.0 bitcast_dynamic-update-slice_fusion.2
  34.5 0.2 pad_multiply_fusion
  34.7 1.3 copy.13.refs_2_
  36.0 1.2 bitcast_dynamic-update-slice_fusion.1
  37.1 1.2 bitcast_dynamic-update-slice_fusion.refs_1_
  38.3 24.3 %shard_map.113 = (f32[2,18,48,256]{3,2,1,0:T(8,128)}, f32[2,18,48,256]{3,2,1,0:T(8,128)}, f32[2,2,16,16,256]{4,3,2,1,0:T(8,128)}, f32[2,2,16,16,256]{4,3,2,1,0:T(8,128)}) custom-call(f32[2,15]{1,0:T(2,128)} %constant.99.clone.refs_0_, f32[8,16,48,256]{3,2,1,0:T(8,128)} %bitcast_dynamic-update-slice_fusion.refs_1_, f32[2,16,48,256]{3,2,1,0:T(8,128)} %copy.13.refs_2_), custom_call_target="tpu_custom_call" | custom-call | flops 117964800 | bytes 14155776 | tf_op jit(solution)/shard_map/pallas_call | solution.py:182
  62.6 1.9 %collective-permute-start.5 = (f32[2,2,16,16,256]{4,3,2,1,0:T(8,128)}, f32[2,2,16,16,256]{4,3,2,1,0:T(8,128)S(1)}, u32[]{:S(2)}, u32[]{:S(2)}) collective-permute-start(f32[2,2,16,16,256]{4,3,2,1,0:T(8,128)} %get-tuple-element.40), channel_id=1, source_target_pairs={{0,4},{4,8},{8,12},{12,16},{16,20},{20,24},{24,28},{1,5},{5,9},{9,... | collective-permute-start | bytes 3145736 | tf_op jit(solution)/shard_map/ppermute | solution.py:272
  64.6 2.6 %collective-permute-start.6 = (f32[2,2,16,16,256]{4,3,2,1,0:T(8,128)}, f32[2,2,16,16,256]{4,3,2,1,0:T(8,128)S(1)}, u32[]{:S(2)}, u32[]{:S(2)}) collective-permute-start(f32[2,2,16,16,256]{4,3,2,1,0:T(8,128)} %get-tuple-element.41), channel_id=1, source_target_pairs={{4,0},{8,4},{12,8},{16,12},{20,16},{24,20},{28,24},{5,1},{9,5},{13... | collective-permute-start | bytes 3145736 | tf_op jit(solution)/shard_map/ppermute | solution.py:273
  67.2 9.4 %collective-permute-done.5.refs_5_ = f32[2,2,16,16,256]{4,3,2,1,0:T(8,128)S(1)} collective-permute-done((f32[2,2,16,16,256]{4,3,2,1,0:T(8,128)}, f32[2,2,16,16,256]{4,3,2,1,0:T(8,128)S(1)}, u32[]{:S(2)}, u32[]{:S(2)}) %collective-permute-start.5) | collective-permute-done | bytes 1048608 | tf_op jit(solution)/shard_map/ppermute | solution.py:272
  76.6 4.3 %collective-permute-done.6.refs_6_ = f32[2,2,16,16,256]{4,3,2,1,0:T(8,128)S(1)} collective-permute-done((f32[2,2,16,16,256]{4,3,2,1,0:T(8,128)}, f32[2,2,16,16,256]{4,3,2,1,0:T(8,128)S(1)}, u32[]{:S(2)}, u32[]{:S(2)}) %collective-permute-start.6) | collective-permute-done | bytes 1048608 | tf_op jit(solution)/shard_map/ppermute | solution.py:273
  80.9 1.0 copy-done.1
  81.9 26.5 %shard_map.114 = (f32[2,18,48,256]{3,2,1,0:T(8,128)}, f32[2,18,48,256]{3,2,1,0:T(8,128)}) custom-call(f32[2,16]{1,0:T(2,128)} %constant.100.clone.refs_0_, f32[8,16,48,256]{3,2,1,0:T(8,128)} %bitcast_dynamic-update-slice_fusion.refs_1_, f32[2,16,48,256]{3,2,1,0:T(8,128)} %copy.13.refs_2_, f32[2,18,48,256]{3,2,1,0:T(8,128)} %get-tuple-element.38.refs_3_, ...), custom_call_target="tpu_custom_call" | custom-call | flops 125829120 | bytes 14155776 | tf_op jit(solution)/shard_map/pallas_call | solution.py:182
  108.4 2.1 %fusion.17 = (f32[2,48,256]{2,1,0:T(8,128)S(1)}, f32[2,16,48,256]{3,2,1,0:T(8,128)S(1)}) fusion(f32[2,18,48,256]{3,2,1,0:T(8,128)} %get-tuple-element.43, f32[2,18,48,256]{3,2,1,0:T(8,128)} %get-tuple-element.42), kind=kLoop, calls=%fused_computation.74 | loop fusion | flops 761856 | bytes 4816896 | tf_op jit(solution)/shard_map/reduce_sum | solution.py:287
  110.6 1.9 %collective-permute-start.7 = (f32[2,16,256]{2,1,0:T(8,128)S(1)}, f32[2,16,256]{2,1,0:T(8,128)S(1)}, u32[]{:S(2)}, u32[]{:S(2)}) collective-permute-start(f32[2,16,256]{2,1,0:T(8,128)S(1)} %slice_multiply_fusion), channel_id=1, source_target_pairs={{0,4},{4,8},{8,12},{12,16},{16,20},{20,24},{24,28},{1,5},{5,9},{9,... | collective-permute-start | bytes 98312 | tf_op jit(solution)/shard_map/ppermute | solution.py:46
  112.5 2.4 %collective-permute-start.8 = (f32[2,16,256]{2,1,0:T(8,128)S(1)}, f32[2,16,256]{2,1,0:T(8,128)S(1)}, u32[]{:S(2)}, u32[]{:S(2)}) collective-permute-start(f32[2,16,256]{2,1,0:T(8,128)S(1)} %slice_multiply_fusion), channel_id=1, source_target_pairs={{4,0},{8,4},{12,8},{16,12},{20,16},{24,20},{28,24},{5,1},{9,5},{13... | collective-permute-start | bytes 98312 | tf_op jit(solution)/shard_map/ppermute | solution.py:47
  114.9 2.8 %collective-permute-done.8 = f32[2,16,256]{2,1,0:T(8,128)S(1)} collective-permute-done((f32[2,16,256]{2,1,0:T(8,128)S(1)}, f32[2,16,256]{2,1,0:T(8,128)S(1)}, u32[]{:S(2)}, u32[]{:S(2)}) %collective-permute-start.8) | collective-permute-done | bytes 32800 | tf_op jit(solution)/shard_map/ppermute | solution.py:47
  117.7 1.3 broadcast_multiply_fusion.refs_2_
  119.1 24.3 %shard_map.115 = (f32[2,18,48,256]{3,2,1,0:T(8,128)}, f32[2,18,48,256]{3,2,1,0:T(8,128)}, f32[2,2,16,16,256]{4,3,2,1,0:T(8,128)}, f32[2,2,16,16,256]{4,3,2,1,0:T(8,128)}) custom-call(f32[2,15]{1,0:T(2,128)} %constant.99.clone.refs_0_, f32[8,16,48,256]{3,2,1,0:T(8,128)} %bitcast_dynamic-update-slice_fusion.refs_1_, ...), custom_call_target="tpu_custom_call" | custom-call | flops 117964800 | bytes 14155776 | tf_op jit(solution)/shard_map/pallas_call | solution.py:182
  143.4 1.9 %collective-permute-start.10 = (f32[2,2,16,16,256]{4,3,2,1,0:T(8,128)}, f32[2,2,16,16,256]{4,3,2,1,0:T(8,128)}, u32[]{:S(2)}, u32[]{:S(2)}) collective-permute-start(f32[2,2,16,16,256]{4,3,2,1,0:T(8,128)} %get-tuple-element.47), channel_id=1, source_target_pairs={{4,0},{8,4},{12,8},{16,12},{20,16},{24,20},{28,24},{5,1},{9,5},{13... | collective-permute-start | bytes 3145736 | tf_op jit(solution)/shard_map/ppermute | solution.py:273
  145.3 3.9 %collective-permute-start.9 = (f32[2,2,16,16,256]{4,3,2,1,0:T(8,128)}, f32[2,2,16,16,256]{4,3,2,1,0:T(8,128)}, u32[]{:S(2)}, u32[]{:S(2)}) collective-permute-start(f32[2,2,16,16,256]{4,3,2,1,0:T(8,128)} %get-tuple-element.46), channel_id=1, source_target_pairs={{0,4},{4,8},{8,12},{12,16},{16,20},{20,24},{24,28},{1,5},{5,9},{9,... | collective-permute-start | bytes 3145736 | tf_op jit(solution)/shard_map/ppermute | solution.py:272
  149.3 0.7 constant_dynamic-slice_fusion
  150.0 9.9 %collective-permute-done.10.refs_6_ = f32[2,2,16,16,256]{4,3,2,1,0:T(8,128)} collective-permute-done((f32[2,2,16,16,256]{4,3,2,1,0:T(8,128)}, f32[2,2,16,16,256]{4,3,2,1,0:T(8,128)}, u32[]{:S(2)}, u32[]{:S(2)}) %collective-permute-start.10) | collective-permute-done | bytes 1048608 | tf_op jit(solution)/shard_map/ppermute | solution.py:273
  159.8 1.2 collective-permute-done.9.refs_5_
  161.0 26.5 %shard_map.116 = (f32[2,18,48,256]{3,2,1,0:T(8,128)}, f32[2,18,48,256]{3,2,1,0:T(8,128)}) custom-call(f32[2,16]{1,0:T(2,128)} %constant.100.clone.refs_0_, f32[8,16,48,256]{3,2,1,0:T(8,128)} %bitcast_dynamic-update-slice_fusion.refs_1_, f32[2,16,48,256]{3,2,1,0:T(8,128)} %broadcast_multiply_fusion.refs_2_, f32[2,18,48,256]{3,2,1,0:T(8,128)} %get-tuple-element.44.refs_3_, ...), custom_call_target="tpu_custom_call" | custom-call | flops 125829120 | bytes 14155776 | tf_op jit(solution)/shard_map/pallas_call | solution.py:182
  187.6 1.0 fusion.8
  188.5 0.7 fusion.15
  (28 shorter events, 0.5 us)
Async XLA Ops:
  0.6 7.1 %collective-permute-start.1 = (f32[8,16,128]{2,1,0:T(8,128)}, f32[8,16,128]{2,1,0:T(8,128)S(1)}, u32[]{:S(2)}, u32[]{:S(2)}) collective-permute-start(f32[8,16,128]{2,1,0:T(8,128)} %param.14), channel_id=1, source_target_pairs={{0,1},{1,0},{2,3},{3,2},{4,5},{5,4},{6,7},{7,6},{8,9},{9,8},{10,11... | collective-permute-start | bytes 196616 | tf_op jit(solution)/shard_map/ppermute | solution.py:206
  2.7 5.0 %collective-permute-start.2 = (f32[8,16,128]{2,1,0:T(8,128)}, f32[8,16,128]{2,1,0:T(8,128)S(1)}, u32[]{:S(2)}, u32[]{:S(2)}) collective-permute-start(f32[8,16,128]{2,1,0:T(8,128)} %param.14), channel_id=1, source_target_pairs={{0,3},{1,2},{2,1},{3,0},{4,7},{5,6},{6,5},{7,4},{8,11},{9,10},{10,... | collective-permute-start | bytes 196616 | tf_op jit(solution)/shard_map/ppermute | solution.py:207
  7.7 3.6 %collective-permute-start = (f32[13,16,128]{2,1,0:T(8,128)S(1)}, f32[13,16,128]{2,1,0:T(8,128)S(1)}, u32[]{:S(2)}, u32[]{:S(2)}) collective-permute-start(f32[13,16,128]{2,1,0:T(8,128)S(1)} %constant_dynamic-update-slice_fusion), channel_id=1, source_target_pairs={{0,2},{2,0},{1,3},{3,1},{4,6},{6,4},{5,7},{7,5},{8,10},{10,8},{9,1... | collective-permute-start | bytes 319496 | tf_op jit(solution)/shard_map/ppermute | solution.py:205
  11.3 9.7 %collective-permute-start.3 = (f32[21,16,256]{2,1,0:T(8,128)S(1)}, f32[21,16,256]{2,1,0:T(8,128)S(1)}, u32[]{:S(2)}, u32[]{:S(2)}) collective-permute-start(f32[21,16,256]{2,1,0:T(8,128)S(1)} %pad_maximum_fusion.1), channel_id=1, source_target_pairs={{0,4},{4,8},{8,12},{12,16},{16,20},{20,24},{24,28},{1,5},{5,9},{9,... | collective-permute-start | bytes 1032200 | tf_op jit(solution)/shard_map/ppermute | solution.py:46
  16.8 8.6 %collective-permute-start.4 = (f32[21,16,256]{2,1,0:T(8,128)S(1)}, f32[21,16,256]{2,1,0:T(8,128)S(1)}, u32[]{:S(2)}, u32[]{:S(2)}) collective-permute-start(f32[21,16,256]{2,1,0:T(8,128)S(1)} %pad_maximum_fusion.1), channel_id=1, source_target_pairs={{4,0},{8,4},{12,8},{16,12},{20,16},{24,20},{28,24},{5,1},{9,5},{13... | collective-permute-start | bytes 1032200 | tf_op jit(solution)/shard_map/ppermute | solution.py:47
  62.6 14.0 %collective-permute-start.5 = (f32[2,2,16,16,256]{4,3,2,1,0:T(8,128)}, f32[2,2,16,16,256]{4,3,2,1,0:T(8,128)S(1)}, u32[]{:S(2)}, u32[]{:S(2)}) collective-permute-start(f32[2,2,16,16,256]{4,3,2,1,0:T(8,128)} %get-tuple-element.40), channel_id=1, source_target_pairs={{0,4},{4,8},{8,12},{12,16},{16,20},{20,24},{24,28},{1,5},{5,9},{9,... | collective-permute-start | bytes 3145736 | tf_op jit(solution)/shard_map/ppermute | solution.py:272
  64.6 16.3 %collective-permute-start.6 = (f32[2,2,16,16,256]{4,3,2,1,0:T(8,128)}, f32[2,2,16,16,256]{4,3,2,1,0:T(8,128)S(1)}, u32[]{:S(2)}, u32[]{:S(2)}) collective-permute-start(f32[2,2,16,16,256]{4,3,2,1,0:T(8,128)} %get-tuple-element.41), channel_id=1, source_target_pairs={{4,0},{8,4},{12,8},{16,12},{20,16},{24,20},{28,24},{5,1},{9,5},{13... | collective-permute-start | bytes 3145736 | tf_op jit(solution)/shard_map/ppermute | solution.py:273
  76.6 4.3 %copy-start = (f32[2,2,16,16,256]{4,3,2,1,0:T(8,128)}, f32[2,2,16,16,256]{4,3,2,1,0:T(8,128)S(1)}, u32[]{:S(2)}) copy-start(f32[2,2,16,16,256]{4,3,2,1,0:T(8,128)S(1)} %collective-permute-done.5.refs_5_) | copy-start | bytes 3145732
  80.9 1.0 copy-start.1
  110.6 4.3 %collective-permute-start.7 = (f32[2,16,256]{2,1,0:T(8,128)S(1)}, f32[2,16,256]{2,1,0:T(8,128)S(1)}, u32[]{:S(2)}, u32[]{:S(2)}) collective-permute-start(f32[2,16,256]{2,1,0:T(8,128)S(1)} %slice_multiply_fusion), channel_id=1, source_target_pairs={{0,4},{4,8},{8,12},{12,16},{16,20},{20,24},{24,28},{1,5},{5,9},{9,... | collective-permute-start | bytes 98312 | tf_op jit(solution)/shard_map/ppermute | solution.py:46
  112.5 5.2 %collective-permute-start.8 = (f32[2,16,256]{2,1,0:T(8,128)S(1)}, f32[2,16,256]{2,1,0:T(8,128)S(1)}, u32[]{:S(2)}, u32[]{:S(2)}) collective-permute-start(f32[2,16,256]{2,1,0:T(8,128)S(1)} %slice_multiply_fusion), channel_id=1, source_target_pairs={{4,0},{8,4},{12,8},{16,12},{20,16},{24,20},{28,24},{5,1},{9,5},{13... | collective-permute-start | bytes 98312 | tf_op jit(solution)/shard_map/ppermute | solution.py:47
  143.4 16.4 %collective-permute-start.10 = (f32[2,2,16,16,256]{4,3,2,1,0:T(8,128)}, f32[2,2,16,16,256]{4,3,2,1,0:T(8,128)}, u32[]{:S(2)}, u32[]{:S(2)}) collective-permute-start(f32[2,2,16,16,256]{4,3,2,1,0:T(8,128)} %get-tuple-element.47), channel_id=1, source_target_pairs={{4,0},{8,4},{12,8},{16,12},{20,16},{24,20},{28,24},{5,1},{9,5},{13... | collective-permute-start | bytes 3145736 | tf_op jit(solution)/shard_map/ppermute | solution.py:273
  145.3 15.7 %collective-permute-start.9 = (f32[2,2,16,16,256]{4,3,2,1,0:T(8,128)}, f32[2,2,16,16,256]{4,3,2,1,0:T(8,128)}, u32[]{:S(2)}, u32[]{:S(2)}) collective-permute-start(f32[2,2,16,16,256]{4,3,2,1,0:T(8,128)} %get-tuple-element.46), channel_id=1, source_target_pairs={{0,4},{4,8},{8,12},{12,16},{16,20},{20,24},{24,28},{1,5},{5,9},{9,... | collective-permute-start | bytes 3145736 | tf_op jit(solution)/shard_map/ppermute | solution.py:272

commit v15 on v14

--- a/solution.py
+++ b/solution.py
@@ -155,6 +155,14 @@
 
         lax.fori_loop(j, end, body, 0)
         j = end
+
+    if not send:
+        def finish(layer, carry):
+            for c in range(comps):
+                x_ref[c, layer + 1] = x_ref[c, layer + 1] + d_ref[c, layer + 1]
+            return carry
+
+        lax.fori_loop(0, layers, finish, 0, unroll=True)
 
     if send:
         def pack(layer, carry):
@@ -277,8 +285,8 @@
                 since = 0
             run.append((keep, push))
             since += 1
-        iterate, step_dir = run_segment(tuple(run), start_valid, k, False, op_stack, rhs, state)
-        return (iterate + step_dir)[:, 1 : layers + 1]
+        iterate, _ = run_segment(tuple(run), start_valid, k, False, op_stack, rhs, state)
+        return iterate[:, 1 : layers + 1]
 
     forcing = jnp.zeros((2,) + eta.shape, jnp.float32)
     forcing = forcing.at[:, 0].set(-(bed_coef * dir_ext)[None] * bv)

time: 190 us -> 189 us (level)
    reduce_sum x1 -> x0, other arithmetic: 2.14 us -> none  [local(): column = jnp.sum(velocity_ext, axis=1) / layers]
where the time goes in v15:
time: 189 us
  Pallas kernels  102 us (54%)
  waiting for transfers between devices  37.7 us (20%)
  starting transfers between devices  25.4 us (13%)
  other arithmetic  16.8 us (9%)
  local copies, waits for them, and re-layouts  6.07 us (3%)
    pallas_call x4, Pallas kernels, run_segment(): pl.pallas_call(lambda *refs: segment_kernel(steps, start_valid, halo, sen...  102 us
    ppermute x2, waiting for transfers between devices, chebyshev(): high = lax.ppermute(down, 'mx', backward)  14.2 us
    ppermute x2, waiting for transfers between devices, chebyshev(): low = lax.ppermute(up, 'mx', forward)  10.6 us
    unnamed x9, other arithmetic  9.28 us
    ppermute x2, starting transfers between devices, exchange_rows(): lax.ppermute(lax.slice_in_dim(own, rows - k, rows, axis=axis), 'mx', forw...  7.4 us
    ppermute x2, waiting for transfers between devices, exchange_rows(): high = lax.ppermute(lax.slice_in_dim(own, 0, k, axis=axis), 'mx', backward)  7.21 us
    ppermute x2, starting transfers between devices, chebyshev(): low = lax.ppermute(up, 'mx', forward)  5.77 us
    ppermute x2, starting transfers between devices, chebyshev(): high = lax.ppermute(down, 'mx', backward)  4.56 us
  transfers between devices with their start and end apart: 11, of which 8 were waited for; matrix products, arithmetic and copies ran while one was open for 2% of the time, Pallas kernels for 0%

profile of v15, /device:TPU:1, one launch (start us, length us, event | category | flops | bytes accessed | tf_op | source)
XLA Modules:
  0.0 188.5 jit_solution(5990799150626757208)
XLA Ops:
  0.6 2.1 %collective-permute-start.1 = (f32[8,16,128]{2,1,0:T(8,128)}, f32[8,16,128]{2,1,0:T(8,128)S(1)}, u32[]{:S(2)}, u32[]{:S(2)}) collective-permute-start(f32[8,16,128]{2,1,0:T(8,128)} %param.14), channel_id=1, source_target_pairs={{0,1},{1,0},{2,3},{3,2},{4,5},{5,4},{6,7},{7,6},{8,9},{9,8},{10,11... | collective-permute-start | bytes 196616 | tf_op jit(solution)/shard_map/ppermute | solution.py:214
  2.7 1.2 collective-permute-start.2
  3.9 0.9 constant_dynamic-update-slice_fusion.4
  4.8 0.7 constant_dynamic-update-slice_fusion.3
  5.5 0.7 constant_dynamic-update-slice_fusion.2
  6.2 0.7 constant_dynamic-update-slice_fusion.1
  7.0 0.7 constant_dynamic-update-slice_fusion
  7.7 3.5 %collective-permute-done = f32[13,16,128]{2,1,0:T(8,128)S(1)} collective-permute-done((f32[13,16,128]{2,1,0:T(8,128)S(1)}, f32[13,16,128]{2,1,0:T(8,128)S(1)}, u32[]{:S(2)}, u32[]{:S(2)}) %collective-permute-start) | collective-permute-done | bytes 106528 | tf_op jit(solution)/shard_map/ppermute | solution.py:213
  11.3 5.5 %collective-permute-start.3 = (f32[21,16,256]{2,1,0:T(8,128)S(1)}, f32[21,16,256]{2,1,0:T(8,128)S(1)}, u32[]{:S(2)}, u32[]{:S(2)}) collective-permute-start(f32[21,16,256]{2,1,0:T(8,128)S(1)} %pad_maximum_fusion.1), channel_id=1, source_target_pairs={{0,4},{4,8},{8,12},{12,16},{16,20},{20,24},{24,28},{1,5},{5,9},{9,... | collective-permute-start | bytes 1032200 | tf_op jit(solution)/shard_map/ppermute | solution.py:46
  16.8 1.9 %collective-permute-start.4 = (f32[21,16,256]{2,1,0:T(8,128)S(1)}, f32[21,16,256]{2,1,0:T(8,128)S(1)}, u32[]{:S(2)}, u32[]{:S(2)}) collective-permute-start(f32[21,16,256]{2,1,0:T(8,128)S(1)} %pad_maximum_fusion.1), channel_id=1, source_target_pairs={{4,0},{8,4},{12,8},{16,12},{20,16},{24,20},{28,24},{5,1},{9,5},{13... | collective-permute-start | bytes 1032200 | tf_op jit(solution)/shard_map/ppermute | solution.py:47
  18.7 2.2 %collective-permute-done.3 = f32[21,16,256]{2,1,0:T(8,128)S(1)} collective-permute-done((f32[21,16,256]{2,1,0:T(8,128)S(1)}, f32[21,16,256]{2,1,0:T(8,128)S(1)}, u32[]{:S(2)}, u32[]{:S(2)}) %collective-permute-start.3) | collective-permute-done | bytes 344096 | tf_op jit(solution)/shard_map/ppermute | solution.py:46
  21.0 4.4 %collective-permute-done.4 = f32[21,16,256]{2,1,0:T(8,128)S(1)} collective-permute-done((f32[21,16,256]{2,1,0:T(8,128)S(1)}, f32[21,16,256]{2,1,0:T(8,128)S(1)}, u32[]{:S(2)}, u32[]{:S(2)}) %collective-permute-start.4) | collective-permute-done | bytes 344096 | tf_op jit(solution)/shard_map/ppermute | solution.py:47
  25.5 0.3 fusion.17
  25.7 0.2 fusion.18
  25.9 0.2 fusion.19
  26.2 0.1 concatenate.90
  26.3 1.1 bitcast_dynamic-update-slice_fusion.7
  27.4 1.2 bitcast_dynamic-update-slice_fusion.6
  28.6 1.4 multiply_add_fusion
  30.1 1.2 bitcast_dynamic-update-slice_fusion.5
  31.3 1.2 bitcast_dynamic-update-slice_fusion.4
  32.5 1.0 bitcast_dynamic-update-slice_fusion.3
  33.5 1.0 bitcast_dynamic-update-slice_fusion.2
  34.5 0.2 pad_multiply_fusion
  34.7 1.3 copy.13.refs_2_
  36.0 1.2 bitcast_dynamic-update-slice_fusion.1
  37.1 1.2 bitcast_dynamic-update-slice_fusion.refs_1_
  38.3 24.3 %shard_map.113 = (f32[2,18,48,256]{3,2,1,0:T(8,128)}, f32[2,18,48,256]{3,2,1,0:T(8,128)}, f32[2,2,16,16,256]{4,3,2,1,0:T(8,128)}, f32[2,2,16,16,256]{4,3,2,1,0:T(8,128)}) custom-call(f32[2,15]{1,0:T(2,128)} %constant.99.clone.refs_0_, f32[8,16,48,256]{3,2,1,0:T(8,128)} %bitcast_dynamic-update-slice_fusion.refs_1_, f32[2,16,48,256]{3,2,1,0:T(8,128)} %copy.13.refs_2_), custom_call_target="tpu_custom_call" | custom-call | flops 117964800 | bytes 14155776 | tf_op jit(solution)/shard_map/pallas_call | solution.py:190
  62.6 1.9 %collective-permute-start.5 = (f32[2,2,16,16,256]{4,3,2,1,0:T(8,128)}, f32[2,2,16,16,256]{4,3,2,1,0:T(8,128)S(1)}, u32[]{:S(2)}, u32[]{:S(2)}) collective-permute-start(f32[2,2,16,16,256]{4,3,2,1,0:T(8,128)} %get-tuple-element.38), channel_id=1, source_target_pairs={{0,4},{4,8},{8,12},{12,16},{16,20},{20,24},{24,28},{1,5},{5,9},{9,... | collective-permute-start | bytes 3145736 | tf_op jit(solution)/shard_map/ppermute | solution.py:280
  64.6 2.6 %collective-permute-start.6 = (f32[2,2,16,16,256]{4,3,2,1,0:T(8,128)}, f32[2,2,16,16,256]{4,3,2,1,0:T(8,128)S(1)}, u32[]{:S(2)}, u32[]{:S(2)}) collective-permute-start(f32[2,2,16,16,256]{4,3,2,1,0:T(8,128)} %get-tuple-element.39), channel_id=1, source_target_pairs={{4,0},{8,4},{12,8},{16,12},{20,16},{24,20},{28,24},{5,1},{9,5},{13... | collective-permute-start | bytes 3145736 | tf_op jit(solution)/shard_map/ppermute | solution.py:281
  67.2 9.4 %collective-permute-done.5.refs_5_ = f32[2,2,16,16,256]{4,3,2,1,0:T(8,128)S(1)} collective-permute-done((f32[2,2,16,16,256]{4,3,2,1,0:T(8,128)}, f32[2,2,16,16,256]{4,3,2,1,0:T(8,128)S(1)}, u32[]{:S(2)}, u32[]{:S(2)}) %collective-permute-start.5) | collective-permute-done | bytes 1048608 | tf_op jit(solution)/shard_map/ppermute | solution.py:280
  76.6 4.3 %collective-permute-done.6.refs_6_ = f32[2,2,16,16,256]{4,3,2,1,0:T(8,128)S(1)} collective-permute-done((f32[2,2,16,16,256]{4,3,2,1,0:T(8,128)}, f32[2,2,16,16,256]{4,3,2,1,0:T(8,128)S(1)}, u32[]{:S(2)}, u32[]{:S(2)}) %collective-permute-start.6) | collective-permute-done | bytes 1048608 | tf_op jit(solution)/shard_map/ppermute | solution.py:281
  80.9 1.0 copy-done.1
  81.9 26.5 %shard_map.114 = (f32[2,18,48,256]{3,2,1,0:T(8,128)}, f32[2,18,48,256]{3,2,1,0:T(8,128)}) custom-call(f32[2,16]{1,0:T(2,128)} %constant.100.clone.refs_0_, f32[8,16,48,256]{3,2,1,0:T(8,128)} %bitcast_dynamic-update-slice_fusion.refs_1_, f32[2,16,48,256]{3,2,1,0:T(8,128)} %copy.13.refs_2_, f32[2,18,48,256]{3,2,1,0:T(8,128)} %get-tuple-element.36.refs_3_, ...), custom_call_target="tpu_custom_call" | custom-call | flops 125829120 | bytes 14155776 | tf_op jit(solution)/shard_map/pallas_call | solution.py:190
  108.4 1.6 fusion.16
  109.9 1.9 %collective-permute-start.7 = (f32[2,16,256]{2,1,0:T(8,128)S(1)}, f32[2,16,256]{2,1,0:T(8,128)S(1)}, u32[]{:S(2)}, u32[]{:S(2)}) collective-permute-start(f32[2,16,256]{2,1,0:T(8,128)S(1)} %slice_multiply_fusion), channel_id=1, source_target_pairs={{0,4},{4,8},{8,12},{12,16},{16,20},{20,24},{24,28},{1,5},{5,9},{9,... | collective-permute-start | bytes 98312 | tf_op jit(solution)/shard_map/ppermute | solution.py:46
  111.9 2.4 %collective-permute-start.8 = (f32[2,16,256]{2,1,0:T(8,128)S(1)}, f32[2,16,256]{2,1,0:T(8,128)S(1)}, u32[]{:S(2)}, u32[]{:S(2)}) collective-permute-start(f32[2,16,256]{2,1,0:T(8,128)S(1)} %slice_multiply_fusion), channel_id=1, source_target_pairs={{4,0},{8,4},{12,8},{16,12},{20,16},{24,20},{28,24},{5,1},{9,5},{13... | collective-permute-start | bytes 98312 | tf_op jit(solution)/shard_map/ppermute | solution.py:47
  114.3 2.8 %collective-permute-done.8 = f32[2,16,256]{2,1,0:T(8,128)S(1)} collective-permute-done((f32[2,16,256]{2,1,0:T(8,128)S(1)}, f32[2,16,256]{2,1,0:T(8,128)S(1)}, u32[]{:S(2)}, u32[]{:S(2)}) %collective-permute-start.8) | collective-permute-done | bytes 32800 | tf_op jit(solution)/shard_map/ppermute | solution.py:47
  117.1 1.3 broadcast_multiply_fusion.refs_2_
  118.5 24.3 %shard_map.115 = (f32[2,18,48,256]{3,2,1,0:T(8,128)}, f32[2,18,48,256]{3,2,1,0:T(8,128)}, f32[2,2,16,16,256]{4,3,2,1,0:T(8,128)}, f32[2,2,16,16,256]{4,3,2,1,0:T(8,128)}) custom-call(f32[2,15]{1,0:T(2,128)} %constant.99.clone.refs_0_, f32[8,16,48,256]{3,2,1,0:T(8,128)} %bitcast_dynamic-update-slice_fusion.refs_1_, ...), custom_call_target="tpu_custom_call" | custom-call | flops 117964800 | bytes 14155776 | tf_op jit(solution)/shard_map/pallas_call | solution.py:190
  142.8 1.9 %collective-permute-start.10 = (f32[2,2,16,16,256]{4,3,2,1,0:T(8,128)}, f32[2,2,16,16,256]{4,3,2,1,0:T(8,128)}, u32[]{:S(2)}, u32[]{:S(2)}) collective-permute-start(f32[2,2,16,16,256]{4,3,2,1,0:T(8,128)} %get-tuple-element.44), channel_id=1, source_target_pairs={{4,0},{8,4},{12,8},{16,12},{20,16},{24,20},{28,24},{5,1},{9,5},{13... | collective-permute-start | bytes 3145736 | tf_op jit(solution)/shard_map/ppermute | solution.py:281
  144.7 3.9 %collective-permute-start.9 = (f32[2,2,16,16,256]{4,3,2,1,0:T(8,128)}, f32[2,2,16,16,256]{4,3,2,1,0:T(8,128)}, u32[]{:S(2)}, u32[]{:S(2)}) collective-permute-start(f32[2,2,16,16,256]{4,3,2,1,0:T(8,128)} %get-tuple-element.43), channel_id=1, source_target_pairs={{0,4},{4,8},{8,12},{12,16},{16,20},{20,24},{24,28},{1,5},{5,9},{9,... | collective-permute-start | bytes 3145736 | tf_op jit(solution)/shard_map/ppermute | solution.py:280
  148.7 0.7 constant_dynamic-slice_fusion
  149.3 9.9 %collective-permute-done.10.refs_6_ = f32[2,2,16,16,256]{4,3,2,1,0:T(8,128)} collective-permute-done((f32[2,2,16,16,256]{4,3,2,1,0:T(8,128)}, f32[2,2,16,16,256]{4,3,2,1,0:T(8,128)}, u32[]{:S(2)}, u32[]{:S(2)}) %collective-permute-start.10) | collective-permute-done | bytes 1048608 | tf_op jit(solution)/shard_map/ppermute | solution.py:281
  159.2 1.2 collective-permute-done.9.refs_5_
  160.4 26.5 %shard_map.116 = (f32[2,18,48,256]{3,2,1,0:T(8,128)}, f32[2,18,48,256]{3,2,1,0:T(8,128)}) custom-call(f32[2,16]{1,0:T(2,128)} %constant.100.clone.refs_0_, f32[8,16,48,256]{3,2,1,0:T(8,128)} %bitcast_dynamic-update-slice_fusion.refs_1_, f32[2,16,48,256]{3,2,1,0:T(8,128)} %broadcast_multiply_fusion.refs_2_, f32[2,18,48,256]{3,2,1,0:T(8,128)} %get-tuple-element.41.refs_3_, ...), custom_call_target="tpu_custom_call" | custom-call | flops 125829120 | bytes 14155776 | tf_op jit(solution)/shard_map/pallas_call | solution.py:190
  186.9 0.9 fusion.7
  187.8 0.7 fusion.14
  (28 shorter events, 0.5 us)
Async XLA Ops:
  0.6 7.1 %collective-permute-start.1 = (f32[8,16,128]{2,1,0:T(8,128)}, f32[8,16,128]{2,1,0:T(8,128)S(1)}, u32[]{:S(2)}, u32[]{:S(2)}) collective-permute-start(f32[8,16,128]{2,1,0:T(8,128)} %param.14), channel_id=1, source_target_pairs={{0,1},{1,0},{2,3},{3,2},{4,5},{5,4},{6,7},{7,6},{8,9},{9,8},{10,11... | collective-permute-start | bytes 196616 | tf_op jit(solution)/shard_map/ppermute | solution.py:214
  2.7 5.0 %collective-permute-start.2 = (f32[8,16,128]{2,1,0:T(8,128)}, f32[8,16,128]{2,1,0:T(8,128)S(1)}, u32[]{:S(2)}, u32[]{:S(2)}) collective-permute-start(f32[8,16,128]{2,1,0:T(8,128)} %param.14), channel_id=1, source_target_pairs={{0,3},{1,2},{2,1},{3,0},{4,7},{5,6},{6,5},{7,4},{8,11},{9,10},{10,... | collective-permute-start | bytes 196616 | tf_op jit(solution)/shard_map/ppermute | solution.py:215
  7.7 3.6 %collective-permute-start = (f32[13,16,128]{2,1,0:T(8,128)S(1)}, f32[13,16,128]{2,1,0:T(8,128)S(1)}, u32[]{:S(2)}, u32[]{:S(2)}) collective-permute-start(f32[13,16,128]{2,1,0:T(8,128)S(1)} %constant_dynamic-update-slice_fusion), channel_id=1, source_target_pairs={{0,2},{2,0},{1,3},{3,1},{4,6},{6,4},{5,7},{7,5},{8,10},{10,8},{9,1... | collective-permute-start | bytes 319496 | tf_op jit(solution)/shard_map/ppermute | solution.py:213
  11.3 9.7 %collective-permute-start.3 = (f32[21,16,256]{2,1,0:T(8,128)S(1)}, f32[21,16,256]{2,1,0:T(8,128)S(1)}, u32[]{:S(2)}, u32[]{:S(2)}) collective-permute-start(f32[21,16,256]{2,1,0:T(8,128)S(1)} %pad_maximum_fusion.1), channel_id=1, source_target_pairs={{0,4},{4,8},{8,12},{12,16},{16,20},{20,24},{24,28},{1,5},{5,9},{9,... | collective-permute-start | bytes 1032200 | tf_op jit(solution)/shard_map/ppermute | solution.py:46
  16.8 8.6 %collective-permute-start.4 = (f32[21,16,256]{2,1,0:T(8,128)S(1)}, f32[21,16,256]{2,1,0:T(8,128)S(1)}, u32[]{:S(2)}, u32[]{:S(2)}) collective-permute-start(f32[21,16,256]{2,1,0:T(8,128)S(1)} %pad_maximum_fusion.1), channel_id=1, source_target_pairs={{4,0},{8,4},{12,8},{16,12},{20,16},{24,20},{28,24},{5,1},{9,5},{13... | collective-permute-start | bytes 1032200 | tf_op jit(solution)/shard_map/ppermute | solution.py:47
  62.6 14.0 %collective-permute-start.5 = (f32[2,2,16,16,256]{4,3,2,1,0:T(8,128)}, f32[2,2,16,16,256]{4,3,2,1,0:T(8,128)S(1)}, u32[]{:S(2)}, u32[]{:S(2)}) collective-permute-start(f32[2,2,16,16,256]{4,3,2,1,0:T(8,128)} %get-tuple-element.38), channel_id=1, source_target_pairs={{0,4},{4,8},{8,12},{12,16},{16,20},{20,24},{24,28},{1,5},{5,9},{9,... | collective-permute-start | bytes 3145736 | tf_op jit(solution)/shard_map/ppermute | solution.py:280
  64.6 16.3 %collective-permute-start.6 = (f32[2,2,16,16,256]{4,3,2,1,0:T(8,128)}, f32[2,2,16,16,256]{4,3,2,1,0:T(8,128)S(1)}, u32[]{:S(2)}, u32[]{:S(2)}) collective-permute-start(f32[2,2,16,16,256]{4,3,2,1,0:T(8,128)} %get-tuple-element.39), channel_id=1, source_target_pairs={{4,0},{8,4},{12,8},{16,12},{20,16},{24,20},{28,24},{5,1},{9,5},{13... | collective-permute-start | bytes 3145736 | tf_op jit(solution)/shard_map/ppermute | solution.py:281
  76.6 4.3 %copy-start = (f32[2,2,16,16,256]{4,3,2,1,0:T(8,128)}, f32[2,2,16,16,256]{4,3,2,1,0:T(8,128)S(1)}, u32[]{:S(2)}) copy-start(f32[2,2,16,16,256]{4,3,2,1,0:T(8,128)S(1)} %collective-permute-done.5.refs_5_) | copy-start | bytes 3145732
  80.9 1.0 copy-start.1
  109.9 4.3 %collective-permute-start.7 = (f32[2,16,256]{2,1,0:T(8,128)S(1)}, f32[2,16,256]{2,1,0:T(8,128)S(1)}, u32[]{:S(2)}, u32[]{:S(2)}) collective-permute-start(f32[2,16,256]{2,1,0:T(8,128)S(1)} %slice_multiply_fusion), channel_id=1, source_target_pairs={{0,4},{4,8},{8,12},{12,16},{16,20},{20,24},{24,28},{1,5},{5,9},{9,... | collective-permute-start | bytes 98312 | tf_op jit(solution)/shard_map/ppermute | solution.py:46
  111.9 5.2 %collective-permute-start.8 = (f32[2,16,256]{2,1,0:T(8,128)S(1)}, f32[2,16,256]{2,1,0:T(8,128)S(1)}, u32[]{:S(2)}, u32[]{:S(2)}) collective-permute-start(f32[2,16,256]{2,1,0:T(8,128)S(1)} %slice_multiply_fusion), channel_id=1, source_target_pairs={{4,0},{8,4},{12,8},{16,12},{20,16},{24,20},{28,24},{5,1},{9,5},{13... | collective-permute-start | bytes 98312 | tf_op jit(solution)/shard_map/ppermute | solution.py:47
  142.8 16.4 %collective-permute-start.10 = (f32[2,2,16,16,256]{4,3,2,1,0:T(8,128)}, f32[2,2,16,16,256]{4,3,2,1,0:T(8,128)}, u32[]{:S(2)}, u32[]{:S(2)}) collective-permute-start(f32[2,2,16,16,256]{4,3,2,1,0:T(8,128)} %get-tuple-element.44), channel_id=1, source_target_pairs={{4,0},{8,4},{12,8},{16,12},{20,16},{24,20},{28,24},{5,1},{9,5},{13... | collective-permute-start | bytes 3145736 | tf_op jit(solution)/shard_map/ppermute | solution.py:281
  144.7 15.7 %collective-permute-start.9 = (f32[2,2,16,16,256]{4,3,2,1,0:T(8,128)}, f32[2,2,16,16,256]{4,3,2,1,0:T(8,128)}, u32[]{:S(2)}, u32[]{:S(2)}) collective-permute-start(f32[2,2,16,16,256]{4,3,2,1,0:T(8,128)} %get-tuple-element.43), channel_id=1, source_target_pairs={{0,4},{4,8},{8,12},{12,16},{16,20},{20,24},{24,28},{1,5},{5,9},{9,... | collective-permute-start | bytes 3145736 | tf_op jit(solution)/shard_map/ppermute | solution.py:280

commit v16 on v15

--- a/solution.py
+++ b/solution.py
@@ -70,7 +70,8 @@
     return jnp.concatenate([z, lax.slice_in_dim(a, 0, n - 1, axis=axis)], axis=axis)
 
 
-def segment_kernel(steps, start_valid, halo, send, table_ref, op_ref, rhs_ref, *refs):
+def segment_kernel(steps, start_valid, halo, send, planes, table_ref, *refs):
+    op_ref, rhs_ref, refs = refs[:planes], refs[planes], refs[planes + 1 :]
     comps, layers = rhs_ref.shape[0], rhs_ref.shape[1]
     rows, cols = rhs_ref.shape[2], rhs_ref.shape[3]
     own = rows - 2 * halo
@@ -101,7 +102,7 @@
         def start(layer, carry):
             for c in range(comps):
                 x_ref[c, layer + 1] = zero
-                d_ref[c, layer + 1] = op_ref[5, layer] * rhs_ref[c, layer] / theta_center
+                d_ref[c, layer + 1] = op_ref[5][layer] * rhs_ref[c, layer] / theta_center
             return carry
 
         lax.fori_loop(0, layers, start, 0, unroll=True)
@@ -114,24 +115,24 @@
 
         def update(layer, carry):
             p = layer + 1
-            c_xm = op_ref[2, layer, span]
-            c_ym = op_ref[3, layer, span]
-            c_xp = op_ref[6, layer, span]
-            c_yp = op_ref[7, layer, span]
+            c_xm = op_ref[2][layer, span]
+            c_ym = op_ref[3][layer, span]
+            c_xp = op_ref[6][layer, span]
+            c_yp = op_ref[7][layer, span]
             for c in range(comps):
                 above = x_ref[c, p + 1, span] + d_ref[c, p + 1, span]
                 x_ref[c, p + 1, span] = above
                 centre = x_ref[c, p, span]
-                beside = op_ref[0, layer, span] * x_ref[c, p - 1, span] + op_ref[1, layer, span] * above
+                beside = op_ref[0][layer, span] * x_ref[c, p - 1, span] + op_ref[1][layer, span] * above
                 beside = beside + c_xm * pltpu.roll(centre, 1, 0)
                 beside = beside + c_xp * pltpu.roll(centre, height - 1, 0)
                 beside = beside + c_ym * pltpu.roll(centre, 1, 1)
                 beside = beside + c_yp * pltpu.roll(centre, cols - 1, 1)
-                resid = rhs_ref[c, layer, span] - (op_ref[4, layer, span] * centre - beside)
+                resid = rhs_ref[c, layer, span] - (op_ref[4][layer, span] * centre - beside)
                 if keep is None:
-                    d_ref[c, p, span] = op_ref[5, layer, span] * resid / theta_center
+                    d_ref[c, p, span] = op_ref[5][layer, span] * resid / theta_center
                 else:
-                    d_ref[c, p, span] = keep * d_ref[c, p, span] + push * (op_ref[5, layer, span] * resid)
+                    d_ref[c, p, span] = keep * d_ref[c, p, span] + push * (op_ref[5][layer, span] * resid)
             return carry
 
         lax.fori_loop(0, layers, update, 0, unroll=True)
@@ -188,14 +189,14 @@
     slab_shape = jax.ShapeDtypeStruct((2, comps, layers, halo, cols), jnp.float32)
     out_shape = (padded_shape, padded_shape) + ((slab_shape, slab_shape) if send else ())
     return pl.pallas_call(
-        lambda *refs: segment_kernel(steps, start_valid, halo, send, *refs),
+        lambda *refs: segment_kernel(steps, start_valid, halo, send, len(op_stack), *refs),
         out_shape=out_shape,
-        in_specs=[smem] + [vmem] * (2 + len(state)),
+        in_specs=[smem] + [vmem] * (len(op_stack) + 1 + len(state)),
         out_specs=tuple(vmem for _ in out_shape),
         cost_estimate=pl.CostEstimate(
             flops=20 * cells * len(steps), bytes_accessed=4 * cells * 9, transcendentals=0
         ),
-    )(table, op_stack, rhs, *state)
+    )(table, *op_stack, rhs, *state)
 
 
 def local(viscosity, friction, base_velocity, grounded, ice_free, direction):
@@ -250,7 +251,7 @@
     jacobi = 1.0 / (act * diag + 1.0 - act)
 
     on = act > 0
-    op_stack = jnp.stack(
+    op_stack = tuple(
         [
             act * c_zm,
             act * c_zp,

time: 189 us -> 187 us (0.989)
  other arithmetic: 16.8 us -> 11.8 us
  starting transfers between devices: 25.4 us -> 29.2 us
    ppermute x2, waiting for transfers between devices: 10.6 us -> 19.1 us  [chebyshev(): low = lax.ppermute(up, 'mx', forward)]
    unnamed x9 -> x2, other arithmetic: 9.28 us -> 1.42 us
    ppermute x2, waiting for transfers between devices: 14.2 us -> 8.68 us  [chebyshev(): high = lax.ppermute(down, 'mx', backward)]
    ppermute x2, waiting for transfers between devices: 7.21 us -> 2.99 us  [exchange_rows(): high = lax.ppermute(lax.slice_in_dim(own, 0, k, axis=axis), 'mx', backward)]
    mul x0 -> x1, other arithmetic: none -> 3.06 us  [local(): act * c_yp * shift(act, 1, 1)]
    ppermute x2, starting transfers between devices: 5.77 us -> 8.59 us  [chebyshev(): low = lax.ppermute(up, 'mx', forward)]
    div x0 -> x1, other arithmetic: none -> 2.37 us  [local(): jacobi = 1.0 / (act * diag + 1.0 - act)]
where the time goes in v16:
time: 187 us; the launch traced here: 186 us
  Pallas kernels  102 us (55%)
  waiting for transfers between devices  36.3 us (19%)
  starting transfers between devices  29.2 us (16%)
  other arithmetic  11.8 us (6%)
  local copies, waits for them, and re-layouts  6.18 us (3%)
    pallas_call x4, Pallas kernels, run_segment(): pl.pallas_call(lambda *refs: segment_kernel(steps, start_valid, halo, sen...  102 us
    ppermute x2, waiting for transfers between devices, chebyshev(): low = lax.ppermute(up, 'mx', forward)  19.1 us
    ppermute x2, waiting for transfers between devices, chebyshev(): high = lax.ppermute(down, 'mx', backward)  8.68 us
    ppermute x2, starting transfers between devices, chebyshev(): low = lax.ppermute(up, 'mx', forward)  8.59 us
    ppermute x2, starting transfers between devices, exchange_rows(): lax.ppermute(lax.slice_in_dim(own, rows - k, rows, axis=axis), 'mx', forw...  6.74 us
    ppermute x2, starting transfers between devices, exchange_rows(): high = lax.ppermute(lax.slice_in_dim(own, 0, k, axis=axis), 'mx', backward)  6.21 us
    ppermute x2, starting transfers between devices, chebyshev(): high = lax.ppermute(down, 'mx', backward)  4.24 us
  transfers between devices with their start and end apart: 11, of which 8 were waited for; matrix products, arithmetic and copies ran while one was open for 2% of the time, Pallas kernels for 0%

profile of v16, /device:TPU:1, one launch (start us, length us, event | category | flops | bytes accessed | tf_op | source)
XLA Modules:
  0.0 186.5 jit_solution(8994326120090156597)
XLA Ops:
  0.6 3.1 %collective-permute-start.2 = (f32[8,16,128]{2,1,0:T(8,128)}, f32[8,16,128]{2,1,0:T(8,128)S(1)}, u32[]{:S(2)}, u32[]{:S(2)}) collective-permute-start(f32[8,16,128]{2,1,0:T(8,128)} %param.14), channel_id=1, source_target_pairs={{0,3},{1,2},{2,1},{3,0},{4,7},{5,6},{6,5},{7,4},{8,11},{9,10},{10,... | collective-permute-start | bytes 196616 | tf_op jit(solution)/shard_map/ppermute | solution.py:216
  3.7 0.3 collective-permute-start.1
  3.9 0.9 constant_dynamic-update-slice_fusion.4
  4.8 0.7 constant_dynamic-update-slice_fusion.3
  5.5 0.7 constant_dynamic-update-slice_fusion.2
  6.2 0.7 constant_dynamic-update-slice_fusion.1
  7.0 0.7 constant_dynamic-update-slice_fusion
  7.7 0.1 collective-permute-start
  7.8 0.0 collective-permute-done.2
  7.8 0.0 collective-permute-done.1
  7.8 3.4 %collective-permute-done = f32[13,16,128]{2,1,0:T(8,128)S(1)} collective-permute-done((f32[13,16,128]{2,1,0:T(8,128)S(1)}, f32[13,16,128]{2,1,0:T(8,128)S(1)}, u32[]{:S(2)}, u32[]{:S(2)}) %collective-permute-start) | collective-permute-done | bytes 106528 | tf_op jit(solution)/shard_map/ppermute | solution.py:214
  11.3 4.3 %collective-permute-start.4 = (f32[21,16,256]{2,1,0:T(8,128)S(1)}, f32[21,16,256]{2,1,0:T(8,128)S(1)}, u32[]{:S(2)}, u32[]{:S(2)}) collective-permute-start(f32[21,16,256]{2,1,0:T(8,128)S(1)} %pad_maximum_fusion.1), channel_id=1, source_target_pairs={{4,0},{8,4},{12,8},{16,12},{20,16},{24,20},{28,24},{5,1},{9,5},{13... | collective-permute-start | bytes 1032200 | tf_op jit(solution)/shard_map/ppermute | solution.py:47
  15.6 3.1 %collective-permute-start.3 = (f32[21,16,256]{2,1,0:T(8,128)S(1)}, f32[21,16,256]{2,1,0:T(8,128)S(1)}, u32[]{:S(2)}, u32[]{:S(2)}) collective-permute-start(f32[21,16,256]{2,1,0:T(8,128)S(1)} %pad_maximum_fusion.1), channel_id=1, source_target_pairs={{0,4},{4,8},{8,12},{12,16},{16,20},{20,24},{24,28},{1,5},{5,9},{9,... | collective-permute-start | bytes 1032200 | tf_op jit(solution)/shard_map/ppermute | solution.py:46
  18.7 3.0 %collective-permute-done.4 = f32[21,16,256]{2,1,0:T(8,128)S(1)} collective-permute-done((f32[21,16,256]{2,1,0:T(8,128)S(1)}, f32[21,16,256]{2,1,0:T(8,128)S(1)}, u32[]{:S(2)}, u32[]{:S(2)}) %collective-permute-start.4) | collective-permute-done | bytes 344096 | tf_op jit(solution)/shard_map/ppermute | solution.py:47
  21.7 1.2 collective-permute-done.3
  23.0 0.1 fusion.20
  23.0 0.1 pad_maximum_fusion
  23.1 0.2 fusion.19
  23.3 0.1 fusion.18
  23.4 0.3 fusion.17
  23.8 0.1 concatenate.90
  23.9 0.2 pad_multiply_fusion
  24.1 1.4 copy.13.refs_9_
  25.5 3.1 %multiply_multiply_fusion = (f32[16,48,256]{2,1,0:T(8,128)}, f32[16,48,256]{2,1,0:T(8,128)S(1)}, f32[16,48,256]{2,1,0:T(8,128)}, f32[16,48,256]{2,1,0:T(8,128)}) fusion(f32[48,256]{1,0:T(8,128)S(1)} %concatenate.94, f32[48,256]{1,0:T(8,128)S(1)} %get-tuple-element.49, f32[16,48,255]{2,1,0:T(8,128)S(1)} %get-tuple-element.64, ...), kind=kLoop, calls=%fused_computation.21 | loop fusion | flops 10027008 | bytes 8710144 | tf_op jit(solution)/shard_map/mul | solution.py:263
  28.5 2.4 %subtract_divide_fusion = (f32[16,48,256]{2,1,0:T(8,128)}, f32[16,48,256]{2,1,0:T(8,128)}, f32[16,48,256]{2,1,0:T(8,128)}, f32[16,48,256]{2,1,0:T(8,128)}, f32[16,48,256]{2,1,0:T(8,128)}) fusion(f32[16,48,256]{2,1,0:T(8,128)S(1)} %fusion.8, f32[48,256]{1,0:T(8,128)S(1)} %get-tuple-element.49, pred[48,256]{1,0:T(8,128)(4,1)S(1)} %broadcast_compare_fusion, ...), kind=kLoop, calls=%fused_computation.23 | loop fusion | flops 5505024 | bytes 7909376 | tf_op jit(solution)/shard_map/div | solution.py:251
  30.9 24.4 %shard_map.113 = (f32[2,18,48,256]{3,2,1,0:T(8,128)}, f32[2,18,48,256]{3,2,1,0:T(8,128)}, f32[2,2,16,16,256]{4,3,2,1,0:T(8,128)}, f32[2,2,16,16,256]{4,3,2,1,0:T(8,128)}) custom-call(f32[2,15]{1,0:T(2,128)} %constant.99.clone.refs_0_, f32[16,48,256]{2,1,0:T(8,128)} %get-tuple-element.80.refs_1_, f32[16,48,256]{2,1,0:T(8,128)} %get-tuple-element.81.refs_2_, ...), custom_call_target="tpu_custom_call" | custom-call | flops 117964800 | bytes 14155776 | tf_op jit(solution)/shard_map/pallas_call | solution.py:191
  55.3 4.4 %collective-permute-start.5 = (f32[2,2,16,16,256]{4,3,2,1,0:T(8,128)}, f32[2,2,16,16,256]{4,3,2,1,0:T(8,128)S(1)}, u32[]{:S(2)}, u32[]{:S(2)}) collective-permute-start(f32[2,2,16,16,256]{4,3,2,1,0:T(8,128)} %get-tuple-element.38), channel_id=1, source_target_pairs={{0,4},{4,8},{8,12},{12,16},{16,20},{20,24},{24,28},{1,5},{5,9},{9,... | collective-permute-start | bytes 3145736 | tf_op jit(solution)/shard_map/ppermute | solution.py:281
  59.7 2.1 %collective-permute-start.6 = (f32[2,2,16,16,256]{4,3,2,1,0:T(8,128)}, f32[2,2,16,16,256]{4,3,2,1,0:T(8,128)S(1)}, u32[]{:S(2)}, u32[]{:S(2)}) collective-permute-start(f32[2,2,16,16,256]{4,3,2,1,0:T(8,128)} %get-tuple-element.39), channel_id=1, source_target_pairs={{4,0},{8,4},{12,8},{16,12},{20,16},{24,20},{28,24},{5,1},{9,5},{13... | collective-permute-start | bytes 3145736 | tf_op jit(solution)/shard_map/ppermute | solution.py:282
  61.8 9.9 %collective-permute-done.5.refs_12_ = f32[2,2,16,16,256]{4,3,2,1,0:T(8,128)S(1)} collective-permute-done((f32[2,2,16,16,256]{4,3,2,1,0:T(8,128)}, f32[2,2,16,16,256]{4,3,2,1,0:T(8,128)S(1)}, u32[]{:S(2)}, u32[]{:S(2)}) %collective-permute-start.5) | collective-permute-done | bytes 1048608 | tf_op jit(solution)/shard_map/ppermute | solution.py:281
  71.8 4.3 %collective-permute-done.6.refs_13_ = f32[2,2,16,16,256]{4,3,2,1,0:T(8,128)S(1)} collective-permute-done((f32[2,2,16,16,256]{4,3,2,1,0:T(8,128)}, f32[2,2,16,16,256]{4,3,2,1,0:T(8,128)S(1)}, u32[]{:S(2)}, u32[]{:S(2)}) %collective-permute-start.6) | collective-permute-done | bytes 1048608 | tf_op jit(solution)/shard_map/ppermute | solution.py:282
  76.1 1.0 copy-done.1
  77.1 26.6 %shard_map.114 = (f32[2,18,48,256]{3,2,1,0:T(8,128)}, f32[2,18,48,256]{3,2,1,0:T(8,128)}) custom-call(f32[2,16]{1,0:T(2,128)} %constant.100.clone.refs_0_, f32[16,48,256]{2,1,0:T(8,128)} %get-tuple-element.80.refs_1_, f32[16,48,256]{2,1,0:T(8,128)} %get-tuple-element.81.refs_2_, f32[16,48,256]{2,1,0:T(8,128)} %get-tuple-element.79.refs_3_, ...), custom_call_target="tpu_custom_call" | custom-call | flops 125829120 | bytes 14155776 | tf_op jit(solution)/shard_map/pallas_call | solution.py:191
  103.6 1.6 fusion.16
  105.2 1.9 %collective-permute-start.8 = (f32[2,16,256]{2,1,0:T(8,128)S(1)}, f32[2,16,256]{2,1,0:T(8,128)S(1)}, u32[]{:S(2)}, u32[]{:S(2)}) collective-permute-start(f32[2,16,256]{2,1,0:T(8,128)S(1)} %slice_multiply_fusion), channel_id=1, source_target_pairs={{4,0},{8,4},{12,8},{16,12},{20,16},{24,20},{28,24},{5,1},{9,5},{13... | collective-permute-start | bytes 98312 | tf_op jit(solution)/shard_map/ppermute | solution.py:47
  107.1 3.6 %collective-permute-start.7 = (f32[2,16,256]{2,1,0:T(8,128)S(1)}, f32[2,16,256]{2,1,0:T(8,128)S(1)}, u32[]{:S(2)}, u32[]{:S(2)}) collective-permute-start(f32[2,16,256]{2,1,0:T(8,128)S(1)} %slice_multiply_fusion), channel_id=1, source_target_pairs={{0,4},{4,8},{8,12},{12,16},{16,20},{20,24},{24,28},{1,5},{5,9},{9,... | collective-permute-start | bytes 98312 | tf_op jit(solution)/shard_map/ppermute | solution.py:46
  110.8 0.0 collective-permute-done.8
  110.8 1.0 collective-permute-done.7
  111.8 1.4 broadcast_multiply_fusion.refs_9_
  113.2 24.4 %shard_map.115 = (f32[2,18,48,256]{3,2,1,0:T(8,128)}, f32[2,18,48,256]{3,2,1,0:T(8,128)}, f32[2,2,16,16,256]{4,3,2,1,0:T(8,128)}, f32[2,2,16,16,256]{4,3,2,1,0:T(8,128)}) custom-call(f32[2,15]{1,0:T(2,128)} %constant.99.clone.refs_0_, f32[16,48,256]{2,1,0:T(8,128)} %get-tuple-element.80.refs_1_, f32[16,48,256]{2,1,0:T(8,128)} %get-tuple-element.81.refs_2_, ...), custom_call_target="tpu_custom_call" | custom-call | flops 117964800 | bytes 14155776 | tf_op jit(solution)/shard_map/pallas_call | solution.py:191
  137.6 4.2 %collective-permute-start.9 = (f32[2,2,16,16,256]{4,3,2,1,0:T(8,128)}, f32[2,2,16,16,256]{4,3,2,1,0:T(8,128)}, u32[]{:S(2)}, u32[]{:S(2)}) collective-permute-start(f32[2,2,16,16,256]{4,3,2,1,0:T(8,128)} %get-tuple-element.43), channel_id=1, source_target_pairs={{0,4},{4,8},{8,12},{12,16},{16,20},{20,24},{24,28},{1,5},{5,9},{9,... | collective-permute-start | bytes 3145736 | tf_op jit(solution)/shard_map/ppermute | solution.py:281
  141.9 2.1 %collective-permute-start.10 = (f32[2,2,16,16,256]{4,3,2,1,0:T(8,128)}, f32[2,2,16,16,256]{4,3,2,1,0:T(8,128)}, u32[]{:S(2)}, u32[]{:S(2)}) collective-permute-start(f32[2,2,16,16,256]{4,3,2,1,0:T(8,128)} %get-tuple-element.44), channel_id=1, source_target_pairs={{4,0},{8,4},{12,8},{16,12},{20,16},{24,20},{28,24},{5,1},{9,5},{13... | collective-permute-start | bytes 3145736 | tf_op jit(solution)/shard_map/ppermute | solution.py:282
  144.0 0.1 fusion.21
  144.1 0.7 constant_dynamic-slice_fusion
  144.8 9.1 %collective-permute-done.9.refs_12_ = f32[2,2,16,16,256]{4,3,2,1,0:T(8,128)} collective-permute-done((f32[2,2,16,16,256]{4,3,2,1,0:T(8,128)}, f32[2,2,16,16,256]{4,3,2,1,0:T(8,128)}, u32[]{:S(2)}, u32[]{:S(2)}) %collective-permute-start.9) | collective-permute-done | bytes 1048608 | tf_op jit(solution)/shard_map/ppermute | solution.py:281
  153.9 4.4 %collective-permute-done.10.refs_13_ = f32[2,2,16,16,256]{4,3,2,1,0:T(8,128)} collective-permute-done((f32[2,2,16,16,256]{4,3,2,1,0:T(8,128)}, f32[2,2,16,16,256]{4,3,2,1,0:T(8,128)}, u32[]{:S(2)}, u32[]{:S(2)}) %collective-permute-start.10) | collective-permute-done | bytes 1048608 | tf_op jit(solution)/shard_map/ppermute | solution.py:282
  158.3 26.6 %shard_map.116 = (f32[2,18,48,256]{3,2,1,0:T(8,128)}, f32[2,18,48,256]{3,2,1,0:T(8,128)}) custom-call(f32[2,16]{1,0:T(2,128)} %constant.100.clone.refs_0_, f32[16,48,256]{2,1,0:T(8,128)} %get-tuple-element.80.refs_1_, f32[16,48,256]{2,1,0:T(8,128)} %get-tuple-element.81.refs_2_, f32[16,48,256]{2,1,0:T(8,128)} %get-tuple-element.79.refs_3_, ...), custom_call_target="tpu_custom_call" | custom-call | flops 125829120 | bytes 14155776 | tf_op jit(solution)/shard_map/pallas_call | solution.py:191
  184.9 0.9 fusion.7
  185.8 0.7 fusion.14
  (21 shorter events, 0.2 us)
Async XLA Ops:
  0.6 7.1 %collective-permute-start.2 = (f32[8,16,128]{2,1,0:T(8,128)}, f32[8,16,128]{2,1,0:T(8,128)S(1)}, u32[]{:S(2)}, u32[]{:S(2)}) collective-permute-start(f32[8,16,128]{2,1,0:T(8,128)} %param.14), channel_id=1, source_target_pairs={{0,3},{1,2},{2,1},{3,0},{4,7},{5,6},{6,5},{7,4},{8,11},{9,10},{10,... | collective-permute-start | bytes 196616 | tf_op jit(solution)/shard_map/ppermute | solution.py:216
  3.7 4.1 %collective-permute-start.1 = (f32[8,16,128]{2,1,0:T(8,128)}, f32[8,16,128]{2,1,0:T(8,128)S(1)}, u32[]{:S(2)}, u32[]{:S(2)}) collective-permute-start(f32[8,16,128]{2,1,0:T(8,128)} %param.14), channel_id=1, source_target_pairs={{0,1},{1,0},{2,3},{3,2},{4,5},{5,4},{6,7},{7,6},{8,9},{9,8},{10,11... | collective-permute-start | bytes 196616 | tf_op jit(solution)/shard_map/ppermute | solution.py:215
  7.7 3.6 %collective-permute-start = (f32[13,16,128]{2,1,0:T(8,128)S(1)}, f32[13,16,128]{2,1,0:T(8,128)S(1)}, u32[]{:S(2)}, u32[]{:S(2)}) collective-permute-start(f32[13,16,128]{2,1,0:T(8,128)S(1)} %constant_dynamic-update-slice_fusion), channel_id=1, source_target_pairs={{0,2},{2,0},{1,3},{3,1},{4,6},{6,4},{5,7},{7,5},{8,10},{10,8},{9,1... | collective-permute-start | bytes 319496 | tf_op jit(solution)/shard_map/ppermute | solution.py:214
  11.3 10.4 %collective-permute-start.4 = (f32[21,16,256]{2,1,0:T(8,128)S(1)}, f32[21,16,256]{2,1,0:T(8,128)S(1)}, u32[]{:S(2)}, u32[]{:S(2)}) collective-permute-start(f32[21,16,256]{2,1,0:T(8,128)S(1)} %pad_maximum_fusion.1), channel_id=1, source_target_pairs={{4,0},{8,4},{12,8},{16,12},{20,16},{24,20},{28,24},{5,1},{9,5},{13... | collective-permute-start | bytes 1032200 | tf_op jit(solution)/shard_map/ppermute | solution.py:47
  15.6 7.3 %collective-permute-start.3 = (f32[21,16,256]{2,1,0:T(8,128)S(1)}, f32[21,16,256]{2,1,0:T(8,128)S(1)}, u32[]{:S(2)}, u32[]{:S(2)}) collective-permute-start(f32[21,16,256]{2,1,0:T(8,128)S(1)} %pad_maximum_fusion.1), channel_id=1, source_target_pairs={{0,4},{4,8},{8,12},{12,16},{16,20},{20,24},{24,28},{1,5},{5,9},{9,... | collective-permute-start | bytes 1032200 | tf_op jit(solution)/shard_map/ppermute | solution.py:46
  55.3 16.4 %collective-permute-start.5 = (f32[2,2,16,16,256]{4,3,2,1,0:T(8,128)}, f32[2,2,16,16,256]{4,3,2,1,0:T(8,128)S(1)}, u32[]{:S(2)}, u32[]{:S(2)}) collective-permute-start(f32[2,2,16,16,256]{4,3,2,1,0:T(8,128)} %get-tuple-element.38), channel_id=1, source_target_pairs={{0,4},{4,8},{8,12},{12,16},{16,20},{20,24},{24,28},{1,5},{5,9},{9,... | collective-permute-start | bytes 3145736 | tf_op jit(solution)/shard_map/ppermute | solution.py:281
  59.7 16.3 %collective-permute-start.6 = (f32[2,2,16,16,256]{4,3,2,1,0:T(8,128)}, f32[2,2,16,16,256]{4,3,2,1,0:T(8,128)S(1)}, u32[]{:S(2)}, u32[]{:S(2)}) collective-permute-start(f32[2,2,16,16,256]{4,3,2,1,0:T(8,128)} %get-tuple-element.39), channel_id=1, source_target_pairs={{4,0},{8,4},{12,8},{16,12},{20,16},{24,20},{28,24},{5,1},{9,5},{13... | collective-permute-start | bytes 3145736 | tf_op jit(solution)/shard_map/ppermute | solution.py:282
  71.8 4.3 %copy-start = (f32[2,2,16,16,256]{4,3,2,1,0:T(8,128)}, f32[2,2,16,16,256]{4,3,2,1,0:T(8,128)S(1)}, u32[]{:S(2)}) copy-start(f32[2,2,16,16,256]{4,3,2,1,0:T(8,128)S(1)} %collective-permute-done.5.refs_12_) | copy-start | bytes 3145732
  76.1 1.0 copy-start.1
  105.2 5.6 %collective-permute-start.8 = (f32[2,16,256]{2,1,0:T(8,128)S(1)}, f32[2,16,256]{2,1,0:T(8,128)S(1)}, u32[]{:S(2)}, u32[]{:S(2)}) collective-permute-start(f32[2,16,256]{2,1,0:T(8,128)S(1)} %slice_multiply_fusion), channel_id=1, source_target_pairs={{4,0},{8,4},{12,8},{16,12},{20,16},{24,20},{28,24},{5,1},{9,5},{13... | collective-permute-start | bytes 98312 | tf_op jit(solution)/shard_map/ppermute | solution.py:47
  107.1 4.7 %collective-permute-start.7 = (f32[2,16,256]{2,1,0:T(8,128)S(1)}, f32[2,16,256]{2,1,0:T(8,128)S(1)}, u32[]{:S(2)}, u32[]{:S(2)}) collective-permute-start(f32[2,16,256]{2,1,0:T(8,128)S(1)} %slice_multiply_fusion), channel_id=1, source_target_pairs={{0,4},{4,8},{8,12},{12,16},{16,20},{20,24},{24,28},{1,5},{5,9},{9,... | collective-permute-start | bytes 98312 | tf_op jit(solution)/shard_map/ppermute | solution.py:46
  137.6 16.3 %collective-permute-start.9 = (f32[2,2,16,16,256]{4,3,2,1,0:T(8,128)}, f32[2,2,16,16,256]{4,3,2,1,0:T(8,128)}, u32[]{:S(2)}, u32[]{:S(2)}) collective-permute-start(f32[2,2,16,16,256]{4,3,2,1,0:T(8,128)} %get-tuple-element.43), channel_id=1, source_target_pairs={{0,4},{4,8},{8,12},{12,16},{16,20},{20,24},{24,28},{1,5},{5,9},{9,... | collective-permute-start | bytes 3145736 | tf_op jit(solution)/shard_map/ppermute | solution.py:281
  141.9 16.4 %collective-permute-start.10 = (f32[2,2,16,16,256]{4,3,2,1,0:T(8,128)}, f32[2,2,16,16,256]{4,3,2,1,0:T(8,128)}, u32[]{:S(2)}, u32[]{:S(2)}) collective-permute-start(f32[2,2,16,16,256]{4,3,2,1,0:T(8,128)} %get-tuple-element.44), channel_id=1, source_target_pairs={{4,0},{8,4},{12,8},{16,12},{20,16},{24,20},{28,24},{5,1},{9,5},{13... | collective-permute-start | bytes 3145736 | tf_op jit(solution)/shard_map/ppermute | solution.py:282

commit v17 on v16

--- a/solution.py
+++ b/solution.py
@@ -187,12 +187,14 @@
     )
     padded_shape = jax.ShapeDtypeStruct((comps, layers + 2, rows, cols), jnp.float32)
     slab_shape = jax.ShapeDtypeStruct((2, comps, layers, halo, cols), jnp.float32)
-    out_shape = (padded_shape, padded_shape) + ((slab_shape, slab_shape) if send else ())
+    out_shape = (padded_shape, padded_shape, slab_shape, slab_shape) if send else (padded_shape,)
+    scratch = [] if send else [pltpu.VMEM(padded_shape.shape, jnp.float32)]
     return pl.pallas_call(
         lambda *refs: segment_kernel(steps, start_valid, halo, send, len(op_stack), *refs),
         out_shape=out_shape,
         in_specs=[smem] + [vmem] * (len(op_stack) + 1 + len(state)),
         out_specs=tuple(vmem for _ in out_shape),
+        scratch_shapes=scratch,
         cost_estimate=pl.CostEstimate(
             flops=20 * cells * len(steps), bytes_accessed=4 * cells * 9, transcendentals=0
         ),
@@ -286,7 +288,7 @@
                 since = 0
             run.append((keep, push))
             since += 1
-        iterate, _ = run_segment(tuple(run), start_valid, k, False, op_stack, rhs, state)
+        iterate = run_segment(tuple(run), start_valid, k, False, op_stack, rhs, state)[0]
         return iterate[:, 1 : layers + 1]
 
     forcing = jnp.zeros((2,) + eta.shape, jnp.float32)

time: 187 us -> 186 us (level)
  no operation moved by 1% of the time
where the time goes in v17:
time: 186 us; the launch traced here: 185 us
  Pallas kernels  101 us (54%)
  waiting for transfers between devices  36.3 us (20%)
  starting transfers between devices  29.2 us (16%)
  other arithmetic  11.7 us (6%)
  local copies, waits for them, and re-layouts  6.06 us (3%)
    pallas_call x4, Pallas kernels, run_segment(): pl.pallas_call(lambda *refs: segment_kernel(steps, start_valid, halo, sen...  101 us
    ppermute x2, waiting for transfers between devices, chebyshev(): low = lax.ppermute(up, 'mx', forward)  19.1 us
    ppermute x2, waiting for transfers between devices, chebyshev(): high = lax.ppermute(down, 'mx', backward)  8.68 us
    ppermute x2, starting transfers between devices, chebyshev(): low = lax.ppermute(up, 'mx', forward)  8.59 us
    ppermute x2, starting transfers between devices, exchange_rows(): lax.ppermute(lax.slice_in_dim(own, rows - k, rows, axis=axis), 'mx', forw...  6.74 us
    ppermute x2, starting transfers between devices, exchange_rows(): high = lax.ppermute(lax.slice_in_dim(own, 0, k, axis=axis), 'mx', backward)  6.21 us
    ppermute x2, starting transfers between devices, chebyshev(): high = lax.ppermute(down, 'mx', backward)  4.24 us
  transfers between devices with their start and end apart: 11, of which 8 were waited for; matrix products, arithmetic and copies ran while one was open for 2% of the time, Pallas kernels for 0%

profile of v17, /device:TPU:1, one launch (start us, length us, event | category | flops | bytes accessed | tf_op | source)
XLA Modules:
  0.0 185.3 jit_solution(15943511812555267097)
XLA Ops:
  0.6 3.1 %collective-permute-start.2 = (f32[8,16,128]{2,1,0:T(8,128)}, f32[8,16,128]{2,1,0:T(8,128)S(1)}, u32[]{:S(2)}, u32[]{:S(2)}) collective-permute-start(f32[8,16,128]{2,1,0:T(8,128)} %param.14), channel_id=1, source_target_pairs={{0,3},{1,2},{2,1},{3,0},{4,7},{5,6},{6,5},{7,4},{8,11},{9,10},{10,... | collective-permute-start | bytes 196616 | tf_op jit(solution)/shard_map/ppermute | solution.py:218
  3.7 0.3 collective-permute-start.1
  3.9 0.9 constant_dynamic-update-slice_fusion.4
  4.8 0.7 constant_dynamic-update-slice_fusion.3
  5.5 0.7 constant_dynamic-update-slice_fusion.2
  6.2 0.7 constant_dynamic-update-slice_fusion.1
  7.0 0.7 constant_dynamic-update-slice_fusion
  7.7 0.1 collective-permute-start
  7.8 0.0 collective-permute-done.2
  7.8 0.0 collective-permute-done.1
  7.8 3.4 %collective-permute-done = f32[13,16,128]{2,1,0:T(8,128)S(1)} collective-permute-done((f32[13,16,128]{2,1,0:T(8,128)S(1)}, f32[13,16,128]{2,1,0:T(8,128)S(1)}, u32[]{:S(2)}, u32[]{:S(2)}) %collective-permute-start) | collective-permute-done | bytes 106528 | tf_op jit(solution)/shard_map/ppermute | solution.py:216
  11.3 4.3 %collective-permute-start.4 = (f32[21,16,256]{2,1,0:T(8,128)S(1)}, f32[21,16,256]{2,1,0:T(8,128)S(1)}, u32[]{:S(2)}, u32[]{:S(2)}) collective-permute-start(f32[21,16,256]{2,1,0:T(8,128)S(1)} %pad_maximum_fusion.1), channel_id=1, source_target_pairs={{4,0},{8,4},{12,8},{16,12},{20,16},{24,20},{28,24},{5,1},{9,5},{13... | collective-permute-start | bytes 1032200 | tf_op jit(solution)/shard_map/ppermute | solution.py:47
  15.6 3.1 %collective-permute-start.3 = (f32[21,16,256]{2,1,0:T(8,128)S(1)}, f32[21,16,256]{2,1,0:T(8,128)S(1)}, u32[]{:S(2)}, u32[]{:S(2)}) collective-permute-start(f32[21,16,256]{2,1,0:T(8,128)S(1)} %pad_maximum_fusion.1), channel_id=1, source_target_pairs={{0,4},{4,8},{8,12},{12,16},{16,20},{20,24},{24,28},{1,5},{5,9},{9,... | collective-permute-start | bytes 1032200 | tf_op jit(solution)/shard_map/ppermute | solution.py:46
  18.7 3.0 %collective-permute-done.4 = f32[21,16,256]{2,1,0:T(8,128)S(1)} collective-permute-done((f32[21,16,256]{2,1,0:T(8,128)S(1)}, f32[21,16,256]{2,1,0:T(8,128)S(1)}, u32[]{:S(2)}, u32[]{:S(2)}) %collective-permute-start.4) | collective-permute-done | bytes 344096 | tf_op jit(solution)/shard_map/ppermute | solution.py:47
  21.7 1.2 collective-permute-done.3
  23.0 0.1 fusion.20
  23.0 0.1 pad_maximum_fusion
  23.1 0.2 fusion.19
  23.3 0.1 fusion.18
  23.4 0.3 fusion.17
  23.8 0.1 concatenate.90
  23.9 0.2 pad_multiply_fusion
  24.1 1.3 copy.13.refs_9_
  25.4 3.0 %multiply_multiply_fusion = (f32[16,48,256]{2,1,0:T(8,128)}, f32[16,48,256]{2,1,0:T(8,128)S(1)}, f32[16,48,256]{2,1,0:T(8,128)}, f32[16,48,256]{2,1,0:T(8,128)}) fusion(f32[48,256]{1,0:T(8,128)S(1)} %concatenate.94, f32[48,256]{1,0:T(8,128)S(1)} %get-tuple-element.45, f32[16,48,255]{2,1,0:T(8,128)S(1)} %get-tuple-element.60, ...), kind=kLoop, calls=%fused_computation.21 | loop fusion | flops 10027008 | bytes 8710144 | tf_op jit(solution)/shard_map/mul | solution.py:265
  28.4 2.4 %subtract_divide_fusion = (f32[16,48,256]{2,1,0:T(8,128)}, f32[16,48,256]{2,1,0:T(8,128)}, f32[16,48,256]{2,1,0:T(8,128)}, f32[16,48,256]{2,1,0:T(8,128)}, f32[16,48,256]{2,1,0:T(8,128)}) fusion(f32[16,48,256]{2,1,0:T(8,128)S(1)} %fusion.8, f32[48,256]{1,0:T(8,128)S(1)} %get-tuple-element.45, pred[48,256]{1,0:T(8,128)(4,1)S(1)} %broadcast_compare_fusion, ...), kind=kLoop, calls=%fused_computation.23 | loop fusion | flops 5505024 | bytes 7909376 | tf_op jit(solution)/shard_map/div | solution.py:253
  30.8 24.5 %shard_map.113 = (f32[2,18,48,256]{3,2,1,0:T(8,128)}, f32[2,18,48,256]{3,2,1,0:T(8,128)}, f32[2,2,16,16,256]{4,3,2,1,0:T(8,128)}, f32[2,2,16,16,256]{4,3,2,1,0:T(8,128)}) custom-call(f32[2,15]{1,0:T(2,128)} %constant.99.clone.refs_0_, f32[16,48,256]{2,1,0:T(8,128)} %get-tuple-element.76.refs_1_, f32[16,48,256]{2,1,0:T(8,128)} %get-tuple-element.77.refs_2_, ...), custom_call_target="tpu_custom_call" | custom-call | flops 117964800 | bytes 14155776 | tf_op jit(solution)/shard_map/pallas_call | solution.py:192
  55.3 4.4 %collective-permute-start.5 = (f32[2,2,16,16,256]{4,3,2,1,0:T(8,128)}, f32[2,2,16,16,256]{4,3,2,1,0:T(8,128)S(1)}, u32[]{:S(2)}, u32[]{:S(2)}) collective-permute-start(f32[2,2,16,16,256]{4,3,2,1,0:T(8,128)} %get-tuple-element.36), channel_id=1, source_target_pairs={{0,4},{4,8},{8,12},{12,16},{16,20},{20,24},{24,28},{1,5},{5,9},{9,... | collective-permute-start | bytes 3145736 | tf_op jit(solution)/shard_map/ppermute | solution.py:283
  59.7 2.1 %collective-permute-start.6 = (f32[2,2,16,16,256]{4,3,2,1,0:T(8,128)}, f32[2,2,16,16,256]{4,3,2,1,0:T(8,128)S(1)}, u32[]{:S(2)}, u32[]{:S(2)}) collective-permute-start(f32[2,2,16,16,256]{4,3,2,1,0:T(8,128)} %get-tuple-element.37), channel_id=1, source_target_pairs={{4,0},{8,4},{12,8},{16,12},{20,16},{24,20},{28,24},{5,1},{9,5},{13... | collective-permute-start | bytes 3145736 | tf_op jit(solution)/shard_map/ppermute | solution.py:284
  61.8 9.9 %collective-permute-done.5.refs_12_ = f32[2,2,16,16,256]{4,3,2,1,0:T(8,128)S(1)} collective-permute-done((f32[2,2,16,16,256]{4,3,2,1,0:T(8,128)}, f32[2,2,16,16,256]{4,3,2,1,0:T(8,128)S(1)}, u32[]{:S(2)}, u32[]{:S(2)}) %collective-permute-start.5) | collective-permute-done | bytes 1048608 | tf_op jit(solution)/shard_map/ppermute | solution.py:283
  71.7 4.3 %collective-permute-done.6.refs_13_ = f32[2,2,16,16,256]{4,3,2,1,0:T(8,128)S(1)} collective-permute-done((f32[2,2,16,16,256]{4,3,2,1,0:T(8,128)}, f32[2,2,16,16,256]{4,3,2,1,0:T(8,128)S(1)}, u32[]{:S(2)}, u32[]{:S(2)}) %collective-permute-start.6) | collective-permute-done | bytes 1048608 | tf_op jit(solution)/shard_map/ppermute | solution.py:284
  76.0 1.0 copy-done.1
  77.0 26.1 %shard_map.114 = f32[2,18,48,256]{3,2,1,0:T(8,128)} custom-call(f32[2,16]{1,0:T(2,128)} %constant.100.clone.refs_0_, f32[16,48,256]{2,1,0:T(8,128)} %get-tuple-element.76.refs_1_, f32[16,48,256]{2,1,0:T(8,128)} %get-tuple-element.77.refs_2_, f32[16,48,256]{2,1,0:T(8,128)} %get-tuple-element.75.refs_3_, f32[16,48,256]{2,1,0:T(8,128)} %get-tuple-element.51.refs_4_, ...), custom_call_target="tpu_custom_call" | custom-call | flops 125829120 | bytes 14155776 | tf_op jit(solution)/shard_map/pallas_call | solution.py:192
  103.1 1.6 fusion.16
  104.6 1.9 %collective-permute-start.8 = (f32[2,16,256]{2,1,0:T(8,128)S(1)}, f32[2,16,256]{2,1,0:T(8,128)S(1)}, u32[]{:S(2)}, u32[]{:S(2)}) collective-permute-start(f32[2,16,256]{2,1,0:T(8,128)S(1)} %slice_multiply_fusion), channel_id=1, source_target_pairs={{4,0},{8,4},{12,8},{16,12},{20,16},{24,20},{28,24},{5,1},{9,5},{13... | collective-permute-start | bytes 98312 | tf_op jit(solution)/shard_map/ppermute | solution.py:47
  106.6 3.6 %collective-permute-start.7 = (f32[2,16,256]{2,1,0:T(8,128)S(1)}, f32[2,16,256]{2,1,0:T(8,128)S(1)}, u32[]{:S(2)}, u32[]{:S(2)}) collective-permute-start(f32[2,16,256]{2,1,0:T(8,128)S(1)} %slice_multiply_fusion), channel_id=1, source_target_pairs={{0,4},{4,8},{8,12},{12,16},{16,20},{20,24},{24,28},{1,5},{5,9},{9,... | collective-permute-start | bytes 98312 | tf_op jit(solution)/shard_map/ppermute | solution.py:46
  110.2 0.0 collective-permute-done.8
  110.2 1.0 collective-permute-done.7
  111.2 1.3 broadcast_multiply_fusion.refs_9_
  112.6 24.4 %shard_map.115 = (f32[2,18,48,256]{3,2,1,0:T(8,128)}, f32[2,18,48,256]{3,2,1,0:T(8,128)}, f32[2,2,16,16,256]{4,3,2,1,0:T(8,128)}, f32[2,2,16,16,256]{4,3,2,1,0:T(8,128)}) custom-call(f32[2,15]{1,0:T(2,128)} %constant.99.clone.refs_0_, f32[16,48,256]{2,1,0:T(8,128)} %get-tuple-element.76.refs_1_, f32[16,48,256]{2,1,0:T(8,128)} %get-tuple-element.77.refs_2_, ...), custom_call_target="tpu_custom_call" | custom-call | flops 117964800 | bytes 14155776 | tf_op jit(solution)/shard_map/pallas_call | solution.py:192
  136.9 4.2 %collective-permute-start.9 = (f32[2,2,16,16,256]{4,3,2,1,0:T(8,128)}, f32[2,2,16,16,256]{4,3,2,1,0:T(8,128)}, u32[]{:S(2)}, u32[]{:S(2)}) collective-permute-start(f32[2,2,16,16,256]{4,3,2,1,0:T(8,128)} %get-tuple-element.40), channel_id=1, source_target_pairs={{0,4},{4,8},{8,12},{12,16},{16,20},{20,24},{24,28},{1,5},{5,9},{9,... | collective-permute-start | bytes 3145736 | tf_op jit(solution)/shard_map/ppermute | solution.py:283
  141.2 2.1 %collective-permute-start.10 = (f32[2,2,16,16,256]{4,3,2,1,0:T(8,128)}, f32[2,2,16,16,256]{4,3,2,1,0:T(8,128)}, u32[]{:S(2)}, u32[]{:S(2)}) collective-permute-start(f32[2,2,16,16,256]{4,3,2,1,0:T(8,128)} %get-tuple-element.41), channel_id=1, source_target_pairs={{4,0},{8,4},{12,8},{16,12},{20,16},{24,20},{28,24},{5,1},{9,5},{13... | collective-permute-start | bytes 3145736 | tf_op jit(solution)/shard_map/ppermute | solution.py:284
  143.3 0.1 fusion.21
  143.4 0.7 constant_dynamic-slice_fusion
  144.1 9.1 %collective-permute-done.9.refs_12_ = f32[2,2,16,16,256]{4,3,2,1,0:T(8,128)} collective-permute-done((f32[2,2,16,16,256]{4,3,2,1,0:T(8,128)}, f32[2,2,16,16,256]{4,3,2,1,0:T(8,128)}, u32[]{:S(2)}, u32[]{:S(2)}) %collective-permute-start.9) | collective-permute-done | bytes 1048608 | tf_op jit(solution)/shard_map/ppermute | solution.py:283
  153.2 4.4 %collective-permute-done.10.refs_13_ = f32[2,2,16,16,256]{4,3,2,1,0:T(8,128)} collective-permute-done((f32[2,2,16,16,256]{4,3,2,1,0:T(8,128)}, f32[2,2,16,16,256]{4,3,2,1,0:T(8,128)}, u32[]{:S(2)}, u32[]{:S(2)}) %collective-permute-start.10) | collective-permute-done | bytes 1048608 | tf_op jit(solution)/shard_map/ppermute | solution.py:284
  157.6 26.1 %shard_map.116 = f32[2,18,48,256]{3,2,1,0:T(8,128)} custom-call(f32[2,16]{1,0:T(2,128)} %constant.100.clone.refs_0_, f32[16,48,256]{2,1,0:T(8,128)} %get-tuple-element.76.refs_1_, f32[16,48,256]{2,1,0:T(8,128)} %get-tuple-element.77.refs_2_, f32[16,48,256]{2,1,0:T(8,128)} %get-tuple-element.75.refs_3_, f32[16,48,256]{2,1,0:T(8,128)} %get-tuple-element.51.refs_4_, ...), custom_call_target="tpu_custom_call" | custom-call | flops 125829120 | bytes 14155776 | tf_op jit(solution)/shard_map/pallas_call | solution.py:192
  183.7 0.9 fusion.7
  184.6 0.7 fusion.14
  (21 shorter events, 0.2 us)
Async XLA Ops:
  0.6 7.1 %collective-permute-start.2 = (f32[8,16,128]{2,1,0:T(8,128)}, f32[8,16,128]{2,1,0:T(8,128)S(1)}, u32[]{:S(2)}, u32[]{:S(2)}) collective-permute-start(f32[8,16,128]{2,1,0:T(8,128)} %param.14), channel_id=1, source_target_pairs={{0,3},{1,2},{2,1},{3,0},{4,7},{5,6},{6,5},{7,4},{8,11},{9,10},{10,... | collective-permute-start | bytes 196616 | tf_op jit(solution)/shard_map/ppermute | solution.py:218
  3.7 4.1 %collective-permute-start.1 = (f32[8,16,128]{2,1,0:T(8,128)}, f32[8,16,128]{2,1,0:T(8,128)S(1)}, u32[]{:S(2)}, u32[]{:S(2)}) collective-permute-start(f32[8,16,128]{2,1,0:T(8,128)} %param.14), channel_id=1, source_target_pairs={{0,1},{1,0},{2,3},{3,2},{4,5},{5,4},{6,7},{7,6},{8,9},{9,8},{10,11... | collective-permute-start | bytes 196616 | tf_op jit(solution)/shard_map/ppermute | solution.py:217
  7.7 3.6 %collective-permute-start = (f32[13,16,128]{2,1,0:T(8,128)S(1)}, f32[13,16,128]{2,1,0:T(8,128)S(1)}, u32[]{:S(2)}, u32[]{:S(2)}) collective-permute-start(f32[13,16,128]{2,1,0:T(8,128)S(1)} %constant_dynamic-update-slice_fusion), channel_id=1, source_target_pairs={{0,2},{2,0},{1,3},{3,1},{4,6},{6,4},{5,7},{7,5},{8,10},{10,8},{9,1... | collective-permute-start | bytes 319496 | tf_op jit(solution)/shard_map/ppermute | solution.py:216
  11.3 10.4 %collective-permute-start.4 = (f32[21,16,256]{2,1,0:T(8,128)S(1)}, f32[21,16,256]{2,1,0:T(8,128)S(1)}, u32[]{:S(2)}, u32[]{:S(2)}) collective-permute-start(f32[21,16,256]{2,1,0:T(8,128)S(1)} %pad_maximum_fusion.1), channel_id=1, source_target_pairs={{4,0},{8,4},{12,8},{16,12},{20,16},{24,20},{28,24},{5,1},{9,5},{13... | collective-permute-start | bytes 1032200 | tf_op jit(solution)/shard_map/ppermute | solution.py:47
  15.6 7.3 %collective-permute-start.3 = (f32[21,16,256]{2,1,0:T(8,128)S(1)}, f32[21,16,256]{2,1,0:T(8,128)S(1)}, u32[]{:S(2)}, u32[]{:S(2)}) collective-permute-start(f32[21,16,256]{2,1,0:T(8,128)S(1)} %pad_maximum_fusion.1), channel_id=1, source_target_pairs={{0,4},{4,8},{8,12},{12,16},{16,20},{20,24},{24,28},{1,5},{5,9},{9,... | collective-permute-start | bytes 1032200 | tf_op jit(solution)/shard_map/ppermute | solution.py:46
  55.3 16.4 %collective-permute-start.5 = (f32[2,2,16,16,256]{4,3,2,1,0:T(8,128)}, f32[2,2,16,16,256]{4,3,2,1,0:T(8,128)S(1)}, u32[]{:S(2)}, u32[]{:S(2)}) collective-permute-start(f32[2,2,16,16,256]{4,3,2,1,0:T(8,128)} %get-tuple-element.36), channel_id=1, source_target_pairs={{0,4},{4,8},{8,12},{12,16},{16,20},{20,24},{24,28},{1,5},{5,9},{9,... | collective-permute-start | bytes 3145736 | tf_op jit(solution)/shard_map/ppermute | solution.py:283
  59.7 16.3 %collective-permute-start.6 = (f32[2,2,16,16,256]{4,3,2,1,0:T(8,128)}, f32[2,2,16,16,256]{4,3,2,1,0:T(8,128)S(1)}, u32[]{:S(2)}, u32[]{:S(2)}) collective-permute-start(f32[2,2,16,16,256]{4,3,2,1,0:T(8,128)} %get-tuple-element.37), channel_id=1, source_target_pairs={{4,0},{8,4},{12,8},{16,12},{20,16},{24,20},{28,24},{5,1},{9,5},{13... | collective-permute-start | bytes 3145736 | tf_op jit(solution)/shard_map/ppermute | solution.py:284
  71.7 4.3 %copy-start = (f32[2,2,16,16,256]{4,3,2,1,0:T(8,128)}, f32[2,2,16,16,256]{4,3,2,1,0:T(8,128)S(1)}, u32[]{:S(2)}) copy-start(f32[2,2,16,16,256]{4,3,2,1,0:T(8,128)S(1)} %collective-permute-done.5.refs_12_) | copy-start | bytes 3145732
  76.0 1.0 copy-start.1
  104.6 5.6 %collective-permute-start.8 = (f32[2,16,256]{2,1,0:T(8,128)S(1)}, f32[2,16,256]{2,1,0:T(8,128)S(1)}, u32[]{:S(2)}, u32[]{:S(2)}) collective-permute-start(f32[2,16,256]{2,1,0:T(8,128)S(1)} %slice_multiply_fusion), channel_id=1, source_target_pairs={{4,0},{8,4},{12,8},{16,12},{20,16},{24,20},{28,24},{5,1},{9,5},{13... | collective-permute-start | bytes 98312 | tf_op jit(solution)/shard_map/ppermute | solution.py:47
  106.6 4.7 %collective-permute-start.7 = (f32[2,16,256]{2,1,0:T(8,128)S(1)}, f32[2,16,256]{2,1,0:T(8,128)S(1)}, u32[]{:S(2)}, u32[]{:S(2)}) collective-permute-start(f32[2,16,256]{2,1,0:T(8,128)S(1)} %slice_multiply_fusion), channel_id=1, source_target_pairs={{0,4},{4,8},{8,12},{12,16},{16,20},{20,24},{24,28},{1,5},{5,9},{9,... | collective-permute-start | bytes 98312 | tf_op jit(solution)/shard_map/ppermute | solution.py:46
  136.9 16.3 %collective-permute-start.9 = (f32[2,2,16,16,256]{4,3,2,1,0:T(8,128)}, f32[2,2,16,16,256]{4,3,2,1,0:T(8,128)}, u32[]{:S(2)}, u32[]{:S(2)}) collective-permute-start(f32[2,2,16,16,256]{4,3,2,1,0:T(8,128)} %get-tuple-element.40), channel_id=1, source_target_pairs={{0,4},{4,8},{8,12},{12,16},{16,20},{20,24},{24,28},{1,5},{5,9},{9,... | collective-permute-start | bytes 3145736 | tf_op jit(solution)/shard_map/ppermute | solution.py:283
  141.2 16.4 %collective-permute-start.10 = (f32[2,2,16,16,256]{4,3,2,1,0:T(8,128)}, f32[2,2,16,16,256]{4,3,2,1,0:T(8,128)}, u32[]{:S(2)}, u32[]{:S(2)}) collective-permute-start(f32[2,2,16,16,256]{4,3,2,1,0:T(8,128)} %get-tuple-element.41), channel_id=1, source_target_pairs={{4,0},{8,4},{12,8},{16,12},{20,16},{24,20},{28,24},{5,1},{9,5},{13... | collective-permute-start | bytes 3145736 | tf_op jit(solution)/shard_map/ppermute | solution.py:284
